TPU v7x, 32 devices: a whole 2x2x4 slice. The times are simulated.
32 devices in a mesh: group: 2 (over x), span: 16 (over z, y, core).
Axes of the slice: x: 2, y: 2, z: 4, core: 2. Of those that a mesh axis runs over, the one named last changes fastest.
Arguments:
- queries: bfloat16 [8192, 2560], P(('group', 'span')), parts along dimension 0, may hold values from -6 to 6
- keys_values: bfloat16 [2, 8192, 2560], P(None, ('group', 'span')), parts along dimension 1, may hold values from -6 to 6
- owner: int32 [2], P('group'), parts along dimension 0, may hold values from 0 to 15
- span_mask: int32 [32, 3], P('group'), parts along dimension 0, may hold values 0 or 1
- lengths: int32 [32], P('group'), parts along dimension 0, may hold values from 128 to 256, as said below
- frames: bfloat16 [6, 16, 52, 384], P('group', 'span'), parts along dimension 0, may hold values from -6 to 6
- past_frames: bfloat16 [4, 16, 52, 384], P('group', 'span'), parts along dimension 0, may hold values from -5 to 5
- norm_gain: float32 [384], replicated, may hold values from 0.5 to 1.5
- conv_weight: bfloat16 [3, 3, 3, 384, 384], replicated, may hold values from -0.0625 to 0.0625
- conv_bias: float32 [384], replicated, may hold values from -3 to 3
Outputs:
- attended: bfloat16 [8192, 2560], P(('group', 'span')), parts along dimension 0
- decoded: bfloat16 [6, 16, 52, 384], P('group', 'span'), parts along dimension 0
There are 2 independent parts, one for each index of `group`. A program takes and returns all parts, laid end to end along the dimension named above; an argument that names none is the same for every part. Nothing has to cross between parts.
Inputs may be any that keep to these rules, and one draw needn't show every extreme that they name: `lengths`: at least one slot holds exactly 256 tokens.
All inputs are finite; a program needn't handle non-finite values.
Results may differ from a plain program's by a relative error of at most 0.005.
Values may be sent and summed in bfloat16 or wider, within the bound.
No kernel may reach another device: no remote copies, remote signals or barrier semaphores. Data moves between devices by JAX's collectives and lax.ppermute only.
A program may use at most 128 MiB of HBM per device.

v0:
```python
import jax
import jax.numpy as jnp
from jax import lax
from jax.sharding import PartitionSpec as P

H = 20
DH = 128
WIN = 4


def from_behind(value, axis, steps):
    count = lax.axis_size(axis)
    pairs = [(source, (source + steps) % count) for source in range(count)]
    return lax.ppermute(value, axis, pairs)


def spread(block, axis, source):
    block = jnp.where(lax.axis_index(axis) == source, block, jnp.zeros_like(block))
    return lax.psum(block, axis)


def extended_2(block, sides, width):
    for axis, dim in sides:
        count = lax.axis_size(axis)
        forward = [(i, i + 1) for i in range(count - 1)]
        backward = [(target, source) for source, target in forward]
        low = lax.ppermute(
            lax.slice_in_dim(block, block.shape[dim] - width, None, axis=dim), axis, forward
        )
        high = lax.ppermute(lax.slice_in_dim(block, 0, width, axis=dim), axis, backward)
        block = jnp.concatenate([low, block, high], axis=dim)
    return block


def shards(
    queries,
    keys_values,
    owner,
    span_mask,
    lengths,
    frames,
    past_frames,
    norm_gain,
    conv_weight,
    conv_bias,
):
    devices = lax.axis_size("span")
    place = lax.axis_index("span")
    anchor = owner[0]
    position = (place - anchor - 1) % devices
    tok_rows = queries.shape[0]
    row_ids = jnp.arange(tok_rows, dtype=jnp.int32)
    blocks = [keys_values]
    valid_list = [row_ids < lengths[place]]
    for offset in range(1, WIN):
        blocks.append(from_behind(keys_values, "span", offset))
    for offset in range(1, WIN):
        source = (place - offset) % devices
        allowed = (position >= offset) & (span_mask[position, offset - 1] == 1)
        valid_list.append(allowed & (row_ids < lengths[source]))
    blocks.append(spread(keys_values, "span", anchor))
    valid_list.append((place != anchor) & (row_ids < lengths[anchor]))
    gathered = jnp.concatenate(blocks, axis=1)
    key_valid = jnp.concatenate(valid_list)
    score_scale = DH ** (-0.5)
    pieces = []
    for head_block in range(H // 4):
        first_col = head_block * 4 * DH
        last_col = first_col + 4 * DH
        query_group = queries[:, first_col:last_col].reshape(tok_rows, 4, DH)
        key_group = gathered[0, :, first_col:last_col].reshape(-1, 4, DH)
        value_group = gathered[1, :, first_col:last_col].reshape(-1, 4, DH)
        scores = (
            jnp.einsum("qhd,khd->hqk", query_group, key_group, preferred_element_type=jnp.float32)
            * score_scale
        )
        scores = jnp.where(key_valid[None, None, :], scores, -jnp.inf)
        row_max = jnp.max(scores, axis=-1, keepdims=True)
        weights = jnp.exp(scores - row_max)
        probs = (weights / jnp.sum(weights, axis=-1, keepdims=True)).astype(jnp.bfloat16)
        blended = jnp.einsum("hqk,khd->qhd", probs, value_group, preferred_element_type=jnp.float32)
        pieces.append(blended.reshape(tok_rows, 4 * DH))
    attended = jnp.concatenate(pieces, axis=1)
    attended = jnp.where(row_ids[:, None] < lengths[place], attended, 0.0).astype(jnp.bfloat16)
    features = frames.astype(jnp.float32)
    squares = jnp.mean(features * features, axis=-1, keepdims=True)
    normed = features * lax.rsqrt(squares + 1e-06) * norm_gain
    activated = jax.nn.silu(normed).astype(jnp.bfloat16)
    stacked = jnp.concatenate([past_frames, activated], axis=0)
    extended = extended_2(stacked, (("span", 1),), 1)
    padded = jnp.pad(extended, ((0, 0), (0, 0), (1, 1), (0, 0)))
    frame_count = frames.shape[0]
    rows_here = frames.shape[1]
    col_count = frames.shape[2]
    channels = frames.shape[3]
    windows = []
    for frame_tap in range(3):
        for row_tap in range(3):
            for col_tap in range(3):
                windows.append(
                    padded[
                        frame_tap : frame_tap + frame_count,
                        row_tap : row_tap + rows_here,
                        col_tap : col_tap + col_count,
                        :,
                    ]
                )
    columns = jnp.concatenate(windows, axis=-1).reshape(-1, 27 * channels)
    convolved = jnp.dot(
        columns, conv_weight.reshape(27 * channels, channels), preferred_element_type=jnp.float32
    )
    decoded = features + conv_bias + convolved.reshape(frame_count, rows_here, col_count, channels)
    return (attended, decoded.astype(jnp.bfloat16))


def solution(mesh):
    placed = (
        P(("group", "span"), None),
        P(None, ("group", "span"), None),
        P("group"),
        P("group", None),
        P("group"),
        P("group", "span", None, None),
        P("group", "span", None, None),
        P(),
        P(),
        P(),
    )
    return jax.shard_map(
        shards,
        mesh=mesh,
        in_specs=placed,
        out_specs=(P(("group", "span"), None), P("group", "span", None, None)),
        check_vma=False,
    )
```

profile of v0, /device:TPU:0, one launch (start us, length us, event | category | flops | bytes accessed | tf_op | source)
XLA Modules:
  0.0 295.0 jit_solution(9412599492333403696)
XLA Ops:
  7.2 3.0 %copy.34 = bf16[2,256,2560]{1,2,0:T(8,128)(2,1)S(1)} copy(bf16[2,256,2560]{2,1,0:T(8,128)(2,1)} %param.11) | data formatting | bytes 5242880 | tf_op args[1]
  10.3 0.5 collective-permute-start
  10.8 2.6 collective-permute-start.1
  13.3 2.4 collective-permute-start.2
  16.1 0.7 pad_maximum_fusion
  16.8 1.3 collective-permute-start.4
  18.1 3.0 %collective-permute-start.3 = (bf16[5,1,52,384]{3,2,0,1:T(8,128)(2,1)}, bf16[5,1,52,384]{3,2,0,1:T(8,128)(2,1)S(1)}, u32[]{:S(2)}, u32[]{:S(2)}) collective-permute-start(bf16[5,1,52,384]{3,2,0,1:T(8,128)(2,1)} %pad_maximum_fusion), channel_id=1, source_target_pairs={{0,1},{1,2},{2,3},{3,4},{4,5},{5,6},{6,7},{7,8},{8,9},{9,10},{10,1... | collective-permute-start | bytes 599048 | tf_op jit(solution)/shard_map/ppermute | solution.py:27
  21.8 3.3 %broadcast_select_fusion = (bf16[2,256,2560]{1,2,0:T(8,128)(2,1)}, bf16[2,1280,2560]{1,2,0:T(8,128)(2,1)}) fusion(bf16[2,256,2560]{1,2,0:T(8,128)(2,1)S(1)} %copy.34, pred[]{:T(512)S(6)} %eq.26), kind=kLoop, calls=%fused_computation.38 | loop fusion | flops 1310719 | bytes 7864321 | tf_op jit(solution)/shard_map/jit(_where)/select_n | solution.py:18
  25.2 2.4 fusion.101
  27.6 1.8 copy.78
  29.4 0.6 fusion.102
  30.0 0.5 iota_compare_fusion.2
  30.6 0.7 constant_dynamic-slice_fusion
  33.1 1.8 copy.79
  34.9 1.8 copy.80
  36.7 1.8 copy.81
  38.5 1.8 copy.82
  40.3 0.5 compare_and_fusion.2
  40.8 0.6 compare_and_fusion.1
  41.5 0.3 dynamic-update-slice.32
  42.1 0.6 compare_and_fusion
  43.0 0.6 constant_dynamic-update-slice_fusion.11
  45.0 6.0 %fusion.32 = bf16[3,1,52,384]{3,2,1,0:T(8,128)(2,1)} fusion(bf16[10368,384,1]{1,0,2:T(8,128)(2,1)} %bitcast.151, bf16[3,1,52,10368]{3,2,0,1:T(8,128)(2,1)S(1)} %slice_dynamic-update-slice_fusion, bf16[3,1,52,384]{3,2,1,0:T(8,128)(2,1)S(1)} %copy-done, f32[384]{0:T(512)S(1)} %copy-done.8), kind=kOutput, calls=%fused_computation.50 | convolution fusion | flops 1242408960 | bytes 11438592 | tf_op jit(solution)/shard_map/dot_general | solution.py:109
  51.0 41.6 %collective-permute-done = bf16[2,256,2560]{1,2,0:T(8,128)(2,1)} collective-permute-done((bf16[2,256,2560]{1,2,0:T(8,128)(2,1)S(1)}, bf16[2,256,2560]{1,2,0:T(8,128)(2,1)}, u32[]{:S(2)}, u32[]{:S(2)}) %collective-permute-start) | collective-permute-done | bytes 2621472 | tf_op jit(solution)/shard_map/ppermute | solution.py:14
  92.6 3.5 %constant_dynamic-update-slice_fusion.3 = bf16[2,1280,2560]{1,2,0:T(8,128)(2,1)} fusion(bf16[2,1280,2560]{1,2,0:T(8,128)(2,1)} %get-tuple-element.17, bf16[2,256,2560]{1,2,0:T(8,128)(2,1)} %collective-permute-done), kind=kLoop, calls=%fused_computation.103 | loop fusion | bytes 5242880
  96.2 3.6 %constant_dynamic-update-slice_fusion.2 = bf16[2,1280,2560]{1,2,0:T(8,128)(2,1)} fusion(bf16[2,1280,2560]{1,2,0:T(8,128)(2,1)} %constant_dynamic-update-slice_fusion.3, bf16[2,256,2560]{1,2,0:T(8,128)(2,1)} %collective-permute-done.1), kind=kLoop, calls=%fused_computation.102 | loop fusion | bytes 5242880
  99.8 38.6 %collective-permute-done.2 = bf16[2,256,2560]{1,2,0:T(8,128)(2,1)} collective-permute-done((bf16[2,256,2560]{1,2,0:T(8,128)(2,1)S(1)}, bf16[2,256,2560]{1,2,0:T(8,128)(2,1)}, u32[]{:S(2)}, u32[]{:S(2)}) %collective-permute-start.2) | collective-permute-done | bytes 2621472 | tf_op jit(solution)/shard_map/ppermute | solution.py:14
  138.4 3.5 %constant_dynamic-update-slice_fusion.1 = bf16[2,1280,2560]{1,2,0:T(8,128)(2,1)} fusion(bf16[2,1280,2560]{1,2,0:T(8,128)(2,1)} %constant_dynamic-update-slice_fusion.2, bf16[2,256,2560]{1,2,0:T(8,128)(2,1)} %collective-permute-done.2), kind=kLoop, calls=%fused_computation.101 | loop fusion | bytes 5242880
  141.8 86.6 %all-reduce.3.cloned.1.call-done = bf16[2,256,2560]{1,2,0:T(8,128)(2,1)} async-done(((bf16[2,256,2560]{1,2,0:T(8,128)(2,1)}), bf16[2,256,2560]{1,2,0:T(8,128)(2,1)}) %all-reduce.3.cloned.1.call-update) | async-done | bytes 2621456 | tf_op jit(solution)/shard_map/psum | solution.py:19
  228.4 3.5 %constant_dynamic-update-slice_fusion = bf16[2,1280,2560]{1,2,0:T(8,128)(2,1)} fusion(bf16[2,1280,2560]{1,2,0:T(8,128)(2,1)} %constant_dynamic-update-slice_fusion.1, bf16[2,256,2560]{1,2,0:T(8,128)(2,1)} %all-reduce.3.cloned.1.call-done), kind=kLoop, calls=%fused_computation.100 | loop fusion | bytes 5242880 | tf_op jit(solution)/shard_map/concatenate | solution.py:63
  231.9 9.1 %fusion.100 = (bf16[1,1280,512]{1,2,0:T(8,128)(2,1)S(1)}, bf16[1,1280,512]{1,2,0:T(8,128)(2,1)}, bf16[1,1280,512]{1,2,0:T(8,128)(2,1)}, bf16[1,1280,512]{1,2,0:T...) fusion(bf16[2,1280,2560]{1,2,0:T(8,128)(2,1)} %constant_dynamic, ...), kind=kLoop, calls=%fused_computation.140 | loop fusion | bytes 26214400 | tf_op jit(solution)/shard_map/slice | solution.py:71
  241.0 2.0 exponential_reduce_fusion.4
  243.0 4.5 %fusion.17 = bf16[4,128,256]{2,1,0:T(8,128)(2,1)} fusion(bf16[1280,4,128]{0,2,1:T(8,128)(2,1)} %bitcast.166, f32[4,256]{1,0:T(4,128)S(1)} %exponential_reduce_fusion.4, bf16[1280,4,128]{0,2,1:T(8,128)(2,1)S(1)} %bitcast.165, bf16[256,4,128]{0,2,1:T(8,128)(2,1)S(1)} %bitcast.168, pred[1280]{0:T(1024)(128)(4,1)S(1)} %constant_dynamic-update-slice_fusion.11), kind=kOutput, calls=%fused_computation.39 | convolution fusion | flops 677644544 | bytes 3151104 | tf_op jit(solution)/shard_map/hqk,khd->qhd/dot_general | solution.py:81
  247.5 1.1 copy.55
  248.6 3.3 %exponential_reduce_fusion.3 = f32[4,256]{1,0:T(4,128)S(1)} fusion(bf16[1280,4,128]{0,2,1:T(8,128)(2,1)} %bitcast.161, bf16[256,4,128]{0,2,1:T(8,128)(2,1)S(1)} %bitcast.175, pred[1280]{0:T(1024)(128)(4,1)S(1)} %constant_dynamic-update-slice_fusion.11), kind=kOutput, calls=%fused_computation.33 | convolution fusion | flops 340788480 | bytes 1578240 | tf_op jit(solution)/shard_map/sub | solution.py:79
  252.0 4.8 %fusion.18 = bf16[4,128,256]{2,1,0:T(8,128)(2,1)} fusion(bf16[1280,4,128]{0,2,1:T(8,128)(2,1)} %bitcast.163, f32[4,256]{1,0:T(4,128)S(1)} %exponential_reduce_fusion.3, bf16[1280,4,128]{0,2,1:T(8,128)(2,1)} %bitcast.162, bf16[256,4,128]{0,2,1:T(8,128)(2,1)S(1)} %bitcast.176, pred[1280]{0:T(1024)(128)(4,1)S(1)} %constant_dynamic-update-slice_fusion.11), kind=kOutput, calls=%fused_computation.40 | convolution fusion | flops 677644544 | bytes 3151104 | tf_op jit(solution)/shard_map/hqk,khd->qhd/dot_general | solution.py:81
  256.8 1.1 copy.56
  257.9 3.3 %exponential_reduce_fusion.2 = f32[4,256]{1,0:T(4,128)S(1)} fusion(bf16[1280,4,128]{0,2,1:T(8,128)(2,1)} %bitcast.158, bf16[256,4,128]{0,2,1:T(8,128)(2,1)S(1)} %bitcast.173, pred[1280]{0:T(1024)(128)(4,1)S(1)} %constant_dynamic-update-slice_fusion.11), kind=kOutput, calls=%fused_computation.32 | convolution fusion | flops 340788480 | bytes 1578240 | tf_op jit(solution)/shard_map/sub | solution.py:79
  261.2 5.0 %fusion.19 = bf16[4,128,256]{2,1,0:T(8,128)(2,1)} fusion(bf16[1280,4,128]{0,2,1:T(8,128)(2,1)} %bitcast.160, f32[4,256]{1,0:T(4,128)S(1)} %exponential_reduce_fusion.2, bf16[1280,4,128]{0,2,1:T(8,128)(2,1)} %bitcast.159, bf16[256,4,128]{0,2,1:T(8,128)(2,1)S(1)} %bitcast.174, pred[1280]{0:T(1024)(128)(4,1)S(1)} %constant_dynamic-update-slice_fusion.11), kind=kOutput, calls=%fused_computation.41 | convolution fusion | flops 677644544 | bytes 3151104 | tf_op jit(solution)/shard_map/hqk,khd->qhd/dot_general | solution.py:81
  266.3 1.1 copy.57
  267.3 3.3 %exponential_reduce_fusion.1 = f32[4,256]{1,0:T(4,128)S(1)} fusion(bf16[1280,4,128]{0,2,1:T(8,128)(2,1)} %bitcast.155, bf16[256,4,128]{0,2,1:T(8,128)(2,1)} %bitcast.171, pred[1280]{0:T(1024)(128)(4,1)S(1)} %constant_dynamic-update-slice_fusion.11), kind=kOutput, calls=%fused_computation.31 | convolution fusion | flops 340788480 | bytes 1578240 | tf_op jit(solution)/shard_map/sub | solution.py:79
  270.7 4.9 %fusion.20 = bf16[4,128,256]{2,1,0:T(8,128)(2,1)} fusion(bf16[1280,4,128]{0,2,1:T(8,128)(2,1)} %bitcast.157, f32[4,256]{1,0:T(4,128)S(1)} %exponential_reduce_fusion.1, bf16[1280,4,128]{0,2,1:T(8,128)(2,1)} %bitcast.156, bf16[256,4,128]{0,2,1:T(8,128)(2,1)} %bitcast.172, pred[1280]{0:T(1024)(128)(4,1)S(1)} %constant_dynamic-update-slice_fusion.11), kind=kOutput, calls=%fused_computation.42 | convolution fusion | flops 677644544 | bytes 3151104 | tf_op jit(solution)/shard_map/hqk,khd->qhd/dot_general | solution.py:81
  275.5 1.8 copy.58
  277.3 2.9 exponential_reduce_fusion
  280.2 4.5 %fusion.21 = bf16[4,128,256]{2,1,0:T(8,128)(2,1)} fusion(bf16[1280,4,128]{0,2,1:T(8,128)(2,1)} %bitcast.154, f32[4,256]{1,0:T(4,128)S(1)} %exponential_reduce_fusion, bf16[1280,4,128]{0,2,1:T(8,128)(2,1)S(1)} %bitcast.153, bf16[256,4,128]{0,2,1:T(8,128)(2,1)} %bitcast.170, pred[1280]{0:T(1024)(128)(4,1)S(1)} %constant_dynamic-update-slice_fusion.11), kind=kOutput, calls=%fused_computation.43 | convolution fusion | flops 677644544 | bytes 3151104 | tf_op jit(solution)/shard_map/hqk,khd->qhd/dot_general | solution.py:81
  284.7 1.1 copy.59
  285.8 1.0 constant_dynamic-update-slice_fusion.6
  286.8 1.3 select_convert_fusion
  (65 shorter events, 2.3 us)
Async XLA Ops:
  7.2 8.6 %copy-start.5 = (bf16[2,1,52,384]{3,0,2,1:T(2,128)(2,1)S(1)}, bf16[2,1,52,384]{3,0,2,1:T(2,128)(2,1)}, u32[]{:S(2)}) copy-start(bf16[2,1,52,384]{3,0,2,1:T(2,128)(2,1)} %param.16) | copy-start | bytes 239620
  7.2 8.6 %copy-start = (bf16[3,1,52,384]{3,2,1,0:T(8,128)(2,1)S(1)}, bf16[3,1,52,384]{3,2,1,0:T(8,128)(2,1)}, u32[]{:S(2)}) copy-start(bf16[3,1,52,384]{3,2,1,0:T(8,128)(2,1)} %param.15) | copy-start | bytes 359428
  7.2 8.7 %copy-start.7 = (f32[384]{0:T(512)S(1)}, f32[384]{0:T(512)}, u32[]{:S(2)}) copy-start(f32[384]{0:T(512)} %param.17) | copy-start | bytes 4612
  7.2 221.2 %all-reduce.3.cloned.1.call-start = ((), (), s32[]{:S(2)}) async-start(), calls=%async_computation | async-start | bytes 5242880 | tf_op jit(solution)/shard_map/psum | solution.py:19
  10.3 82.4 %collective-permute-start = (bf16[2,256,2560]{1,2,0:T(8,128)(2,1)S(1)}, bf16[2,256,2560]{1,2,0:T(8,128)(2,1)}, u32[]{:S(2)}, u32[]{:S(2)}) collective-permute-start(bf16[2,256,2560]{1,2,0:T(8,128)(2,1)S(1)} %copy.34), channel_id=1, source_target_pairs={{0,1},{1,2},{2,3},{3,4},{4,5},{5,6},{6,7},{7,8},{8,9},{9,10},{10,1... | collective-permute-start | bytes 7864328 | tf_op jit(solution)/shard_map/ppermute | solution.py:14
  10.8 85.4 %collective-permute-start.1 = (bf16[2,256,2560]{1,2,0:T(8,128)(2,1)S(1)}, bf16[2,256,2560]{1,2,0:T(8,128)(2,1)}, u32[]{:S(2)}, u32[]{:S(2)}) collective-permute-start(bf16[2,256,2560]{1,2,0:T(8,128)(2,1)S(1)} %copy.34), channel_id=1, source_target_pairs={{0,2},{1,3},{2,4},{3,5},{4,6},{5,7},{6,8},{7,9},{8,10},{9,11},{10,... | collective-permute-start | bytes 7864328 | tf_op jit(solution)/shard_map/ppermute | solution.py:14
  13.3 125.0 %collective-permute-start.2 = (bf16[2,256,2560]{1,2,0:T(8,128)(2,1)S(1)}, bf16[2,256,2560]{1,2,0:T(8,128)(2,1)}, u32[]{:S(2)}, u32[]{:S(2)}) collective-permute-start(bf16[2,256,2560]{1,2,0:T(8,128)(2,1)S(1)} %copy.34), channel_id=1, source_target_pairs={{0,3},{1,4},{2,5},{3,6},{4,7},{5,8},{6,9},{7,10},{8,11},{9,12},{10... | collective-permute-start | bytes 7864328 | tf_op jit(solution)/shard_map/ppermute | solution.py:14
  16.8 26.8 %collective-permute-start.4 = (bf16[5,1,52,384]{3,2,0,1:T(8,128)(2,1)}, bf16[5,1,52,384]{3,2,0,1:T(8,128)(2,1)S(1)}, u32[]{:S(2)}, u32[]{:S(2)}) collective-permute-start(bf16[5,1,52,384]{3,2,0,1:T(8,128)(2,1)} %pad_maximum_fusion), channel_id=1, source_target_pairs={{1,0},{2,1},{3,2},{4,3},{5,4},{6,5},{7,6},{8,7},{9,8},{10,9},{11,1... | collective-permute-start | bytes 599048 | tf_op jit(solution)/shard_map/ppermute | solution.py:30
  18.1 25.5 %collective-permute-start.3 = (bf16[5,1,52,384]{3,2,0,1:T(8,128)(2,1)}, bf16[5,1,52,384]{3,2,0,1:T(8,128)(2,1)S(1)}, u32[]{:S(2)}, u32[]{:S(2)}) collective-permute-start(bf16[5,1,52,384]{3,2,0,1:T(8,128)(2,1)} %pad_maximum_fusion), channel_id=1, source_target_pairs={{0,1},{1,2},{2,3},{3,4},{4,5},{5,6},{6,7},{7,8},{8,9},{9,10},{10,1... | collective-permute-start | bytes 599048 | tf_op jit(solution)/shard_map/ppermute | solution.py:27
  25.1 4.3 %copy-start.6 = (s32[16]{0:T(128)S(1)}, s32[16]{0:T(128)}, u32[]{:S(2)}) copy-start(s32[16]{0:T(128)} %param.14) | copy-start | bytes 196
  25.1 5.5 %copy-start.9 = (s32[16,3]{0,1:T(4,128)S(1)}, s32[16,3]{0,1:T(4,128)}, u32[]{:S(2)}) copy-start(s32[16,3]{0,1:T(4,128)} %param.13) | copy-start | bytes 580
  43.9 1.1 copy-start.8
  231.9 9.1 %copy-start.1 = (bf16[256,512]{0,1:T(8,128)(2,1)S(1)}, bf16[256,512]{0,1:T(8,128)(2,1)}, u32[]{:S(2)}) copy-start(bf16[256,512]{0,1:T(8,128)(2,1)} %copy.78) | copy-start | bytes 786436
  243.0 5.6 %copy-start.3 = (bf16[256,512]{0,1:T(8,128)(2,1)S(1)}, bf16[256,512]{0,1:T(8,128)(2,1)}, u32[]{:S(2)}) copy-start(bf16[256,512]{0,1:T(8,128)(2,1)} %copy.79) | copy-start | bytes 786436
  248.6 3.3 %copy-start.4 = (bf16[256,512]{0,1:T(8,128)(2,1)S(1)}, bf16[256,512]{0,1:T(8,128)(2,1)}, u32[]{:S(2)}) copy-start(bf16[256,512]{0,1:T(8,128)(2,1)} %copy.79) | copy-start | bytes 786436
  252.0 6.0 %copy-start.2 = (bf16[256,512]{0,1:T(8,128)(2,1)S(1)}, bf16[256,512]{0,1:T(8,128)(2,1)}, u32[]{:S(2)}) copy-start(bf16[256,512]{0,1:T(8,128)(2,1)} %copy.80) | copy-start | bytes 786436
Sparse Core Ops, SparseCore 0:
  25.2 203.1 all-reduce.2
where the time goes:
time: 296 us; the launch traced here: 295 us
  waiting for transfers between devices  167 us (56%)
  local copies, waits for them, and re-layouts  47.7 us (16%)
  matrix products  44.5 us (15%)
  between operations  17.1 us (6%)
  starting transfers between devices  9.86 us (3%)
  other arithmetic  9.04 us (3%)
    psum x1, waiting for transfers between devices, spread(): return lax.psum(block, axis)  86.6 us
    ppermute x3, waiting for transfers between devices, from_behind(): return lax.ppermute(value, axis, pairs)  80.2 us
    unnamed x61, local copies, waits for them, and re-layouts  25.3 us
    dot_general x5, matrix products, shards(): jnp.einsum('hqk,khd->qhd', probs, value_group, preferred_element_type=jnp...  23.7 us
    sub x5, matrix products, shards(): weights = jnp.exp(scores - row_max)  14.8 us
    slice x1, local copies, waits for them, and re-layouts, shards(): key_group = gathered[0, :, first_col:last_col].reshape(-1, 4, DH)  9.06 us
    reshape x5, local copies, waits for them, and re-layouts, shards(): pieces.append(blended.reshape(tok_rows, 4 * DH))  6.15 us
    dot_general x1, matrix products, shards(): jnp.dot(columns, conv_weight.reshape(27 * channels, channels), preferred_...  5.99 us
  transfers between devices with their start and end apart: 6, of which 3 were waited for; matrix products, arithmetic and copies ran while one was open for 13% of the time, Pallas kernels for 0%

commit v1 on v0

--- a/solution.py
+++ b/solution.py
@@ -6,12 +6,6 @@
 H = 20
 DH = 128
 WIN = 4
-
-
-def from_behind(value, axis, steps):
-    count = lax.axis_size(axis)
-    pairs = [(source, (source + steps) % count) for source in range(count)]
-    return lax.ppermute(value, axis, pairs)
 
 
 def spread(block, axis, source):
@@ -32,6 +26,45 @@
     return block
 
 
+def move(value, pairs):
+    return lax.ppermute(value, "span", pairs)
+
+
+def window_blocks(kv, devices):
+    rows = devices // 4
+    lane = lax.axis_index("span") % 4
+
+    def at(r, l):
+        return 4 * (r % rows) + l
+
+    rng = range(rows)
+    rail1 = move(kv, [(at(r, 3), at(r + 1, 2)) for r in rng])
+    rail0 = move(kv, [(at(r, 1), at(r + 1, 0)) for r in rng])
+    y_up = move(kv, [(at(r, 0), at(r, 2)) for r in rng] + [(at(r, 1), at(r, 3)) for r in rng])
+    y_down = move(kv, [(at(r, 2), at(r, 1)) for r in rng])
+    chip = move(kv, [(at(r, 0), at(r, 1)) for r in rng] + [(at(r, 2), at(r, 3)) for r in rng])
+    swap = move(y_up, [(at(r, 3), at(r, 2)) for r in rng] + [(at(r, 2), at(r, 3)) for r in rng])
+    down2 = move(rail1, [(at(r, 2), at(r, 0)) for r in rng])
+    rail0b = move(y_down, [(at(r, 1), at(r + 1, 0)) for r in rng])
+    pair = move(jnp.stack([down2, rail0b]), [(at(r, 0), at(r, 1)) for r in rng])
+
+    def pick(*options):
+        out = options[0]
+        for l in range(1, 4):
+            out = jnp.where(lane == l, options[l], out)
+        return out
+
+    b1 = pick(down2, chip, swap, chip)
+    b2 = pick(rail0b, pair[0], y_up, y_up)
+    b3 = pick(rail0, pair[1], rail1, swap)
+    return b1, b2, b3
+
+
+def part_stats(q, k, valid, scale):
+    scores = jnp.einsum("qhd,khd->hqk", q, k, preferred_element_type=jnp.float32) * scale
+    return jnp.where(valid[None, None, :], scores, -jnp.inf)
+
+
 def shards(
     queries,
     keys_values,
@@ -50,36 +83,41 @@
     position = (place - anchor - 1) % devices
     tok_rows = queries.shape[0]
     row_ids = jnp.arange(tok_rows, dtype=jnp.int32)
-    blocks = [keys_values]
+    anchor_kv = spread(keys_values, "span", anchor)
+    b1, b2, b3 = window_blocks(keys_values, devices)
+    blocks = [keys_values, b1, b2, b3]
     valid_list = [row_ids < lengths[place]]
-    for offset in range(1, WIN):
-        blocks.append(from_behind(keys_values, "span", offset))
     for offset in range(1, WIN):
         source = (place - offset) % devices
         allowed = (position >= offset) & (span_mask[position, offset - 1] == 1)
         valid_list.append(allowed & (row_ids < lengths[source]))
-    blocks.append(spread(keys_values, "span", anchor))
-    valid_list.append((place != anchor) & (row_ids < lengths[anchor]))
-    gathered = jnp.concatenate(blocks, axis=1)
-    key_valid = jnp.concatenate(valid_list)
+    anchor_valid = (place != anchor) & (row_ids < lengths[anchor])
+    window_kv = jnp.concatenate(blocks, axis=1)
+    window_valid = jnp.concatenate(valid_list)
     score_scale = DH ** (-0.5)
     pieces = []
     for head_block in range(H // 4):
         first_col = head_block * 4 * DH
         last_col = first_col + 4 * DH
-        query_group = queries[:, first_col:last_col].reshape(tok_rows, 4, DH)
-        key_group = gathered[0, :, first_col:last_col].reshape(-1, 4, DH)
-        value_group = gathered[1, :, first_col:last_col].reshape(-1, 4, DH)
-        scores = (
-            jnp.einsum("qhd,khd->hqk", query_group, key_group, preferred_element_type=jnp.float32)
-            * score_scale
+        q = queries[:, first_col:last_col].reshape(tok_rows, 4, DH)
+        wk = window_kv[0, :, first_col:last_col].reshape(-1, 4, DH)
+        wv = window_kv[1, :, first_col:last_col].reshape(-1, 4, DH)
+        ak = anchor_kv[0, :, first_col:last_col].reshape(-1, 4, DH)
+        av = anchor_kv[1, :, first_col:last_col].reshape(-1, 4, DH)
+        ws = part_stats(q, wk, window_valid, score_scale)
+        a_s = part_stats(q, ak, anchor_valid, score_scale)
+        top = jnp.maximum(
+            jnp.max(ws, axis=-1, keepdims=True), jnp.max(a_s, axis=-1, keepdims=True)
         )
-        scores = jnp.where(key_valid[None, None, :], scores, -jnp.inf)
-        row_max = jnp.max(scores, axis=-1, keepdims=True)
-        weights = jnp.exp(scores - row_max)
-        probs = (weights / jnp.sum(weights, axis=-1, keepdims=True)).astype(jnp.bfloat16)
-        blended = jnp.einsum("hqk,khd->qhd", probs, value_group, preferred_element_type=jnp.float32)
-        pieces.append(blended.reshape(tok_rows, 4 * DH))
+        w_exp = jnp.exp(ws - top)
+        a_exp = jnp.exp(a_s - top)
+        total = jnp.sum(w_exp, axis=-1, keepdims=True) + jnp.sum(a_exp, axis=-1, keepdims=True)
+        w_probs = (w_exp / total).astype(jnp.bfloat16)
+        a_probs = (a_exp / total).astype(jnp.bfloat16)
+        blended = jnp.einsum(
+            "hqk,khd->hqd", w_probs, wv, preferred_element_type=jnp.float32
+        ) + jnp.einsum("hqk,khd->hqd", a_probs, av, preferred_element_type=jnp.float32)
+        pieces.append(jnp.transpose(blended, (1, 0, 2)).reshape(tok_rows, 4 * DH))
     attended = jnp.concatenate(pieces, axis=1)
     attended = jnp.where(row_ids[:, None] < lengths[place], attended, 0.0).astype(jnp.bfloat16)
     features = frames.astype(jnp.float32)

time: 296 us -> 257 us (0.87)
  waiting for transfers between devices: 167 us -> 105 us
  starting transfers between devices: 9.86 us -> 40.9 us
  other arithmetic: 9.04 us -> 28 us
  local copies, waits for them, and re-layouts: 47.7 us -> 33.5 us
  matrix products: 44.5 us -> 31.5 us
    psum x1, waiting for transfers between devices: 86.6 us -> 49.8 us  [spread(): return lax.psum(block, axis)]
    ppermute x3 -> x9, starting transfers between devices: 5.5 us -> 35.9 us  [move(): return lax.ppermute(value, 'span', pairs)]
    ppermute x3 -> x9, waiting for transfers between devices: 80.2 us -> 55.3 us  [move(): return lax.ppermute(value, 'span', pairs)]
    sub x5 -> x0, matrix products: 14.8 us -> none  [shards(): weights = jnp.exp(scores - row_max)]
    reduce_sum x0 -> x6, other arithmetic: none -> 7.25 us  [the longest x1 6.44 us: shards(): jnp.sum(w_exp, axis=-1, keepdims=True)]
    select_n x0 -> x1, other arithmetic: none -> 6.41 us  [pick(): out = jnp.where(lane == l, options[l], out)]
    unnamed x61 -> x106, local copies, waits for them, and re-layouts: 25.3 us -> 19.8 us
    dot_general x5 -> x20, matrix products: 23.7 us -> 28.8 us  [the longest x10 15 us: part_stats(): jnp.einsum('qhd,khd->hqk', q, k, preferred_element_type=jnp.float32) * scale]
  transfers between devices with their start and end apart: 6 -> 12, of which waited for: 3 -> 3; matrix products, arithmetic and copies ran while one was open for 13% -> 15% of each run, Pallas kernels for 0% -> 0%
where the time goes in v1:
time: 257 us
  waiting for transfers between devices  105 us (41%)
  starting transfers between devices  40.9 us (16%)
  local copies, waits for them, and re-layouts  33.5 us (13%)
  matrix products  31.5 us (12%)
  other arithmetic  28 us (11%)
  between operations  17.5 us (7%)
    ppermute x9, waiting for transfers between devices, move(): return lax.ppermute(value, 'span', pairs)  55.3 us
    psum x1, waiting for transfers between devices, spread(): return lax.psum(block, axis)  49.8 us
    ppermute x9, starting transfers between devices, move(): return lax.ppermute(value, 'span', pairs)  35.9 us
    unnamed x106, local copies, waits for them, and re-layouts  19.8 us
    dot_general x10, matrix products, part_stats(): jnp.einsum('qhd,khd->hqk', q, k, preferred_element_type=jnp.float32) * scale  15 us
    dot_general x5, matrix products, shards(): jnp.einsum('hqk,khd->hqd', w_probs, wv, preferred_element_type=jnp.float32)  8.75 us
    reduce_sum x1, other arithmetic, shards(): jnp.sum(w_exp, axis=-1, keepdims=True)  6.44 us
    select_n x1, other arithmetic, pick(): out = jnp.where(lane == l, options[l], out)  6.41 us
  transfers between devices with their start and end apart: 12, of which 3 were waited for; matrix products, arithmetic and copies ran while one was open for 15% of the time, Pallas kernels for 0%

profile of v1, /device:TPU:0, one launch (start us, length us, event | category | flops | bytes accessed | tf_op | source)
XLA Modules:
  0.0 256.6 jit_solution(3849628814859727125)
XLA Ops:
  7.2 3.0 %copy.45 = bf16[2,256,2560]{1,2,0:T(8,128)(2,1)S(1)} copy(bf16[2,256,2560]{2,1,0:T(8,128)(2,1)} %param.11) | data formatting | bytes 5242880 | tf_op args[1]
  10.3 2.2 collective-permute-start.3
  12.4 2.2 collective-permute-start.5
  15.7 1.3 collective-permute-start.10
  17.0 3.7 %collective-permute-start.9 = (bf16[5,1,52,384]{3,2,0,1:T(8,128)(2,1)}, bf16[5,1,52,384]{3,2,0,1:T(8,128)(2,1)}, u32[]{:S(2)}, u32[]{:S(2)}) collective-permute-start(bf16[5,1,52,384]{3,2,0,1:T(8,128)(2,1)} %pad_maximum_fusion.2), channel_id=1, source_target_pairs={{0,1},{1,2},{2,3},{3,4},{4,5},{5,6},{6,7},{7,8},{8,9},{9,10},{10,1... | collective-permute-start | bytes 599048 | tf_op jit(solution)/shard_map/ppermute | solution.py:21
  20.8 8.1 %collective-permute-start.1 = (bf16[2,256,2560]{1,2,0:T(8,128)(2,1)S(1)}, bf16[2,256,2560]{1,2,0:T(8,128)(2,1)}, u32[]{:S(2)}, u32[]{:S(2)}) collective-permute-start(bf16[2,256,2560]{1,2,0:T(8,128)(2,1)S(1)} %copy.45), channel_id=1, source_target_pairs={{0,2},{4,6},{8,10},{12,14},{1,3},{5,7},{9,11},{13,15},{16,18},{20,... | collective-permute-start | bytes 7864328 | tf_op jit(solution)/shard_map/ppermute | solution.py:30
  29.6 1.7 broadcast_select_fusion
  31.4 2.2 fusion.86
  36.3 1.1 copy.124
  38.2 1.1 copy.123
  39.3 1.8 copy.121
  43.0 1.3 compare_and_fusion.1
  45.0 11.7 %collective-permute-start = (bf16[2,256,2560]{1,2,0:T(8,128)(2,1)S(1)}, bf16[2,256,2560]{1,2,0:T(8,128)(2,1)}, u32[]{:S(2)}, u32[]{:S(2)}) collective-permute-start(bf16[2,256,2560]{1,2,0:T(8,128)(2,1)S(1)} %copy.45), channel_id=1, source_target_pairs={{0,1},{4,5},{8,9},{12,13},{2,3},{6,7},{10,11},{14,15},{16,17},{20,... | collective-permute-start | bytes 7864328 | tf_op jit(solution)/shard_map/ppermute | solution.py:30
  56.7 1.3 collective-permute-start.8
  58.0 1.3 select_maximum_fusion
  59.3 1.3 collective-permute-start.4
  60.6 1.3 collective-permute-start.6
  66.0 27.1 %collective-permute-done.4 = bf16[2,256,2560]{1,2,0:T(8,128)(2,1)S(1)} collective-permute-done((bf16[2,256,2560]{1,2,0:T(8,128)(2,1)}, bf16[2,256,2560]{1,2,0:T(8,128)(2,1)S(1)}, u32[]{:S(2)}, u32[]{:S(2)}) %collective-permute-start.4) | collective-permute-done | bytes 2621472 | tf_op jit(solution)/shard_map/ppermute | solution.py:30
  93.1 28.2 %collective-permute-done.6 = bf16[2,256,2560]{1,2,0:T(8,128)(2,1)S(1)} collective-permute-done((bf16[2,256,2560]{1,2,0:T(8,128)(2,1)}, bf16[2,256,2560]{1,2,0:T(8,128)(2,1)S(1)}, u32[]{:S(2)}, u32[]{:S(2)}) %collective-permute-start.6) | collective-permute-done | bytes 2621472 | tf_op jit(solution)/shard_map/ppermute | solution.py:30
  121.4 3.1 %pad_maximum_fusion.1 = bf16[2,2,256,2560]{2,3,1,0:T(8,128)(2,1)} fusion(bf16[1,2,256,2560]{2,3,1,0:T(8,128)(2,1)S(1)} %bitcast.206, bf16[1,2,256,2560]{2,3,1,0:T(8,128)(2,1)S(1)} %bitcast.205), kind=kLoop, calls=%fused_computation.1 | loop fusion | flops 2621440 | bytes 10485760 | tf_op jit(solution)/shard_map/stack | solution.py:49
  125.3 5.5 %collective-permute-start.7 = (bf16[2,2,256,2560]{2,3,1,0:T(8,128)(2,1)}, bf16[2,2,256,2560]{2,3,1,0:T(8,128)(2,1)}, u32[]{:S(2)}, u32[]{:S(2)}) collective-permute-start(bf16[2,2,256,2560]{2,3,1,0:T(8,128)(2,1)} %pad_maximum_fusion.1), channel_id=1, source_target_pairs={{0,1},{4,5},{8,9},{12,13},{16,17},{20,21},{24,25},{28,29}} | collective-permute-start | bytes 15728648 | tf_op jit(solution)/shard_map/ppermute | solution.py:30
  133.2 2.2 collective-permute-start.2
  136.5 2.8 %fusion.46 = bf16[3,1,52,384]{3,2,1,0:T(8,128)(2,1)} fusion(bf16[10368,384,1]{1,0,2:T(8,128)(2,1)S(1)} %bitcast.204, bf16[3,1,52,10368]{3,2,0,1:T(8,128)(2,1)S(1)} %slice_dynamic-update-slice_fusion, bf16[3,1,52,384]{3,2,1,0:T(8,128)(2,1)S(1)} %copy-done.19, f32[384]{0:T(512)S(1)} %copy-done.30), kind=kOutput, calls=%fused_computation.75 | convolution fusion | flops 1242408960 | bytes 11438592 | tf_op jit(solution)/shard_map/dot_general | solution.py:147
  139.3 49.8 %all-reduce.3.cloned.1.call-done = bf16[2,256,2560]{1,2,0:T(8,128)(2,1)} async-done(((bf16[2,256,2560]{1,2,0:T(8,128)(2,1)}), bf16[2,256,2560]{1,2,0:T(8,128)(2,1)}) %all-reduce.3.cloned.1.call-update) | async-done | bytes 2621456 | tf_op jit(solution)/shard_map/psum | solution.py:13
  189.1 2.8 %fusion.85 = (bf16[1,256,512]{1,2,0:T(8,128)(2,1)S(1)}, bf16[1,256,512]{1,2,0:T(8,128)(2,1)S(1)}, bf16[1,256,512]{1,2,0:T(8,128)(2,1)}, bf16[1,256,512]{1,2,0:T(...) fusion(bf16[2,256,2560]{1,2,0:T(8,128)(2,1)} %all-reduce.3.clon, ...), kind=kLoop, calls=%fused_computation.172 | loop fusion | bytes 5242880 | tf_op jit(solution)/shard_map/slice | solution.py:106
  191.8 1.3 fusion.89
  193.5 1.4 fusion.90
  194.9 1.4 fusion.92
  196.3 1.4 fusion.91
  197.7 6.4 %select_select_fusion = (bf16[2,256,2560]{1,2,0:T(8,128)(2,1)S(1)}, bf16[2,256,2560]{1,2,0:T(8,128)(2,1)S(1)}, bf16[2,256,2560]{1,2,0:T(8,128)(2,1)S(1)}) fusion(bf16[2,256,2560]{1,2,0:T(8,128)(2,1)} %collective-permute-done.1, bf16[2,256,2560]{1,2,0:T(8,128)(2,1)S(1)} %copy-done.9, bf16[2,2,256,2560]{2,3,1,0:T(8,128)(2,1)} %collective-permute-done.7, ...), kind=kLoop, calls=%fused_computation.27 | loop fusion | flops 11796480 | bytes 31457284 | tf_op jit(solution)/shard_map/jit(_where)/select_n | solution.py:54
  204.1 1.5 pad_maximum_fusion
  205.6 2.3 fusion.84
  210.2 1.8 bitcast_reduce_fusion
  213.1 5.2 %fusion.11 = (f32[4,256]{1,0:T(4,128)S(1)}, f32[4,256]{1,0:T(4,128)S(1)}, f32[4,256]{1,0:T(4,128)S(1)}, f32[4,256]{1,0:T(4,128)S(1)}, f32[4,256]{1,0:T(4,128)S(1)}, /*index=5*/f32[4,1024,256]{2,1,0:T(8,128)}) fusion(f32[4,1024,256]{2,1,0:T(8,128)S(1)} %get-tuple-element.52, f32[4,256]{1,0:T(4,128)S(1)} %max.44, pred[1024]{0:T(1024)(128)(4,1)S(1)} %pad_add_fusion, ...), kind=kOutput, calls=%fused_computation.34 | convolution fusion | flops 286256128 | bytes 22311936 | tf_op jit(solution)/shard_map/qhd,khd->hqk/dot_general | solution.py:64
  218.6 1.3 fusion.32
  220.3 6.4 %fusion.10 = (f32[4,256]{1,0:T(4,128)S(1)}, f32[4,256]{1,0:T(4,128)S(1)}, f32[4,256]{1,0:T(4,128)S(1)}) fusion(f32[4,1024,256]{2,1,0:T(8,128)} %copy-done.4, f32[4,256]{1,0:T(4,128)S(1)} %max.43, pred[1024]{0:T(1024)(128)(4,1)S(1)} %pad_add_fusion, f32[4,256]{1,0:T(4,128)S(1)} %max.41, f32[4,1024,256]{2,1,0:T(8,128)} %get-tuple-element.57, ...), kind=kLoop, calls=%fused_computation.33 | loop fusion | flops 12579840 | bytes 12608512 | tf_op jit(solution)/shard_map/reduce_sum | solution.py:114
  227.2 1.8 copy-done.5
  229.0 2.0 fusion.33
  231.0 1.9 copy.85
  233.1 1.4 fusion.59
  235.2 2.1 fusion.34
  237.2 1.9 copy.84
  239.3 1.4 fusion.58
  241.4 2.0 fusion.35
  243.4 1.1 copy.83
  244.7 1.4 fusion.57
  246.8 1.3 fusion.36
  248.4 1.3 select_convert_fusion
  (151 shorter events, 20.9 us)
Async XLA Ops:
  7.2 7.5 %copy-start.18 = (bf16[3,1,52,384]{3,2,1,0:T(8,128)(2,1)S(1)}, bf16[3,1,52,384]{3,2,1,0:T(8,128)(2,1)}, u32[]{:S(2)}) copy-start(bf16[3,1,52,384]{3,2,1,0:T(8,128)(2,1)} %param.15) | copy-start | bytes 359428
  7.2 7.6 %copy-start.27 = (bf16[2,1,52,384]{3,0,2,1:T(2,128)(2,1)S(1)}, bf16[2,1,52,384]{3,0,2,1:T(2,128)(2,1)}, u32[]{:S(2)}) copy-start(bf16[2,1,52,384]{3,0,2,1:T(2,128)(2,1)} %param.16) | copy-start | bytes 239620
  7.2 7.7 %copy-start.29 = (f32[384]{0:T(512)S(1)}, f32[384]{0:T(512)}, u32[]{:S(2)}) copy-start(f32[384]{0:T(512)} %param.17) | copy-start | bytes 4612
  7.2 181.9 %all-reduce.3.cloned.1.call-start = ((), (), s32[]{:S(2)}) async-start(), calls=%async_computation | async-start | bytes 5242880 | tf_op jit(solution)/shard_map/psum | solution.py:13
  10.3 49.1 %collective-permute-start.3 = (bf16[2,256,2560]{1,2,0:T(8,128)(2,1)S(1)}, bf16[2,256,2560]{1,2,0:T(8,128)(2,1)}, u32[]{:S(2)}, u32[]{:S(2)}) collective-permute-start(bf16[2,256,2560]{1,2,0:T(8,128)(2,1)S(1)} %copy.45), channel_id=1, source_target_pairs={{3,6},{7,10},{11,14},{15,2},{19,22},{23,26},{27,30},{31,18}} | collective-permute-start | bytes 7864328 | tf_op jit(solution)/shard_map/ppermute | solution.py:30
  12.4 48.2 %collective-permute-start.5 = (bf16[2,256,2560]{1,2,0:T(8,128)(2,1)S(1)}, bf16[2,256,2560]{1,2,0:T(8,128)(2,1)}, u32[]{:S(2)}, u32[]{:S(2)}) collective-permute-start(bf16[2,256,2560]{1,2,0:T(8,128)(2,1)S(1)} %copy.45), channel_id=1, source_target_pairs={{2,1},{6,5},{10,9},{14,13},{18,17},{22,21},{26,25},{30,29}} | collective-permute-start | bytes 7864328 | tf_op jit(solution)/shard_map/ppermute | solution.py:30
  14.8 2.2 copy-start.16
  15.7 29.2 %collective-permute-start.10 = (bf16[5,1,52,384]{3,2,0,1:T(8,128)(2,1)}, bf16[5,1,52,384]{3,2,0,1:T(8,128)(2,1)}, u32[]{:S(2)}, u32[]{:S(2)}) collective-permute-start(bf16[5,1,52,384]{3,2,0,1:T(8,128)(2,1)} %pad_maximum_fusion.2), channel_id=1, source_target_pairs={{1,0},{2,1},{3,2},{4,3},{5,4},{6,5},{7,6},{8,7},{9,8},{10,9},{11,1... | collective-permute-start | bytes 599048 | tf_op jit(solution)/shard_map/ppermute | solution.py:24
  17.0 39.6 %collective-permute-start.9 = (bf16[5,1,52,384]{3,2,0,1:T(8,128)(2,1)}, bf16[5,1,52,384]{3,2,0,1:T(8,128)(2,1)}, u32[]{:S(2)}, u32[]{:S(2)}) collective-permute-start(bf16[5,1,52,384]{3,2,0,1:T(8,128)(2,1)} %pad_maximum_fusion.2), channel_id=1, source_target_pairs={{0,1},{1,2},{2,3},{3,4},{4,5},{5,6},{6,7},{7,8},{8,9},{9,10},{10,1... | collective-permute-start | bytes 599048 | tf_op jit(solution)/shard_map/ppermute | solution.py:21
  20.8 112.4 %collective-permute-start.1 = (bf16[2,256,2560]{1,2,0:T(8,128)(2,1)S(1)}, bf16[2,256,2560]{1,2,0:T(8,128)(2,1)}, u32[]{:S(2)}, u32[]{:S(2)}) collective-permute-start(bf16[2,256,2560]{1,2,0:T(8,128)(2,1)S(1)} %copy.45), channel_id=1, source_target_pairs={{0,2},{4,6},{8,10},{12,14},{1,3},{5,7},{9,11},{13,15},{16,18},{20,... | collective-permute-start | bytes 7864328 | tf_op jit(solution)/shard_map/ppermute | solution.py:30
  31.3 2.5 copy-start.33
  31.3 9.8 %copy-start.28 = (s32[16]{0:T(128)S(1)}, s32[16]{0:T(128)}, u32[]{:S(2)}) copy-start(s32[16]{0:T(128)} %param.14) | copy-start | bytes 196
  41.1 24.9 %copy-start.17 = (bf16[2,1,52,384]{3,2,0,1:T(8,128)(2,1)S(1)}, bf16[2,1,52,384]{3,2,0,1:T(8,128)(2,1)}, u32[]{:S(2)}) copy-start(bf16[2,1,52,384]{3,2,0,1:T(8,128)(2,1)} %copy-done.16) | copy-start | bytes 239620
  42.4 79.0 %copy-start.31 = (pred[256]{0:T(512)(128)(4,1)}, pred[256]{0:T(512)(128)(4,1)S(1)}, u32[]{:S(2)}) copy-start(pred[256]{0:T(512)(128)(4,1)S(1)} %iota_compare_fusion.2) | copy-start | bytes 772
  45.0 152.7 %collective-permute-start = (bf16[2,256,2560]{1,2,0:T(8,128)(2,1)S(1)}, bf16[2,256,2560]{1,2,0:T(8,128)(2,1)}, u32[]{:S(2)}, u32[]{:S(2)}) collective-permute-start(bf16[2,256,2560]{1,2,0:T(8,128)(2,1)S(1)} %copy.45), channel_id=1, source_target_pairs={{0,1},{4,5},{8,9},{12,13},{2,3},{6,7},{10,11},{14,15},{16,17},{20,... | collective-permute-start | bytes 7864328 | tf_op jit(solution)/shard_map/ppermute | solution.py:30
  56.7 141.0 %collective-permute-start.8 = (bf16[2,256,2560]{1,2,0:T(8,128)(2,1)S(1)}, bf16[2,256,2560]{1,2,0:T(8,128)(2,1)}, u32[]{:S(2)}, u32[]{:S(2)}) collective-permute-start(bf16[2,256,2560]{1,2,0:T(8,128)(2,1)S(1)} %copy.45), channel_id=1, source_target_pairs={{1,4},{5,8},{9,12},{13,0},{17,20},{21,24},{25,28},{29,16}} | collective-permute-start | bytes 7864328 | tf_op jit(solution)/shard_map/ppermute | solution.py:30
  59.3 33.8 %collective-permute-start.4 = (bf16[2,256,2560]{1,2,0:T(8,128)(2,1)}, bf16[2,256,2560]{1,2,0:T(8,128)(2,1)S(1)}, u32[]{:S(2)}, u32[]{:S(2)}) collective-permute-start(bf16[2,256,2560]{1,2,0:T(8,128)(2,1)} %collective-permute-done.3), channel_id=1, source_target_pairs={{2,0},{6,4},{10,8},{14,12},{18,16},{22,20},{26,24},{30,28}} | collective-permute-start | bytes 7864328 | tf_op jit(solution)/shard_map/ppermute | solution.py:30
  60.6 60.7 %collective-permute-start.6 = (bf16[2,256,2560]{1,2,0:T(8,128)(2,1)}, bf16[2,256,2560]{1,2,0:T(8,128)(2,1)S(1)}, u32[]{:S(2)}, u32[]{:S(2)}) collective-permute-start(bf16[2,256,2560]{1,2,0:T(8,128)(2,1)} %collective-permute-done.5), channel_id=1, source_target_pairs={{1,4},{5,8},{9,12},{13,0},{17,20},{21,24},{25,28},{29,16}} | collective-permute-start | bytes 7864328 | tf_op jit(solution)/shard_map/ppermute | solution.py:30
  66.0 70.5 %slice-start = ((s8[7962624]{0:T(1024)(128)(4,1)}), s8[4194304]{0:T(1024)(128)(4,1)S(1)}, s32[]{:S(2)}) async-start(s8[7962624]{0:T(1024)(128)(4,1)} %bitcast.202), calls=%async_computation.1 | async-start | bytes 8388608
  93.1 31.4 %copy-start.6 = (bf16[2,256,2560]{1,2,0:T(8,128)(2,1)}, bf16[2,256,2560]{1,2,0:T(8,128)(2,1)S(1)}, u32[]{:S(2)}) copy-start(bf16[2,256,2560]{1,2,0:T(8,128)(2,1)S(1)} %collective-permute-done.4) | copy-start | bytes 7864324
  121.3 4.0 %copy-start.8 = (bf16[2,256,2560]{1,2,0:T(8,128)(2,1)}, bf16[2,256,2560]{1,2,0:T(8,128)(2,1)S(1)}, u32[]{:S(2)}) copy-start(bf16[2,256,2560]{1,2,0:T(8,128)(2,1)S(1)} %collective-permute-done.6) | copy-start | bytes 7864324
  121.3 11.6 %copy-start.19 = (bf16[3,1,52,384]{3,2,1,0:T(8,128)(2,1)S(1)}, bf16[3,1,52,384]{3,2,1,0:T(8,128)(2,1)}, u32[]{:S(2)}) copy-start(bf16[3,1,52,384]{3,2,1,0:T(8,128)(2,1)} %param.15) | copy-start | bytes 359428
  121.3 15.1 %slice-start.1 = ((s8[7962624]{0:T(1024)(128)(4,1)}), s8[3768320]{0:T(1024)(128)(4,1)S(1)}, s32[]{:S(2)}) async-start(s8[7962624]{0:T(1024)(128)(4,1)} %bitcast.202), calls=%async_computation.2 | async-start | bytes 7536640
  121.4 15.1 %copy-start.30 = (f32[384]{0:T(512)S(1)}, f32[384]{0:T(512)}, u32[]{:S(2)}) copy-start(f32[384]{0:T(512)} %param.19) | copy-start | bytes 4612
  125.3 72.3 %collective-permute-start.7 = (bf16[2,2,256,2560]{2,3,1,0:T(8,128)(2,1)}, bf16[2,2,256,2560]{2,3,1,0:T(8,128)(2,1)}, u32[]{:S(2)}, u32[]{:S(2)}) collective-permute-start(bf16[2,2,256,2560]{2,3,1,0:T(8,128)(2,1)} %pad_maximum_fusion.1), channel_id=1, source_target_pairs={{0,1},{4,5},{8,9},{12,13},{16,17},{20,21},{24,25},{28,29}} | collective-permute-start | bytes 15728648 | tf_op jit(solution)/shard_map/ppermute | solution.py:30
  133.2 64.4 %collective-permute-start.2 = (bf16[2,256,2560]{1,2,0:T(8,128)(2,1)}, bf16[2,256,2560]{1,2,0:T(8,128)(2,1)}, u32[]{:S(2)}, u32[]{:S(2)}) collective-permute-start(bf16[2,256,2560]{1,2,0:T(8,128)(2,1)} %collective-permute-done.1), channel_id=1, source_target_pairs={{3,2},{7,6},{11,10},{15,14},{2,3},{6,7},{10,11},{14,15},{19,18},{2... | collective-permute-start | bytes 7864328 | tf_op jit(solution)/shard_map/ppermute | solution.py:30
  191.8 3.1 %copy-start.15 = (bf16[256,512]{0,1:T(8,128)(2,1)S(1)}, bf16[256,512]{0,1:T(8,128)(2,1)}, u32[]{:S(2)}) copy-start(bf16[256,512]{0,1:T(8,128)(2,1)} %copy.122) | copy-start | bytes 786436
  191.8 4.5 %copy-start.25 = (bf16[256,512]{0,1:T(8,128)(2,1)S(1)}, bf16[256,512]{0,1:T(8,128)(2,1)}, u32[]{:S(2)}) copy-start(bf16[256,512]{0,1:T(8,128)(2,1)} %copy.121) | copy-start | bytes 786436
  193.1 4.5 %copy-start.7 = (bf16[2,256,2560]{1,2,0:T(8,128)(2,1)S(1)}, bf16[2,256,2560]{1,2,0:T(8,128)(2,1)}, u32[]{:S(2)}) copy-start(bf16[2,256,2560]{1,2,0:T(8,128)(2,1)} %copy-done.6) | copy-start | bytes 7864324
  193.2 4.5 %copy-start.9 = (bf16[2,256,2560]{1,2,0:T(8,128)(2,1)S(1)}, bf16[2,256,2560]{1,2,0:T(8,128)(2,1)}, u32[]{:S(2)}) copy-start(bf16[2,256,2560]{1,2,0:T(8,128)(2,1)} %copy-done.8) | copy-start | bytes 7864324
  208.6 3.5 %copy-start = (f32[4,1024,256]{2,1,0:T(8,128)}, f32[4,1024,256]{2,1,0:T(8,128)S(1)}, u32[]{:S(2)}) copy-start(f32[4,1024,256]{2,1,0:T(8,128)S(1)} %fusion.93) | copy-start | bytes 12582916
  209.4 2.8 %copy-start.2 = (f32[4,1024,256]{2,1,0:T(8,128)}, f32[4,1024,256]{2,1,0:T(8,128)S(1)}, u32[]{:S(2)}) copy-start(f32[4,1024,256]{2,1,0:T(8,128)S(1)} %fusion.94) | copy-start | bytes 12582916
  210.2 2.9 %copy-start.4 = (f32[4,1024,256]{2,1,0:T(8,128)}, f32[4,1024,256]{2,1,0:T(8,128)S(1)}, u32[]{:S(2)}) copy-start(f32[4,1024,256]{2,1,0:T(8,128)S(1)} %fusion.95) | copy-start | bytes 12582916
  218.6 1.5 copy-start.14
  220.3 6.5 %copy-start.26 = (bf16[1,256,512]{1,2,0:T(8,128)(2,1)S(1)}, bf16[1,256,512]{1,2,0:T(8,128)(2,1)}, u32[]{:S(2)}) copy-start(bf16[1,256,512]{1,2,0:T(8,128)(2,1)} %get-tuple-element.31) | copy-start | bytes 786436
  220.3 6.8 %copy-start.22 = (bf16[1,1024,512]{1,2,0:T(8,128)(2,1)S(1)}, bf16[1,1024,512]{1,2,0:T(8,128)(2,1)}, u32[]{:S(2)}) copy-start(bf16[1,1024,512]{1,2,0:T(8,128)(2,1)} %get-tuple-element.18) | copy-start | bytes 3145732
  226.8 2.2 copy-start.5
  229.0 3.9 %copy-start.13 = (f32[4,256,256]{1,2,0:T(8,128)S(1)}, f32[4,256,256]{1,2,0:T(8,128)}, u32[]{:S(2)}) copy-start(f32[4,256,256]{1,2,0:T(8,128)} %get-tuple-element.63) | copy-start | bytes 3145732
  231.0 3.5 %copy-start.21 = (bf16[1,1024,512]{1,2,0:T(8,128)(2,1)S(1)}, bf16[1,1024,512]{1,2,0:T(8,128)(2,1)}, u32[]{:S(2)}) copy-start(bf16[1,1024,512]{1,2,0:T(8,128)(2,1)} %get-tuple-element.20) | copy-start | bytes 3145732
  232.9 2.3 copy-start.3
  235.2 3.9 %copy-start.12 = (f32[4,256,256]{1,2,0:T(8,128)S(1)}, f32[4,256,256]{1,2,0:T(8,128)}, u32[]{:S(2)}) copy-start(f32[4,256,256]{1,2,0:T(8,128)} %get-tuple-element.61) | copy-start | bytes 3145732
  237.2 3.5 %copy-start.20 = (bf16[1,1024,512]{1,2,0:T(8,128)(2,1)S(1)}, bf16[1,1024,512]{1,2,0:T(8,128)(2,1)}, u32[]{:S(2)}) copy-start(bf16[1,1024,512]{1,2,0:T(8,128)(2,1)} %get-tuple-element.22) | copy-start | bytes 3145732
  239.1 2.3 copy-start.10
  241.4 3.1 %copy-start.11 = (f32[4,256,256]{1,2,0:T(8,128)S(1)}, f32[4,256,256]{1,2,0:T(8,128)}, u32[]{:S(2)}) copy-start(f32[4,256,256]{1,2,0:T(8,128)} %get-tuple-element.56) | copy-start | bytes 3145732
  244.5 2.3 copy-start.1
  246.8 1.5 copy-start.24
  246.8 1.6 copy-start.23
  246.8 1.6 copy-start.32
Sparse Core Ops, SparseCore 0:
  31.4 157.5 all-reduce.2

commit v2 on v1

--- a/solution.py
+++ b/solution.py
@@ -6,6 +6,7 @@
 H = 20
 DH = 128
 WIN = 4
+HG = 10
 
 
 def spread(block, axis, source):
@@ -83,7 +84,9 @@
     position = (place - anchor - 1) % devices
     tok_rows = queries.shape[0]
     row_ids = jnp.arange(tok_rows, dtype=jnp.int32)
-    anchor_kv = spread(keys_values, "span", anchor)
+    anchor_k = spread(keys_values[0], "span", anchor)
+    later_v, anchor_k = lax.optimization_barrier((keys_values[1], anchor_k))
+    anchor_v = spread(later_v, "span", anchor)
     b1, b2, b3 = window_blocks(keys_values, devices)
     blocks = [keys_values, b1, b2, b3]
     valid_list = [row_ids < lengths[place]]
@@ -95,15 +98,14 @@
     window_kv = jnp.concatenate(blocks, axis=1)
     window_valid = jnp.concatenate(valid_list)
     score_scale = DH ** (-0.5)
-    pieces = []
-    for head_block in range(H // 4):
-        first_col = head_block * 4 * DH
-        last_col = first_col + 4 * DH
-        q = queries[:, first_col:last_col].reshape(tok_rows, 4, DH)
-        wk = window_kv[0, :, first_col:last_col].reshape(-1, 4, DH)
-        wv = window_kv[1, :, first_col:last_col].reshape(-1, 4, DH)
-        ak = anchor_kv[0, :, first_col:last_col].reshape(-1, 4, DH)
-        av = anchor_kv[1, :, first_col:last_col].reshape(-1, 4, DH)
+    partial = []
+    for head_block in range(H // HG):
+        first_col = head_block * HG * DH
+        last_col = first_col + HG * DH
+        q = queries[:, first_col:last_col].reshape(tok_rows, HG, DH)
+        wk = window_kv[0, :, first_col:last_col].reshape(-1, HG, DH)
+        wv = window_kv[1, :, first_col:last_col].reshape(-1, HG, DH)
+        ak = anchor_k[:, first_col:last_col].reshape(-1, HG, DH)
         ws = part_stats(q, wk, window_valid, score_scale)
         a_s = part_stats(q, ak, anchor_valid, score_scale)
         top = jnp.maximum(
@@ -114,10 +116,18 @@
         total = jnp.sum(w_exp, axis=-1, keepdims=True) + jnp.sum(a_exp, axis=-1, keepdims=True)
         w_probs = (w_exp / total).astype(jnp.bfloat16)
         a_probs = (a_exp / total).astype(jnp.bfloat16)
-        blended = jnp.einsum(
-            "hqk,khd->hqd", w_probs, wv, preferred_element_type=jnp.float32
-        ) + jnp.einsum("hqk,khd->hqd", a_probs, av, preferred_element_type=jnp.float32)
-        pieces.append(jnp.transpose(blended, (1, 0, 2)).reshape(tok_rows, 4 * DH))
+        w_out = jnp.einsum("hqk,khd->hqd", w_probs, wv, preferred_element_type=jnp.float32)
+        partial.append((w_out, a_probs))
+    anchor_v, partial = lax.optimization_barrier((anchor_v, partial))
+    pieces = []
+    for head_block, (w_out, a_probs) in enumerate(partial):
+        first_col = head_block * HG * DH
+        last_col = first_col + HG * DH
+        av = anchor_v[:, first_col:last_col].reshape(-1, HG, DH)
+        blended = w_out + jnp.einsum(
+            "hqk,khd->hqd", a_probs, av, preferred_element_type=jnp.float32
+        )
+        pieces.append(jnp.transpose(blended, (1, 0, 2)).reshape(tok_rows, HG * DH))
     attended = jnp.concatenate(pieces, axis=1)
     attended = jnp.where(row_ids[:, None] < lengths[place], attended, 0.0).astype(jnp.bfloat16)
     features = frames.astype(jnp.float32)

time: 257 us -> 298 us (1.16)
  waiting for transfers between devices: 105 us -> 150 us
  starting transfers between devices: 40.9 us -> 31 us
  other arithmetic: 28 us -> 32.4 us
    psum x1 -> x2, waiting for transfers between devices: 49.8 us -> 92.1 us  [spread(): return lax.psum(block, axis)]
    ppermute x9, starting transfers between devices: 35.9 us -> 25.9 us  [move(): return lax.ppermute(value, 'span', pairs)]
    dot_general x5 -> x2, matrix products: 8.75 us -> 15.1 us  [shards(): jnp.einsum('hqk,khd->hqd', w_probs, wv, preferred_element_type=jnp.float32)]
    reshape x5 -> x0, local copies, waits for them, and re-layouts: 5.13 us -> none  [shards(): pieces.append(jnp.transpose(blended, (1, 0, 2)).reshape(tok_rows, 4 * DH))]
    dot_general x10 -> x4, matrix products: 15 us -> 10.4 us  [part_stats(): jnp.einsum('qhd,khd->hqk', q, k, preferred_element_type=jnp.float32) * scale]
    slice x3 -> x6, local copies, waits for them, and re-layouts: 7.19 us -> 11.3 us  [the longest x3 4.64 us: shards(): av = anchor_v[:, first_col:last_col].reshape(-1, HG, DH)]
    convert_element_type x0 -> x1, other arithmetic: none -> 2.98 us  [shards(): a_probs = (a_exp / total).astype(jnp.bfloat16)]
    unnamed x106 -> x54, local copies, waits for them, and re-layouts: 19.8 us -> 17.4 us
  transfers between devices with their start and end apart: 12 -> 13, of which waited for: 3 -> 4; matrix products, arithmetic and copies ran while one was open for 15% -> 27% of each run, Pallas kernels for 0% -> 0%
where the time goes in v2:
time: 298 us; the launch traced here: 297 us
  waiting for transfers between devices  150 us (50%)
  local copies, waits for them, and re-layouts  34 us (11%)
  matrix products  33 us (11%)
  other arithmetic  32.4 us (11%)
  starting transfers between devices  31 us (10%)
  between operations  17.1 us (6%)
    psum x2, waiting for transfers between devices, spread(): return lax.psum(block, axis)  92.1 us
    ppermute x9, waiting for transfers between devices, move(): return lax.ppermute(value, 'span', pairs)  57.6 us
    ppermute x9, starting transfers between devices, move(): return lax.ppermute(value, 'span', pairs)  25.9 us
    unnamed x54, local copies, waits for them, and re-layouts  17.4 us
    dot_general x2, matrix products, shards(): jnp.einsum('hqk,khd->hqd', w_probs, wv, preferred_element_type=jnp.float32)  15.1 us
    dot_general x4, matrix products, part_stats(): jnp.einsum('qhd,khd->hqk', q, k, preferred_element_type=jnp.float32) * scale  10.4 us
    reduce_sum x1, other arithmetic, shards(): jnp.sum(w_exp, axis=-1, keepdims=True)  7.39 us
    select_n x1, other arithmetic, pick(): out = jnp.where(lane == l, options[l], out)  6.38 us
  transfers between devices with their start and end apart: 13, of which 4 were waited for; matrix products, arithmetic and copies ran while one was open for 27% of the time, Pallas kernels for 0%

profile of v2, /device:TPU:0, one launch (start us, length us, event | category | flops | bytes accessed | tf_op | source)
XLA Modules:
  0.0 297.3 jit_solution(355756754644313053)
XLA Ops:
  7.2 1.0 fusion.36
  9.1 1.1 fusion.43
  10.9 1.3 collective-permute-start.10
  12.2 3.7 %collective-permute-start.9 = (bf16[5,1,52,384]{3,2,0,1:T(8,128)(2,1)}, bf16[5,1,52,384]{3,2,0,1:T(8,128)(2,1)}, u32[]{:S(2)}, u32[]{:S(2)}) collective-permute-start(bf16[5,1,52,384]{3,2,0,1:T(8,128)(2,1)} %pad_maximum_fusion.2), channel_id=1, source_target_pairs={{0,1},{1,2},{2,3},{3,4},{4,5},{5,6},{6,7},{7,8},{8,9},{9,10},{10,1... | collective-permute-start | bytes 599048 | tf_op jit(solution)/shard_map/ppermute | solution.py:22
  15.9 3.0 copy.23
  18.9 2.2 collective-permute-start.3
  21.1 2.2 collective-permute-start.5
  23.3 8.1 %collective-permute-start.1 = (bf16[2,256,2560]{1,2,0:T(8,128)(2,1)S(1)}, bf16[2,256,2560]{1,2,0:T(8,128)(2,1)}, u32[]{:S(2)}, u32[]{:S(2)}) collective-permute-start(bf16[2,256,2560]{1,2,0:T(8,128)(2,1)S(1)} %copy.23), channel_id=1, source_target_pairs={{0,2},{4,6},{8,10},{12,14},{1,3},{5,7},{9,11},{13,15},{16,18},{20,... | collective-permute-start | bytes 7864328 | tf_op jit(solution)/shard_map/ppermute | solution.py:31
  32.1 1.1 fusion.19
  33.4 2.2 fusion.55
  35.7 1.1 copy.72
  39.2 1.3 copy.73
  41.2 1.2 compare_and_fusion.3
  42.4 1.2 compare_and_fusion.1
  43.6 2.5 slice_bitcast_fusion.2
  46.8 3.6 %collective-permute-start = (bf16[2,256,2560]{1,2,0:T(8,128)(2,1)S(1)}, bf16[2,256,2560]{1,2,0:T(8,128)(2,1)}, u32[]{:S(2)}, u32[]{:S(2)}) collective-permute-start(bf16[2,256,2560]{1,2,0:T(8,128)(2,1)S(1)} %copy.23), channel_id=1, source_target_pairs={{0,1},{4,5},{8,9},{12,13},{2,3},{6,7},{10,11},{14,15},{16,17},{20,... | collective-permute-start | bytes 7864328 | tf_op jit(solution)/shard_map/ppermute | solution.py:31
  50.3 1.3 collective-permute-start.8
  51.6 1.3 select_maximum_fusion
  53.9 1.3 collective-permute-start.4
  55.2 1.3 collective-permute-start.6
  58.8 35.7 %collective-permute-done.4 = bf16[2,256,2560]{1,2,0:T(8,128)(2,1)S(1)} collective-permute-done((bf16[2,256,2560]{1,2,0:T(8,128)(2,1)}, bf16[2,256,2560]{1,2,0:T(8,128)(2,1)S(1)}, u32[]{:S(2)}, u32[]{:S(2)}) %collective-permute-start.4) | collective-permute-done | bytes 2621472 | tf_op jit(solution)/shard_map/ppermute | solution.py:31
  94.5 21.8 %collective-permute-done.6 = bf16[2,256,2560]{1,2,0:T(8,128)(2,1)S(1)} collective-permute-done((bf16[2,256,2560]{1,2,0:T(8,128)(2,1)}, bf16[2,256,2560]{1,2,0:T(8,128)(2,1)S(1)}, u32[]{:S(2)}, u32[]{:S(2)}) %collective-permute-start.6) | collective-permute-done | bytes 2621472 | tf_op jit(solution)/shard_map/ppermute | solution.py:31
  116.3 3.1 %pad_maximum_fusion.1 = bf16[2,2,256,2560]{2,3,1,0:T(8,128)(2,1)} fusion(bf16[1,2,256,2560]{2,3,1,0:T(8,128)(2,1)S(1)} %bitcast.138, bf16[1,2,256,2560]{2,3,1,0:T(8,128)(2,1)S(1)} %bitcast.137), kind=kLoop, calls=%fused_computation.13 | loop fusion | flops 2621440 | bytes 10485760 | tf_op jit(solution)/shard_map/stack | solution.py:50
  120.3 3.7 %collective-permute-start.7 = (bf16[2,2,256,2560]{2,3,1,0:T(8,128)(2,1)}, bf16[2,2,256,2560]{2,3,1,0:T(8,128)(2,1)}, u32[]{:S(2)}, u32[]{:S(2)}) collective-permute-start(bf16[2,2,256,2560]{2,3,1,0:T(8,128)(2,1)} %pad_maximum_fusion.1), channel_id=1, source_target_pairs={{0,1},{4,5},{8,9},{12,13},{16,17},{20,21},{24,25},{28,29}} | collective-permute-start | bytes 15728648 | tf_op jit(solution)/shard_map/ppermute | solution.py:31
  127.4 2.2 collective-permute-start.2
  129.6 2.7 fusion.30
  132.3 48.4 %all-reduce.4.cloned.1.call-done = bf16[256,2560]{0,1:T(8,128)(2,1)} async-done(((bf16[256,2560]{0,1:T(8,128)(2,1)}), bf16[256,2560]{0,1:T(8,128)(2,1)}) %all-reduce.4.cloned.1.call-update) | async-done | bytes 1310736 | tf_op jit(solution)/shard_map/psum | solution.py:14
  180.7 1.2 broadcast_select_fusion
  181.9 1.4 fusion.54
  184.0 1.0 bitcast_reduce_fusion.2
  185.7 1.7 copy-done.4
  187.4 6.4 %select_select_fusion = (bf16[2,256,2560]{1,2,0:T(8,128)(2,1)S(1)}, bf16[2,256,2560]{1,2,0:T(8,128)(2,1)S(1)}, bf16[2,256,2560]{1,2,0:T(8,128)(2,1)S(1)}) fusion(bf16[2,256,2560]{1,2,0:T(8,128)(2,1)} %collective-permute-done.1, bf16[2,256,2560]{1,2,0:T(8,128)(2,1)S(1)} %copy-done.4, bf16[2,2,256,2560]{2,3,1,0:T(8,128)(2,1)} %collective-permute-done.7, ...), kind=kLoop, calls=%fused_computation.16 | loop fusion | flops 11796480 | bytes 31457284 | tf_op jit(solution)/shard_map/jit(_where)/select_n | solution.py:55
  193.8 1.5 pad_maximum_fusion
  195.3 3.0 fusion.52
  198.3 2.7 fusion.57
  200.9 6.2 %bitcast_reduce_fusion = (f32[10,256]{1,0:T(8,128)S(1)}, f32[10,256]{1,0:T(8,128)S(1)}, f32[10,1024,256]{2,1,0:T(8,128)}) fusion(pred[1024]{0:T(1024)(128)(4,1)S(1)} %pad_add_fusion, f32[10,1024,256]{2,1,0:T(8,128)S(1)} %fusion.57, bf16[1024,10,128]{0,2,1:T(8,128)(2,1)S(1)} %bitcast.139, bf16[256,10,128]{0,2,1:T(8,128)(2,1)S(1)} %bitcast.142), kind=kOutput, calls=%fused_computation.2 | convolution fusion | flops 686812160 | bytes 24269824 | tf_op jit(solution)/shard_map/qhd,khd->hqk/dot_general | solution.py:65
  207.1 1.2 fusion.16
  208.3 7.4 %fusion.3 = (f32[10,256]{1,0:T(8,128)S(1)}, f32[10,256]{1,0:T(8,128)S(1)}) fusion(f32[10,1024,256]{2,1,0:T(8,128)} %get-tuple-element.51, f32[10,256]{1,0:T(8,128)S(1)} %max.17, pred[1024]{0:T(1024)(128)(4,1)S(1)} %pad_add_fusion, f32[10,256]{1,0:T(8,128)S(1)} %max.16, f32[10,1024,256]{2,1,0:T(8,128)S(1)} %fusion.57), kind=kLoop, calls=%fused_computation.12 | loop fusion | flops 20966400 | bytes 21013504 | tf_op jit(solution)/shard_map/reduce_sum | solution.py:116
  215.7 9.1 %fusion.5 = f32[10,256,128]{2,1,0:T(8,128)} fusion(bf16[1024,10,128]{0,2,1:T(8,128)(2,1)} %bitcast.146, f32[10,1024,256]{2,1,0:T(8,128)} %get-tuple-element.51, f32[10,256]{1,0:T(8,128)S(1)} %add.107, f32[10,256]{1,0:T(8,128)S(1)} %max.17, pred[1024]{0:T(1024)(128)(4,1)S(1)} %pad_add_fusion), kind=kOutput, calls=%fused_computation.15 | convolution fusion | flops 684195840 | bytes 14439424 | tf_op jit(solution)/shard_map/hqk,khd->hqd/dot_general | solution.py:119
  224.8 6.1 %fusion.4 = f32[10,256,128]{2,1,0:T(8,128)} fusion(bf16[1024,10,128]{0,2,1:T(8,128)(2,1)} %bitcast.145, f32[10,1024,256]{2,1,0:T(8,128)S(1)} %fusion.57, f32[10,256]{1,0:T(8,128)S(1)} %add.106, f32[10,256]{1,0:T(8,128)S(1)} %max.16, pred[1024]{0:T(1024)(128)(4,1)S(1)} %pad_add_fusion), kind=kOutput, calls=%fused_computation.14 | convolution fusion | flops 684195840 | bytes 14439424 | tf_op jit(solution)/shard_map/hqk,khd->hqd/dot_general | solution.py:119
  230.9 3.0 %divide_convert_fusion.4 = (bf16[10,256,256]{1,2,0:T(8,128)(2,1)S(1)}, bf16[10,256,256]{1,2,0:T(8,128)(2,1)S(1)}) fusion(f32[10,256,256]{2,1,0:T(8,128)} %copy-done, f32[10,256]{1,0:T(8,128)S(1)} %add.107, f32[10,256]{1,0:T(8,128)S(1)} %max.17, pred[256]{0:T(512)(128)(4,1)S(1)} %compare_and_fusion, f32[10,256]{1,0:T(8,128)S(1)} %add.106, ...), kind=kLoop, calls=%fused_computation.33 | loop fusion | flops 6553600 | bytes 7905536 | tf_op jit(solution)/shard_map/convert_element_type | solution.py:118
  233.8 43.7 %all-reduce.6.cloned.1.call-done = bf16[256,2560]{1,0:T(8,128)(2,1)} async-done(((bf16[256,2560]{1,0:T(8,128)(2,1)}), bf16[256,2560]{1,0:T(8,128)(2,1)}) %all-reduce.6.cloned.1.call-update) | async-done | bytes 1310736 | tf_op jit(solution)/shard_map/psum | solution.py:14
  277.6 2.2 fusion.53
  279.8 2.2 copy.44
  282.0 2.9 fusion.18
  284.9 1.3 copy.47
  286.5 1.9 fusion.17
  288.9 1.6 copy.54
  (81 shorter events, 13.0 us)
Async XLA Ops:
  7.2 173.5 %all-reduce.4.cloned.1.call-start = ((), (), s32[]{:S(2)}) async-start(), calls=%async_computation | async-start | bytes 2621440 | tf_op jit(solution)/shard_map/psum | solution.py:14
  10.9 35.8 %collective-permute-start.10 = (bf16[5,1,52,384]{3,2,0,1:T(8,128)(2,1)}, bf16[5,1,52,384]{3,2,0,1:T(8,128)(2,1)}, u32[]{:S(2)}, u32[]{:S(2)}) collective-permute-start(bf16[5,1,52,384]{3,2,0,1:T(8,128)(2,1)} %pad_maximum_fusion.2), channel_id=1, source_target_pairs={{1,0},{2,1},{3,2},{4,3},{5,4},{6,5},{7,6},{8,7},{9,8},{10,9},{11,1... | collective-permute-start | bytes 599048 | tf_op jit(solution)/shard_map/ppermute | solution.py:25
  12.2 38.1 %collective-permute-start.9 = (bf16[5,1,52,384]{3,2,0,1:T(8,128)(2,1)}, bf16[5,1,52,384]{3,2,0,1:T(8,128)(2,1)}, u32[]{:S(2)}, u32[]{:S(2)}) collective-permute-start(bf16[5,1,52,384]{3,2,0,1:T(8,128)(2,1)} %pad_maximum_fusion.2), channel_id=1, source_target_pairs={{0,1},{1,2},{2,3},{3,4},{4,5},{5,6},{6,7},{7,8},{8,9},{9,10},{10,1... | collective-permute-start | bytes 599048 | tf_op jit(solution)/shard_map/ppermute | solution.py:22
  18.9 34.9 %collective-permute-start.3 = (bf16[2,256,2560]{1,2,0:T(8,128)(2,1)S(1)}, bf16[2,256,2560]{1,2,0:T(8,128)(2,1)}, u32[]{:S(2)}, u32[]{:S(2)}) collective-permute-start(bf16[2,256,2560]{1,2,0:T(8,128)(2,1)S(1)} %copy.23), channel_id=1, source_target_pairs={{3,6},{7,10},{11,14},{15,2},{19,22},{23,26},{27,30},{31,18}} | collective-permute-start | bytes 7864328 | tf_op jit(solution)/shard_map/ppermute | solution.py:31
  21.1 34.0 %collective-permute-start.5 = (bf16[2,256,2560]{1,2,0:T(8,128)(2,1)S(1)}, bf16[2,256,2560]{1,2,0:T(8,128)(2,1)}, u32[]{:S(2)}, u32[]{:S(2)}) collective-permute-start(bf16[2,256,2560]{1,2,0:T(8,128)(2,1)S(1)} %copy.23), channel_id=1, source_target_pairs={{2,1},{6,5},{10,9},{14,13},{18,17},{22,21},{26,25},{30,29}} | collective-permute-start | bytes 7864328 | tf_op jit(solution)/shard_map/ppermute | solution.py:31
  23.3 104.0 %collective-permute-start.1 = (bf16[2,256,2560]{1,2,0:T(8,128)(2,1)S(1)}, bf16[2,256,2560]{1,2,0:T(8,128)(2,1)}, u32[]{:S(2)}, u32[]{:S(2)}) collective-permute-start(bf16[2,256,2560]{1,2,0:T(8,128)(2,1)S(1)} %copy.23), channel_id=1, source_target_pairs={{0,2},{4,6},{8,10},{12,14},{1,3},{5,7},{9,11},{13,15},{16,18},{20,... | collective-permute-start | bytes 7864328 | tf_op jit(solution)/shard_map/ppermute | solution.py:31
  33.2 3.5 %copy-start.10 = (s32[16,3]{0,1:T(4,128)S(1)}, s32[16,3]{0,1:T(4,128)}, u32[]{:S(2)}) copy-start(s32[16,3]{0,1:T(4,128)} %param.13) | copy-start | bytes 580
  33.3 244.3 %all-reduce.6.cloned.1.call-start = ((), (), s32[]{:S(2)}) async-start(), calls=%async_computation.1 | async-start | bytes 2621440 | tf_op jit(solution)/shard_map/psum | solution.py:14
  33.4 7.1 %copy-start.7 = (s32[16]{0:T(128)S(1)}, s32[16]{0:T(128)}, u32[]{:S(2)}) copy-start(s32[16]{0:T(128)} %param.14) | copy-start | bytes 196
  46.8 138.2 %collective-permute-start = (bf16[2,256,2560]{1,2,0:T(8,128)(2,1)S(1)}, bf16[2,256,2560]{1,2,0:T(8,128)(2,1)}, u32[]{:S(2)}, u32[]{:S(2)}) collective-permute-start(bf16[2,256,2560]{1,2,0:T(8,128)(2,1)S(1)} %copy.23), channel_id=1, source_target_pairs={{0,1},{4,5},{8,9},{12,13},{2,3},{6,7},{10,11},{14,15},{16,17},{20,... | collective-permute-start | bytes 7864328 | tf_op jit(solution)/shard_map/ppermute | solution.py:31
  50.3 134.6 %collective-permute-start.8 = (bf16[2,256,2560]{1,2,0:T(8,128)(2,1)S(1)}, bf16[2,256,2560]{1,2,0:T(8,128)(2,1)}, u32[]{:S(2)}, u32[]{:S(2)}) collective-permute-start(bf16[2,256,2560]{1,2,0:T(8,128)(2,1)S(1)} %copy.23), channel_id=1, source_target_pairs={{1,4},{5,8},{9,12},{13,0},{17,20},{21,24},{25,28},{29,16}} | collective-permute-start | bytes 7864328 | tf_op jit(solution)/shard_map/ppermute | solution.py:31
  53.9 40.6 %collective-permute-start.4 = (bf16[2,256,2560]{1,2,0:T(8,128)(2,1)}, bf16[2,256,2560]{1,2,0:T(8,128)(2,1)S(1)}, u32[]{:S(2)}, u32[]{:S(2)}) collective-permute-start(bf16[2,256,2560]{1,2,0:T(8,128)(2,1)} %collective-permute-done.3), channel_id=1, source_target_pairs={{2,0},{6,4},{10,8},{14,12},{18,16},{22,20},{26,24},{30,28}} | collective-permute-start | bytes 7864328 | tf_op jit(solution)/shard_map/ppermute | solution.py:31
  55.2 61.2 %collective-permute-start.6 = (bf16[2,256,2560]{1,2,0:T(8,128)(2,1)}, bf16[2,256,2560]{1,2,0:T(8,128)(2,1)S(1)}, u32[]{:S(2)}, u32[]{:S(2)}) collective-permute-start(bf16[2,256,2560]{1,2,0:T(8,128)(2,1)} %collective-permute-done.5), channel_id=1, source_target_pairs={{1,4},{5,8},{9,12},{13,0},{17,20},{21,24},{25,28},{29,16}} | collective-permute-start | bytes 7864328 | tf_op jit(solution)/shard_map/ppermute | solution.py:31
  58.6 71.0 %slice-start = ((s8[7962624]{0:T(1024)(128)(4,1)}), s8[4194304]{0:T(1024)(128)(4,1)S(1)}, s32[]{:S(2)}) async-start(s8[7962624]{0:T(1024)(128)(4,1)} %bitcast.134), calls=%async_computation.2 | async-start | bytes 8388608
  94.5 25.0 %copy-start.1 = (bf16[2,256,2560]{1,2,0:T(8,128)(2,1)}, bf16[2,256,2560]{1,2,0:T(8,128)(2,1)S(1)}, u32[]{:S(2)}) copy-start(bf16[2,256,2560]{1,2,0:T(8,128)(2,1)S(1)} %collective-permute-done.4) | copy-start | bytes 7864324
  116.3 4.0 %copy-start.3 = (bf16[2,256,2560]{1,2,0:T(8,128)(2,1)}, bf16[2,256,2560]{1,2,0:T(8,128)(2,1)S(1)}, u32[]{:S(2)}) copy-start(bf16[2,256,2560]{1,2,0:T(8,128)(2,1)S(1)} %collective-permute-done.6) | copy-start | bytes 7864324
  116.3 9.8 %copy-start.6 = (bf16[3,1,52,384]{3,2,1,0:T(8,128)(2,1)S(1)}, bf16[3,1,52,384]{3,2,1,0:T(8,128)(2,1)}, u32[]{:S(2)}) copy-start(bf16[3,1,52,384]{3,2,1,0:T(8,128)(2,1)} %param.15) | copy-start | bytes 359428
  116.3 9.8 %copy-start.8 = (f32[384]{0:T(512)S(1)}, f32[384]{0:T(512)}, u32[]{:S(2)}) copy-start(f32[384]{0:T(512)} %param.17) | copy-start | bytes 4612
  116.3 13.3 %slice-start.1 = ((s8[7962624]{0:T(1024)(128)(4,1)}), s8[3768320]{0:T(1024)(128)(4,1)S(1)}, s32[]{:S(2)}) async-start(s8[7962624]{0:T(1024)(128)(4,1)} %bitcast.134), calls=%async_computation.3 | async-start | bytes 7536640
  120.3 9.3 %copy-start.9 = (f32[384]{0:T(512)S(1)}, f32[384]{0:T(512)}, u32[]{:S(2)}) copy-start(f32[384]{0:T(512)} %param.19) | copy-start | bytes 4612
  120.3 64.7 %collective-permute-start.7 = (bf16[2,2,256,2560]{2,3,1,0:T(8,128)(2,1)}, bf16[2,2,256,2560]{2,3,1,0:T(8,128)(2,1)}, u32[]{:S(2)}, u32[]{:S(2)}) collective-permute-start(bf16[2,2,256,2560]{2,3,1,0:T(8,128)(2,1)} %pad_maximum_fusion.1), channel_id=1, source_target_pairs={{0,1},{4,5},{8,9},{12,13},{16,17},{20,21},{24,25},{28,29}} | collective-permute-start | bytes 15728648 | tf_op jit(solution)/shard_map/ppermute | solution.py:31
  127.4 57.6 %collective-permute-start.2 = (bf16[2,256,2560]{1,2,0:T(8,128)(2,1)}, bf16[2,256,2560]{1,2,0:T(8,128)(2,1)}, u32[]{:S(2)}, u32[]{:S(2)}) collective-permute-start(bf16[2,256,2560]{1,2,0:T(8,128)(2,1)} %collective-permute-done.1), channel_id=1, source_target_pairs={{3,2},{7,6},{11,10},{15,14},{2,3},{6,7},{10,11},{14,15},{19,18},{2... | collective-permute-start | bytes 7864328 | tf_op jit(solution)/shard_map/ppermute | solution.py:31
  181.9 1.5 copy-start.5
  183.9 1.7 copy-start.2
  183.9 3.5 %copy-start.4 = (bf16[2,256,2560]{1,2,0:T(8,128)(2,1)S(1)}, bf16[2,256,2560]{1,2,0:T(8,128)(2,1)}, u32[]{:S(2)}) copy-start(bf16[2,256,2560]{1,2,0:T(8,128)(2,1)} %copy-done.3) | copy-start | bytes 7864324
  184.9 22.2 %copy-start = (f32[10,256,256]{2,1,0:T(8,128)}, f32[10,256,256]{2,1,0:T(8,128)S(1)}, u32[]{:S(2)}) copy-start(f32[10,256,256]{2,1,0:T(8,128)S(1)} %get-tuple-element.52) | copy-start | bytes 7864324
Sparse Core Ops, SparseCore 0:
  33.4 147.2 all-reduce.3
  184.2 93.3 all-reduce.5

commit v3 on v2

--- a/solution.py
+++ b/solution.py
@@ -66,6 +66,12 @@
     return jnp.where(valid[None, None, :], scores, -jnp.inf)
 
 
+def weighted(weights, values):
+    return jnp.einsum(
+        "hqk,khd->hqd", weights.astype(jnp.bfloat16), values, preferred_element_type=jnp.float32
+    )
+
+
 def shards(
     queries,
     keys_values,
@@ -84,9 +90,7 @@
     position = (place - anchor - 1) % devices
     tok_rows = queries.shape[0]
     row_ids = jnp.arange(tok_rows, dtype=jnp.int32)
-    anchor_k = spread(keys_values[0], "span", anchor)
-    later_v, anchor_k = lax.optimization_barrier((keys_values[1], anchor_k))
-    anchor_v = spread(later_v, "span", anchor)
+    anchor_kv = spread(keys_values, "span", anchor)
     b1, b2, b3 = window_blocks(keys_values, devices)
     blocks = [keys_values, b1, b2, b3]
     valid_list = [row_ids < lengths[place]]
@@ -105,28 +109,26 @@
         q = queries[:, first_col:last_col].reshape(tok_rows, HG, DH)
         wk = window_kv[0, :, first_col:last_col].reshape(-1, HG, DH)
         wv = window_kv[1, :, first_col:last_col].reshape(-1, HG, DH)
-        ak = anchor_k[:, first_col:last_col].reshape(-1, HG, DH)
         ws = part_stats(q, wk, window_valid, score_scale)
-        a_s = part_stats(q, ak, anchor_valid, score_scale)
-        top = jnp.maximum(
-            jnp.max(ws, axis=-1, keepdims=True), jnp.max(a_s, axis=-1, keepdims=True)
-        )
-        w_exp = jnp.exp(ws - top)
-        a_exp = jnp.exp(a_s - top)
-        total = jnp.sum(w_exp, axis=-1, keepdims=True) + jnp.sum(a_exp, axis=-1, keepdims=True)
-        w_probs = (w_exp / total).astype(jnp.bfloat16)
-        a_probs = (a_exp / total).astype(jnp.bfloat16)
-        w_out = jnp.einsum("hqk,khd->hqd", w_probs, wv, preferred_element_type=jnp.float32)
-        partial.append((w_out, a_probs))
-    anchor_v, partial = lax.optimization_barrier((anchor_v, partial))
+        w_max = jnp.max(ws, axis=-1, keepdims=True)
+        w_exp = jnp.exp(ws - w_max)
+        w_sum = jnp.sum(w_exp, axis=-1, keepdims=True)
+        partial.append((w_max, w_sum, weighted(w_exp, wv)))
+    anchor_kv, partial = lax.optimization_barrier((anchor_kv, partial))
     pieces = []
-    for head_block, (w_out, a_probs) in enumerate(partial):
+    for head_block, (w_max, w_sum, w_out) in enumerate(partial):
         first_col = head_block * HG * DH
         last_col = first_col + HG * DH
-        av = anchor_v[:, first_col:last_col].reshape(-1, HG, DH)
-        blended = w_out + jnp.einsum(
-            "hqk,khd->hqd", a_probs, av, preferred_element_type=jnp.float32
-        )
+        q = queries[:, first_col:last_col].reshape(tok_rows, HG, DH)
+        ak = anchor_kv[0, :, first_col:last_col].reshape(-1, HG, DH)
+        av = anchor_kv[1, :, first_col:last_col].reshape(-1, HG, DH)
+        a_s = part_stats(q, ak, anchor_valid, score_scale)
+        top = jnp.maximum(w_max, jnp.max(a_s, axis=-1, keepdims=True))
+        a_exp = jnp.exp(a_s - top)
+        a_sum = jnp.sum(a_exp, axis=-1, keepdims=True)
+        a_out = weighted(a_exp, av)
+        w_scale = jnp.exp(w_max - top)
+        blended = (w_out * w_scale + a_out) / (w_sum * w_scale + a_sum)
         pieces.append(jnp.transpose(blended, (1, 0, 2)).reshape(tok_rows, HG * DH))
     attended = jnp.concatenate(pieces, axis=1)
     attended = jnp.where(row_ids[:, None] < lengths[place], attended, 0.0).astype(jnp.bfloat16)

time: 298 us -> 220 us (0.74)
  waiting for transfers between devices: 150 us -> 69.7 us
  starting transfers between devices: 31 us -> 44.1 us
  local copies, waits for them, and re-layouts: 34 us -> 27.5 us
  other arithmetic: 32.4 us -> 28.5 us
    psum x2 -> x1, waiting for transfers between devices: 92.1 us -> 28.3 us  [spread(): return lax.psum(block, axis)]
    ppermute x9, waiting for transfers between devices: 57.6 us -> 41.4 us  [move(): return lax.ppermute(value, 'span', pairs)]
    ppermute x9, starting transfers between devices: 25.9 us -> 39 us  [move(): return lax.ppermute(value, 'span', pairs)]
    slice x4 -> x1, local copies, waits for them, and re-layouts: 6.08 us -> 2.7 us  [shards(): av = anchor_kv[1, :, first_col:last_col].reshape(-1, HG, DH)]
    convert_element_type x1 -> x0, other arithmetic: 2.98 us -> none  [shards(): a_probs = (a_exp / total).astype(jnp.bfloat16)]
    unnamed x54 -> x60, local copies, waits for them, and re-layouts: 17.4 us -> 15.5 us
  transfers between devices with their start and end apart: 13 -> 12, of which waited for: 4 -> 4; matrix products, arithmetic and copies ran while one was open for 27% -> 31% of each run, Pallas kernels for 0% -> 0%
where the time goes in v3:
time: 220 us; the launch traced here: 219 us
  waiting for transfers between devices  69.7 us (32%)
  starting transfers between devices  44.1 us (20%)
  matrix products  32.4 us (15%)
  other arithmetic  28.5 us (13%)
  local copies, waits for them, and re-layouts  27.5 us (12%)
  between operations  17.2 us (8%)
    ppermute x9, waiting for transfers between devices, move(): return lax.ppermute(value, 'span', pairs)  41.4 us
    ppermute x9, starting transfers between devices, move(): return lax.ppermute(value, 'span', pairs)  39 us
    psum x1, waiting for transfers between devices, spread(): return lax.psum(block, axis)  28.3 us
    dot_general x4, matrix products, weighted(): jnp.einsum('hqk,khd->hqd', weights.astype(jnp.bfloat16), values, preferre...  18.4 us
    unnamed x60, local copies, waits for them, and re-layouts  15.5 us
    dot_general x4, matrix products, part_stats(): jnp.einsum('qhd,khd->hqk', q, k, preferred_element_type=jnp.float32) * scale  11.2 us
    reduce_sum x1, other arithmetic, shards(): w_sum = jnp.sum(w_exp, axis=-1, keepdims=True)  7.1 us
    select_n x1, other arithmetic, pick(): out = jnp.where(lane == l, options[l], out)  5.96 us
  transfers between devices with their start and end apart: 12, of which 4 were waited for; matrix products, arithmetic and copies ran while one was open for 31% of the time, Pallas kernels for 0%

profile of v3, /device:TPU:0, one launch (start us, length us, event | category | flops | bytes accessed | tf_op | source)
XLA Modules:
  0.0 219.4 jit_solution(16236503728800616848)
XLA Ops:
  7.2 3.0 %copy.23 = bf16[2,256,2560]{1,2,0:T(8,128)(2,1)S(1)} copy(bf16[2,256,2560]{2,1,0:T(8,128)(2,1)} %param.11) | data formatting | bytes 5242880 | tf_op args[1]
  10.3 2.1 collective-permute-start.3
  12.4 2.2 collective-permute-start.5
  14.9 0.7 pad_maximum_fusion.2
  15.6 1.3 collective-permute-start.10
  16.9 3.7 %collective-permute-start.9 = (bf16[5,1,52,384]{3,2,0,1:T(8,128)(2,1)}, bf16[5,1,52,384]{3,2,0,1:T(8,128)(2,1)}, u32[]{:S(2)}, u32[]{:S(2)}) collective-permute-start(bf16[5,1,52,384]{3,2,0,1:T(8,128)(2,1)} %pad_maximum_fusion.2), channel_id=1, source_target_pairs={{0,1},{1,2},{2,3},{3,4},{4,5},{5,6},{6,7},{7,8},{8,9},{9,10},{10,1... | collective-permute-start | bytes 599048 | tf_op jit(solution)/shard_map/ppermute | solution.py:22
  20.6 8.2 %collective-permute-start.1 = (bf16[2,256,2560]{1,2,0:T(8,128)(2,1)S(1)}, bf16[2,256,2560]{1,2,0:T(8,128)(2,1)}, u32[]{:S(2)}, u32[]{:S(2)}) collective-permute-start(bf16[2,256,2560]{1,2,0:T(8,128)(2,1)S(1)} %copy.23), channel_id=1, source_target_pairs={{0,2},{4,6},{8,10},{12,14},{1,3},{5,7},{9,11},{13,15},{16,18},{20,... | collective-permute-start | bytes 7864328 | tf_op jit(solution)/shard_map/ppermute | solution.py:31
  29.4 1.3 collective-permute-start.4
  30.8 1.3 collective-permute-start.6
  32.1 1.6 broadcast_select_fusion
  33.8 2.4 %fusion.89 = (bf16[256,1280]{1,0:T(8,128)(2,1)}, bf16[256,1280]{1,0:T(8,128)(2,1)}) fusion(bf16[256,2560]{1,0:T(8,128)(2,1)} %param.10), kind=kLoop, calls=%fused_computation.152 | loop fusion | bytes 2621440 | tf_op jit(solution)/shard_map/slice | solution.py:109
  36.3 1.3 copy.70
  40.2 2.2 copy.71
  43.0 1.2 compare_and_fusion.3
  44.1 1.3 compare_and_fusion.1
  46.1 18.7 %collective-permute-start = (bf16[2,256,2560]{1,2,0:T(8,128)(2,1)S(1)}, bf16[2,256,2560]{1,2,0:T(8,128)(2,1)S(1)}, u32[]{:S(2)}, u32[]{:S(2)}) collective-permute-start(bf16[2,256,2560]{1,2,0:T(8,128)(2,1)S(1)} %copy.23), channel_id=1, source_target_pairs={{0,1},{4,5},{8,9},{12,13},{2,3},{6,7},{10,11},{14,15},{16,17},{20,... | collective-permute-start | bytes 7864328 | tf_op jit(solution)/shard_map/ppermute | solution.py:31
  64.9 1.3 collective-permute-start.8
  66.2 1.3 select_maximum_fusion
  67.5 0.9 slice_dynamic-update-slice_fusion.22
  68.6 17.8 %collective-permute-done.4 = bf16[2,256,2560]{1,2,0:T(8,128)(2,1)} collective-permute-done((bf16[2,256,2560]{1,2,0:T(8,128)(2,1)}, bf16[2,256,2560]{1,2,0:T(8,128)(2,1)}, u32[]{:S(2)}, u32[]{:S(2)}) %collective-permute-start.4) | collective-permute-done | bytes 2621472 | tf_op jit(solution)/shard_map/ppermute | solution.py:31
  86.4 13.4 %collective-permute-done.6 = bf16[2,256,2560]{1,2,0:T(8,128)(2,1)} collective-permute-done((bf16[2,256,2560]{1,2,0:T(8,128)(2,1)}, bf16[2,256,2560]{1,2,0:T(8,128)(2,1)}, u32[]{:S(2)}, u32[]{:S(2)}) %collective-permute-start.6) | collective-permute-done | bytes 2621472 | tf_op jit(solution)/shard_map/ppermute | solution.py:31
  99.9 5.8 %pad_maximum_fusion.1 = bf16[2,2,256,2560]{2,3,1,0:T(8,128)(2,1)} fusion(bf16[1,2,256,2560]{2,3,1,0:T(8,128)(2,1)} %bitcast.9, bf16[1,2,256,2560]{2,3,1,0:T(8,128)(2,1)} %bitcast.8), kind=kLoop, calls=%fused_computation.15 | loop fusion | flops 2621440 | bytes 10485760 | tf_op jit(solution)/shard_map/stack | solution.py:50
  105.7 1.7 collective-permute-start.7
  107.5 0.9 slice_dynamic-update-slice_fusion.17
  108.5 0.9 slice_dynamic-update-slice_fusion.14
  109.6 0.9 slice_dynamic-update-slice_fusion.9
  110.6 2.2 %collective-permute-start.2 = (bf16[2,256,2560]{1,2,0:T(8,128)(2,1)}, bf16[2,256,2560]{1,2,0:T(8,128)(2,1)}, u32[]{:S(2)}, u32[]{:S(2)}) collective-permute-start(bf16[2,256,2560]{1,2,0:T(8,128)(2,1)} %collective-permute-done.1), channel_id=1, source_target_pairs={{3,2},{7,6},{11,10},{15,14},{2,3},{6,7},{10,11},{14,15},{19,18},{2... | collective-permute-start | bytes 7864328 | tf_op jit(solution)/shard_map/ppermute | solution.py:31
  112.8 0.9 slice_dynamic-update-slice_fusion.6
  114.1 0.9 slice_dynamic-update-slice_fusion.1
  115.1 2.8 %fusion.55 = bf16[3,1,52,384]{3,2,1,0:T(8,128)(2,1)} fusion(bf16[10368,384,1]{1,0,2:T(8,128)(2,1)S(1)} %bitcast.176, bf16[3,1,52,10368]{3,2,0,1:T(8,128)(2,1)S(1)} %slice_dynamic-update-slice_fusion, bf16[3,1,52,384]{3,2,1,0:T(8,128)(2,1)S(1)} %copy-done.5, f32[384]{0:T(512)S(1)} %copy-done.10), kind=kOutput, calls=%fused_computation.69 | convolution fusion | flops 1242408960 | bytes 11438592 | tf_op jit(solution)/shard_map/dot_general | solution.py:159
  117.9 10.1 %collective-permute-done.8 = bf16[2,256,2560]{1,2,0:T(8,128)(2,1)} collective-permute-done((bf16[2,256,2560]{1,2,0:T(8,128)(2,1)S(1)}, bf16[2,256,2560]{1,2,0:T(8,128)(2,1)}, u32[]{:S(2)}, u32[]{:S(2)}) %collective-permute-start.8) | collective-permute-done | bytes 2621472 | tf_op jit(solution)/shard_map/ppermute | solution.py:31
  128.0 6.0 %select_select_fusion = (bf16[2,256,2560]{1,2,0:T(8,128)(2,1)S(1)}, bf16[2,256,2560]{1,2,0:T(8,128)(2,1)S(1)}, bf16[2,256,2560]{1,2,0:T(8,128)(2,1)S(1)}) fusion(bf16[2,256,2560]{1,2,0:T(8,128)(2,1)} %collective-permute-done.1, bf16[2,256,2560]{1,2,0:T(8,128)(2,1)} %collective-permute-done.6, bf16[2,2,256,2560]{2,3,1,0:T(8,128)(2,1)S(1)} %collective-permute-done.7, ...), kind=kLoop, calls=%fused_computation.24 | loop fusion | flops 11796480 | bytes 31457284 | tf_op jit(solution)/shard_map/jit(_where)/select_n | solution.py:55
  133.9 1.5 pad_maximum_fusion
  135.4 2.9 %fusion.87 = (bf16[1,1024,1280]{1,2,0:T(8,128)(2,1)}, bf16[1,1024,1280]{1,2,0:T(8,128)(2,1)S(1)}, bf16[1,1024,1280]{1,2,0:T(8,128)(2,1)}, bf16[1,1024,1280]{1,2,0:T(8,128)(2,1)S(1)}) fusion(bf16[2,1024,2560]{1,2,0:T(8,128)(2,1)S(1)} %pad_maximum_fusion), kind=kLoop, calls=%fused_computation.150 | loop fusion | bytes 20971520 | tf_op jit(solution)/shard_map/slice | solution.py:111
  138.3 1.6 fusion.91
  139.9 6.2 %bitcast_reduce_fusion = (f32[10,256]{1,0:T(8,128)S(1)}, f32[10,256]{1,0:T(8,128)S(1)}, f32[10,1024,256]{2,1,0:T(8,128)}) fusion(pred[1024]{0:T(1024)(128)(4,1)S(1)} %pad_add_fusion, f32[10,1024,256]{2,1,0:T(8,128)S(1)} %fusion.91, bf16[1024,10,128]{0,2,1:T(8,128)(2,1)S(1)} %bitcast.177, bf16[256,10,128]{0,2,1:T(8,128)(2,1)S(1)} %bitcast.181), kind=kOutput, calls=%fused_computation.2 | convolution fusion | flops 686812160 | bytes 24269824 | tf_op jit(solution)/shard_map/qhd,khd->hqk/dot_general | solution.py:65
  146.1 5.9 %fusion.8 = f32[10,256,128]{2,1,0:T(8,128)} fusion(bf16[1024,10,128]{0,2,1:T(8,128)(2,1)} %bitcast.184, f32[10,1024,256]{2,1,0:T(8,128)S(1)} %fusion.91, f32[10,256]{1,0:T(8,128)S(1)} %get-tuple-element.23, pred[1024]{0:T(1024)(128)(4,1)S(1)} %pad_add_fusion), kind=kOutput, calls=%fused_computation.14 | convolution fusion | flops 681574400 | bytes 14429184 | tf_op jit(solution)/shard_map/hqk,khd->hqd/dot_general | solution.py:70
  152.0 8.0 %fusion.6 = f32[10,256,128]{2,1,0:T(8,128)} fusion(bf16[1024,10,128]{0,2,1:T(8,128)(2,1)S(1)} %bitcast.183, f32[10,1024,256]{2,1,0:T(8,128)} %get-tuple-element.51, f32[10,256]{1,0:T(8,128)S(1)} %get-tuple-element.22, pred[1024]{0:T(1024)(128)(4,1)S(1)} %pad_add_fusion), kind=kOutput, calls=%fused_computation.13 | convolution fusion | flops 681574400 | bytes 14429184 | tf_op jit(solution)/shard_map/hqk,khd->hqd/dot_general | solution.py:70
  159.9 7.1 %fusion.5 = (f32[10,256]{1,0:T(8,128)S(1)}, f32[10,256]{1,0:T(8,128)S(1)}) fusion(f32[10,1024,256]{2,1,0:T(8,128)} %get-tuple-element.51, f32[10,256]{1,0:T(8,128)S(1)} %get-tuple-element.22, pred[1024]{0:T(1024)(128)(4,1)S(1)} %pad_add_fusion, f32[10,256]{1,0:T(8,128)S(1)} %get-tuple-element.23, f32[10,1024,256]{2,1,0:T(8,128)S(1)} %fusion.91), kind=kLoop, calls=%fused_computation.12 | loop fusion | flops 20966400 | bytes 21013504 | tf_op jit(solution)/shard_map/reduce_sum | solution.py:115
  167.0 28.3 %all-reduce.3.cloned.1.call-done = bf16[2,256,2560]{1,2,0:T(8,128)(2,1)} async-done(((bf16[2,256,2560]{1,2,0:T(8,128)(2,1)}), bf16[2,256,2560]{1,2,0:T(8,128)(2,1)}) %all-reduce.3.cloned.1.call-update) | async-done | bytes 2621456 | tf_op jit(solution)/shard_map/psum | solution.py:14
  195.4 2.7 %fusion.88 = (bf16[1,256,1280]{1,2,0:T(8,128)(2,1)S(1)}, bf16[1,256,1280]{1,2,0:T(8,128)(2,1)}, bf16[1,256,1280]{1,2,0:T(8,128)(2,1)S(1)}, bf16[1,256,1280]{1,2,0:T(8,128)(2,1)S(1)}) fusion(bf16[2,256,2560]{1,2,0:T(8,128)(2,1)} %all-reduce.3.cloned.1.call-done), kind=kLoop, calls=%fused_computation.151 | loop fusion | bytes 5242880 | tf_op jit(solution)/shard_map/slice | solution.py:124
  198.1 0.7 bitcast_reduce_fusion.3
  199.2 2.8 %fusion.27 = (f32[10,256]{1,0:T(8,128)S(1)}, f32[10,256]{1,0:T(8,128)S(1)}, f32[10,256,256]{2,1,0:T(8,128)}) fusion(f32[10,256,256]{2,1,0:T(8,128)S(1)} %get-tuple-element.53, f32[10,256]{1,0:T(8,128)S(1)} %fusion.75, pred[256]{0:T(512)(128)(4,1)S(1)} %compare_and_fusion, bf16[256,10,128]{0,2,1:T(8,128)(2,1)S(1)} %bitcast.190, ...), kind=kOutput, calls=%fused_computation.45 | convolution fusion | flops 172354560 | bytes 6584576 | tf_op jit(solution)/shard_map/qhd,khd->hqk/dot_general | solution.py:65
  202.0 2.3 %fusion.32 = bf16[256,10,128]{2,0,1:T(8,128)(2,1)} fusion(bf16[256,10,128]{0,2,1:T(8,128)(2,1)S(1)} %bitcast.189, f32[10,256,256]{2,1,0:T(8,128)S(1)} %get-tuple-element.53, f32[10,256]{1,0:T(8,128)S(1)} %fusion.75, f32[10,256,128]{2,1,0:T(8,128)S(1)} %copy-done.13, pred[256]{0:T(512)(128)(4,1)S(1)} %compare_and_fusion, ...), kind=kOutput, calls=%fused_computation.54 | convolution fusion | flops 171704320 | bytes 5273856 | tf_op jit(solution)/shard_map/hqk,khd->hqd/dot_general | solution.py:70
  204.3 1.3 copy.44
  207.1 2.3 %fusion.34 = bf16[256,10,128]{2,0,1:T(8,128)(2,1)} fusion(bf16[256,10,128]{0,2,1:T(8,128)(2,1)S(1)} %bitcast.188, f32[10,256,256]{2,1,0:T(8,128)S(1)} %copy-done.3, f32[10,256]{1,0:T(8,128)S(1)} %fusion.76, f32[10,256,128]{2,1,0:T(8,128)S(1)} %copy-done.12, pred[256]{0:T(512)(128)(4,1)S(1)} %compare_and_fusion, f32[10,256]{1,0:T(8,128)S(1)} %get-tuple-element.42, ...), kind=kOutput, calls=%fused_computation.56 | convolution fusion | flops 171704320 | bytes 5273856 | tf_op jit(solution)/shard_map/hqk,khd->hqd/dot_general | solution.py:70
  209.4 1.3 copy.49
  211.0 1.6 copy.52
  (78 shorter events, 5.3 us)
Async XLA Ops:
  7.2 7.4 %copy-start.7 = (bf16[2,1,52,384]{3,0,2,1:T(2,128)(2,1)S(1)}, bf16[2,1,52,384]{3,0,2,1:T(2,128)(2,1)}, u32[]{:S(2)}) copy-start(bf16[2,1,52,384]{3,0,2,1:T(2,128)(2,1)} %param.16) | copy-start | bytes 239620
  7.2 7.4 %copy-start.4 = (bf16[3,1,52,384]{3,2,1,0:T(8,128)(2,1)S(1)}, bf16[3,1,52,384]{3,2,1,0:T(8,128)(2,1)}, u32[]{:S(2)}) copy-start(bf16[3,1,52,384]{3,2,1,0:T(8,128)(2,1)} %param.15) | copy-start | bytes 359428
  7.2 7.5 %copy-start.9 = (f32[384]{0:T(512)S(1)}, f32[384]{0:T(512)}, u32[]{:S(2)}) copy-start(f32[384]{0:T(512)} %param.17) | copy-start | bytes 4612
  7.2 188.2 %all-reduce.3.cloned.1.call-start = ((), (), s32[]{:S(2)}) async-start(), calls=%async_computation | async-start | bytes 5242880 | tf_op jit(solution)/shard_map/psum | solution.py:14
  10.3 19.2 %collective-permute-start.3 = (bf16[2,256,2560]{1,2,0:T(8,128)(2,1)S(1)}, bf16[2,256,2560]{1,2,0:T(8,128)(2,1)}, u32[]{:S(2)}, u32[]{:S(2)}) collective-permute-start(bf16[2,256,2560]{1,2,0:T(8,128)(2,1)S(1)} %copy.23), channel_id=1, source_target_pairs={{3,6},{7,10},{11,14},{15,2},{19,22},{23,26},{27,30},{31,18}} | collective-permute-start | bytes 7864328 | tf_op jit(solution)/shard_map/ppermute | solution.py:31
  12.4 18.4 %collective-permute-start.5 = (bf16[2,256,2560]{1,2,0:T(8,128)(2,1)S(1)}, bf16[2,256,2560]{1,2,0:T(8,128)(2,1)}, u32[]{:S(2)}, u32[]{:S(2)}) collective-permute-start(bf16[2,256,2560]{1,2,0:T(8,128)(2,1)S(1)} %copy.23), channel_id=1, source_target_pairs={{2,1},{6,5},{10,9},{14,13},{18,17},{22,21},{26,25},{30,29}} | collective-permute-start | bytes 7864328 | tf_op jit(solution)/shard_map/ppermute | solution.py:31
  15.6 30.5 %collective-permute-start.10 = (bf16[5,1,52,384]{3,2,0,1:T(8,128)(2,1)}, bf16[5,1,52,384]{3,2,0,1:T(8,128)(2,1)}, u32[]{:S(2)}, u32[]{:S(2)}) collective-permute-start(bf16[5,1,52,384]{3,2,0,1:T(8,128)(2,1)} %pad_maximum_fusion.2), channel_id=1, source_target_pairs={{1,0},{2,1},{3,2},{4,3},{5,4},{6,5},{7,6},{8,7},{9,8},{10,9},{11,1... | collective-permute-start | bytes 599048 | tf_op jit(solution)/shard_map/ppermute | solution.py:25
  16.9 48.0 %collective-permute-start.9 = (bf16[5,1,52,384]{3,2,0,1:T(8,128)(2,1)}, bf16[5,1,52,384]{3,2,0,1:T(8,128)(2,1)}, u32[]{:S(2)}, u32[]{:S(2)}) collective-permute-start(bf16[5,1,52,384]{3,2,0,1:T(8,128)(2,1)} %pad_maximum_fusion.2), channel_id=1, source_target_pairs={{0,1},{1,2},{2,3},{3,4},{4,5},{5,6},{6,7},{7,8},{8,9},{9,10},{10,1... | collective-permute-start | bytes 599048 | tf_op jit(solution)/shard_map/ppermute | solution.py:22
  20.6 90.0 %collective-permute-start.1 = (bf16[2,256,2560]{1,2,0:T(8,128)(2,1)S(1)}, bf16[2,256,2560]{1,2,0:T(8,128)(2,1)}, u32[]{:S(2)}, u32[]{:S(2)}) collective-permute-start(bf16[2,256,2560]{1,2,0:T(8,128)(2,1)S(1)} %copy.23), channel_id=1, source_target_pairs={{0,2},{4,6},{8,10},{12,14},{1,3},{5,7},{9,11},{13,15},{16,18},{20,... | collective-permute-start | bytes 7864328 | tf_op jit(solution)/shard_map/ppermute | solution.py:31
  29.4 57.0 %collective-permute-start.4 = (bf16[2,256,2560]{1,2,0:T(8,128)(2,1)}, bf16[2,256,2560]{1,2,0:T(8,128)(2,1)}, u32[]{:S(2)}, u32[]{:S(2)}) collective-permute-start(bf16[2,256,2560]{1,2,0:T(8,128)(2,1)} %collective-permute-done.3), channel_id=1, source_target_pairs={{2,0},{6,4},{10,8},{14,12},{18,16},{22,20},{26,24},{30,28}} | collective-permute-start | bytes 7864328 | tf_op jit(solution)/shard_map/ppermute | solution.py:31
  30.8 69.1 %collective-permute-start.6 = (bf16[2,256,2560]{1,2,0:T(8,128)(2,1)}, bf16[2,256,2560]{1,2,0:T(8,128)(2,1)}, u32[]{:S(2)}, u32[]{:S(2)}) collective-permute-start(bf16[2,256,2560]{1,2,0:T(8,128)(2,1)} %collective-permute-done.5), channel_id=1, source_target_pairs={{1,4},{5,8},{9,12},{13,0},{17,20},{21,24},{25,28},{29,16}} | collective-permute-start | bytes 7864328 | tf_op jit(solution)/shard_map/ppermute | solution.py:31
  33.7 3.9 %copy-start.11 = (s32[16,3]{0,1:T(4,128)S(1)}, s32[16,3]{0,1:T(4,128)}, u32[]{:S(2)}) copy-start(s32[16,3]{0,1:T(4,128)} %param.13) | copy-start | bytes 580
  33.8 8.5 %copy-start.8 = (s32[16]{0:T(128)S(1)}, s32[16]{0:T(128)}, u32[]{:S(2)}) copy-start(s32[16]{0:T(128)} %param.14) | copy-start | bytes 196
  46.1 71.8 %collective-permute-start = (bf16[2,256,2560]{1,2,0:T(8,128)(2,1)S(1)}, bf16[2,256,2560]{1,2,0:T(8,128)(2,1)S(1)}, u32[]{:S(2)}, u32[]{:S(2)}) collective-permute-start(bf16[2,256,2560]{1,2,0:T(8,128)(2,1)S(1)} %copy.23), channel_id=1, source_target_pairs={{0,1},{4,5},{8,9},{12,13},{2,3},{6,7},{10,11},{14,15},{16,17},{20,... | collective-permute-start | bytes 7864328 | tf_op jit(solution)/shard_map/ppermute | solution.py:31
  64.9 63.1 %collective-permute-start.8 = (bf16[2,256,2560]{1,2,0:T(8,128)(2,1)S(1)}, bf16[2,256,2560]{1,2,0:T(8,128)(2,1)}, u32[]{:S(2)}, u32[]{:S(2)}) collective-permute-start(bf16[2,256,2560]{1,2,0:T(8,128)(2,1)S(1)} %copy.23), channel_id=1, source_target_pairs={{1,4},{5,8},{9,12},{13,0},{17,20},{21,24},{25,28},{29,16}} | collective-permute-start | bytes 7864328 | tf_op jit(solution)/shard_map/ppermute | solution.py:31
  99.9 15.2 %slice-start = ((s8[7962624]{0:T(1024)(128)(4,1)}), s8[4194304]{0:T(1024)(128)(4,1)S(1)}, s32[]{:S(2)}) async-start(s8[7962624]{0:T(1024)(128)(4,1)} %bitcast.174), calls=%async_computation.1 | async-start | bytes 8388608
  99.9 15.2 %slice-start.1 = ((s8[7962624]{0:T(1024)(128)(4,1)}), s8[3768320]{0:T(1024)(128)(4,1)S(1)}, s32[]{:S(2)}) async-start(s8[7962624]{0:T(1024)(128)(4,1)} %bitcast.174), calls=%async_computation.2 | async-start | bytes 7536640
  105.7 8.2 %copy-start.5 = (bf16[3,1,52,384]{3,2,1,0:T(8,128)(2,1)S(1)}, bf16[3,1,52,384]{3,2,1,0:T(8,128)(2,1)}, u32[]{:S(2)}) copy-start(bf16[3,1,52,384]{3,2,1,0:T(8,128)(2,1)} %param.15) | copy-start | bytes 359428
  105.7 22.3 %collective-permute-start.7 = (bf16[2,2,256,2560]{2,3,1,0:T(8,128)(2,1)}, bf16[2,2,256,2560]{2,3,1,0:T(8,128)(2,1)S(1)}, u32[]{:S(2)}, u32[]{:S(2)}) collective-permute-start(bf16[2,2,256,2560]{2,3,1,0:T(8,128)(2,1)} %pad_maximum_fusion.1), channel_id=1, source_target_pairs={{0,1},{4,5},{8,9},{12,13},{16,17},{20,21},{24,25},{28,29}} | collective-permute-start | bytes 15728648 | tf_op jit(solution)/shard_map/ppermute | solution.py:31
  107.4 7.7 %copy-start.10 = (f32[384]{0:T(512)S(1)}, f32[384]{0:T(512)}, u32[]{:S(2)}) copy-start(f32[384]{0:T(512)} %param.19) | copy-start | bytes 4612
  110.6 17.4 %collective-permute-start.2 = (bf16[2,256,2560]{1,2,0:T(8,128)(2,1)}, bf16[2,256,2560]{1,2,0:T(8,128)(2,1)}, u32[]{:S(2)}, u32[]{:S(2)}) collective-permute-start(bf16[2,256,2560]{1,2,0:T(8,128)(2,1)} %collective-permute-done.1), channel_id=1, source_target_pairs={{3,2},{7,6},{11,10},{15,14},{2,3},{6,7},{10,11},{14,15},{19,18},{2... | collective-permute-start | bytes 7864328 | tf_op jit(solution)/shard_map/ppermute | solution.py:31
  138.3 1.6 copy-start
  146.1 5.9 %copy-start.2 = (bf16[1,1024,1280]{1,2,0:T(8,128)(2,1)S(1)}, bf16[1,1024,1280]{1,2,0:T(8,128)(2,1)}, u32[]{:S(2)}) copy-start(bf16[1,1024,1280]{1,2,0:T(8,128)(2,1)} %get-tuple-element.26) | copy-start | bytes 7864324
  198.1 1.1 copy-start.1
  199.2 2.8 %copy-start.13 = (f32[10,256,128]{2,1,0:T(8,128)S(1)}, f32[10,256,128]{2,1,0:T(8,128)}, u32[]{:S(2)}) copy-start(f32[10,256,128]{2,1,0:T(8,128)} %fusion.8) | copy-start | bytes 3932164
  202.0 3.7 %copy-start.3 = (f32[10,256,256]{2,1,0:T(8,128)S(1)}, f32[10,256,256]{2,1,0:T(8,128)}, u32[]{:S(2)}) copy-start(f32[10,256,256]{2,1,0:T(8,128)} %get-tuple-element.54) | copy-start | bytes 7864324
  205.6 1.1 copy-start.6
  205.6 1.5 copy-start.12
Sparse Core Ops, SparseCore 0:
  33.8 161.4 all-reduce.2

commit v4 on v3

--- a/solution.py
+++ b/solution.py
@@ -90,8 +90,11 @@
     position = (place - anchor - 1) % devices
     tok_rows = queries.shape[0]
     row_ids = jnp.arange(tok_rows, dtype=jnp.int32)
-    anchor_kv = spread(keys_values, "span", anchor)
-    b1, b2, b3 = window_blocks(keys_values, devices)
+    is_anchor = place == anchor
+    masked = jnp.where(is_anchor, keys_values, jnp.zeros_like(keys_values))
+    anchor_kv = lax.psum(masked, "span")
+    sent = jnp.where(is_anchor, lax.optimization_barrier(masked), keys_values)
+    b1, b2, b3 = window_blocks(sent, devices)
     blocks = [keys_values, b1, b2, b3]
     valid_list = [row_ids < lengths[place]]
     for offset in range(1, WIN):

time: 220 us -> 221 us (level)
  waiting for transfers between devices: 69.7 us -> 18 us
  starting transfers between devices: 44.1 us -> 95.3 us
    ppermute x1, starting transfers between devices: 3.73 us -> 36.1 us  [extended_2(): lax.ppermute(lax.slice_in_dim(block, block.shape[dim] - width, None, axis...]
    psum x1, waiting for transfers between devices: 28.3 us -> 0.02 us  [shards(): anchor_kv = lax.psum(masked, 'span')]
    ppermute x9, waiting for transfers between devices: 41.4 us -> 17.9 us  [move(): return lax.ppermute(value, 'span', pairs)]
    ppermute x9, starting transfers between devices: 39 us -> 57.9 us  [move(): return lax.ppermute(value, 'span', pairs)]
    unnamed x60 -> x58, local copies, waits for them, and re-layouts: 15.5 us -> 15.3 us
  transfers between devices with their start and end apart: 12 -> 12, of which waited for: 4 -> 1; matrix products, arithmetic and copies ran while one was open for 31% -> 30% of each run, Pallas kernels for 0% -> 0%
where the time goes in v4:
time: 221 us; the launch traced here: 220 us
  starting transfers between devices  95.3 us (43%)
  matrix products  32.2 us (15%)
  other arithmetic  30.2 us (14%)
  local copies, waits for them, and re-layouts  27.4 us (12%)
  waiting for transfers between devices  18 us (8%)
  between operations  17.1 us (8%)
    ppermute x9, starting transfers between devices, move(): return lax.ppermute(value, 'span', pairs)  57.9 us
    ppermute x1, starting transfers between devices, extended_2(): lax.ppermute(lax.slice_in_dim(block, block.shape[dim] - width, None, axis...  36.1 us
    dot_general x4, matrix products, weighted(): jnp.einsum('hqk,khd->hqd', weights.astype(jnp.bfloat16), values, preferre...  19.7 us
    ppermute x9, waiting for transfers between devices, move(): return lax.ppermute(value, 'span', pairs)  17.9 us
    unnamed x58, local copies, waits for them, and re-layouts  15.3 us
    dot_general x4, matrix products, part_stats(): jnp.einsum('qhd,khd->hqk', q, k, preferred_element_type=jnp.float32) * scale  9.69 us
    reduce_sum x1, other arithmetic, shards(): w_sum = jnp.sum(w_exp, axis=-1, keepdims=True)  7.09 us
    another operation x1, other arithmetic, window_blocks(): pair = move(jnp.stack([down2, rail0b]), [(at(r, 0), at(r, 1)) for r in rng])  5.83 us
  transfers between devices with their start and end apart: 12, of which 1 were waited for; matrix products, arithmetic and copies ran while one was open for 30% of the time, Pallas kernels for 0%

profile of v4, /device:TPU:0, one launch (start us, length us, event | category | flops | bytes accessed | tf_op | source)
XLA Modules:
  0.0 220.1 jit_solution(4187726682689938500)
XLA Ops:
  7.2 3.0 %copy.23 = bf16[2,256,2560]{1,2,0:T(8,128)(2,1)S(1)} copy(bf16[2,256,2560]{2,1,0:T(8,128)(2,1)} %param.11) | data formatting | bytes 5242880 | tf_op args[1]
  10.8 1.7 broadcast_select_fusion.1
  12.5 1.7 broadcast_select_fusion
  14.3 2.3 %collective-permute-start.5 = (bf16[2,256,2560]{1,2,0:T(8,128)(2,1)}, bf16[2,256,2560]{1,2,0:T(8,128)(2,1)}, u32[]{:S(2)}, u32[]{:S(2)}) collective-permute-start(bf16[2,256,2560]{1,2,0:T(8,128)(2,1)} %broadcast_select_fusion), channel_id=1, source_target_pairs={{2,1},{6,5},{10,9},{14,13},{18,17},{22,21},{26,25},{30,29}} | collective-permute-start | bytes 7864328 | tf_op jit(solution)/shard_map/ppermute | solution.py:31
  16.6 2.2 %collective-permute-start.3 = (bf16[2,256,2560]{1,2,0:T(8,128)(2,1)}, bf16[2,256,2560]{1,2,0:T(8,128)(2,1)}, u32[]{:S(2)}, u32[]{:S(2)}) collective-permute-start(bf16[2,256,2560]{1,2,0:T(8,128)(2,1)} %broadcast_select_fusion), channel_id=1, source_target_pairs={{3,6},{7,10},{11,14},{15,2},{19,22},{23,26},{27,30},{31,18}} | collective-permute-start | bytes 7864328 | tf_op jit(solution)/shard_map/ppermute | solution.py:31
  18.9 7.8 %collective-permute-start.1 = (bf16[2,256,2560]{1,2,0:T(8,128)(2,1)}, bf16[2,256,2560]{1,2,0:T(8,128)(2,1)}, u32[]{:S(2)}, u32[]{:S(2)}) collective-permute-start(bf16[2,256,2560]{1,2,0:T(8,128)(2,1)} %broadcast_select_fusion), channel_id=1, source_target_pairs={{0,2},{4,6},{8,10},{12,14},{1,3},{5,7},{9,11},{13,15},{16,18},{20,... | collective-permute-start | bytes 7864328 | tf_op jit(solution)/shard_map/ppermute | solution.py:31
  26.8 1.3 collective-permute-start.6
  28.1 1.3 collective-permute-start.4
  29.6 0.7 pad_maximum_fusion.2
  30.4 1.3 collective-permute-start.10
  31.6 36.1 %collective-permute-start.9 = (bf16[5,1,52,384]{3,2,0,1:T(8,128)(2,1)}, bf16[5,1,52,384]{3,2,0,1:T(8,128)(2,1)}, u32[]{:S(2)}, u32[]{:S(2)}) collective-permute-start(bf16[5,1,52,384]{3,2,0,1:T(8,128)(2,1)} %pad_maximum_fusion.2), channel_id=1, source_target_pairs={{0,1},{1,2},{2,3},{3,4},{4,5},{5,6},{6,7},{7,8},{8,9},{9,10},{10,1... | collective-permute-start | bytes 599048 | tf_op jit(solution)/shard_map/ppermute | solution.py:22
  70.3 2.4 %fusion.89 = (bf16[256,1280]{1,0:T(8,128)(2,1)}, bf16[256,1280]{1,0:T(8,128)(2,1)}) fusion(bf16[256,2560]{1,0:T(8,128)(2,1)} %param.10), kind=kLoop, calls=%fused_computation.153 | loop fusion | bytes 2621440 | tf_op jit(solution)/shard_map/slice | solution.py:112
  72.7 1.3 copy.66
  74.0 2.2 copy.67
  76.2 0.7 fusion.90
  76.9 1.2 compare_and_fusion.3
  78.1 1.3 compare_and_fusion.1
  80.1 1.3 collective-permute-start.8
  81.4 37.8 %collective-permute-start = (bf16[2,256,2560]{1,2,0:T(8,128)(2,1)}, bf16[2,256,2560]{1,2,0:T(8,128)(2,1)}, u32[]{:S(2)}, u32[]{:S(2)}) collective-permute-start(bf16[2,256,2560]{1,2,0:T(8,128)(2,1)} %broadcast_select_fusion), channel_id=1, source_target_pairs={{0,1},{4,5},{8,9},{12,13},{2,3},{6,7},{10,11},{14,15},{16,17},{20,... | collective-permute-start | bytes 7864328 | tf_op jit(solution)/shard_map/ppermute | solution.py:31
  119.2 1.3 select_maximum_fusion
  120.6 0.9 slice_dynamic-update-slice_fusion.22
  121.7 5.8 %pad_maximum_fusion.1 = bf16[2,2,256,2560]{2,3,1,0:T(8,128)(2,1)} fusion(bf16[1,2,256,2560]{2,3,1,0:T(8,128)(2,1)} %bitcast.9, bf16[1,2,256,2560]{2,3,1,0:T(8,128)(2,1)} %bitcast.8), kind=kLoop, calls=%fused_computation.15 | loop fusion | flops 2621440 | bytes 10485760 | tf_op jit(solution)/shard_map/stack | solution.py:50
  127.5 1.7 collective-permute-start.7
  129.3 0.9 slice_dynamic-update-slice_fusion.17
  130.3 0.9 slice_dynamic-update-slice_fusion.14
  131.5 0.9 slice_dynamic-update-slice_fusion.9
  132.5 2.1 collective-permute-start.2
  134.6 0.9 slice_dynamic-update-slice_fusion.6
  135.9 0.9 slice_dynamic-update-slice_fusion.1
  136.9 2.8 %fusion.55 = bf16[3,1,52,384]{3,2,1,0:T(8,128)(2,1)} fusion(bf16[10368,384,1]{1,0,2:T(8,128)(2,1)S(1)} %bitcast.176, bf16[3,1,52,10368]{3,2,0,1:T(8,128)(2,1)S(1)} %slice_dynamic-update-slice_fusion, bf16[3,1,52,384]{3,2,1,0:T(8,128)(2,1)S(1)} %copy-done.6, f32[384]{0:T(512)S(1)} %copy-done.10), kind=kOutput, calls=%fused_computation.70 | convolution fusion | flops 1242408960 | bytes 11438592 | tf_op jit(solution)/shard_map/dot_general | solution.py:162
  139.7 17.9 %collective-permute-done.8 = bf16[2,256,2560]{1,2,0:T(8,128)(2,1)S(1)} collective-permute-done((bf16[2,256,2560]{1,2,0:T(8,128)(2,1)}, bf16[2,256,2560]{1,2,0:T(8,128)(2,1)S(1)}, u32[]{:S(2)}, u32[]{:S(2)}) %collective-permute-start.8) | collective-permute-done | bytes 2621472 | tf_op jit(solution)/shard_map/ppermute | solution.py:31
  157.6 5.7 %select_select_fusion = (bf16[2,256,2560]{1,2,0:T(8,128)(2,1)S(1)}, bf16[2,256,2560]{1,2,0:T(8,128)(2,1)S(1)}, bf16[2,256,2560]{1,2,0:T(8,128)(2,1)S(1)}) fusion(bf16[2,256,2560]{1,2,0:T(8,128)(2,1)} %collective-permute-done.1, bf16[2,256,2560]{1,2,0:T(8,128)(2,1)} %collective-permute-done.6, bf16[2,2,256,2560]{2,3,1,0:T(8,128)(2,1)S(1)} %collective-permute-done.7, ...), kind=kLoop, calls=%fused_computation.24 | loop fusion | flops 11796480 | bytes 31457284 | tf_op jit(solution)/shard_map/jit(_where)/select_n | solution.py:55
  163.3 1.5 pad_maximum_fusion
  164.8 2.9 %fusion.87 = (bf16[1,1024,1280]{1,2,0:T(8,128)(2,1)}, bf16[1,1024,1280]{1,2,0:T(8,128)(2,1)S(1)}, bf16[1,1024,1280]{1,2,0:T(8,128)(2,1)}, bf16[1,1024,1280]{1,2,0:T(8,128)(2,1)S(1)}) fusion(bf16[2,1024,2560]{1,2,0:T(8,128)(2,1)S(1)} %pad_maximum_fusion), kind=kLoop, calls=%fused_computation.151 | loop fusion | bytes 20971520 | tf_op jit(solution)/shard_map/slice | solution.py:114
  167.7 1.6 fusion.91
  169.3 6.2 %bitcast_reduce_fusion = (f32[10,256]{1,0:T(8,128)S(1)}, f32[10,256]{1,0:T(8,128)S(1)}, f32[10,1024,256]{2,1,0:T(8,128)}) fusion(pred[1024]{0:T(1024)(128)(4,1)S(1)} %pad_add_fusion, f32[10,1024,256]{2,1,0:T(8,128)S(1)} %fusion.91, bf16[1024,10,128]{0,2,1:T(8,128)(2,1)S(1)} %bitcast.177, bf16[256,10,128]{0,2,1:T(8,128)(2,1)S(1)} %bitcast.181), kind=kOutput, calls=%fused_computation.2 | convolution fusion | flops 686812160 | bytes 24269824 | tf_op jit(solution)/shard_map/qhd,khd->hqk/dot_general | solution.py:65
  175.5 5.9 %fusion.8 = f32[10,256,128]{2,1,0:T(8,128)} fusion(bf16[1024,10,128]{0,2,1:T(8,128)(2,1)} %bitcast.184, f32[10,1024,256]{2,1,0:T(8,128)S(1)} %fusion.91, f32[10,256]{1,0:T(8,128)S(1)} %get-tuple-element.23, pred[1024]{0:T(1024)(128)(4,1)S(1)} %pad_add_fusion), kind=kOutput, calls=%fused_computation.14 | convolution fusion | flops 681574400 | bytes 14429184 | tf_op jit(solution)/shard_map/hqk,khd->hqd/dot_general | solution.py:70
  181.4 7.9 %fusion.6 = f32[10,256,128]{2,1,0:T(8,128)} fusion(bf16[1024,10,128]{0,2,1:T(8,128)(2,1)S(1)} %bitcast.183, f32[10,1024,256]{2,1,0:T(8,128)} %get-tuple-element.51, f32[10,256]{1,0:T(8,128)S(1)} %get-tuple-element.22, pred[1024]{0:T(1024)(128)(4,1)S(1)} %pad_add_fusion), kind=kOutput, calls=%fused_computation.13 | convolution fusion | flops 681574400 | bytes 14429184 | tf_op jit(solution)/shard_map/hqk,khd->hqd/dot_general | solution.py:70
  189.3 7.1 %fusion.5 = (f32[10,256]{1,0:T(8,128)S(1)}, f32[10,256]{1,0:T(8,128)S(1)}) fusion(f32[10,1024,256]{2,1,0:T(8,128)} %get-tuple-element.51, f32[10,256]{1,0:T(8,128)S(1)} %get-tuple-element.22, pred[1024]{0:T(1024)(128)(4,1)S(1)} %pad_add_fusion, f32[10,256]{1,0:T(8,128)S(1)} %get-tuple-element.23, f32[10,1024,256]{2,1,0:T(8,128)S(1)} %fusion.91), kind=kLoop, calls=%fused_computation.12 | loop fusion | flops 20966400 | bytes 21013504 | tf_op jit(solution)/shard_map/reduce_sum | solution.py:118
  196.4 2.7 %fusion.88 = (bf16[1,256,1280]{1,2,0:T(8,128)(2,1)}, bf16[1,256,1280]{1,2,0:T(8,128)(2,1)S(1)}, bf16[1,256,1280]{1,2,0:T(8,128)(2,1)S(1)}, bf16[1,256,1280]{1,2,0:T(8,128)(2,1)S(1)}) fusion(bf16[2,256,2560]{1,2,0:T(8,128)(2,1)} %all-reduce.3.cloned.1.call-done), kind=kLoop, calls=%fused_computation.152 | loop fusion | bytes 5242880 | tf_op jit(solution)/shard_map/slice | solution.py:127
  199.2 0.7 bitcast_reduce_fusion.3
  200.2 1.3 fusion.27
  202.2 0.7 copy-done.12
  202.9 2.3 %fusion.34 = bf16[256,10,128]{2,0,1:T(8,128)(2,1)} fusion(bf16[256,10,128]{0,2,1:T(8,128)(2,1)S(1)} %bitcast.189, f32[10,256,256]{2,1,0:T(8,128)S(1)} %get-tuple-element.54, f32[10,256]{1,0:T(8,128)S(1)} %fusion.76, f32[10,256,128]{2,1,0:T(8,128)S(1)} %copy-done.12, pred[256]{0:T(512)(128)(4,1)S(1)} %compare_and_fusion, ...), kind=kOutput, calls=%fused_computation.57 | convolution fusion | flops 171704320 | bytes 5273856 | tf_op jit(solution)/shard_map/hqk,khd->hqd/dot_general | solution.py:70
  205.1 1.3 copy.45
  206.5 3.6 %fusion.32 = bf16[256,10,128]{2,0,1:T(8,128)(2,1)} fusion(bf16[256,10,128]{0,2,1:T(8,128)(2,1)} %bitcast.188, f32[10,256,256]{2,1,0:T(8,128)S(1)} %copy-done.4, f32[10,256]{1,0:T(8,128)S(1)} %fusion.75, f32[10,256,128]{2,1,0:T(8,128)} %fusion.8, pred[256]{0:T(512)(128)(4,1)S(1)} %compare_and_fusion, f32[10,256]{1,0:T(8,128)S(1)} %get-tuple-element.40, ...), kind=kOutput, calls=%fused_computation.55 | convolution fusion | flops 171704320 | bytes 5273856 | tf_op jit(solution)/shard_map/hqk,khd->hqd/dot_general | solution.py:70
  210.1 1.3 copy.40
  211.7 1.6 copy.48
  (77 shorter events, 3.9 us)
Async XLA Ops:
  14.3 12.4 %copy-start.5 = (bf16[3,1,52,384]{3,2,1,0:T(8,128)(2,1)S(1)}, bf16[3,1,52,384]{3,2,1,0:T(8,128)(2,1)}, u32[]{:S(2)}) copy-start(bf16[3,1,52,384]{3,2,1,0:T(8,128)(2,1)} %param.15) | copy-start | bytes 359428
  14.3 15.2 %copy-start.9 = (f32[384]{0:T(512)S(1)}, f32[384]{0:T(512)}, u32[]{:S(2)}) copy-start(f32[384]{0:T(512)} %param.17) | copy-start | bytes 4612
  14.3 15.3 %copy-start.7 = (bf16[2,1,52,384]{3,0,2,1:T(2,128)(2,1)S(1)}, bf16[2,1,52,384]{3,0,2,1:T(2,128)(2,1)}, u32[]{:S(2)}) copy-start(bf16[2,1,52,384]{3,0,2,1:T(2,128)(2,1)} %param.16) | copy-start | bytes 239620
  14.3 53.4 %copy-start.11 = (s32[16,3]{0,1:T(4,128)S(1)}, s32[16,3]{0,1:T(4,128)}, u32[]{:S(2)}) copy-start(s32[16,3]{0,1:T(4,128)} %param.13) | copy-start | bytes 580
  14.3 182.1 %all-reduce.3.cloned.1.call-start = ((), (), s32[]{:S(2)}) async-start(), calls=%async_computation | async-start | bytes 5242880 | tf_op jit(solution)/shard_map/psum | solution.py:95
  14.3 12.5 %collective-permute-start.5 = (bf16[2,256,2560]{1,2,0:T(8,128)(2,1)}, bf16[2,256,2560]{1,2,0:T(8,128)(2,1)}, u32[]{:S(2)}, u32[]{:S(2)}) collective-permute-start(bf16[2,256,2560]{1,2,0:T(8,128)(2,1)} %broadcast_select_fusion), channel_id=1, source_target_pairs={{2,1},{6,5},{10,9},{14,13},{18,17},{22,21},{26,25},{30,29}} | collective-permute-start | bytes 7864328 | tf_op jit(solution)/shard_map/ppermute | solution.py:31
  16.6 11.5 %collective-permute-start.3 = (bf16[2,256,2560]{1,2,0:T(8,128)(2,1)}, bf16[2,256,2560]{1,2,0:T(8,128)(2,1)}, u32[]{:S(2)}, u32[]{:S(2)}) collective-permute-start(bf16[2,256,2560]{1,2,0:T(8,128)(2,1)} %broadcast_select_fusion), channel_id=1, source_target_pairs={{3,6},{7,10},{11,14},{15,2},{19,22},{23,26},{27,30},{31,18}} | collective-permute-start | bytes 7864328 | tf_op jit(solution)/shard_map/ppermute | solution.py:31
  18.9 113.6 %collective-permute-start.1 = (bf16[2,256,2560]{1,2,0:T(8,128)(2,1)}, bf16[2,256,2560]{1,2,0:T(8,128)(2,1)}, u32[]{:S(2)}, u32[]{:S(2)}) collective-permute-start(bf16[2,256,2560]{1,2,0:T(8,128)(2,1)} %broadcast_select_fusion), channel_id=1, source_target_pairs={{0,2},{4,6},{8,10},{12,14},{1,3},{5,7},{9,11},{13,15},{16,18},{20,... | collective-permute-start | bytes 7864328 | tf_op jit(solution)/shard_map/ppermute | solution.py:31
  26.8 94.8 %collective-permute-start.6 = (bf16[2,256,2560]{1,2,0:T(8,128)(2,1)}, bf16[2,256,2560]{1,2,0:T(8,128)(2,1)}, u32[]{:S(2)}, u32[]{:S(2)}) collective-permute-start(bf16[2,256,2560]{1,2,0:T(8,128)(2,1)} %collective-permute-done.5), channel_id=1, source_target_pairs={{1,4},{5,8},{9,12},{13,0},{17,20},{21,24},{25,28},{29,16}} | collective-permute-start | bytes 7864328 | tf_op jit(solution)/shard_map/ppermute | solution.py:31
  28.1 93.5 %collective-permute-start.4 = (bf16[2,256,2560]{1,2,0:T(8,128)(2,1)}, bf16[2,256,2560]{1,2,0:T(8,128)(2,1)}, u32[]{:S(2)}, u32[]{:S(2)}) collective-permute-start(bf16[2,256,2560]{1,2,0:T(8,128)(2,1)} %collective-permute-done.3), channel_id=1, source_target_pairs={{2,0},{6,4},{10,8},{14,12},{18,16},{22,20},{26,24},{30,28}} | collective-permute-start | bytes 7864328 | tf_op jit(solution)/shard_map/ppermute | solution.py:31
  30.4 49.7 %collective-permute-start.10 = (bf16[5,1,52,384]{3,2,0,1:T(8,128)(2,1)}, bf16[5,1,52,384]{3,2,0,1:T(8,128)(2,1)}, u32[]{:S(2)}, u32[]{:S(2)}) collective-permute-start(bf16[5,1,52,384]{3,2,0,1:T(8,128)(2,1)} %pad_maximum_fusion.2), channel_id=1, source_target_pairs={{1,0},{2,1},{3,2},{4,3},{5,4},{6,5},{7,6},{8,7},{9,8},{10,9},{11,1... | collective-permute-start | bytes 599048 | tf_op jit(solution)/shard_map/ppermute | solution.py:25
  31.6 49.7 %collective-permute-start.9 = (bf16[5,1,52,384]{3,2,0,1:T(8,128)(2,1)}, bf16[5,1,52,384]{3,2,0,1:T(8,128)(2,1)}, u32[]{:S(2)}, u32[]{:S(2)}) collective-permute-start(bf16[5,1,52,384]{3,2,0,1:T(8,128)(2,1)} %pad_maximum_fusion.2), channel_id=1, source_target_pairs={{0,1},{1,2},{2,3},{3,4},{4,5},{5,6},{6,7},{7,8},{8,9},{9,10},{10,1... | collective-permute-start | bytes 599048 | tf_op jit(solution)/shard_map/ppermute | solution.py:22
  70.3 6.0 %copy-start.8 = (s32[16]{0:T(128)S(1)}, s32[16]{0:T(128)}, u32[]{:S(2)}) copy-start(s32[16]{0:T(128)} %param.14) | copy-start | bytes 196
  80.1 77.5 %collective-permute-start.8 = (bf16[2,256,2560]{1,2,0:T(8,128)(2,1)}, bf16[2,256,2560]{1,2,0:T(8,128)(2,1)S(1)}, u32[]{:S(2)}, u32[]{:S(2)}) collective-permute-start(bf16[2,256,2560]{1,2,0:T(8,128)(2,1)} %broadcast_select_fusion), channel_id=1, source_target_pairs={{1,4},{5,8},{9,12},{13,0},{17,20},{21,24},{25,28},{29,16}} | collective-permute-start | bytes 7864328 | tf_op jit(solution)/shard_map/ppermute | solution.py:31
  81.4 76.2 %collective-permute-start = (bf16[2,256,2560]{1,2,0:T(8,128)(2,1)}, bf16[2,256,2560]{1,2,0:T(8,128)(2,1)}, u32[]{:S(2)}, u32[]{:S(2)}) collective-permute-start(bf16[2,256,2560]{1,2,0:T(8,128)(2,1)} %broadcast_select_fusion), channel_id=1, source_target_pairs={{0,1},{4,5},{8,9},{12,13},{2,3},{6,7},{10,11},{14,15},{16,17},{20,... | collective-permute-start | bytes 7864328 | tf_op jit(solution)/shard_map/ppermute | solution.py:31
  121.7 15.2 %slice-start = ((s8[7962624]{0:T(1024)(128)(4,1)}), s8[4194304]{0:T(1024)(128)(4,1)S(1)}, s32[]{:S(2)}) async-start(s8[7962624]{0:T(1024)(128)(4,1)} %bitcast.174), calls=%async_computation.1 | async-start | bytes 8388608
  121.7 15.2 %slice-start.1 = ((s8[7962624]{0:T(1024)(128)(4,1)}), s8[3768320]{0:T(1024)(128)(4,1)S(1)}, s32[]{:S(2)}) async-start(s8[7962624]{0:T(1024)(128)(4,1)} %bitcast.174), calls=%async_computation.2 | async-start | bytes 7536640
  127.5 8.1 %copy-start.6 = (bf16[3,1,52,384]{3,2,1,0:T(8,128)(2,1)S(1)}, bf16[3,1,52,384]{3,2,1,0:T(8,128)(2,1)}, u32[]{:S(2)}) copy-start(bf16[3,1,52,384]{3,2,1,0:T(8,128)(2,1)} %param.15) | copy-start | bytes 359428
  127.5 30.1 %collective-permute-start.7 = (bf16[2,2,256,2560]{2,3,1,0:T(8,128)(2,1)}, bf16[2,2,256,2560]{2,3,1,0:T(8,128)(2,1)S(1)}, u32[]{:S(2)}, u32[]{:S(2)}) collective-permute-start(bf16[2,2,256,2560]{2,3,1,0:T(8,128)(2,1)} %pad_maximum_fusion.1), channel_id=1, source_target_pairs={{0,1},{4,5},{8,9},{12,13},{16,17},{20,21},{24,25},{28,29}} | collective-permute-start | bytes 15728648 | tf_op jit(solution)/shard_map/ppermute | solution.py:31
  129.3 7.6 %copy-start.10 = (f32[384]{0:T(512)S(1)}, f32[384]{0:T(512)}, u32[]{:S(2)}) copy-start(f32[384]{0:T(512)} %param.19) | copy-start | bytes 4612
  132.5 25.1 %collective-permute-start.2 = (bf16[2,256,2560]{1,2,0:T(8,128)(2,1)}, bf16[2,256,2560]{1,2,0:T(8,128)(2,1)}, u32[]{:S(2)}, u32[]{:S(2)}) collective-permute-start(bf16[2,256,2560]{1,2,0:T(8,128)(2,1)} %collective-permute-done.1), channel_id=1, source_target_pairs={{3,2},{7,6},{11,10},{15,14},{2,3},{6,7},{10,11},{14,15},{19,18},{2... | collective-permute-start | bytes 7864328 | tf_op jit(solution)/shard_map/ppermute | solution.py:31
  167.7 1.6 copy-start
  175.5 5.9 %copy-start.2 = (bf16[1,1024,1280]{1,2,0:T(8,128)(2,1)S(1)}, bf16[1,1024,1280]{1,2,0:T(8,128)(2,1)}, u32[]{:S(2)}) copy-start(bf16[1,1024,1280]{1,2,0:T(8,128)(2,1)} %get-tuple-element.26) | copy-start | bytes 7864324
  199.2 1.1 copy-start.1
  199.8 1.7 copy-start.3
  201.5 1.3 copy-start.12
  202.9 3.6 %copy-start.4 = (f32[10,256,256]{2,1,0:T(8,128)S(1)}, f32[10,256,256]{2,1,0:T(8,128)}, u32[]{:S(2)}) copy-start(f32[10,256,256]{2,1,0:T(8,128)} %copy-done.3) | copy-start | bytes 7864324
Sparse Core Ops, SparseCore 0:
  19.0 117.7 all-reduce.2

commit v5 on v4

--- a/solution.py
+++ b/solution.py
@@ -38,16 +38,8 @@
     def at(r, l):
         return 4 * (r % rows) + l
 
-    rng = range(rows)
-    rail1 = move(kv, [(at(r, 3), at(r + 1, 2)) for r in rng])
-    rail0 = move(kv, [(at(r, 1), at(r + 1, 0)) for r in rng])
-    y_up = move(kv, [(at(r, 0), at(r, 2)) for r in rng] + [(at(r, 1), at(r, 3)) for r in rng])
-    y_down = move(kv, [(at(r, 2), at(r, 1)) for r in rng])
-    chip = move(kv, [(at(r, 0), at(r, 1)) for r in rng] + [(at(r, 2), at(r, 3)) for r in rng])
-    swap = move(y_up, [(at(r, 3), at(r, 2)) for r in rng] + [(at(r, 2), at(r, 3)) for r in rng])
-    down2 = move(rail1, [(at(r, 2), at(r, 0)) for r in rng])
-    rail0b = move(y_down, [(at(r, 1), at(r + 1, 0)) for r in rng])
-    pair = move(jnp.stack([down2, rail0b]), [(at(r, 0), at(r, 1)) for r in rng])
+    def pairs(*moves):
+        return [(at(r, a), at(r + step, b)) for a, b, step in moves for r in range(rows)]
 
     def pick(*options):
         out = options[0]
@@ -55,9 +47,13 @@
             out = jnp.where(lane == l, options[l], out)
         return out
 
-    b1 = pick(down2, chip, swap, chip)
-    b2 = pick(rail0b, pair[0], y_up, y_up)
-    b3 = pick(rail0, pair[1], rail1, swap)
+    cross = move(kv, pairs((0, 2, 0), (1, 3, 0), (2, 1, 0)))
+    along = move(kv, pairs((0, 1, 0), (2, 3, 0), (1, 0, 1), (3, 2, 1)))
+    second = move(pick(cross, cross, along, cross), pairs((3, 2, 0), (2, 0, 0), (1, 1, 1)))
+    third = move(pick(second, second, cross, cross), pairs((0, 1, 0), (1, 0, 0), (2, 3, 0)))
+    b1 = pick(second, along, second, along)
+    b2 = pick(third, third, cross, cross)
+    b3 = pick(along, second, along, third)
     return b1, b2, b3
 
 

time: 221 us -> 218 us (0.986)
  waiting for transfers between devices: 18 us -> 88.1 us
  starting transfers between devices: 95.3 us -> 25.6 us
  other arithmetic: 30.2 us -> 25.7 us
    ppermute x9 -> x4, waiting for transfers between devices: 17.9 us -> 87.4 us  [move(): return lax.ppermute(value, 'span', pairs)]
    ppermute x9 -> x4, starting transfers between devices: 57.9 us -> 19.4 us  [move(): return lax.ppermute(value, 'span', pairs)]
    ppermute x1, starting transfers between devices: 36.1 us -> 4.86 us  [extended_2(): lax.ppermute(lax.slice_in_dim(block, block.shape[dim] - width, None, axis...]
    another operation x1 -> x0, other arithmetic: 5.83 us -> none  [window_blocks(): pair = move(jnp.stack([down2, rail0b]), [(at(r, 0), at(r, 1)) for r in rng])]
    select_n x1 -> x3, other arithmetic: 5.71 us -> 7.08 us  [pick(): out = jnp.where(lane == l, options[l], out)]
    unnamed x58 -> x54, local copies, waits for them, and re-layouts: 15.3 us -> 15.3 us
  transfers between devices with their start and end apart: 12 -> 7, of which waited for: 1 -> 3; matrix products, arithmetic and copies ran while one was open for 30% -> 29% of each run, Pallas kernels for 0% -> 0%
where the time goes in v5:
time: 218 us; the launch traced here: 217 us
  waiting for transfers between devices  88.1 us (40%)
  matrix products  32.7 us (15%)
  local copies, waits for them, and re-layouts  27.4 us (13%)
  other arithmetic  25.7 us (12%)
  starting transfers between devices  25.6 us (12%)
  between operations  17.1 us (8%)
    ppermute x4, waiting for transfers between devices, move(): return lax.ppermute(value, 'span', pairs)  87.4 us
    dot_general x4, matrix products, weighted(): jnp.einsum('hqk,khd->hqd', weights.astype(jnp.bfloat16), values, preferre...  20.3 us
    ppermute x4, starting transfers between devices, move(): return lax.ppermute(value, 'span', pairs)  19.4 us
    unnamed x54, local copies, waits for them, and re-layouts  15.3 us
    dot_general x4, matrix products, part_stats(): jnp.einsum('qhd,khd->hqk', q, k, preferred_element_type=jnp.float32) * scale  9.68 us
    reduce_sum x1, other arithmetic, shards(): w_sum = jnp.sum(w_exp, axis=-1, keepdims=True)  7.09 us
    select_n x3, other arithmetic, pick(): out = jnp.where(lane == l, options[l], out)  7.08 us
    ppermute x1, starting transfers between devices, extended_2(): lax.ppermute(lax.slice_in_dim(block, block.shape[dim] - width, None, axis...  4.86 us
  transfers between devices with their start and end apart: 7, of which 3 were waited for; matrix products, arithmetic and copies ran while one was open for 29% of the time, Pallas kernels for 0%

profile of v5, /device:TPU:0, one launch (start us, length us, event | category | flops | bytes accessed | tf_op | source)
XLA Modules:
  0.0 216.7 jit_solution(12612084807676540960)
XLA Ops:
  7.2 3.0 %copy.23 = bf16[2,256,2560]{1,2,0:T(8,128)(2,1)S(1)} copy(bf16[2,256,2560]{2,1,0:T(8,128)(2,1)} %param.11) | data formatting | bytes 5242880 | tf_op args[1]
  10.8 1.6 broadcast_select_fusion.1
  12.4 1.8 broadcast_select_fusion
  14.3 0.7 all-reduce.3.cloned.1.call-update
  15.5 5.9 %collective-permute-start.1 = (bf16[2,256,2560]{1,2,0:T(8,128)(2,1)}, bf16[2,256,2560]{1,2,0:T(8,128)(2,1)}, u32[]{:S(2)}, u32[]{:S(2)}) collective-permute-start(bf16[2,256,2560]{1,2,0:T(8,128)(2,1)} %broadcast_select_fusion), channel_id=1, source_target_pairs={{0,2},{4,6},{8,10},{12,14},{1,3},{5,7},{9,11},{13,15},{2,1},{6,5},... | collective-permute-start | bytes 7864328 | tf_op jit(solution)/shard_map/ppermute | solution.py:31
  21.7 0.7 pad_maximum_fusion.1
  22.5 1.3 collective-permute-start.5
  23.7 4.9 %collective-permute-start.4 = (bf16[5,1,52,384]{3,2,0,1:T(8,128)(2,1)}, bf16[5,1,52,384]{3,2,0,1:T(8,128)(2,1)}, u32[]{:S(2)}, u32[]{:S(2)}) collective-permute-start(bf16[5,1,52,384]{3,2,0,1:T(8,128)(2,1)} %pad_maximum_fusion.1), channel_id=1, source_target_pairs={{0,1},{1,2},{2,3},{3,4},{4,5},{5,6},{6,7},{7,8},{8,9},{9,10},{10,1... | collective-permute-start | bytes 599048 | tf_op jit(solution)/shard_map/ppermute | solution.py:22
  28.6 0.7 constant_dynamic-slice_fusion.2
  31.3 2.5 %fusion.87 = (bf16[256,1280]{1,0:T(8,128)(2,1)}, bf16[256,1280]{1,0:T(8,128)(2,1)}) fusion(bf16[256,2560]{1,0:T(8,128)(2,1)} %param.10), kind=kLoop, calls=%fused_computation.151 | loop fusion | bytes 2621440 | tf_op jit(solution)/shard_map/slice | solution.py:108
  33.8 1.3 copy.66
  35.1 2.2 copy.67
  37.3 0.7 fusion.88
  37.9 1.3 compare_and_fusion.3
  39.2 1.4 compare_and_fusion.1
  40.6 0.7 compare_and_fusion
  41.3 1.3 select_maximum_fusion
  42.6 0.9 slice_dynamic-update-slice_fusion.22
  43.7 24.4 %collective-permute-done = bf16[2,256,2560]{1,2,0:T(8,128)(2,1)} collective-permute-done((bf16[2,256,2560]{1,2,0:T(8,128)(2,1)}, bf16[2,256,2560]{1,2,0:T(8,128)(2,1)}, u32[]{:S(2)}, u32[]{:S(2)}) %collective-permute-start) | collective-permute-done | bytes 2621472 | tf_op jit(solution)/shard_map/ppermute | solution.py:31
  68.0 18.5 %collective-permute-done.1 = bf16[2,256,2560]{1,2,0:T(8,128)(2,1)} collective-permute-done((bf16[2,256,2560]{1,2,0:T(8,128)(2,1)}, bf16[2,256,2560]{1,2,0:T(8,128)(2,1)}, u32[]{:S(2)}, u32[]{:S(2)}) %collective-permute-start.1) | collective-permute-done | bytes 2621472 | tf_op jit(solution)/shard_map/ppermute | solution.py:31
  86.6 2.2 select_select_fusion.4
  88.8 1.3 collective-permute-start.2
  90.1 0.9 slice_dynamic-update-slice_fusion.17
  91.1 0.9 slice_dynamic-update-slice_fusion.14
  92.2 1.1 slice_dynamic-update-slice_fusion.9
  93.4 44.5 %collective-permute-done.2 = bf16[2,256,2560]{1,2,0:T(8,128)(2,1)S(1)} collective-permute-done((bf16[2,256,2560]{1,2,0:T(8,128)(2,1)S(1)}, bf16[2,256,2560]{1,2,0:T(8,128)(2,1)S(1)}, u32[]{:S(2)}, u32[]{:S(2)}) %collective-permute-start.2) | collective-permute-done | bytes 2621472 | tf_op jit(solution)/shard_map/ppermute | solution.py:31
  137.9 2.0 select_select_fusion.2
  139.9 11.6 %collective-permute-start.3 = (bf16[2,256,2560]{1,2,0:T(8,128)(2,1)S(1)}, bf16[2,256,2560]{1,2,0:T(8,128)(2,1)S(1)}, u32[]{:S(2)}, u32[]{:S(2)}) collective-permute-start(bf16[2,256,2560]{1,2,0:T(8,128)(2,1)S(1)} %select_select_fusion.2), channel_id=1, source_target_pairs={{0,1},{4,5},{8,9},{12,13},{1,0},{5,4},{9,8},{13,12},{2,3},{6,7},{1... | collective-permute-start | bytes 7864328 | tf_op jit(solution)/shard_map/ppermute | solution.py:31
  151.5 0.9 slice_dynamic-update-slice_fusion.6
  152.8 0.9 slice_dynamic-update-slice_fusion.1
  153.8 2.7 %fusion.53 = bf16[3,1,52,384]{3,2,1,0:T(8,128)(2,1)} fusion(bf16[10368,384,1]{1,0,2:T(8,128)(2,1)S(1)} %bitcast.160, bf16[3,1,52,10368]{3,2,0,1:T(8,128)(2,1)S(1)} %slice_dynamic-update-slice_fusion, bf16[3,1,52,384]{3,2,1,0:T(8,128)(2,1)S(1)} %copy-done.4, f32[384]{0:T(512)S(1)} %copy-done.8), kind=kOutput, calls=%fused_computation.68 | convolution fusion | flops 1242408960 | bytes 11438592 | tf_op jit(solution)/shard_map/dot_general | solution.py:158
  156.6 2.9 %fusion.18 = (bf16[2,256,2560]{1,2,0:T(8,128)(2,1)S(1)}, bf16[2,256,2560]{1,2,0:T(8,128)(2,1)S(1)}, bf16[2,256,2560]{1,2,0:T(8,128)(2,1)S(1)}) fusion(bf16[2,256,2560]{1,2,0:T(8,128)(2,1)} %collective-permute-done, bf16[2,256,2560]{1,2,0:T(8,128)(2,1)S(1)} %collective-permute-done.2, pred[]{:T(512)S(6)} %eq.57, pred[]{:T(512)S(6)} %eq.56, pred[]{:T(512)S(6)} %eq.55, ...), kind=kLoop, calls=%fused_computation.27 | loop fusion | flops 10485760 | bytes 18350084 | tf_op jit(solution)/shard_map/jit(_where)/select_n | solution.py:47
  159.5 1.5 pad_maximum_fusion
  161.0 2.9 %fusion.85 = (bf16[1,1024,1280]{1,2,0:T(8,128)(2,1)}, bf16[1,1024,1280]{1,2,0:T(8,128)(2,1)S(1)}, bf16[1,1024,1280]{1,2,0:T(8,128)(2,1)}, bf16[1,1024,1280]{1,2,0:T(8,128)(2,1)S(1)}) fusion(bf16[2,1024,2560]{1,2,0:T(8,128)(2,1)S(1)} %pad_maximum_fusion), kind=kLoop, calls=%fused_computation.149 | loop fusion | bytes 20971520 | tf_op jit(solution)/shard_map/slice | solution.py:110
  163.9 1.6 fusion.89
  165.5 6.2 %bitcast_reduce_fusion = (f32[10,256]{1,0:T(8,128)S(1)}, f32[10,256]{1,0:T(8,128)S(1)}, f32[10,1024,256]{2,1,0:T(8,128)}) fusion(pred[1024]{0:T(1024)(128)(4,1)S(1)} %pad_add_fusion, f32[10,1024,256]{2,1,0:T(8,128)S(1)} %fusion.89, bf16[1024,10,128]{0,2,1:T(8,128)(2,1)S(1)} %bitcast.161, bf16[256,10,128]{0,2,1:T(8,128)(2,1)S(1)} %bitcast.165), kind=kOutput, calls=%fused_computation.2 | convolution fusion | flops 686812160 | bytes 24269824 | tf_op jit(solution)/shard_map/qhd,khd->hqk/dot_general | solution.py:61
  171.6 5.7 %fusion.8 = f32[10,256,128]{2,1,0:T(8,128)} fusion(bf16[1024,10,128]{0,2,1:T(8,128)(2,1)} %bitcast.168, f32[10,1024,256]{2,1,0:T(8,128)S(1)} %fusion.89, f32[10,256]{1,0:T(8,128)S(1)} %get-tuple-element.23, pred[1024]{0:T(1024)(128)(4,1)S(1)} %pad_add_fusion), kind=kOutput, calls=%fused_computation.14 | convolution fusion | flops 681574400 | bytes 14429184 | tf_op jit(solution)/shard_map/hqk,khd->hqd/dot_general | solution.py:66
  177.4 8.7 %fusion.6 = f32[10,256,128]{2,1,0:T(8,128)} fusion(bf16[1024,10,128]{0,2,1:T(8,128)(2,1)} %bitcast.167, f32[10,1024,256]{2,1,0:T(8,128)} %get-tuple-element.51, f32[10,256]{1,0:T(8,128)S(1)} %get-tuple-element.22, pred[1024]{0:T(1024)(128)(4,1)S(1)} %pad_add_fusion), kind=kOutput, calls=%fused_computation.13 | convolution fusion | flops 681574400 | bytes 14429184 | tf_op jit(solution)/shard_map/hqk,khd->hqd/dot_general | solution.py:66
  186.0 7.1 %fusion.5 = (f32[10,256]{1,0:T(8,128)S(1)}, f32[10,256]{1,0:T(8,128)S(1)}) fusion(f32[10,1024,256]{2,1,0:T(8,128)} %get-tuple-element.51, f32[10,256]{1,0:T(8,128)S(1)} %get-tuple-element.22, pred[1024]{0:T(1024)(128)(4,1)S(1)} %pad_add_fusion, f32[10,256]{1,0:T(8,128)S(1)} %get-tuple-element.23, f32[10,1024,256]{2,1,0:T(8,128)S(1)} %fusion.89), kind=kLoop, calls=%fused_computation.12 | loop fusion | flops 20966400 | bytes 21013504 | tf_op jit(solution)/shard_map/reduce_sum | solution.py:114
  193.2 2.7 %fusion.86 = (bf16[1,256,1280]{1,2,0:T(8,128)(2,1)}, bf16[1,256,1280]{1,2,0:T(8,128)(2,1)S(1)}, bf16[1,256,1280]{1,2,0:T(8,128)(2,1)S(1)}, bf16[1,256,1280]{1,2,0:T(8,128)(2,1)S(1)}) fusion(bf16[2,256,2560]{1,2,0:T(8,128)(2,1)} %all-reduce.3.cloned.1.call-done), kind=kLoop, calls=%fused_computation.150 | loop fusion | bytes 5242880 | tf_op jit(solution)/shard_map/slice | solution.py:123
  195.9 0.7 bitcast_reduce_fusion.3
  196.6 1.3 fusion.25
  198.7 0.7 copy-done.10
  199.4 2.3 %fusion.32 = bf16[256,10,128]{2,0,1:T(8,128)(2,1)} fusion(bf16[256,10,128]{0,2,1:T(8,128)(2,1)S(1)} %bitcast.173, f32[10,256,256]{2,1,0:T(8,128)S(1)} %get-tuple-element.54, f32[10,256]{1,0:T(8,128)S(1)} %fusion.74, f32[10,256,128]{2,1,0:T(8,128)S(1)} %copy-done.10, pred[256]{0:T(512)(128)(4,1)S(1)} %compare_and_fusion, ...), kind=kOutput, calls=%fused_computation.55 | convolution fusion | flops 171704320 | bytes 5273856 | tf_op jit(solution)/shard_map/hqk,khd->hqd/dot_general | solution.py:66
  201.6 1.3 copy.45
  203.0 3.6 %fusion.30 = bf16[256,10,128]{2,0,1:T(8,128)(2,1)} fusion(bf16[256,10,128]{0,2,1:T(8,128)(2,1)} %bitcast.172, f32[10,256,256]{2,1,0:T(8,128)S(1)} %copy-done.2, f32[10,256]{1,0:T(8,128)S(1)} %fusion.73, f32[10,256,128]{2,1,0:T(8,128)} %fusion.8, pred[256]{0:T(512)(128)(4,1)S(1)} %compare_and_fusion, f32[10,256]{1,0:T(8,128)S(1)} %get-tuple-element.40, ...), kind=kOutput, calls=%fused_computation.53 | convolution fusion | flops 171704320 | bytes 5273856 | tf_op jit(solution)/shard_map/hqk,khd->hqd/dot_general | solution.py:66
  206.6 1.3 copy.40
  208.2 1.6 copy.48
  (64 shorter events, 2.8 us)
Async XLA Ops:
  14.2 7.2 %copy-start.3 = (bf16[3,1,52,384]{3,2,1,0:T(8,128)(2,1)S(1)}, bf16[3,1,52,384]{3,2,1,0:T(8,128)(2,1)}, u32[]{:S(2)}) copy-start(bf16[3,1,52,384]{3,2,1,0:T(8,128)(2,1)} %param.15) | copy-start | bytes 359428
  14.2 7.3 %copy-start.7 = (f32[384]{0:T(512)S(1)}, f32[384]{0:T(512)}, u32[]{:S(2)}) copy-start(f32[384]{0:T(512)} %param.17) | copy-start | bytes 4612
  14.2 7.5 %copy-start.5 = (bf16[2,1,52,384]{3,0,2,1:T(2,128)(2,1)S(1)}, bf16[2,1,52,384]{3,0,2,1:T(2,128)(2,1)}, u32[]{:S(2)}) copy-start(bf16[2,1,52,384]{3,0,2,1:T(2,128)(2,1)} %param.16) | copy-start | bytes 239620
  14.2 14.4 %copy-start.9 = (s32[16,3]{0,1:T(4,128)S(1)}, s32[16,3]{0,1:T(4,128)}, u32[]{:S(2)}) copy-start(s32[16,3]{0,1:T(4,128)} %param.13) | copy-start | bytes 580
  14.2 178.9 %all-reduce.3.cloned.1.call-start = ((), (), s32[]{:S(2)}) async-start(), calls=%async_computation | async-start | bytes 5242880 | tf_op jit(solution)/shard_map/psum | solution.py:91
  14.9 53.1 %collective-permute-start = (bf16[2,256,2560]{1,2,0:T(8,128)(2,1)}, bf16[2,256,2560]{1,2,0:T(8,128)(2,1)}, u32[]{:S(2)}, u32[]{:S(2)}) collective-permute-start(bf16[2,256,2560]{1,2,0:T(8,128)(2,1)} %broadcast_select_fusion), channel_id=1, source_target_pairs={{0,1},{4,5},{8,9},{12,13},{2,3},{6,7},{10,11},{14,15},{1,4},{5,8},... | collective-permute-start | bytes 7864328 | tf_op jit(solution)/shard_map/ppermute | solution.py:31
  15.5 71.1 %collective-permute-start.1 = (bf16[2,256,2560]{1,2,0:T(8,128)(2,1)}, bf16[2,256,2560]{1,2,0:T(8,128)(2,1)}, u32[]{:S(2)}, u32[]{:S(2)}) collective-permute-start(bf16[2,256,2560]{1,2,0:T(8,128)(2,1)} %broadcast_select_fusion), channel_id=1, source_target_pairs={{0,2},{4,6},{8,10},{12,14},{1,3},{5,7},{9,11},{13,15},{2,1},{6,5},... | collective-permute-start | bytes 7864328 | tf_op jit(solution)/shard_map/ppermute | solution.py:31
  22.5 18.8 %collective-permute-start.5 = (bf16[5,1,52,384]{3,2,0,1:T(8,128)(2,1)}, bf16[5,1,52,384]{3,2,0,1:T(8,128)(2,1)}, u32[]{:S(2)}, u32[]{:S(2)}) collective-permute-start(bf16[5,1,52,384]{3,2,0,1:T(8,128)(2,1)} %pad_maximum_fusion.1), channel_id=1, source_target_pairs={{1,0},{2,1},{3,2},{4,3},{5,4},{6,5},{7,6},{8,7},{9,8},{10,9},{11,1... | collective-permute-start | bytes 599048 | tf_op jit(solution)/shard_map/ppermute | solution.py:25
  23.7 17.5 %collective-permute-start.4 = (bf16[5,1,52,384]{3,2,0,1:T(8,128)(2,1)}, bf16[5,1,52,384]{3,2,0,1:T(8,128)(2,1)}, u32[]{:S(2)}, u32[]{:S(2)}) collective-permute-start(bf16[5,1,52,384]{3,2,0,1:T(8,128)(2,1)} %pad_maximum_fusion.1), channel_id=1, source_target_pairs={{0,1},{1,2},{2,3},{3,4},{4,5},{5,6},{6,7},{7,8},{8,9},{9,10},{10,1... | collective-permute-start | bytes 599048 | tf_op jit(solution)/shard_map/ppermute | solution.py:22
  31.3 6.0 %copy-start.6 = (s32[16]{0:T(128)S(1)}, s32[16]{0:T(128)}, u32[]{:S(2)}) copy-start(s32[16]{0:T(128)} %param.14) | copy-start | bytes 196
  86.6 67.2 %slice-start = ((s8[7962624]{0:T(1024)(128)(4,1)}), s8[4194304]{0:T(1024)(128)(4,1)S(1)}, s32[]{:S(2)}) async-start(s8[7962624]{0:T(1024)(128)(4,1)} %bitcast.158), calls=%async_computation.1 | async-start | bytes 8388608
  88.8 49.1 %collective-permute-start.2 = (bf16[2,256,2560]{1,2,0:T(8,128)(2,1)S(1)}, bf16[2,256,2560]{1,2,0:T(8,128)(2,1)S(1)}, u32[]{:S(2)}, u32[]{:S(2)}) collective-permute-start(bf16[2,256,2560]{1,2,0:T(8,128)(2,1)S(1)} %select_select_fusion.4), channel_id=1, source_target_pairs={{3,2},{7,6},{11,10},{15,14},{2,0},{6,4},{10,8},{14,12},{1,5},{5,9}... | collective-permute-start | bytes 7864328 | tf_op jit(solution)/shard_map/ppermute | solution.py:31
  92.2 61.6 %slice-start.1 = ((s8[7962624]{0:T(1024)(128)(4,1)}), s8[3768320]{0:T(1024)(128)(4,1)S(1)}, s32[]{:S(2)}) async-start(s8[7962624]{0:T(1024)(128)(4,1)} %bitcast.158), calls=%async_computation.2 | async-start | bytes 7536640
  93.4 59.2 %copy-start.4 = (bf16[3,1,52,384]{3,2,1,0:T(8,128)(2,1)S(1)}, bf16[3,1,52,384]{3,2,1,0:T(8,128)(2,1)}, u32[]{:S(2)}) copy-start(bf16[3,1,52,384]{3,2,1,0:T(8,128)(2,1)} %param.15) | copy-start | bytes 359428
  93.4 60.4 %copy-start.8 = (f32[384]{0:T(512)S(1)}, f32[384]{0:T(512)}, u32[]{:S(2)}) copy-start(f32[384]{0:T(512)} %param.19) | copy-start | bytes 4612
  139.9 16.7 %collective-permute-start.3 = (bf16[2,256,2560]{1,2,0:T(8,128)(2,1)S(1)}, bf16[2,256,2560]{1,2,0:T(8,128)(2,1)S(1)}, u32[]{:S(2)}, u32[]{:S(2)}) collective-permute-start(bf16[2,256,2560]{1,2,0:T(8,128)(2,1)S(1)} %select_select_fusion.2), channel_id=1, source_target_pairs={{0,1},{4,5},{8,9},{12,13},{1,0},{5,4},{9,8},{13,12},{2,3},{6,7},{1... | collective-permute-start | bytes 7864328 | tf_op jit(solution)/shard_map/ppermute | solution.py:31
  163.9 1.6 copy-start
  196.5 1.5 copy-start.1
  198.1 1.3 copy-start.10
  199.4 3.6 %copy-start.2 = (f32[10,256,256]{2,1,0:T(8,128)S(1)}, f32[10,256,256]{2,1,0:T(8,128)}, u32[]{:S(2)}) copy-start(f32[10,256,256]{2,1,0:T(8,128)} %copy-done.1) | copy-start | bytes 7864324
Sparse Core Ops, SparseCore 0:
  18.7 129.9 all-reduce.2

commit v6 on v5

--- a/solution.py
+++ b/solution.py
@@ -6,7 +6,7 @@
 H = 20
 DH = 128
 WIN = 4
-HG = 10
+HG = 20
 
 
 def spread(block, axis, source):
@@ -31,7 +31,7 @@
     return lax.ppermute(value, "span", pairs)
 
 
-def window_blocks(kv, devices):
+def window_blocks(kv, devices, after, after_second):
     rows = devices // 4
     lane = lax.axis_index("span") % 4
 
@@ -50,11 +50,11 @@
     cross = move(kv, pairs((0, 2, 0), (1, 3, 0), (2, 1, 0)))
     along = move(kv, pairs((0, 1, 0), (2, 3, 0), (1, 0, 1), (3, 2, 1)))
     second = move(pick(cross, cross, along, cross), pairs((3, 2, 0), (2, 0, 0), (1, 1, 1)))
-    third = move(pick(second, second, cross, cross), pairs((0, 1, 0), (1, 0, 0), (2, 3, 0)))
-    b1 = pick(second, along, second, along)
-    b2 = pick(third, third, cross, cross)
-    b3 = pick(along, second, along, third)
-    return b1, b2, b3
+    carry = after(along, cross)
+    payload, carry = lax.optimization_barrier((pick(second, second, cross, cross), carry))
+    third = move(payload, pairs((0, 1, 0), (1, 0, 0), (2, 3, 0)))
+    carry = after_second(carry, cross, second)
+    return third, carry
 
 
 def part_stats(q, k, valid, scale):
@@ -66,6 +66,23 @@
     return jnp.einsum(
         "hqk,khd->hqd", weights.astype(jnp.bfloat16), values, preferred_element_type=jnp.float32
     )
+
+
+def attend(q, kv, valid, state):
+    k = kv[0].reshape(-1, HG, DH)
+    v = kv[1].reshape(-1, HG, DH)
+    scores = part_stats(q, k, valid, DH ** (-0.5))
+    top = jnp.max(scores, axis=-1, keepdims=True)
+    if state is not None:
+        top = jnp.maximum(state[0], top)
+    weights = jnp.exp(scores - top)
+    total = jnp.sum(weights, axis=-1, keepdims=True)
+    out = weighted(weights, v)
+    if state is not None:
+        rescale = jnp.exp(state[0] - top)
+        total = state[1] * rescale + total
+        out = state[2] * rescale + out
+    return top, total, out
 
 
 def shards(
@@ -90,45 +107,39 @@
     masked = jnp.where(is_anchor, keys_values, jnp.zeros_like(keys_values))
     anchor_kv = lax.psum(masked, "span")
     sent = jnp.where(is_anchor, lax.optimization_barrier(masked), keys_values)
-    b1, b2, b3 = window_blocks(sent, devices)
-    blocks = [keys_values, b1, b2, b3]
     valid_list = [row_ids < lengths[place]]
     for offset in range(1, WIN):
         source = (place - offset) % devices
         allowed = (position >= offset) & (span_mask[position, offset - 1] == 1)
         valid_list.append(allowed & (row_ids < lengths[source]))
+    valid_list.append(jnp.zeros_like(valid_list[0]))
+    lane = place % 4
+
+    def offset_of(*per_lane):
+        out = valid_list[per_lane[0]]
+        for l in range(1, 4):
+            out = jnp.where(lane == l, valid_list[per_lane[l]], out)
+        return out
+
+    query_heads = queries.reshape(tok_rows, HG, DH)
+
+    def first_group(along, cross):
+        group_kv = jnp.concatenate([keys_values, along], axis=1)
+        group_valid = jnp.concatenate([valid_list[0], offset_of(3, 1, 3, 1)])
+        return attend(query_heads, group_kv, group_valid, None)
+
+    def second_group(state, cross, second):
+        group_kv = jnp.concatenate([cross, second], axis=1)
+        group_valid = jnp.concatenate([offset_of(4, 4, 2, 2), offset_of(1, 3, 1, 4)])
+        return attend(query_heads, group_kv, group_valid, state)
+
+    third, state = window_blocks(sent, devices, first_group, second_group)
+    state = attend(query_heads, third, offset_of(2, 2, 4, 3), state)
     anchor_valid = (place != anchor) & (row_ids < lengths[anchor])
-    window_kv = jnp.concatenate(blocks, axis=1)
-    window_valid = jnp.concatenate(valid_list)
-    score_scale = DH ** (-0.5)
-    partial = []
-    for head_block in range(H // HG):
-        first_col = head_block * HG * DH
-        last_col = first_col + HG * DH
-        q = queries[:, first_col:last_col].reshape(tok_rows, HG, DH)
-        wk = window_kv[0, :, first_col:last_col].reshape(-1, HG, DH)
-        wv = window_kv[1, :, first_col:last_col].reshape(-1, HG, DH)
-        ws = part_stats(q, wk, window_valid, score_scale)
-        w_max = jnp.max(ws, axis=-1, keepdims=True)
-        w_exp = jnp.exp(ws - w_max)
-        w_sum = jnp.sum(w_exp, axis=-1, keepdims=True)
-        partial.append((w_max, w_sum, weighted(w_exp, wv)))
-    anchor_kv, partial = lax.optimization_barrier((anchor_kv, partial))
-    pieces = []
-    for head_block, (w_max, w_sum, w_out) in enumerate(partial):
-        first_col = head_block * HG * DH
-        last_col = first_col + HG * DH
-        q = queries[:, first_col:last_col].reshape(tok_rows, HG, DH)
-        ak = anchor_kv[0, :, first_col:last_col].reshape(-1, HG, DH)
-        av = anchor_kv[1, :, first_col:last_col].reshape(-1, HG, DH)
-        a_s = part_stats(q, ak, anchor_valid, score_scale)
-        top = jnp.maximum(w_max, jnp.max(a_s, axis=-1, keepdims=True))
-        a_exp = jnp.exp(a_s - top)
-        a_sum = jnp.sum(a_exp, axis=-1, keepdims=True)
-        a_out = weighted(a_exp, av)
-        w_scale = jnp.exp(w_max - top)
-        blended = (w_out * w_scale + a_out) / (w_sum * w_scale + a_sum)
-        pieces.append(jnp.transpose(blended, (1, 0, 2)).reshape(tok_rows, HG * DH))
+    anchor_kv, state = lax.optimization_barrier((anchor_kv, state))
+    top, total, out = attend(query_heads, anchor_kv, anchor_valid, state)
+    blended = out / total
+    pieces = [jnp.transpose(blended, (1, 0, 2)).reshape(tok_rows, HG * DH)]
     attended = jnp.concatenate(pieces, axis=1)
     attended = jnp.where(row_ids[:, None] < lengths[place], attended, 0.0).astype(jnp.bfloat16)
     features = frames.astype(jnp.float32)

time: 218 us -> 228 us (1.046)
  waiting for transfers between devices: 88.1 us -> 74.6 us
  other arithmetic: 25.7 us -> 36.4 us
  matrix products: 32.7 us -> 40.7 us
  local copies, waits for them, and re-layouts: 27.4 us -> 30.5 us
  starting transfers between devices: 25.6 us -> 28.3 us
    ppermute x4, waiting for transfers between devices: 87.4 us -> 73.9 us  [move(): return lax.ppermute(value, 'span', pairs)]
    unnamed x54 -> x53, local copies, waits for them, and re-layouts: 15.3 us -> 24.5 us
    unnamed x4 -> x5, other arithmetic: 0.22 us -> 7.15 us
    concatenate x2 -> x4, other arithmetic: 1.5 us -> 8.01 us  [the longest x1 4.92 us: second_group(): group_kv = jnp.concatenate([cross, second], axis=1)]
    slice x3, local copies, waits for them, and re-layouts: 8.1 us -> 2.39 us  [attend(): v = kv[1].reshape(-1, HG, DH)]
    dot_general x1, matrix products: 2.74 us -> 7.35 us  [shards(): jnp.dot(columns, conv_weight.reshape(27 * channels, channels), preferred_...]
    reduce_sum x2 -> x4, other arithmetic: 7.7 us -> 10.6 us  [attend(): total = jnp.sum(weights, axis=-1, keepdims=True)]
    select_n x3, other arithmetic: 7.08 us -> 4.21 us  [offset_of(): out = jnp.where(lane == l, valid_list[per_lane[l]], out)]
  transfers between devices with their start and end apart: 7 -> 7, of which waited for: 3 -> 2; matrix products, arithmetic and copies ran while one was open for 29% -> 39% of each run, Pallas kernels for 0% -> 0%
where the time goes in v6:
time: 228 us; the launch traced here: 227 us
  waiting for transfers between devices  74.6 us (33%)
  matrix products  40.7 us (18%)
  other arithmetic  36.4 us (16%)
  local copies, waits for them, and re-layouts  30.5 us (13%)
  starting transfers between devices  28.3 us (12%)
  between operations  17 us (7%)
    ppermute x4, waiting for transfers between devices, move(): return lax.ppermute(value, 'span', pairs)  73.9 us
    unnamed x53, local copies, waits for them, and re-layouts  24.5 us
    dot_general x4, matrix products, weighted(): jnp.einsum('hqk,khd->hqd', weights.astype(jnp.bfloat16), values, preferre...  22.1 us
    ppermute x4, starting transfers between devices, move(): return lax.ppermute(value, 'span', pairs)  21 us
    dot_general x4, matrix products, part_stats(): jnp.einsum('qhd,khd->hqk', q, k, preferred_element_type=jnp.float32) * scale  11.2 us
    reduce_sum x4, other arithmetic, attend(): total = jnp.sum(weights, axis=-1, keepdims=True)  10.6 us
    dot_general x1, matrix products, shards(): jnp.dot(columns, conv_weight.reshape(27 * channels, channels), preferred_...  7.35 us
    unnamed x5, other arithmetic  7.15 us
  transfers between devices with their start and end apart: 7, of which 2 were waited for; matrix products, arithmetic and copies ran while one was open for 39% of the time, Pallas kernels for 0%

profile of v6, /device:TPU:0, one launch (start us, length us, event | category | flops | bytes accessed | tf_op | source)
XLA Modules:
  0.0 227.5 jit_solution(9448711875836062265)
XLA Ops:
  7.2 3.0 %copy.25 = bf16[2,256,2560]{1,2,0:T(8,128)(2,1)S(1)} copy(bf16[2,256,2560]{2,1,0:T(8,128)(2,1)} %param.11) | data formatting | bytes 5242880 | tf_op args[1]
  10.8 1.7 broadcast_select_fusion.1
  12.5 1.8 broadcast_select_fusion
  14.3 0.7 all-reduce.3.cloned.1.call-update
  15.0 6.4 %collective-permute-start = (bf16[2,256,2560]{1,2,0:T(8,128)(2,1)}, bf16[2,256,2560]{1,2,0:T(8,128)(2,1)}, u32[]{:S(2)}, u32[]{:S(2)}) collective-permute-start(bf16[2,256,2560]{1,2,0:T(8,128)(2,1)} %broadcast_select_fusion), channel_id=1, source_target_pairs={{0,2},{4,6},{8,10},{12,14},{1,3},{5,7},{9,11},{13,15},{2,1},{6,5},... | collective-permute-start | bytes 7864328 | tf_op jit(solution)/shard_map/ppermute | solution.py:31
  21.7 0.7 pad_maximum_fusion.1
  22.5 1.3 collective-permute-start.5
  23.7 6.0 %collective-permute-start.4 = (bf16[5,1,52,384]{3,2,0,1:T(8,128)(2,1)}, bf16[5,1,52,384]{3,2,0,1:T(8,128)(2,1)S(1)}, u32[]{:S(2)}, u32[]{:S(2)}) collective-permute-start(bf16[5,1,52,384]{3,2,0,1:T(8,128)(2,1)} %pad_maximum_fusion.1), channel_id=1, source_target_pairs={{0,1},{1,2},{2,3},{3,4},{4,5},{5,6},{6,7},{7,8},{8,9},{9,10},{10,1... | collective-permute-start | bytes 599048 | tf_op jit(solution)/shard_map/ppermute | solution.py:22
  33.1 1.2 fusion.78
  34.3 1.8 select_select_fusion.3
  36.1 1.2 select_select_fusion.5
  37.9 2.4 %copy.28 = bf16[256,2560]{0,1:T(8,128)(2,1)} copy(bf16[256,2560]{1,0:T(8,128)(2,1)} %param.10) | data formatting | bytes 2621440 | tf_op args[0]
  42.6 0.7 slice_dynamic-update-slice_fusion.21
  44.7 0.7 slice_dynamic-update-slice_fusion.19
  46.8 0.7 slice_dynamic-update-slice_fusion.16
  48.9 0.7 slice_dynamic-update-slice_fusion.13
  50.3 0.7 fusion.71
  51.0 0.7 slice_dynamic-update-slice_fusion.11
  53.1 0.7 slice_dynamic-update-slice_fusion.8
  54.5 0.7 slice_dynamic-update-slice_fusion.6
  56.6 0.8 constant_dynamic-update-slice_fusion.2
  57.4 0.7 slice_dynamic-update-slice_fusion.3
  58.8 30.4 %collective-permute-done = bf16[2,256,2560]{1,2,0:T(8,128)(2,1)} collective-permute-done((bf16[2,256,2560]{1,2,0:T(8,128)(2,1)}, bf16[2,256,2560]{1,2,0:T(8,128)(2,1)}, u32[]{:S(2)}, u32[]{:S(2)}) %collective-permute-start) | collective-permute-done | bytes 2621472 | tf_op jit(solution)/shard_map/ppermute | solution.py:31
  89.1 5.0 %constant_dynamic-update-slice_fusion.1 = (bf16[2,512,2560]{1,2,0:T(8,128)(2,1)}, bf16[2,256,2560]{1,2,0:T(8,128)(2,1)}) fusion(bf16[2,256,2560]{1,2,0:T(8,128)(2,1)} %collective-permute-done, bf16[2,256,2560]{1,2,0:T(8,128)(2,1)} %collective-permute-done.1, pred[]{:T(512)S(6)} %eq.54, pred[]{:T(512)S(6)} %eq.53), kind=kLoop, calls=%fused_computation.115 | loop fusion | flops 2621439 | bytes 10485762
  94.1 1.6 collective-permute-start.2
  95.7 3.1 %pad_maximum_fusion = (bf16[1,512,2560]{1,2,0:T(8,128)(2,1)}, bf16[1,512,2560]{1,2,0:T(8,128)(2,1)S(1)}) fusion(bf16[2,256,2560]{1,2,0:T(8,128)(2,1)} %collective-permute-done.1, bf16[2,256,2560]{1,2,0:T(8,128)(2,1)S(1)} %copy.25), kind=kLoop, calls=%fused_computation.43 | loop fusion | flops 10485760 | bytes 10485760 | tf_op jit(solution)/shard_map/concatenate | solution.py:127
  98.8 2.5 %bitcast_reduce_fusion.1 = (f32[20,256]{1,0:T(8,128)S(1)}, f32[20,512,256]{2,1,0:T(8,128)S(1)}) fusion(pred[512]{0:T(512)(128)(4,1)S(1)} %pad_add_fusion, bf16[512,20,128]{0,2,1:T(8,128)(2,1)S(1)} %bitcast.177, bf16[256,20,128]{0,2,1:T(8,128)(2,1)S(1)} %bitcast.170), kind=kOutput, calls=%fused_computation.4 | convolution fusion | flops 678947840 | bytes 14438912 | tf_op jit(solution)/shard_map/qhd,khd->hqk/dot_general | solution.py:61
  101.2 2.2 fusion.3
  103.4 4.5 %fusion.8 = f32[20,256,128]{2,1,0:T(8,128)} fusion(bf16[512,20,128]{0,2,1:T(8,128)(2,1)S(1)} %bitcast.183, f32[20,512,256]{2,1,0:T(8,128)S(1)} %get-tuple-element.49, f32[20,256]{1,0:T(8,128)S(1)} %get-tuple-element.48, pred[512]{0:T(512)(128)(4,1)S(1)} %pad_add_fusion), kind=kOutput, calls=%fused_computation.13 | convolution fusion | flops 681574400 | bytes 15749632 | tf_op jit(solution)/shard_map/hqk,khd->hqd/dot_general | solution.py:66
  107.9 43.6 %collective-permute-done.2 = bf16[2,256,2560]{1,2,0:T(8,128)(2,1)} collective-permute-done((bf16[2,256,2560]{1,2,0:T(8,128)(2,1)}, bf16[2,256,2560]{1,2,0:T(8,128)(2,1)}, u32[]{:S(2)}, u32[]{:S(2)}) %collective-permute-start.2) | collective-permute-done | bytes 2621472 | tf_op jit(solution)/shard_map/ppermute | solution.py:31
  151.5 4.9 %constant_dynamic-update-slice_fusion = (bf16[2,512,2560]{1,2,0:T(8,128)(2,1)}, bf16[2,256,2560]{1,2,0:T(8,128)(2,1)S(1)}) fusion(bf16[2,512,2560]{1,2,0:T(8,128)(2,1)} %get-tuple-element.34, bf16[2,256,2560]{1,2,0:T(8,128)(2,1)} %collective-permute-done.2, bf16[2,256,2560]{1,2,0:T(8,128)(2,1)} %collective-permute-done, pred[]{:T(512)S(6)} %eq.54, pred[]{:T(512)S(6)} %eq.53), kind=kLoop, calls=%fused_computation.114 | loop fusion | flops 2621440 | bytes 10485762 | tf_op jit(solution)/shard_map/concatenate | solution.py:132
  156.4 13.0 %collective-permute-start.3 = (bf16[2,256,2560]{1,2,0:T(8,128)(2,1)S(1)}, bf16[2,256,2560]{1,2,0:T(8,128)(2,1)S(1)}, u32[]{:S(2)}, u32[]{:S(2)}) collective-permute-start(bf16[2,256,2560]{1,2,0:T(8,128)(2,1)S(1)} %get-tuple-element.11), channel_id=1, source_target_pairs={{0,1},{4,5},{8,9},{12,13},{1,0},{5,4},{9,8},{13,12},{2,3},{6,7},{1... | collective-permute-start | bytes 7864328 | tf_op jit(solution)/shard_map/ppermute | solution.py:31
  169.4 0.7 slice_dynamic-update-slice_fusion.1
  170.2 0.7 slice_dynamic-update-slice_fusion
  170.9 7.4 %fusion.52 = bf16[3,1,52,384]{3,2,1,0:T(8,128)(2,1)} fusion(bf16[10368,384,1]{1,0,2:T(8,128)(2,1)} %bitcast.174, bf16[3,1,52,10368]{3,2,0,1:T(8,128)(2,1)} %slice_dynamic-update-slice_fusion, bf16[3,1,52,384]{3,2,1,0:T(8,128)(2,1)S(1)} %copy-done.5, f32[384]{0:T(512)S(1)} %copy-done.9), kind=kOutput, calls=%fused_computation.64 | convolution fusion | flops 1242408960 | bytes 11438592 | tf_op jit(solution)/shard_map/dot_general | solution.py:169
  178.6 1.0 copy-done.1
  179.5 6.2 %bitcast_reduce_fusion = (f32[20,256]{1,0:T(8,128)S(1)}, f32[20,512,256]{2,1,0:T(8,128)}) fusion(pred[512]{0:T(512)(128)(4,1)S(1)} %pad_add_fusion.1, bf16[512,20,128]{0,2,1:T(8,128)(2,1)S(1)} %bitcast.178, bf16[256,20,128]{0,2,1:T(8,128)(2,1)S(1)} %bitcast.171), kind=kOutput, calls=%fused_computation.1 | convolution fusion | flops 678947840 | bytes 14438912 | tf_op jit(solution)/shard_map/qhd,khd->hqk/dot_general | solution.py:61
  185.9 1.3 bitcast_reduce_fusion.3
  187.2 1.2 fusion.21
  188.4 6.1 %fusion.5 = f32[20,256]{1,0:T(8,128)S(1)} fusion(f32[20,512,256]{2,1,0:T(8,128)} %get-tuple-element.51, f32[20,256]{1,0:T(8,128)S(1)} %get-tuple-element.39, pred[512]{0:T(512)(128)(4,1)S(1)} %pad_add_fusion.1), kind=kLoop, calls=%fused_computation.11 | loop fusion | flops 10480640 | bytes 10527232 | tf_op jit(solution)/shard_map/reduce_sum | solution.py:79
  194.6 8.6 %fusion.6 = f32[20,256,128]{2,1,0:T(8,128)} fusion(bf16[512,20,128]{0,2,1:T(8,128)(2,1)S(1)} %bitcast.182, f32[20,512,256]{2,1,0:T(8,128)} %get-tuple-element.51, f32[20,256]{1,0:T(8,128)S(1)} %get-tuple-element.39, pred[512]{0:T(512)(128)(4,1)S(1)} %pad_add_fusion.1), kind=kOutput, calls=%fused_computation.12 | convolution fusion | flops 681574400 | bytes 15749632 | tf_op jit(solution)/shard_map/hqk,khd->hqd/dot_general | solution.py:66
  203.2 5.2 %multiply_add_fusion = f32[20,256,128]{2,1,0:T(8,128)} fusion(f32[20,256,128]{2,1,0:T(8,128)} %fusion.6, f32[20,256,128]{2,1,0:T(8,128)S(1)} %copy-done.3, bf16[256,20,128]{0,2,1:T(8,128)(2,1)S(1)} %bitcast.181, f32[20,256,256]{2,1,0:T(8,128)S(1)} %get-tuple-element.53, f32[20,256]{1,0:T(8,128)S(1)} %bitcast.186, ...), kind=kOutput, calls=%fused_computation.48 | convolution fusion | flops 343408640 | bytes 14479616 | tf_op jit(solution)/shard_map/hqk,khd->hqd/dot_general | solution.py:66
  208.4 1.9 fusion.90
  210.3 1.3 bitcast_reduce_fusion.2
  211.7 1.2 fusion.22
  213.4 3.7 %divide_bitcast_fusion = bf16[256,20,128]{2,0,1:T(8,128)(2,1)} fusion(f32[20,256,128]{2,1,0:T(8,128)S(1)} %copy-done.4, f32[20,256]{1,0:T(8,128)S(1)} %get-tuple-element.37, f32[20,256]{1,0:T(8,128)S(1)} %get-tuple-element.36, bf16[256,20,128]{0,2,1:T(8,128)(2,1)S(1)} %bitcast.184, f32[20,256,256]{2,1,0:T(8,128)S(1)} %get-tuple-element.55, ...), kind=kOutput, calls=%fused_computation.46 | convolution fusion | flops 343408640 | bytes 10547456 | tf_op jit(solution)/shard_map/hqk,khd->hqd/dot_general | solution.py:66
  217.1 1.6 copy.45
  219.0 1.6 copy.48
  (66 shorter events, 14.9 us)
Async XLA Ops:
  12.5 8.9 %copy-start.6 = (bf16[2,1,52,384]{3,0,2,1:T(2,128)(2,1)S(1)}, bf16[2,1,52,384]{3,0,2,1:T(2,128)(2,1)}, u32[]{:S(2)}) copy-start(bf16[2,1,52,384]{3,0,2,1:T(2,128)(2,1)} %param.16) | copy-start | bytes 239620
  12.5 8.9 %copy-start.5 = (bf16[3,1,52,384]{3,2,1,0:T(8,128)(2,1)S(1)}, bf16[3,1,52,384]{3,2,1,0:T(8,128)(2,1)}, u32[]{:S(2)}) copy-start(bf16[3,1,52,384]{3,2,1,0:T(8,128)(2,1)} %param.15) | copy-start | bytes 359428
  12.5 9.1 %copy-start.8 = (f32[384]{0:T(512)S(1)}, f32[384]{0:T(512)}, u32[]{:S(2)}) copy-start(f32[384]{0:T(512)} %param.17) | copy-start | bytes 4612
  14.3 15.6 %copy-start.10 = (s32[16,3]{0,1:T(4,128)S(1)}, s32[16,3]{0,1:T(4,128)}, u32[]{:S(2)}) copy-start(s32[16,3]{0,1:T(4,128)} %param.13) | copy-start | bytes 580
  14.3 18.1 %copy-start.7 = (s32[16]{0:T(128)S(1)}, s32[16]{0:T(128)}, u32[]{:S(2)}) copy-start(s32[16]{0:T(128)} %param.14) | copy-start | bytes 196
  14.3 194.1 %all-reduce.3.cloned.1.call-start = ((), (), s32[]{:S(2)}) async-start(), calls=%async_computation | async-start | bytes 5242880 | tf_op jit(solution)/shard_map/psum | solution.py:108
  15.0 74.1 %collective-permute-start = (bf16[2,256,2560]{1,2,0:T(8,128)(2,1)}, bf16[2,256,2560]{1,2,0:T(8,128)(2,1)}, u32[]{:S(2)}, u32[]{:S(2)}) collective-permute-start(bf16[2,256,2560]{1,2,0:T(8,128)(2,1)} %broadcast_select_fusion), channel_id=1, source_target_pairs={{0,2},{4,6},{8,10},{12,14},{1,3},{5,7},{9,11},{13,15},{2,1},{6,5},... | collective-permute-start | bytes 7864328 | tf_op jit(solution)/shard_map/ppermute | solution.py:31
  21.4 67.7 %collective-permute-start.1 = (bf16[2,256,2560]{1,2,0:T(8,128)(2,1)}, bf16[2,256,2560]{1,2,0:T(8,128)(2,1)}, u32[]{:S(2)}, u32[]{:S(2)}) collective-permute-start(bf16[2,256,2560]{1,2,0:T(8,128)(2,1)} %broadcast_select_fusion), channel_id=1, source_target_pairs={{0,1},{4,5},{8,9},{12,13},{2,3},{6,7},{10,11},{14,15},{1,4},{5,8},... | collective-permute-start | bytes 7864328 | tf_op jit(solution)/shard_map/ppermute | solution.py:31
  22.5 18.6 %collective-permute-start.5 = (bf16[5,1,52,384]{3,2,0,1:T(8,128)(2,1)}, bf16[5,1,52,384]{3,2,0,1:T(8,128)(2,1)S(1)}, u32[]{:S(2)}, u32[]{:S(2)}) collective-permute-start(bf16[5,1,52,384]{3,2,0,1:T(8,128)(2,1)} %pad_maximum_fusion.1), channel_id=1, source_target_pairs={{1,0},{2,1},{3,2},{4,3},{5,4},{6,5},{7,6},{8,7},{9,8},{10,9},{11,1... | collective-permute-start | bytes 599048 | tf_op jit(solution)/shard_map/ppermute | solution.py:25
  23.7 17.3 %collective-permute-start.4 = (bf16[5,1,52,384]{3,2,0,1:T(8,128)(2,1)}, bf16[5,1,52,384]{3,2,0,1:T(8,128)(2,1)S(1)}, u32[]{:S(2)}, u32[]{:S(2)}) collective-permute-start(bf16[5,1,52,384]{3,2,0,1:T(8,128)(2,1)} %pad_maximum_fusion.1), channel_id=1, source_target_pairs={{0,1},{1,2},{2,3},{3,4},{4,5},{5,6},{6,7},{7,8},{8,9},{9,10},{10,1... | collective-permute-start | bytes 599048 | tf_op jit(solution)/shard_map/ppermute | solution.py:22
  94.1 4.7 %copy-start = (bf16[256,2560]{0,1:T(8,128)(2,1)S(1)}, bf16[256,2560]{0,1:T(8,128)(2,1)}, u32[]{:S(2)}) copy-start(bf16[256,2560]{0,1:T(8,128)(2,1)} %copy.28) | copy-start | bytes 3932164
  94.1 57.4 %collective-permute-start.2 = (bf16[2,256,2560]{1,2,0:T(8,128)(2,1)}, bf16[2,256,2560]{1,2,0:T(8,128)(2,1)}, u32[]{:S(2)}, u32[]{:S(2)}) collective-permute-start(bf16[2,256,2560]{1,2,0:T(8,128)(2,1)} %get-tuple-element.35), channel_id=1, source_target_pairs={{3,2},{7,6},{11,10},{15,14},{2,0},{6,4},{10,8},{14,12},{1,5},{5,9}... | collective-permute-start | bytes 7864328 | tf_op jit(solution)/shard_map/ppermute | solution.py:31
  101.2 2.2 copy-start.2
  151.5 19.4 %copy-start.9 = (f32[384]{0:T(512)S(1)}, f32[384]{0:T(512)}, u32[]{:S(2)}) copy-start(f32[384]{0:T(512)} %param.19) | copy-start | bytes 4612
  156.4 29.4 %collective-permute-start.3 = (bf16[2,256,2560]{1,2,0:T(8,128)(2,1)S(1)}, bf16[2,256,2560]{1,2,0:T(8,128)(2,1)S(1)}, u32[]{:S(2)}, u32[]{:S(2)}) collective-permute-start(bf16[2,256,2560]{1,2,0:T(8,128)(2,1)S(1)} %get-tuple-element.11), channel_id=1, source_target_pairs={{0,1},{4,5},{8,9},{12,13},{1,0},{5,4},{9,8},{13,12},{2,3},{6,7},{1... | collective-permute-start | bytes 7864328 | tf_op jit(solution)/shard_map/ppermute | solution.py:31
  170.1 8.1 %slice-start = ((s8[5242880]{0:T(1024)(128)(4,1)}), s8[4194304]{0:T(1024)(128)(4,1)S(1)}, s32[]{:S(2)}) async-start(s8[5242880]{0:T(1024)(128)(4,1)} %bitcast.175), calls=%async_computation.1 | async-start | bytes 8388608
  170.9 7.4 %slice-start.1 = ((s8[5242880]{0:T(1024)(128)(4,1)}), s8[1048576]{0:T(1024)(128)(4,1)S(1)}, s32[]{:S(2)}) async-start(s8[5242880]{0:T(1024)(128)(4,1)} %bitcast.175), calls=%async_computation.2 | async-start | bytes 2097152
  178.2 1.3 copy-start.1
  194.6 8.6 %copy-start.3 = (f32[20,256,128]{2,1,0:T(8,128)S(1)}, f32[20,256,128]{2,1,0:T(8,128)}, u32[]{:S(2)}) copy-start(f32[20,256,128]{2,1,0:T(8,128)} %fusion.8) | copy-start | bytes 7864324
  211.6 1.7 copy-start.4
Sparse Core Ops, SparseCore 0:
  18.8 123.1 all-reduce.2

commit v7 on v6

--- a/solution.py
+++ b/solution.py
@@ -6,7 +6,7 @@
 H = 20
 DH = 128
 WIN = 4
-HG = 20
+HG = 10
 
 
 def spread(block, axis, source):
@@ -31,7 +31,7 @@
     return lax.ppermute(value, "span", pairs)
 
 
-def window_blocks(kv, devices, after, after_second):
+def window_blocks(kv, devices):
     rows = devices // 4
     lane = lax.axis_index("span") % 4
 
@@ -50,11 +50,8 @@
     cross = move(kv, pairs((0, 2, 0), (1, 3, 0), (2, 1, 0)))
     along = move(kv, pairs((0, 1, 0), (2, 3, 0), (1, 0, 1), (3, 2, 1)))
     second = move(pick(cross, cross, along, cross), pairs((3, 2, 0), (2, 0, 0), (1, 1, 1)))
-    carry = after(along, cross)
-    payload, carry = lax.optimization_barrier((pick(second, second, cross, cross), carry))
-    third = move(payload, pairs((0, 1, 0), (1, 0, 0), (2, 3, 0)))
-    carry = after_second(carry, cross, second)
-    return third, carry
+    third = move(pick(second, second, cross, cross), pairs((0, 1, 0), (1, 0, 0), (2, 3, 0)))
+    return along, cross, second, third
 
 
 def part_stats(q, k, valid, scale):
@@ -107,6 +104,7 @@
     masked = jnp.where(is_anchor, keys_values, jnp.zeros_like(keys_values))
     anchor_kv = lax.psum(masked, "span")
     sent = jnp.where(is_anchor, lax.optimization_barrier(masked), keys_values)
+    along, cross, second, third = window_blocks(sent, devices)
     valid_list = [row_ids < lengths[place]]
     for offset in range(1, WIN):
         source = (place - offset) % devices
@@ -121,25 +119,25 @@
             out = jnp.where(lane == l, valid_list[per_lane[l]], out)
         return out
 
-    query_heads = queries.reshape(tok_rows, HG, DH)
-
-    def first_group(along, cross):
-        group_kv = jnp.concatenate([keys_values, along], axis=1)
-        group_valid = jnp.concatenate([valid_list[0], offset_of(3, 1, 3, 1)])
-        return attend(query_heads, group_kv, group_valid, None)
-
-    def second_group(state, cross, second):
-        group_kv = jnp.concatenate([cross, second], axis=1)
-        group_valid = jnp.concatenate([offset_of(4, 4, 2, 2), offset_of(1, 3, 1, 4)])
-        return attend(query_heads, group_kv, group_valid, state)
-
-    third, state = window_blocks(sent, devices, first_group, second_group)
-    state = attend(query_heads, third, offset_of(2, 2, 4, 3), state)
+    groups = [
+        (jnp.concatenate([keys_values, along], axis=1),
+         jnp.concatenate([valid_list[0], offset_of(3, 1, 3, 1)])),
+        (jnp.concatenate([cross, second, third], axis=1),
+         jnp.concatenate([offset_of(4, 4, 2, 2), offset_of(1, 3, 1, 4), offset_of(2, 2, 4, 3)])),
+    ]
     anchor_valid = (place != anchor) & (row_ids < lengths[anchor])
-    anchor_kv, state = lax.optimization_barrier((anchor_kv, state))
-    top, total, out = attend(query_heads, anchor_kv, anchor_valid, state)
-    blended = out / total
-    pieces = [jnp.transpose(blended, (1, 0, 2)).reshape(tok_rows, HG * DH)]
+    heads = [slice(h * HG * DH, (h + 1) * HG * DH) for h in range(H // HG)]
+    query_heads = [queries[:, cols].reshape(tok_rows, HG, DH) for cols in heads]
+    states = [None] * len(heads)
+    for group_kv, group_valid in groups:
+        for h, cols in enumerate(heads):
+            states[h] = attend(query_heads[h], group_kv[:, :, cols], group_valid, states[h])
+    anchor_kv, states = lax.optimization_barrier((anchor_kv, states))
+    pieces = []
+    for h, cols in enumerate(heads):
+        top, total, out = attend(query_heads[h], anchor_kv[:, :, cols], anchor_valid, states[h])
+        blended = out / total
+        pieces.append(jnp.transpose(blended, (1, 0, 2)).reshape(tok_rows, HG * DH))
     attended = jnp.concatenate(pieces, axis=1)
     attended = jnp.where(row_ids[:, None] < lengths[place], attended, 0.0).astype(jnp.bfloat16)
     features = frames.astype(jnp.float32)

time: 228 us -> 213 us (0.934)
  matrix products: 40.7 us -> 29.3 us
  waiting for transfers between devices: 74.6 us -> 84.9 us
  other arithmetic: 36.4 us -> 26.7 us
  local copies, waits for them, and re-layouts: 30.5 us -> 27.2 us
  starting transfers between devices: 28.3 us -> 26 us
    ppermute x4, waiting for transfers between devices: 73.9 us -> 84.2 us  [move(): return lax.ppermute(value, 'span', pairs)]
    unnamed x53 -> x70, local copies, waits for them, and re-layouts: 24.5 us -> 15.6 us
    unnamed x5, other arithmetic: 7.15 us -> 0.22 us
    select_n x0 -> x2, other arithmetic: none -> 5.47 us  [pick(): out = jnp.where(lane == l, options[l], out)]
    dot_general x4 -> x6, matrix products: 22.1 us -> 17.1 us  [weighted(): jnp.einsum('hqk,khd->hqd', weights.astype(jnp.bfloat16), values, preferre...]
    concatenate x4 -> x3, other arithmetic: 8.01 us -> 3 us  [the longest x1 2.97 us: shards(): jnp.concatenate([keys_values, along], axis=1)]
    dot_general x1, matrix products: 7.35 us -> 2.77 us  [shards(): jnp.dot(columns, conv_weight.reshape(27 * channels, channels), preferred_...]
    reduce_sum x4 -> x3, other arithmetic: 10.6 us -> 6.75 us  [attend(): total = jnp.sum(weights, axis=-1, keepdims=True)]
  transfers between devices with their start and end apart: 7 -> 7, of which waited for: 2 -> 2; matrix products, arithmetic and copies ran while one was open for 39% -> 28% of each run, Pallas kernels for 0% -> 0%
where the time goes in v7:
time: 213 us; the launch traced here: 211 us
  waiting for transfers between devices  84.9 us (40%)
  matrix products  29.3 us (14%)
  local copies, waits for them, and re-layouts  27.2 us (13%)
  other arithmetic  26.7 us (13%)
  starting transfers between devices  26 us (12%)
  between operations  17.3 us (8%)
    ppermute x4, waiting for transfers between devices, move(): return lax.ppermute(value, 'span', pairs)  84.2 us
    ppermute x4, starting transfers between devices, move(): return lax.ppermute(value, 'span', pairs)  19.8 us
    dot_general x6, matrix products, weighted(): jnp.einsum('hqk,khd->hqd', weights.astype(jnp.bfloat16), values, preferre...  17.1 us
    unnamed x70, local copies, waits for them, and re-layouts  15.6 us
    dot_general x6, matrix products, part_stats(): jnp.einsum('qhd,khd->hqk', q, k, preferred_element_type=jnp.float32) * scale  9.47 us
    reduce_sum x3, other arithmetic, attend(): total = jnp.sum(weights, axis=-1, keepdims=True)  6.75 us
    select_n x2, other arithmetic, pick(): out = jnp.where(lane == l, options[l], out)  5.47 us
    slice x2, local copies, waits for them, and re-layouts, attend(): v = kv[1].reshape(-1, HG, DH)  4.96 us
  transfers between devices with their start and end apart: 7, of which 2 were waited for; matrix products, arithmetic and copies ran while one was open for 28% of the time, Pallas kernels for 0%

profile of v7, /device:TPU:0, one launch (start us, length us, event | category | flops | bytes accessed | tf_op | source)
XLA Modules:
  0.0 211.4 jit_solution(13323676650205712571)
XLA Ops:
  7.2 3.0 %copy.25 = bf16[2,256,2560]{1,2,0:T(8,128)(2,1)S(1)} copy(bf16[2,256,2560]{2,1,0:T(8,128)(2,1)} %param.11) | data formatting | bytes 5242880 | tf_op args[1]
  10.8 1.7 broadcast_select_fusion.1
  12.5 1.8 broadcast_select_fusion
  14.4 0.7 all-reduce.3.cloned.1.call-update
  15.1 6.4 %collective-permute-start.1 = (bf16[2,256,2560]{1,2,0:T(8,128)(2,1)}, bf16[2,256,2560]{1,2,0:T(8,128)(2,1)}, u32[]{:S(2)}, u32[]{:S(2)}) collective-permute-start(bf16[2,256,2560]{1,2,0:T(8,128)(2,1)} %broadcast_select_fusion), channel_id=1, source_target_pairs={{0,2},{4,6},{8,10},{12,14},{1,3},{5,7},{9,11},{13,15},{2,1},{6,5},... | collective-permute-start | bytes 7864328 | tf_op jit(solution)/shard_map/ppermute | solution.py:31
  21.8 0.7 pad_maximum_fusion.1
  22.6 1.3 collective-permute-start.5
  23.8 4.9 %collective-permute-start.4 = (bf16[5,1,52,384]{3,2,0,1:T(8,128)(2,1)}, bf16[5,1,52,384]{3,2,0,1:T(8,128)(2,1)}, u32[]{:S(2)}, u32[]{:S(2)}) collective-permute-start(bf16[5,1,52,384]{3,2,0,1:T(8,128)(2,1)} %pad_maximum_fusion.1), channel_id=1, source_target_pairs={{0,1},{1,2},{2,3},{3,4},{4,5},{5,6},{6,7},{7,8},{8,9},{9,10},{10,1... | collective-permute-start | bytes 599048 | tf_op jit(solution)/shard_map/ppermute | solution.py:22
  31.5 1.3 fusion.111
  32.8 1.3 fusion.110
  34.7 2.4 %fusion.126 = (bf16[256,1280]{1,0:T(8,128)(2,1)}, bf16[256,1280]{1,0:T(8,128)(2,1)}) fusion(bf16[256,2560]{1,0:T(8,128)(2,1)} %param.10), kind=kLoop, calls=%fused_computation.207 | loop fusion | bytes 2621440 | tf_op jit(solution)/shard_map/slice | solution.py:130
  37.1 1.3 copy.84
  38.5 2.2 %copy.85 = bf16[256,1280]{0,1:T(8,128)(2,1)} copy(bf16[256,1280]{1,0:T(8,128)(2,1)} %get-tuple-element.51) | data formatting | bytes 1310720
  40.7 0.7 iota_compare_fusion.2
  41.4 1.3 select_select_fusion.3
  43.3 1.3 select_maximum_fusion
  44.6 0.9 slice_dynamic-update-slice_fusion.22
  45.7 0.9 slice_dynamic-update-slice_fusion.17
  46.7 0.9 slice_dynamic-update-slice_fusion.14
  47.8 41.4 %collective-permute-done.1 = bf16[2,256,2560]{1,2,0:T(8,128)(2,1)} collective-permute-done((bf16[2,256,2560]{1,2,0:T(8,128)(2,1)}, bf16[2,256,2560]{1,2,0:T(8,128)(2,1)}, u32[]{:S(2)}, u32[]{:S(2)}) %collective-permute-start.1) | collective-permute-done | bytes 2621472 | tf_op jit(solution)/shard_map/ppermute | solution.py:31
  89.2 2.7 %select_select_fusion.1 = (bf16[2,256,2560]{1,2,0:T(8,128)(2,1)S(1)}, bf16[2,768,2560]{1,2,0:T(8,128)(2,1)S(1)}) fusion(bf16[2,256,2560]{1,2,0:T(8,128)(2,1)} %collective-permute-done.1, bf16[2,256,2560]{1,2,0:T(8,128)(2,1)} %collective-permute-done, pred[]{:T(512)S(6)} %eq.56, pred[]{:T(512)S(6)} %eq.53), kind=kLoop, calls=%fused_computation.39 | loop fusion | flops 2621439 | bytes 10485762 | tf_op jit(solution)/shard_map/jit(_where)/select_n | solution.py:47
  92.0 1.3 collective-permute-start.2
  93.3 0.9 slice_dynamic-update-slice_fusion.9
  94.3 0.9 slice_dynamic-update-slice_fusion.6
  95.6 1.1 slice_dynamic-update-slice_fusion.1
  96.8 42.8 %collective-permute-done.2 = bf16[2,256,2560]{1,2,0:T(8,128)(2,1)S(1)} collective-permute-done((bf16[2,256,2560]{1,2,0:T(8,128)(2,1)S(1)}, bf16[2,256,2560]{1,2,0:T(8,128)(2,1)S(1)}, u32[]{:S(2)}, u32[]{:S(2)}) %collective-permute-start.2) | collective-permute-done | bytes 2621472 | tf_op jit(solution)/shard_map/ppermute | solution.py:31
  139.6 2.7 %select_select_fusion = (bf16[2,256,2560]{1,2,0:T(8,128)(2,1)S(1)}, bf16[2,768,2560]{1,2,0:T(8,128)(2,1)S(1)}) fusion(bf16[2,256,2560]{1,2,0:T(8,128)(2,1)} %collective-permute-done.1, bf16[2,256,2560]{1,2,0:T(8,128)(2,1)S(1)} %collective-permute-done.2, pred[]{:T(512)S(6)} %eq.56, pred[]{:T(512)S(6)} %eq.53, bf16[2,768,2560]{1,2,0:T(8,128)(2,1)S(1)} %get-tuple-element.49), kind=kLoop, calls=%fused_computation.38 | loop fusion | flops 2621440 | bytes 10485762 | tf_op jit(solution)/shard_map/jit(_where)/select_n | solution.py:47
  142.3 12.1 %collective-permute-start.3 = (bf16[2,256,2560]{1,2,0:T(8,128)(2,1)S(1)}, bf16[2,256,2560]{1,2,0:T(8,128)(2,1)S(1)}, u32[]{:S(2)}, u32[]{:S(2)}) collective-permute-start(bf16[2,256,2560]{1,2,0:T(8,128)(2,1)S(1)} %get-tuple-element.46), channel_id=1, source_target_pairs={{0,1},{4,5},{8,9},{12,13},{1,0},{5,4},{9,8},{13,12},{2,3},{6,7},{1... | collective-permute-start | bytes 7864328 | tf_op jit(solution)/shard_map/ppermute | solution.py:31
  154.5 2.8 %fusion.84 = bf16[3,1,52,384]{3,2,1,0:T(8,128)(2,1)} fusion(bf16[10368,384,1]{1,0,2:T(8,128)(2,1)S(1)} %bitcast.234, bf16[3,1,52,10368]{3,2,0,1:T(8,128)(2,1)S(1)} %slice_dynamic-update-slice_fusion, bf16[3,1,52,384]{3,2,1,0:T(8,128)(2,1)S(1)} %copy-done.5, f32[384]{0:T(512)S(1)} %copy-done.13), kind=kOutput, calls=%fused_computation.98 | convolution fusion | flops 1242408960 | bytes 11438592 | tf_op jit(solution)/shard_map/dot_general | solution.py:167
  157.2 3.0 %pad_maximum_fusion = (bf16[1,512,1280]{1,2,0:T(8,128)(2,1)}, bf16[1,512,1280]{1,2,0:T(8,128)(2,1)S(1)}, bf16[1,512,1280]{1,2,0:T(8,128)(2,1)}, bf16[1,512,1280]{1,2,0:T(8,128)(2,1)S(1)}) fusion(bf16[2,256,2560]{1,2,0:T(8,128)(2,1)} %collective-permute-done, bf16[2,256,2560]{1,2,0:T(8,128)(2,1)S(1)} %copy.25), kind=kLoop, calls=%fused_computation.85 | loop fusion | flops 10485760 | bytes 10485760 | tf_op jit(solution)/shard_map/concatenate | solution.py:123
  160.2 0.9 fusion.128
  161.3 2.1 %bitcast_reduce_fusion.2 = (f32[10,256]{1,0:T(8,128)S(1)}, f32[10,256]{1,0:T(8,128)S(1)}, f32[10,512,256]{2,1,0:T(8,128)S(1)}) fusion(pred[512]{0:T(512)(128)(4,1)S(1)} %pad_add_fusion.1, f32[10,512,256]{2,1,0:T(8,128)S(1)} %fusion.128, bf16[512,10,128]{0,2,1:T(8,128)(2,1)S(1)} %bitcast.243, bf16[256,10,128]{0,2,1:T(8,128)(2,1)S(1)} %bitcast.240), kind=kOutput, calls=%fused_computation.19 | convolution fusion | flops 343403520 | bytes 12472832 | tf_op jit(solution)/shard_map/qhd,khd->hqk/dot_general | solution.py:58
  163.4 2.4 %fusion.11 = (f32[10,256]{1,0:T(8,128)S(1)}, f32[10,256]{1,0:T(8,128)S(1)}) fusion(f32[10,512,256]{2,1,0:T(8,128)S(1)} %get-tuple-element.68, f32[10,256]{1,0:T(8,128)S(1)} %get-tuple-element.28, pred[512]{0:T(512)(128)(4,1)S(1)} %pad_add_fusion.1, f32[10,256]{1,0:T(8,128)S(1)} %get-tuple-element.29, f32[10,512,256]{2,1,0:T(8,128)S(1)} %fusion.128), kind=kLoop, calls=%fused_computation.29 | loop fusion | flops 10480640 | bytes 10527232 | tf_op jit(solution)/shard_map/reduce_sum | solution.py:76
  166.0 2.3 %fusion.124 = (bf16[1,768,1280]{1,2,0:T(8,128)(2,1)}, bf16[1,768,1280]{1,2,0:T(8,128)(2,1)S(1)}, bf16[1,768,1280]{1,2,0:T(8,128)(2,1)}, bf16[1,768,1280]{1,2,0:T(8,128)(2,1)S(1)}) fusion(bf16[2,768,2560]{1,2,0:T(8,128)(2,1)S(1)} %constant_dynamic-update-slice_fusion), kind=kLoop, calls=%fused_computation.205 | loop fusion | bytes 15728640 | tf_op jit(solution)/shard_map/slice | solution.py:70
  168.3 1.2 fusion.129
  169.5 3.3 %bitcast_reduce_fusion = (f32[10,256]{1,0:T(8,128)S(1)}, f32[10,256]{1,0:T(8,128)S(1)}, f32[10,768,256]{2,1,0:T(8,128)S(1)}) fusion(pred[768]{0:T(1024)(128)(4,1)S(1)} %pad_add_fusion, f32[10,768,256]{2,1,0:T(8,128)S(1)} %fusion.129, bf16[768,10,128]{0,2,1:T(8,128)(2,1)S(1)} %bitcast.239, bf16[256,10,128]{0,2,1:T(8,128)(2,1)S(1)} %bitcast.241), kind=kOutput, calls=%fused_computation.1 | convolution fusion | flops 515107840 | bytes 18371328 | tf_op jit(solution)/shard_map/qhd,khd->hqk/dot_general | solution.py:58
  172.9 3.3 %fusion.14 = f32[10,256,128]{2,1,0:T(8,128)} fusion(bf16[768,10,128]{0,2,1:T(8,128)(2,1)S(1)} %bitcast.249, f32[10,768,256]{2,1,0:T(8,128)S(1)} %fusion.129, f32[10,256]{1,0:T(8,128)S(1)} %get-tuple-element.33, pred[768]{0:T(1024)(128)(4,1)S(1)} %pad_add_fusion), kind=kOutput, calls=%fused_computation.31 | convolution fusion | flops 511180800 | bytes 11152128 | tf_op jit(solution)/shard_map/hqk,khd->hqd/dot_general | solution.py:63
  176.2 3.8 %fusion.5 = (f32[10,256]{1,0:T(8,128)S(1)}, f32[10,256]{1,0:T(8,128)S(1)}) fusion(f32[10,768,256]{2,1,0:T(8,128)S(1)} %get-tuple-element.69, f32[10,256]{1,0:T(8,128)S(1)} %get-tuple-element.31, pred[768]{0:T(1024)(128)(4,1)S(1)} %pad_add_fusion, f32[10,256]{1,0:T(8,128)S(1)} %get-tuple-element.33, f32[10,768,256]{2,1,0:T(8,128)S(1)} %fusion.129), kind=kLoop, calls=%fused_computation.17 | loop fusion | flops 15723520 | bytes 15770368 | tf_op jit(solution)/shard_map/reduce_sum | solution.py:76
  180.0 2.9 %fusion.58 = f32[10,256,128]{2,1,0:T(8,128)} fusion(f32[10,256,128]{2,1,0:T(8,128)S(1)} %copy-done.16, bf16[512,10,128]{0,2,1:T(8,128)(2,1)S(1)} %bitcast.251, f32[10,512,256]{2,1,0:T(8,128)S(1)} %fusion.128, f32[10,256]{1,0:T(8,128)S(1)} %get-tuple-element.29, pred[512]{0:T(512)(128)(4,1)S(1)} %pad_add_fusion.1, f32[10,256]{1,0:T(8,128)S(1)} %get-tuple-element.32), kind=kOutput, calls=%fused_computation.81 | convolution fusion | flops 341442560 | bytes 9196032 | tf_op jit(solution)/shard_map/hqk,khd->hqd/dot_general | solution.py:63
  182.9 2.2 %fusion.12 = f32[10,256,128]{2,1,0:T(8,128)S(1)} fusion(bf16[768,10,128]{0,2,1:T(8,128)(2,1)S(1)} %bitcast.248, f32[10,768,256]{2,1,0:T(8,128)S(1)} %get-tuple-element.69, f32[10,256]{1,0:T(8,128)S(1)} %get-tuple-element.31, pred[768]{0:T(1024)(128)(4,1)S(1)} %pad_add_fusion), kind=kOutput, calls=%fused_computation.30 | convolution fusion | flops 511180800 | bytes 11152128 | tf_op jit(solution)/shard_map/hqk,khd->hqd/dot_general | solution.py:63
  185.2 2.8 %fusion.55 = f32[10,256,128]{2,1,0:T(8,128)} fusion(f32[10,256,128]{2,1,0:T(8,128)S(1)} %fusion.12, bf16[512,10,128]{0,2,1:T(8,128)(2,1)S(1)} %bitcast.250, f32[10,512,256]{2,1,0:T(8,128)S(1)} %bitcast.231, f32[10,256]{1,0:T(8,128)S(1)} %get-tuple-element.28, pred[512]{0:T(512)(128)(4,1)S(1)} %pad_add_fusion.1, f32[10,256]{1,0:T(8,128)S(1)} %get-tuple-element.30), kind=kOutput, calls=%fused_computation.80 | convolution fusion | flops 341442560 | bytes 9196032 | tf_op jit(solution)/shard_map/hqk,khd->hqd/dot_general | solution.py:63
  187.9 2.7 %fusion.125 = (bf16[1,256,1280]{1,2,0:T(8,128)(2,1)}, bf16[1,256,1280]{1,2,0:T(8,128)(2,1)S(1)}, bf16[1,256,1280]{1,2,0:T(8,128)(2,1)S(1)}, bf16[1,256,1280]{1,2,0:T(8,128)(2,1)S(1)}) fusion(bf16[2,256,2560]{1,2,0:T(8,128)(2,1)} %all-reduce.3.cloned.1.call-done), kind=kLoop, calls=%fused_computation.206 | loop fusion | bytes 5242880 | tf_op jit(solution)/shard_map/slice | solution.py:70
  191.3 1.3 fusion.41
  194.1 2.3 %fusion.48 = bf16[256,10,128]{2,0,1:T(8,128)(2,1)} fusion(bf16[256,10,128]{0,2,1:T(8,128)(2,1)S(1)} %bitcast.253, f32[10,256,256]{2,1,0:T(8,128)S(1)} %get-tuple-element.72, f32[10,256]{1,0:T(8,128)S(1)} %fusion.107, f32[10,256,128]{2,1,0:T(8,128)S(1)} %copy-done.15, pred[256]{0:T(512)(128)(4,1)S(1)} %compare_and_fusion, ...), kind=kOutput, calls=%fused_computation.77 | convolution fusion | flops 171704320 | bytes 5273856 | tf_op jit(solution)/shard_map/hqk,khd->hqd/dot_general | solution.py:63
  196.4 1.3 copy.55
  197.8 3.6 %fusion.46 = bf16[256,10,128]{2,0,1:T(8,128)(2,1)} fusion(bf16[256,10,128]{0,2,1:T(8,128)(2,1)} %bitcast.252, f32[10,256,256]{2,1,0:T(8,128)S(1)} %copy-done.3, f32[10,256]{1,0:T(8,128)S(1)} %fusion.106, f32[10,256,128]{2,1,0:T(8,128)} %fusion.58, pred[256]{0:T(512)(128)(4,1)S(1)} %compare_and_fusion, f32[10,256]{1,0:T(8,128)S(1)} %get-tuple-element.53, ...), kind=kOutput, calls=%fused_computation.75 | convolution fusion | flops 171704320 | bytes 5273856 | tf_op jit(solution)/shard_map/hqk,khd->hqd/dot_general | solution.py:63
  201.4 1.3 copy.50
  203.0 1.6 copy.58
  (93 shorter events, 6.0 us)
Async XLA Ops:
  14.4 7.2 %copy-start.10 = (bf16[2,1,52,384]{3,0,2,1:T(2,128)(2,1)S(1)}, bf16[2,1,52,384]{3,0,2,1:T(2,128)(2,1)}, u32[]{:S(2)}) copy-start(bf16[2,1,52,384]{3,0,2,1:T(2,128)(2,1)} %param.16) | copy-start | bytes 239620
  14.4 7.2 %copy-start.4 = (bf16[3,1,52,384]{3,2,1,0:T(8,128)(2,1)S(1)}, bf16[3,1,52,384]{3,2,1,0:T(8,128)(2,1)}, u32[]{:S(2)}) copy-start(bf16[3,1,52,384]{3,2,1,0:T(8,128)(2,1)} %param.15) | copy-start | bytes 359428
  14.4 7.3 %copy-start.12 = (f32[384]{0:T(512)S(1)}, f32[384]{0:T(512)}, u32[]{:S(2)}) copy-start(f32[384]{0:T(512)} %param.17) | copy-start | bytes 4612
  14.4 14.4 %copy-start.14 = (s32[16,3]{0,1:T(4,128)S(1)}, s32[16,3]{0,1:T(4,128)}, u32[]{:S(2)}) copy-start(s32[16,3]{0,1:T(4,128)} %param.13) | copy-start | bytes 580
  14.4 16.4 %copy-start.11 = (s32[16]{0:T(128)S(1)}, s32[16]{0:T(128)}, u32[]{:S(2)}) copy-start(s32[16]{0:T(128)} %param.14) | copy-start | bytes 196
  14.4 173.6 %all-reduce.3.cloned.1.call-start = ((), (), s32[]{:S(2)}) async-start(), calls=%async_computation | async-start | bytes 5242880 | tf_op jit(solution)/shard_map/psum | solution.py:105
  15.1 74.1 %collective-permute-start.1 = (bf16[2,256,2560]{1,2,0:T(8,128)(2,1)}, bf16[2,256,2560]{1,2,0:T(8,128)(2,1)}, u32[]{:S(2)}, u32[]{:S(2)}) collective-permute-start(bf16[2,256,2560]{1,2,0:T(8,128)(2,1)} %broadcast_select_fusion), channel_id=1, source_target_pairs={{0,2},{4,6},{8,10},{12,14},{1,3},{5,7},{9,11},{13,15},{2,1},{6,5},... | collective-permute-start | bytes 7864328 | tf_op jit(solution)/shard_map/ppermute | solution.py:31
  21.5 67.7 %collective-permute-start = (bf16[2,256,2560]{1,2,0:T(8,128)(2,1)}, bf16[2,256,2560]{1,2,0:T(8,128)(2,1)}, u32[]{:S(2)}, u32[]{:S(2)}) collective-permute-start(bf16[2,256,2560]{1,2,0:T(8,128)(2,1)} %broadcast_select_fusion), channel_id=1, source_target_pairs={{0,1},{4,5},{8,9},{12,13},{2,3},{6,7},{10,11},{14,15},{1,4},{5,8},... | collective-permute-start | bytes 7864328 | tf_op jit(solution)/shard_map/ppermute | solution.py:31
  22.6 20.7 %collective-permute-start.5 = (bf16[5,1,52,384]{3,2,0,1:T(8,128)(2,1)}, bf16[5,1,52,384]{3,2,0,1:T(8,128)(2,1)}, u32[]{:S(2)}, u32[]{:S(2)}) collective-permute-start(bf16[5,1,52,384]{3,2,0,1:T(8,128)(2,1)} %pad_maximum_fusion.1), channel_id=1, source_target_pairs={{1,0},{2,1},{3,2},{4,3},{5,4},{6,5},{7,6},{8,7},{9,8},{10,9},{11,1... | collective-permute-start | bytes 599048 | tf_op jit(solution)/shard_map/ppermute | solution.py:25
  23.8 19.4 %collective-permute-start.4 = (bf16[5,1,52,384]{3,2,0,1:T(8,128)(2,1)}, bf16[5,1,52,384]{3,2,0,1:T(8,128)(2,1)}, u32[]{:S(2)}, u32[]{:S(2)}) collective-permute-start(bf16[5,1,52,384]{3,2,0,1:T(8,128)(2,1)} %pad_maximum_fusion.1), channel_id=1, source_target_pairs={{0,1},{1,2},{2,3},{3,4},{4,5},{5,6},{6,7},{7,8},{8,9},{9,10},{10,1... | collective-permute-start | bytes 599048 | tf_op jit(solution)/shard_map/ppermute | solution.py:22
  47.8 47.5 %copy-start.5 = (bf16[3,1,52,384]{3,2,1,0:T(8,128)(2,1)S(1)}, bf16[3,1,52,384]{3,2,1,0:T(8,128)(2,1)}, u32[]{:S(2)}) copy-start(bf16[3,1,52,384]{3,2,1,0:T(8,128)(2,1)} %param.15) | copy-start | bytes 359428
  89.2 65.2 %slice-start.2 = ((s8[7962624]{0:T(1024)(128)(4,1)}), s8[4194304]{0:T(1024)(128)(4,1)S(1)}, s32[]{:S(2)}) async-start(s8[7962624]{0:T(1024)(128)(4,1)} %bitcast.232), calls=%async_computation.3 | async-start | bytes 8388608
  92.0 47.6 %collective-permute-start.2 = (bf16[2,256,2560]{1,2,0:T(8,128)(2,1)S(1)}, bf16[2,256,2560]{1,2,0:T(8,128)(2,1)S(1)}, u32[]{:S(2)}, u32[]{:S(2)}) collective-permute-start(bf16[2,256,2560]{1,2,0:T(8,128)(2,1)S(1)} %get-tuple-element.48), channel_id=1, source_target_pairs={{3,2},{7,6},{11,10},{15,14},{2,0},{6,4},{10,8},{14,12},{1,5},{5,9}... | collective-permute-start | bytes 7864328 | tf_op jit(solution)/shard_map/ppermute | solution.py:31
  95.3 59.1 %slice-start.3 = ((s8[7962624]{0:T(1024)(128)(4,1)}), s8[3768320]{0:T(1024)(128)(4,1)S(1)}, s32[]{:S(2)}) async-start(s8[7962624]{0:T(1024)(128)(4,1)} %bitcast.232), calls=%async_computation.4 | async-start | bytes 7536640
  139.6 14.9 %copy-start.13 = (f32[384]{0:T(512)S(1)}, f32[384]{0:T(512)}, u32[]{:S(2)}) copy-start(f32[384]{0:T(512)} %param.19) | copy-start | bytes 4612
  142.3 23.5 %collective-permute-start.3 = (bf16[2,256,2560]{1,2,0:T(8,128)(2,1)S(1)}, bf16[2,256,2560]{1,2,0:T(8,128)(2,1)S(1)}, u32[]{:S(2)}, u32[]{:S(2)}) collective-permute-start(bf16[2,256,2560]{1,2,0:T(8,128)(2,1)S(1)} %get-tuple-element.46), channel_id=1, source_target_pairs={{0,1},{4,5},{8,9},{12,13},{1,0},{5,4},{9,8},{13,12},{2,3},{6,7},{1... | collective-permute-start | bytes 7864328 | tf_op jit(solution)/shard_map/ppermute | solution.py:31
  160.2 1.1 copy-start.1
  163.4 2.4 %copy-start = (f32[10,512,256]{2,1,0:T(8,128)}, f32[10,512,256]{2,1,0:T(8,128)S(1)}, u32[]{:S(2)}) copy-start(f32[10,512,256]{2,1,0:T(8,128)S(1)} %get-tuple-element.68) | copy-start | bytes 15728644
  169.5 3.3 %copy-start.7 = (bf16[1,768,1280]{1,2,0:T(8,128)(2,1)S(1)}, bf16[1,768,1280]{1,2,0:T(8,128)(2,1)}, u32[]{:S(2)}) copy-start(bf16[1,768,1280]{1,2,0:T(8,128)(2,1)} %get-tuple-element.36) | copy-start | bytes 5898244
  176.2 3.8 %copy-start.9 = (bf16[1,512,1280]{1,2,0:T(8,128)(2,1)S(1)}, bf16[1,512,1280]{1,2,0:T(8,128)(2,1)}, u32[]{:S(2)}) copy-start(bf16[1,512,1280]{1,2,0:T(8,128)(2,1)} %get-tuple-element.40) | copy-start | bytes 3932164
  176.2 3.8 %copy-start.16 = (f32[10,256,128]{2,1,0:T(8,128)S(1)}, f32[10,256,128]{2,1,0:T(8,128)}, u32[]{:S(2)}) copy-start(f32[10,256,128]{2,1,0:T(8,128)} %fusion.14) | copy-start | bytes 3932164
  180.0 2.9 %copy-start.6 = (bf16[1,768,1280]{1,2,0:T(8,128)(2,1)S(1)}, bf16[1,768,1280]{1,2,0:T(8,128)(2,1)}, u32[]{:S(2)}) copy-start(bf16[1,768,1280]{1,2,0:T(8,128)(2,1)} %get-tuple-element.34) | copy-start | bytes 5898244
  180.0 5.1 %slice-start = ((s8[5242880]{0:T(1024)(128)(4,1)}), s8[4194304]{0:T(1024)(128)(4,1)S(1)}, s32[]{:S(2)}) async-start(s8[5242880]{0:T(1024)(128)(4,1)} %bitcast.230), calls=%async_computation.1 | async-start | bytes 8388608
  182.9 2.2 %slice-start.1 = ((s8[5242880]{0:T(1024)(128)(4,1)}), s8[1048576]{0:T(1024)(128)(4,1)S(1)}, s32[]{:S(2)}) async-start(s8[5242880]{0:T(1024)(128)(4,1)} %bitcast.230), calls=%async_computation.2 | async-start | bytes 2097152
  182.9 2.2 %copy-start.8 = (bf16[1,512,1280]{1,2,0:T(8,128)(2,1)S(1)}, bf16[1,512,1280]{1,2,0:T(8,128)(2,1)}, u32[]{:S(2)}) copy-start(bf16[1,512,1280]{1,2,0:T(8,128)(2,1)} %get-tuple-element.38) | copy-start | bytes 3932164
  191.3 1.5 copy-start.2
  192.8 1.3 copy-start.15
  194.1 3.6 %copy-start.3 = (f32[10,256,256]{2,1,0:T(8,128)S(1)}, f32[10,256,256]{2,1,0:T(8,128)}, u32[]{:S(2)}) copy-start(f32[10,256,256]{2,1,0:T(8,128)} %copy-done.2) | copy-start | bytes 7864324
Sparse Core Ops, SparseCore 0:
  18.8 131.9 all-reduce.2

commit v8 on v7

--- a/solution.py
+++ b/solution.py
@@ -120,10 +120,10 @@
         return out
 
     groups = [
-        (jnp.concatenate([keys_values, along], axis=1),
-         jnp.concatenate([valid_list[0], offset_of(3, 1, 3, 1)])),
-        (jnp.concatenate([cross, second, third], axis=1),
-         jnp.concatenate([offset_of(4, 4, 2, 2), offset_of(1, 3, 1, 4), offset_of(2, 2, 4, 3)])),
+        (keys_values, valid_list[0]),
+        (jnp.concatenate([along, cross, second, third], axis=1),
+         jnp.concatenate([offset_of(3, 1, 3, 1), offset_of(4, 4, 2, 2), offset_of(1, 3, 1, 4),
+                          offset_of(2, 2, 4, 3)])),
     ]
     anchor_valid = (place != anchor) & (row_ids < lengths[anchor])
     heads = [slice(h * HG * DH, (h + 1) * HG * DH) for h in range(H // HG)]

time: 213 us -> 224 us (1.052)
  matrix products: 29.3 us -> 38.6 us
  other arithmetic: 26.7 us -> 30.9 us
  waiting for transfers between devices: 84.9 us -> 82.1 us
  starting transfers between devices: 26 us -> 28.3 us
    dot_general x6, matrix products: 17.1 us -> 24.4 us  [weighted(): jnp.einsum('hqk,khd->hqd', weights.astype(jnp.bfloat16), values, preferre...]
    select_n x2, other arithmetic: 5.47 us -> 10 us  [pick(): out = jnp.where(lane == l, options[l], out)]
    reduce_sum x3, other arithmetic: 6.75 us -> 10.1 us  [attend(): total = jnp.sum(weights, axis=-1, keepdims=True)]
    concatenate x3 -> x1, other arithmetic: 3 us -> 0.01 us  [shards(): jnp.concatenate([offset_of(3, 1, 3, 1), offset_of(4, 4, 2, 2), offset_of(...]
    ppermute x4, waiting for transfers between devices: 84.2 us -> 81.4 us  [move(): return lax.ppermute(value, 'span', pairs)]
    slice x2 -> x3, local copies, waits for them, and re-layouts: 4.96 us -> 7.23 us  [attend(): v = kv[1].reshape(-1, HG, DH)]
    unnamed x70 -> x79, local copies, waits for them, and re-layouts: 15.6 us -> 13.9 us
  transfers between devices with their start and end apart: 7 -> 7, of which waited for: 2 -> 2; matrix products, arithmetic and copies ran while one was open for 28% -> 33% of each run, Pallas kernels for 0% -> 0%
where the time goes in v8:
time: 224 us
  waiting for transfers between devices  82.1 us (37%)
  matrix products  38.6 us (17%)
  other arithmetic  30.9 us (14%)
  starting transfers between devices  28.3 us (13%)
  local copies, waits for them, and re-layouts  27 us (12%)
  between operations  17.3 us (8%)
    ppermute x4, waiting for transfers between devices, move(): return lax.ppermute(value, 'span', pairs)  81.4 us
    dot_general x6, matrix products, weighted(): jnp.einsum('hqk,khd->hqd', weights.astype(jnp.bfloat16), values, preferre...  24.4 us
    ppermute x4, starting transfers between devices, move(): return lax.ppermute(value, 'span', pairs)  22 us
    unnamed x79, local copies, waits for them, and re-layouts  13.9 us
    dot_general x6, matrix products, part_stats(): jnp.einsum('qhd,khd->hqk', q, k, preferred_element_type=jnp.float32) * scale  11.6 us
    reduce_sum x3, other arithmetic, attend(): total = jnp.sum(weights, axis=-1, keepdims=True)  10.1 us
    select_n x2, other arithmetic, pick(): out = jnp.where(lane == l, options[l], out)  10 us
    slice x3, local copies, waits for them, and re-layouts, attend(): v = kv[1].reshape(-1, HG, DH)  7.23 us
  transfers between devices with their start and end apart: 7, of which 2 were waited for; matrix products, arithmetic and copies ran while one was open for 33% of the time, Pallas kernels for 0%

profile of v8, /device:TPU:0, one launch (start us, length us, event | category | flops | bytes accessed | tf_op | source)
XLA Modules:
  0.0 224.1 jit_solution(6199660129351317215)
XLA Ops:
  7.2 3.0 %copy.25 = bf16[2,256,2560]{1,2,0:T(8,128)(2,1)S(1)} copy(bf16[2,256,2560]{2,1,0:T(8,128)(2,1)} %param.11) | data formatting | bytes 5242880 | tf_op args[1]
  10.8 1.6 broadcast_select_fusion.1
  12.4 1.8 broadcast_select_fusion
  14.3 0.7 all-reduce.3.cloned.1.call-update
  15.0 6.4 %collective-permute-start.1 = (bf16[2,256,2560]{1,2,0:T(8,128)(2,1)}, bf16[2,256,2560]{1,2,0:T(8,128)(2,1)}, u32[]{:S(2)}, u32[]{:S(2)}) collective-permute-start(bf16[2,256,2560]{1,2,0:T(8,128)(2,1)} %broadcast_select_fusion), channel_id=1, source_target_pairs={{0,2},{4,6},{8,10},{12,14},{1,3},{5,7},{9,11},{13,15},{2,1},{6,5},... | collective-permute-start | bytes 7864328 | tf_op jit(solution)/shard_map/ppermute | solution.py:31
  21.7 0.7 pad_maximum_fusion
  22.4 1.3 collective-permute-start.5
  23.7 4.9 %collective-permute-start.4 = (bf16[5,1,52,384]{3,2,0,1:T(8,128)(2,1)}, bf16[5,1,52,384]{3,2,0,1:T(8,128)(2,1)}, u32[]{:S(2)}, u32[]{:S(2)}) collective-permute-start(bf16[5,1,52,384]{3,2,0,1:T(8,128)(2,1)} %pad_maximum_fusion), channel_id=1, source_target_pairs={{0,1},{1,2},{2,3},{3,4},{4,5},{5,6},{6,7},{7,8},{8,9},{9,10},{10,1... | collective-permute-start | bytes 599048 | tf_op jit(solution)/shard_map/ppermute | solution.py:22
  28.6 1.6 fusion.115
  32.9 1.4 fusion.116
  34.8 0.7 fusion.117
  36.8 1.2 select_select_fusion.3
  38.0 1.3 fusion.99
  39.3 1.0 fusion.24
  40.4 1.8 fusion.28
  42.1 1.3 compare_and_fusion
  43.5 1.3 select_maximum_fusion
  44.8 0.9 slice_dynamic-update-slice_fusion.22
  45.9 43.2 %collective-permute-done.1 = bf16[2,256,2560]{1,2,0:T(8,128)(2,1)} collective-permute-done((bf16[2,256,2560]{1,2,0:T(8,128)(2,1)}, bf16[2,256,2560]{1,2,0:T(8,128)(2,1)}, u32[]{:S(2)}, u32[]{:S(2)}) %collective-permute-start.1) | collective-permute-done | bytes 2621472 | tf_op jit(solution)/shard_map/ppermute | solution.py:31
  89.1 5.0 %select_select_fusion.1 = (bf16[2,256,2560]{1,2,0:T(8,128)(2,1)}, bf16[2,1024,2560]{1,2,0:T(8,128)(2,1)S(1)}) fusion(bf16[2,256,2560]{1,2,0:T(8,128)(2,1)} %collective-permute-done.1, bf16[2,256,2560]{1,2,0:T(8,128)(2,1)} %collective-permute-done, pred[]{:T(512)S(6)} %eq.56, pred[]{:T(512)S(6)} %eq.53), kind=kLoop, calls=%fused_computation.23 | loop fusion | flops 2621439 | bytes 10485762 | tf_op jit(solution)/shard_map/jit(_where)/select_n | solution.py:47
  94.1 1.3 collective-permute-start.2
  95.4 0.9 slice_dynamic-update-slice_fusion.17
  96.4 0.9 slice_dynamic-update-slice_fusion.14
  97.5 0.9 slice_dynamic-update-slice_fusion.9
  98.5 2.3 %constant_dynamic-update-slice_fusion.2 = bf16[2,1024,2560]{1,2,0:T(8,128)(2,1)S(1)} fusion(bf16[2,1024,2560]{1,2,0:T(8,128)(2,1)S(1)} %get-tuple-element.49, bf16[2,256,2560]{1,2,0:T(8,128)(2,1)} %collective-permute-done.1), kind=kLoop, calls=%fused_computation.136 | loop fusion | bytes 5242880
  100.8 38.2 %collective-permute-done.2 = bf16[2,256,2560]{1,2,0:T(8,128)(2,1)} collective-permute-done((bf16[2,256,2560]{1,2,0:T(8,128)(2,1)}, bf16[2,256,2560]{1,2,0:T(8,128)(2,1)}, u32[]{:S(2)}, u32[]{:S(2)}) %collective-permute-start.2) | collective-permute-done | bytes 2621472 | tf_op jit(solution)/shard_map/ppermute | solution.py:31
  139.0 5.0 %select_select_fusion = (bf16[2,256,2560]{1,2,0:T(8,128)(2,1)}, bf16[2,1024,2560]{1,2,0:T(8,128)(2,1)S(1)}) fusion(bf16[2,256,2560]{1,2,0:T(8,128)(2,1)} %collective-permute-done.1, bf16[2,256,2560]{1,2,0:T(8,128)(2,1)} %collective-permute-done.2, pred[]{:T(512)S(6)} %eq.56, pred[]{:T(512)S(6)} %eq.53, ...), kind=kLoop, calls=%fused_computation.22 | loop fusion | flops 2621440 | bytes 10485762 | tf_op jit(solution)/shard_map/jit(_where)/select_n | solution.py:47
  144.0 14.4 %collective-permute-start.3 = (bf16[2,256,2560]{1,2,0:T(8,128)(2,1)}, bf16[2,256,2560]{1,2,0:T(8,128)(2,1)S(1)}, u32[]{:S(2)}, u32[]{:S(2)}) collective-permute-start(bf16[2,256,2560]{1,2,0:T(8,128)(2,1)} %get-tuple-element.46), channel_id=1, source_target_pairs={{0,1},{4,5},{8,9},{12,13},{1,0},{5,4},{9,8},{13,12},{2,3},{6,7},{1... | collective-permute-start | bytes 7864328 | tf_op jit(solution)/shard_map/ppermute | solution.py:31
  158.5 0.9 slice_dynamic-update-slice_fusion.6
  159.7 0.9 slice_dynamic-update-slice_fusion.1
  160.8 2.7 %fusion.73 = bf16[3,1,52,384]{3,2,1,0:T(8,128)(2,1)} fusion(bf16[10368,384,1]{1,0,2:T(8,128)(2,1)S(1)} %bitcast.208, bf16[3,1,52,10368]{3,2,0,1:T(8,128)(2,1)S(1)} %slice_dynamic-update-slice_fusion, bf16[3,1,52,384]{3,2,1,0:T(8,128)(2,1)S(1)} %copy-done.8, f32[384]{0:T(512)S(1)} %copy-done.19), kind=kOutput, calls=%fused_computation.84 | convolution fusion | flops 1242408960 | bytes 11438592 | tf_op jit(solution)/shard_map/dot_general | solution.py:167
  163.8 3.0 %fusion.113 = (bf16[1,1024,1280]{1,2,0:T(8,128)(2,1)}, bf16[1,1024,1280]{1,2,0:T(8,128)(2,1)S(1)}, bf16[1,1024,1280]{1,2,0:T(8,128)(2,1)}, bf16[1,1024,1280]{1,2,0:T(8,128)(2,1)S(1)}) fusion(bf16[2,1024,2560]{1,2,0:T(8,128)(2,1)S(1)} %constant_dynamic-update-slice_fusion), kind=kLoop, calls=%fused_computation.191 | loop fusion | bytes 20971520 | tf_op jit(solution)/shard_map/slice | solution.py:70
  166.8 1.6 fusion.119
  168.4 6.2 %bitcast_reduce_fusion = (f32[10,256]{1,0:T(8,128)S(1)}, f32[10,256]{1,0:T(8,128)S(1)}, f32[10,1024,256]{2,1,0:T(8,128)}) fusion(pred[1024]{0:T(1024)(128)(4,1)S(1)} %pad_add_fusion, f32[10,1024,256]{2,1,0:T(8,128)S(1)} %fusion.119, bf16[1024,10,128]{0,2,1:T(8,128)(2,1)S(1)} %bitcast.209, bf16[256,10,128]{0,2,1:T(8,128)(2,1)S(1)} %bitcast.215), kind=kOutput, calls=%fused_computation.1 | convolution fusion | flops 686812160 | bytes 24269824 | tf_op jit(solution)/shard_map/qhd,khd->hqk/dot_general | solution.py:58
  174.6 7.4 %fusion.5 = (f32[10,256]{1,0:T(8,128)S(1)}, f32[10,256]{1,0:T(8,128)S(1)}) fusion(f32[10,1024,256]{2,1,0:T(8,128)} %get-tuple-element.69, f32[10,256]{1,0:T(8,128)S(1)} %get-tuple-element.31, pred[1024]{0:T(1024)(128)(4,1)S(1)} %pad_add_fusion, f32[10,256]{1,0:T(8,128)S(1)} %get-tuple-element.33, f32[10,1024,256]{2,1,0:T(8,128)S(1)} %fusion.119), kind=kLoop, calls=%fused_computation.11 | loop fusion | flops 20966400 | bytes 21013504 | tf_op jit(solution)/shard_map/reduce_sum | solution.py:76
  182.0 2.2 convolution_multiply_fusion.1
  184.2 6.4 %fusion.37 = f32[10,256,128]{2,1,0:T(8,128)} fusion(f32[10,256,128]{2,1,0:T(8,128)} %convolution_multiply_fusion.1, bf16[1024,10,128]{0,2,1:T(8,128)(2,1)} %bitcast.218, f32[10,1024,256]{2,1,0:T(8,128)S(1)} %fusion.119, f32[10,256]{1,0:T(8,128)S(1)} %get-tuple-element.33, pred[1024]{0:T(1024)(128)(4,1)S(1)} %pad_add_fusion), kind=kOutput, calls=%fused_computation.62 | convolution fusion | flops 681902080 | bytes 15739904 | tf_op jit(solution)/shard_map/hqk,khd->hqd/dot_general | solution.py:63
  190.7 2.3 %convolution_multiply_fusion = f32[10,256,128]{2,1,0:T(8,128)S(1)} fusion(bf16[256,10,128]{0,2,1:T(8,128)(2,1)} %bitcast.224, f32[10,256,256]{1,2,0:T(8,128)S(1)} %copy-done.1, f32[10,256]{1,0:T(8,128)S(1)} %get-tuple-element.28, pred[256]{0:T(512)(128)(4,1)S(1)} %copy-done.18, f32[10,256]{1,0:T(8,128)S(1)} %get-tuple-element.30), kind=kOutput, calls=%fused_computation.56 | convolution fusion | flops 170721280 | bytes 4608256 | tf_op jit(solution)/shard_map/hqk,khd->hqd/dot_general | solution.py:63
  193.0 8.1 %fusion.40 = f32[10,256,128]{2,1,0:T(8,128)} fusion(f32[10,256,128]{2,1,0:T(8,128)S(1)} %convolution_multiply_fusion, bf16[1024,10,128]{0,2,1:T(8,128)(2,1)S(1)} %bitcast.217, f32[10,1024,256]{2,1,0:T(8,128)} %get-tuple-element.69, f32[10,256]{1,0:T(8,128)S(1)} %get-tuple-element.31, pred[1024]{0:T(1024)(128)(4,1)S(1)} %pad_add_fusion), kind=kOutput, calls=%fused_computation.63 | convolution fusion | flops 681902080 | bytes 15739904 | tf_op jit(solution)/shard_map/hqk,khd->hqd/dot_general | solution.py:63
  201.1 2.7 %fusion.114 = (bf16[1,256,1280]{1,2,0:T(8,128)(2,1)}, bf16[1,256,1280]{1,2,0:T(8,128)(2,1)S(1)}, bf16[1,256,1280]{1,2,0:T(8,128)(2,1)S(1)}, bf16[1,256,1280]{1,2,0:T(8,128)(2,1)S(1)}) fusion(bf16[2,256,2560]{1,2,0:T(8,128)(2,1)} %all-reduce.3.cloned.1.call-done), kind=kLoop, calls=%fused_computation.192 | loop fusion | bytes 5242880 | tf_op jit(solution)/shard_map/slice | solution.py:70
  203.8 0.7 bitcast_reduce_fusion.3
  204.5 1.6 fusion.29
  206.1 1.0 fusion.31
  207.4 2.0 fusion.36
  209.4 1.3 copy.58
  210.8 3.3 %fusion.34 = bf16[256,10,128]{2,0,1:T(8,128)(2,1)} fusion(bf16[256,10,128]{0,2,1:T(8,128)(2,1)} %bitcast.226, f32[10,256,256]{1,2,0:T(8,128)S(1)} %copy-done.4, f32[10,256]{1,0:T(8,128)S(1)} %fusion.95, f32[10,256,128]{2,1,0:T(8,128)} %fusion.37, pred[256]{0:T(512)(128)(4,1)S(1)} %copy-done.20, f32[10,256]{1,0:T(8,128)S(1)} %get-tuple-element.53, ...), kind=kOutput, calls=%fused_computation.59 | convolution fusion | flops 171704320 | bytes 5273856 | tf_op jit(solution)/shard_map/hqk,khd->hqd/dot_general | solution.py:63
  214.1 1.3 copy.53
  215.7 1.6 copy.61
  (99 shorter events, 4.6 us)
Async XLA Ops:
  14.2 7.1 %copy-start.12 = (bf16[2,1,52,384]{3,0,2,1:T(2,128)(2,1)S(1)}, bf16[2,1,52,384]{3,0,2,1:T(2,128)(2,1)}, u32[]{:S(2)}) copy-start(bf16[2,1,52,384]{3,0,2,1:T(2,128)(2,1)} %param.16) | copy-start | bytes 239620
  14.2 7.1 %copy-start.7 = (bf16[3,1,52,384]{3,2,1,0:T(8,128)(2,1)S(1)}, bf16[3,1,52,384]{3,2,1,0:T(8,128)(2,1)}, u32[]{:S(2)}) copy-start(bf16[3,1,52,384]{3,2,1,0:T(8,128)(2,1)} %param.15) | copy-start | bytes 359428
  14.2 7.3 %copy-start.16 = (f32[384]{0:T(512)S(1)}, f32[384]{0:T(512)}, u32[]{:S(2)}) copy-start(f32[384]{0:T(512)} %param.17) | copy-start | bytes 4612
  14.2 186.9 %all-reduce.3.cloned.1.call-start = ((), (), s32[]{:S(2)}) async-start(), calls=%async_computation | async-start | bytes 5242880 | tf_op jit(solution)/shard_map/psum | solution.py:105
  15.0 74.1 %collective-permute-start.1 = (bf16[2,256,2560]{1,2,0:T(8,128)(2,1)}, bf16[2,256,2560]{1,2,0:T(8,128)(2,1)}, u32[]{:S(2)}, u32[]{:S(2)}) collective-permute-start(bf16[2,256,2560]{1,2,0:T(8,128)(2,1)} %broadcast_select_fusion), channel_id=1, source_target_pairs={{0,2},{4,6},{8,10},{12,14},{1,3},{5,7},{9,11},{13,15},{2,1},{6,5},... | collective-permute-start | bytes 7864328 | tf_op jit(solution)/shard_map/ppermute | solution.py:31
  21.3 67.7 %collective-permute-start = (bf16[2,256,2560]{1,2,0:T(8,128)(2,1)}, bf16[2,256,2560]{1,2,0:T(8,128)(2,1)}, u32[]{:S(2)}, u32[]{:S(2)}) collective-permute-start(bf16[2,256,2560]{1,2,0:T(8,128)(2,1)} %broadcast_select_fusion), channel_id=1, source_target_pairs={{0,1},{4,5},{8,9},{12,13},{2,3},{6,7},{10,11},{14,15},{1,4},{5,8},... | collective-permute-start | bytes 7864328 | tf_op jit(solution)/shard_map/ppermute | solution.py:31
  22.4 21.0 %collective-permute-start.5 = (bf16[5,1,52,384]{3,2,0,1:T(8,128)(2,1)}, bf16[5,1,52,384]{3,2,0,1:T(8,128)(2,1)}, u32[]{:S(2)}, u32[]{:S(2)}) collective-permute-start(bf16[5,1,52,384]{3,2,0,1:T(8,128)(2,1)} %pad_maximum_fusion), channel_id=1, source_target_pairs={{1,0},{2,1},{3,2},{4,3},{5,4},{6,5},{7,6},{8,7},{9,8},{10,9},{11,1... | collective-permute-start | bytes 599048 | tf_op jit(solution)/shard_map/ppermute | solution.py:25
  23.7 19.8 %collective-permute-start.4 = (bf16[5,1,52,384]{3,2,0,1:T(8,128)(2,1)}, bf16[5,1,52,384]{3,2,0,1:T(8,128)(2,1)}, u32[]{:S(2)}, u32[]{:S(2)}) collective-permute-start(bf16[5,1,52,384]{3,2,0,1:T(8,128)(2,1)} %pad_maximum_fusion), channel_id=1, source_target_pairs={{0,1},{1,2},{2,3},{3,4},{4,5},{5,6},{6,7},{7,8},{8,9},{9,10},{10,1... | collective-permute-start | bytes 599048 | tf_op jit(solution)/shard_map/ppermute | solution.py:22
  28.6 1.6 copy-start.21
  32.8 2.0 copy-start.15
  32.8 3.4 %copy-start.6 = (bf16[1,256,1280]{1,2,0:T(8,128)(2,1)S(1)}, bf16[1,256,1280]{1,2,0:T(8,128)(2,1)}, u32[]{:S(2)}) copy-start(bf16[1,256,1280]{1,2,0:T(8,128)(2,1)} %get-tuple-element.45) | copy-start | bytes 1966084
  34.5 4.8 %copy-start.5 = (bf16[1,256,1280]{1,2,0:T(8,128)(2,1)S(1)}, bf16[1,256,1280]{1,2,0:T(8,128)(2,1)}, u32[]{:S(2)}) copy-start(bf16[1,256,1280]{1,2,0:T(8,128)(2,1)} %get-tuple-element.43) | copy-start | bytes 1966084
  36.2 4.2 %copy-start.17 = (pred[256]{0:T(512)(128)(4,1)}, pred[256]{0:T(512)(128)(4,1)S(1)}, u32[]{:S(2)}) copy-start(pred[256]{0:T(512)(128)(4,1)S(1)} %iota_compare_fusion.2) | copy-start | bytes 772
  40.3 1.8 copy-start
  40.3 1.8 copy-start.10
  94.1 45.0 %collective-permute-start.2 = (bf16[2,256,2560]{1,2,0:T(8,128)(2,1)}, bf16[2,256,2560]{1,2,0:T(8,128)(2,1)}, u32[]{:S(2)}, u32[]{:S(2)}) collective-permute-start(bf16[2,256,2560]{1,2,0:T(8,128)(2,1)} %get-tuple-element.48), channel_id=1, source_target_pairs={{3,2},{7,6},{11,10},{15,14},{2,0},{6,4},{10,8},{14,12},{1,5},{5,9}... | collective-permute-start | bytes 7864328 | tf_op jit(solution)/shard_map/ppermute | solution.py:31
  98.5 62.2 %slice-start = ((s8[7962624]{0:T(1024)(128)(4,1)}), s8[4194304]{0:T(1024)(128)(4,1)S(1)}, s32[]{:S(2)}) async-start(s8[7962624]{0:T(1024)(128)(4,1)} %bitcast.206), calls=%async_computation.1 | async-start | bytes 8388608
  100.8 58.7 %copy-start.8 = (bf16[3,1,52,384]{3,2,1,0:T(8,128)(2,1)S(1)}, bf16[3,1,52,384]{3,2,1,0:T(8,128)(2,1)}, u32[]{:S(2)}) copy-start(bf16[3,1,52,384]{3,2,1,0:T(8,128)(2,1)} %param.15) | copy-start | bytes 359428
  100.8 59.9 %slice-start.1 = ((s8[7962624]{0:T(1024)(128)(4,1)}), s8[3768320]{0:T(1024)(128)(4,1)S(1)}, s32[]{:S(2)}) async-start(s8[7962624]{0:T(1024)(128)(4,1)} %bitcast.206), calls=%async_computation.2 | async-start | bytes 7536640
  100.8 59.9 %copy-start.19 = (f32[384]{0:T(512)S(1)}, f32[384]{0:T(512)}, u32[]{:S(2)}) copy-start(f32[384]{0:T(512)} %param.19) | copy-start | bytes 4612
  144.0 19.4 %collective-permute-start.3 = (bf16[2,256,2560]{1,2,0:T(8,128)(2,1)}, bf16[2,256,2560]{1,2,0:T(8,128)(2,1)S(1)}, u32[]{:S(2)}, u32[]{:S(2)}) collective-permute-start(bf16[2,256,2560]{1,2,0:T(8,128)(2,1)} %get-tuple-element.46), channel_id=1, source_target_pairs={{0,1},{4,5},{8,9},{12,13},{1,0},{5,4},{9,8},{13,12},{2,3},{6,7},{1... | collective-permute-start | bytes 7864328 | tf_op jit(solution)/shard_map/ppermute | solution.py:31
  168.4 6.2 %copy-start.11 = (f32[10,256]{1,0:T(8,128)S(1)}, f32[10,256]{1,0:T(8,128)}, u32[]{:S(2)}) copy-start(f32[10,256]{1,0:T(8,128)} %copy-done.10) | copy-start | bytes 30724
  174.6 7.4 %copy-start.14 = (f32[10,256]{1,0:T(8,128)S(1)}, f32[10,256]{1,0:T(8,128)}, u32[]{:S(2)}) copy-start(f32[10,256]{1,0:T(8,128)} %get-tuple-element.27) | copy-start | bytes 30724
  174.6 7.4 %copy-start.9 = (bf16[1,256,1280]{1,2,0:T(8,128)(2,1)S(1)}, bf16[1,256,1280]{1,2,0:T(8,128)(2,1)}, u32[]{:S(2)}) copy-start(bf16[1,256,1280]{1,2,0:T(8,128)(2,1)} %get-tuple-element.44) | copy-start | bytes 1966084
  174.6 7.4 %copy-start.18 = (pred[256]{0:T(512)(128)(4,1)S(1)}, pred[256]{0:T(512)(128)(4,1)}, u32[]{:S(2)}) copy-start(pred[256]{0:T(512)(128)(4,1)} %copy-done.17) | copy-start | bytes 772
  184.2 6.4 %copy-start.13 = (f32[10,256]{1,0:T(8,128)S(1)}, f32[10,256]{1,0:T(8,128)}, u32[]{:S(2)}) copy-start(f32[10,256]{1,0:T(8,128)} %get-tuple-element.26) | copy-start | bytes 30724
  184.2 6.4 %copy-start.1 = (f32[10,256,256]{1,2,0:T(8,128)S(1)}, f32[10,256,256]{1,2,0:T(8,128)}, u32[]{:S(2)}) copy-start(f32[10,256,256]{1,2,0:T(8,128)} %copy-done) | copy-start | bytes 7864324
  190.6 2.4 %copy-start.2 = (bf16[1,1024,1280]{1,2,0:T(8,128)(2,1)S(1)}, bf16[1,1024,1280]{1,2,0:T(8,128)(2,1)}, u32[]{:S(2)}) copy-start(bf16[1,1024,1280]{1,2,0:T(8,128)(2,1)} %get-tuple-element.34) | copy-start | bytes 7864324
  201.1 2.7 %copy-start.20 = (pred[256]{0:T(512)(128)(4,1)S(1)}, pred[256]{0:T(512)(128)(4,1)}, u32[]{:S(2)}) copy-start(pred[256]{0:T(512)(128)(4,1)} %compare_and_fusion) | copy-start | bytes 772
  204.5 1.6 copy-start.3
  206.1 1.3 copy-start.22
  207.4 3.4 %copy-start.4 = (f32[10,256,256]{1,2,0:T(8,128)S(1)}, f32[10,256,256]{1,2,0:T(8,128)}, u32[]{:S(2)}) copy-start(f32[10,256,256]{1,2,0:T(8,128)} %copy-done.3) | copy-start | bytes 7864324
Sparse Core Ops, SparseCore 0:
  18.7 133.5 all-reduce.2

commit v9 on v7

--- a/solution.py
+++ b/solution.py
@@ -6,7 +6,7 @@
 H = 20
 DH = 128
 WIN = 4
-HG = 10
+HG = 20
 
 
 def spread(block, axis, source):
@@ -122,8 +122,9 @@
     groups = [
         (jnp.concatenate([keys_values, along], axis=1),
          jnp.concatenate([valid_list[0], offset_of(3, 1, 3, 1)])),
-        (jnp.concatenate([cross, second, third], axis=1),
-         jnp.concatenate([offset_of(4, 4, 2, 2), offset_of(1, 3, 1, 4), offset_of(2, 2, 4, 3)])),
+        (jnp.concatenate([cross, second], axis=1),
+         jnp.concatenate([offset_of(4, 4, 2, 2), offset_of(1, 3, 1, 4)])),
+        (third, offset_of(2, 2, 4, 3)),
     ]
     anchor_valid = (place != anchor) & (row_ids < lengths[anchor])
     heads = [slice(h * HG * DH, (h + 1) * HG * DH) for h in range(H // HG)]

time: 213 us -> 205 us (0.962)
  waiting for transfers between devices: 84.9 us -> 76 us
  other arithmetic: 26.7 us -> 32.5 us
  local copies, waits for them, and re-layouts: 27.2 us -> 21.7 us
  matrix products: 29.3 us -> 31.7 us
    ppermute x4, waiting for transfers between devices: 84.2 us -> 76 us  [move(): return lax.ppermute(value, 'span', pairs)]
    concatenate x1 -> x2, other arithmetic: 0.01 us -> 5.69 us  [the longest x1 5.68 us: shards(): jnp.concatenate([cross, second], axis=1)]
    select_n x2 -> x0, other arithmetic: 5.47 us -> none  [pick(): out = jnp.where(lane == l, options[l], out)]
    unnamed x70 -> x49, local copies, waits for them, and re-layouts: 15.6 us -> 10.4 us
    unnamed x5 -> x4, other arithmetic: 0.22 us -> 5.17 us
    dot_general x1, matrix products: 2.77 us -> 6.09 us  [shards(): jnp.dot(columns, conv_weight.reshape(27 * channels, channels), preferred_...]
    slice x2 -> x3, local copies, waits for them, and re-layouts: 4.96 us -> 8.27 us  [attend(): v = kv[1].reshape(-1, HG, DH)]
    ppermute x1, starting transfers between devices: 4.91 us -> 2.37 us  [extended_2(): lax.ppermute(lax.slice_in_dim(block, block.shape[dim] - width, None, axis...]
  transfers between devices with their start and end apart: 7 -> 7, of which waited for: 2 -> 3; matrix products, arithmetic and copies ran while one was open for 28% -> 34% of each run, Pallas kernels for 0% -> 0%
where the time goes in v9:
time: 205 us; the launch traced here: 203 us
  waiting for transfers between devices  76 us (37%)
  other arithmetic  32.5 us (16%)
  matrix products  31.7 us (15%)
  starting transfers between devices  24.4 us (12%)
  local copies, waits for them, and re-layouts  21.7 us (11%)
  between operations  17.2 us (8%)
    ppermute x4, waiting for transfers between devices, move(): return lax.ppermute(value, 'span', pairs)  76 us
    ppermute x4, starting transfers between devices, move(): return lax.ppermute(value, 'span', pairs)  20.8 us
    dot_general x4, matrix products, weighted(): jnp.einsum('hqk,khd->hqd', weights.astype(jnp.bfloat16), values, preferre...  18 us
    unnamed x49, local copies, waits for them, and re-layouts  10.4 us
    slice x3, local copies, waits for them, and re-layouts, attend(): v = kv[1].reshape(-1, HG, DH)  8.27 us
    dot_general x4, matrix products, part_stats(): jnp.einsum('qhd,khd->hqk', q, k, preferred_element_type=jnp.float32) * scale  7.55 us
    reduce_sum x4, other arithmetic, attend(): total = jnp.sum(weights, axis=-1, keepdims=True)  6.77 us
    dot_general x1, matrix products, shards(): jnp.dot(columns, conv_weight.reshape(27 * channels, channels), preferred_...  6.09 us
  transfers between devices with their start and end apart: 7, of which 3 were waited for; matrix products, arithmetic and copies ran while one was open for 34% of the time, Pallas kernels for 0%

profile of v9, /device:TPU:0, one launch (start us, length us, event | category | flops | bytes accessed | tf_op | source)
XLA Modules:
  0.0 203.5 jit_solution(6636131742743340111)
XLA Ops:
  7.2 1.0 fusion.60
  8.2 0.9 copy.47
  9.1 1.1 fusion.67
  10.2 2.4 %collective-permute-start.4 = (bf16[5,1,52,384]{3,2,0,1:T(8,128)(2,1)S(1)}, bf16[5,1,52,384]{3,2,0,1:T(8,128)(2,1)S(1)}, u32[]{:S(2)}, u32[]{:S(2)}) collective-permute-start(bf16[5,1,52,384]{3,2,0,1:T(8,128)(2,1)S(1)} %pad_maximum_fusion.1), channel_id=1, source_target_pairs={{0,1},{1,2},{2,3},{3,4},{4,5},{5,6},{6,7},{7,8},{8,9},{9,10},{10,1... | collective-permute-start | bytes 599048 | tf_op jit(solution)/shard_map/ppermute | solution.py:22
  12.6 1.3 collective-permute-start.5
  14.5 3.0 %copy.25 = bf16[2,256,2560]{1,2,0:T(8,128)(2,1)S(1)} copy(bf16[2,256,2560]{2,1,0:T(8,128)(2,1)} %param.11) | data formatting | bytes 5242880 | tf_op args[1]
  17.5 1.7 broadcast_select_fusion.1
  19.2 1.8 broadcast_select_fusion
  21.0 3.2 %collective-permute-start = (bf16[2,256,2560]{1,2,0:T(8,128)(2,1)}, bf16[2,256,2560]{1,2,0:T(8,128)(2,1)}, u32[]{:S(2)}, u32[]{:S(2)}) collective-permute-start(bf16[2,256,2560]{1,2,0:T(8,128)(2,1)} %broadcast_select_fusion), channel_id=1, source_target_pairs={{0,1},{4,5},{8,9},{12,13},{2,3},{6,7},{10,11},{14,15},{1,4},{5,8},... | collective-permute-start | bytes 7864328 | tf_op jit(solution)/shard_map/ppermute | solution.py:31
  24.2 6.8 %collective-permute-start.1 = (bf16[2,256,2560]{1,2,0:T(8,128)(2,1)}, bf16[2,256,2560]{1,2,0:T(8,128)(2,1)}, u32[]{:S(2)}, u32[]{:S(2)}) collective-permute-start(bf16[2,256,2560]{1,2,0:T(8,128)(2,1)} %broadcast_select_fusion), channel_id=1, source_target_pairs={{0,2},{4,6},{8,10},{12,14},{1,3},{5,7},{9,11},{13,15},{2,1},{6,5},... | collective-permute-start | bytes 7864328 | tf_op jit(solution)/shard_map/ppermute | solution.py:31
  31.2 0.7 constant_dynamic-slice_fusion.2
  33.8 0.7 fusion.90
  34.5 1.2 fusion.77
  35.7 1.8 select_select_fusion.3
  37.5 1.2 select_select_fusion.5
  38.8 0.7 iota_compare_fusion.2
  39.5 2.4 %copy.28 = bf16[256,2560]{0,1:T(8,128)(2,1)} copy(bf16[256,2560]{1,0:T(8,128)(2,1)} %param.10) | data formatting | bytes 2621440 | tf_op args[0]
  41.9 0.7 compare_and_fusion
  44.1 6.1 %fusion.52 = bf16[3,1,52,384]{3,2,1,0:T(8,128)(2,1)} fusion(bf16[10368,384,1]{1,0,2:T(8,128)(2,1)} %bitcast.178, bf16[3,1,52,10368]{3,2,0,1:T(8,128)(2,1)S(1)} %slice_dynamic-update-slice_fusion, bf16[3,1,52,384]{3,2,1,0:T(8,128)(2,1)S(1)} %copy-done.6, f32[384]{0:T(512)S(1)} %copy-done.9), kind=kOutput, calls=%fused_computation.64 | convolution fusion | flops 1242408960 | bytes 11438592 | tf_op jit(solution)/shard_map/dot_general | solution.py:168
  50.1 23.5 %collective-permute-done = bf16[2,256,2560]{1,2,0:T(8,128)(2,1)} collective-permute-done((bf16[2,256,2560]{1,2,0:T(8,128)(2,1)}, bf16[2,256,2560]{1,2,0:T(8,128)(2,1)}, u32[]{:S(2)}, u32[]{:S(2)}) %collective-permute-start) | collective-permute-done | bytes 2621472 | tf_op jit(solution)/shard_map/ppermute | solution.py:31
  73.7 23.7 %collective-permute-done.1 = bf16[2,256,2560]{1,2,0:T(8,128)(2,1)} collective-permute-done((bf16[2,256,2560]{1,2,0:T(8,128)(2,1)}, bf16[2,256,2560]{1,2,0:T(8,128)(2,1)}, u32[]{:S(2)}, u32[]{:S(2)}) %collective-permute-start.1) | collective-permute-done | bytes 2621472 | tf_op jit(solution)/shard_map/ppermute | solution.py:31
  97.4 5.0 %constant_dynamic-update-slice_fusion.1 = (bf16[2,512,2560]{1,2,0:T(8,128)(2,1)}, bf16[2,256,2560]{1,2,0:T(8,128)(2,1)}) fusion(bf16[2,256,2560]{1,2,0:T(8,128)(2,1)} %collective-permute-done.1, bf16[2,256,2560]{1,2,0:T(8,128)(2,1)} %collective-permute-done, pred[]{:T(512)S(6)} %eq.56, pred[]{:T(512)S(6)} %eq.53), kind=kLoop, calls=%fused_computation.115 | loop fusion | flops 2621439 | bytes 10485762
  102.3 1.6 collective-permute-start.2
  103.9 3.0 %pad_maximum_fusion = (bf16[1,512,2560]{1,2,0:T(8,128)(2,1)}, bf16[1,512,2560]{1,2,0:T(8,128)(2,1)S(1)}) fusion(bf16[2,256,2560]{1,2,0:T(8,128)(2,1)} %collective-permute-done, bf16[2,256,2560]{1,2,0:T(8,128)(2,1)S(1)} %copy.25), kind=kLoop, calls=%fused_computation.43 | loop fusion | flops 10485760 | bytes 10485760 | tf_op jit(solution)/shard_map/concatenate | solution.py:123
  107.0 2.5 %bitcast_reduce_fusion.1 = (f32[20,256]{1,0:T(8,128)S(1)}, f32[20,512,256]{2,1,0:T(8,128)S(1)}) fusion(pred[512]{0:T(512)(128)(4,1)S(1)} %pad_add_fusion, bf16[512,20,128]{0,2,1:T(8,128)(2,1)S(1)} %bitcast.179, bf16[256,20,128]{0,2,1:T(8,128)(2,1)S(1)} %bitcast.174), kind=kOutput, calls=%fused_computation.4 | convolution fusion | flops 678947840 | bytes 14438912 | tf_op jit(solution)/shard_map/qhd,khd->hqk/dot_general | solution.py:58
  109.5 2.2 %fusion.3 = f32[20,256]{1,0:T(8,128)S(1)} fusion(f32[20,512,256]{2,1,0:T(8,128)S(1)} %get-tuple-element.43, f32[20,256]{1,0:T(8,128)S(1)} %get-tuple-element.42, pred[512]{0:T(512)(128)(4,1)S(1)} %pad_add_fusion), kind=kLoop, calls=%fused_computation.9 | loop fusion | flops 10480640 | bytes 10527232 | tf_op jit(solution)/shard_map/reduce_sum | solution.py:76
  111.6 4.2 %fusion.8 = f32[20,256,128]{2,1,0:T(8,128)} fusion(bf16[512,20,128]{0,2,1:T(8,128)(2,1)S(1)} %bitcast.185, f32[20,512,256]{2,1,0:T(8,128)S(1)} %get-tuple-element.43, f32[20,256]{1,0:T(8,128)S(1)} %get-tuple-element.42, pred[512]{0:T(512)(128)(4,1)S(1)} %pad_add_fusion), kind=kOutput, calls=%fused_computation.13 | convolution fusion | flops 681574400 | bytes 15749632 | tf_op jit(solution)/shard_map/hqk,khd->hqd/dot_general | solution.py:63
  115.9 28.7 %collective-permute-done.2 = bf16[2,256,2560]{1,2,0:T(8,128)(2,1)} collective-permute-done((bf16[2,256,2560]{1,2,0:T(8,128)(2,1)}, bf16[2,256,2560]{1,2,0:T(8,128)(2,1)}, u32[]{:S(2)}, u32[]{:S(2)}) %collective-permute-start.2) | collective-permute-done | bytes 2621472 | tf_op jit(solution)/shard_map/ppermute | solution.py:31
  144.6 5.7 %constant_dynamic-update-slice_fusion = (bf16[2,512,2560]{1,2,0:T(8,128)(2,1)}, bf16[2,256,2560]{1,2,0:T(8,128)(2,1)}) fusion(bf16[2,512,2560]{1,2,0:T(8,128)(2,1)} %get-tuple-element.28, bf16[2,256,2560]{1,2,0:T(8,128)(2,1)} %collective-permute-done.2, bf16[2,256,2560]{1,2,0:T(8,128)(2,1)} %collective-permute-done.1, pred[]{:T(512)S(6)} %eq.56, pred[]{:T(512)S(6)} %eq.53), kind=kLoop, calls=%fused_computation.114 | loop fusion | flops 2621440 | bytes 10485762 | tf_op jit(solution)/shard_map/concatenate | solution.py:125
  150.3 9.1 %collective-permute-start.3 = (bf16[2,256,2560]{1,2,0:T(8,128)(2,1)}, bf16[2,256,2560]{1,2,0:T(8,128)(2,1)}, u32[]{:S(2)}, u32[]{:S(2)}) collective-permute-start(bf16[2,256,2560]{1,2,0:T(8,128)(2,1)} %get-tuple-element.27), channel_id=1, source_target_pairs={{0,1},{4,5},{8,9},{12,13},{1,0},{5,4},{9,8},{13,12},{2,3},{6,7},{1... | collective-permute-start | bytes 7864328 | tf_op jit(solution)/shard_map/ppermute | solution.py:31
  159.4 4.5 %fusion.87 = (bf16[1,512,2560]{1,2,0:T(8,128)(2,1)}, bf16[1,512,2560]{1,2,0:T(8,128)(2,1)S(1)}) fusion(bf16[2,512,2560]{1,2,0:T(8,128)(2,1)} %get-tuple-element.26), kind=kLoop, calls=%fused_computation.158 | loop fusion | bytes 10485760 | tf_op jit(solution)/shard_map/slice | solution.py:70
  163.9 2.5 %bitcast_reduce_fusion = (f32[20,256]{1,0:T(8,128)S(1)}, f32[20,512,256]{2,1,0:T(8,128)S(1)}) fusion(pred[512]{0:T(512)(128)(4,1)S(1)} %pad_add_fusion.1, bf16[512,20,128]{0,2,1:T(8,128)(2,1)S(1)} %bitcast.180, bf16[256,20,128]{0,2,1:T(8,128)(2,1)S(1)} %bitcast.175), kind=kOutput, calls=%fused_computation.1 | convolution fusion | flops 678947840 | bytes 14438912 | tf_op jit(solution)/shard_map/qhd,khd->hqk/dot_general | solution.py:58
  166.4 2.2 %fusion.5 = f32[20,256]{1,0:T(8,128)S(1)} fusion(f32[20,512,256]{2,1,0:T(8,128)S(1)} %get-tuple-element.45, f32[20,256]{1,0:T(8,128)S(1)} %get-tuple-element.15, pred[512]{0:T(512)(128)(4,1)S(1)} %pad_add_fusion.1), kind=kLoop, calls=%fused_computation.11 | loop fusion | flops 10480640 | bytes 10527232 | tf_op jit(solution)/shard_map/reduce_sum | solution.py:76
  168.7 6.0 %fusion.6 = f32[20,256,128]{2,1,0:T(8,128)} fusion(bf16[512,20,128]{0,2,1:T(8,128)(2,1)} %bitcast.184, f32[20,512,256]{2,1,0:T(8,128)S(1)} %get-tuple-element.45, f32[20,256]{1,0:T(8,128)S(1)} %get-tuple-element.15, pred[512]{0:T(512)(128)(4,1)S(1)} %pad_add_fusion.1), kind=kOutput, calls=%fused_computation.12 | convolution fusion | flops 681574400 | bytes 15749632 | tf_op jit(solution)/shard_map/hqk,khd->hqd/dot_general | solution.py:63
  174.7 1.9 fusion.89
  176.6 1.3 bitcast_reduce_fusion.3
  177.9 1.2 fusion.21
  179.2 0.5 copy-done.3
  179.6 0.8 copy-done.4
  180.4 4.0 %multiply_add_fusion = f32[20,256,128]{2,1,0:T(8,128)} fusion(f32[20,256,128]{2,1,0:T(8,128)S(1)} %copy-done.4, f32[20,256,128]{2,1,0:T(8,128)S(1)} %copy-done.3, bf16[256,20,128]{0,2,1:T(8,128)(2,1)S(1)} %bitcast.183, f32[20,256,256]{2,1,0:T(8,128)S(1)} %get-tuple-element.47, f32[20,256]{1,0:T(8,128)S(1)} %get-tuple-element.17, ...), kind=kOutput, calls=%fused_computation.48 | convolution fusion | flops 343408640 | bytes 14479616 | tf_op jit(solution)/shard_map/hqk,khd->hqd/dot_general | solution.py:63
  184.4 1.9 fusion.88
  186.3 1.3 bitcast_reduce_fusion.2
  187.6 1.2 fusion.22
  188.8 0.5 copy-done.5
  189.4 3.7 %divide_bitcast_fusion = bf16[256,20,128]{2,0,1:T(8,128)(2,1)} fusion(f32[20,256,128]{2,1,0:T(8,128)S(1)} %copy-done.5, f32[20,256]{1,0:T(8,128)S(1)} %get-tuple-element.33, f32[20,256]{1,0:T(8,128)S(1)} %get-tuple-element.32, bf16[256,20,128]{0,2,1:T(8,128)(2,1)S(1)} %bitcast.186, f32[20,256,256]{2,1,0:T(8,128)S(1)} %get-tuple-element.49, ...), kind=kOutput, calls=%fused_computation.46 | convolution fusion | flops 343408640 | bytes 10547456 | tf_op jit(solution)/shard_map/hqk,khd->hqd/dot_general | solution.py:63
  193.1 1.6 copy.45
  194.7 0.3 fusion.31
  195.0 1.6 copy.48
  (62 shorter events, 1.4 us)
Async XLA Ops:
  10.2 32.4 %collective-permute-start.4 = (bf16[5,1,52,384]{3,2,0,1:T(8,128)(2,1)S(1)}, bf16[5,1,52,384]{3,2,0,1:T(8,128)(2,1)S(1)}, u32[]{:S(2)}, u32[]{:S(2)}) collective-permute-start(bf16[5,1,52,384]{3,2,0,1:T(8,128)(2,1)S(1)} %pad_maximum_fusion.1), channel_id=1, source_target_pairs={{0,1},{1,2},{2,3},{3,4},{4,5},{5,6},{6,7},{7,8},{8,9},{9,10},{10,1... | collective-permute-start | bytes 599048 | tf_op jit(solution)/shard_map/ppermute | solution.py:22
  12.6 30.0 %collective-permute-start.5 = (bf16[5,1,52,384]{3,2,0,1:T(8,128)(2,1)S(1)}, bf16[5,1,52,384]{3,2,0,1:T(8,128)(2,1)S(1)}, u32[]{:S(2)}, u32[]{:S(2)}) collective-permute-start(bf16[5,1,52,384]{3,2,0,1:T(8,128)(2,1)S(1)} %pad_maximum_fusion.1), channel_id=1, source_target_pairs={{1,0},{2,1},{3,2},{4,3},{5,4},{6,5},{7,6},{8,7},{9,8},{10,9},{11,1... | collective-permute-start | bytes 599048 | tf_op jit(solution)/shard_map/ppermute | solution.py:25
  19.2 12.0 %copy-start.10 = (s32[16,3]{0,1:T(4,128)S(1)}, s32[16,3]{0,1:T(4,128)}, u32[]{:S(2)}) copy-start(s32[16,3]{0,1:T(4,128)} %param.13) | copy-start | bytes 580
  19.2 14.6 %copy-start.7 = (s32[16]{0:T(128)S(1)}, s32[16]{0:T(128)}, u32[]{:S(2)}) copy-start(s32[16]{0:T(128)} %param.14) | copy-start | bytes 196
  21.0 163.5 %all-reduce.3.cloned.1.call-start = ((), (), s32[]{:S(2)}) async-start(), calls=%async_computation | async-start | bytes 5242880 | tf_op jit(solution)/shard_map/psum | solution.py:105
  21.0 52.7 %collective-permute-start = (bf16[2,256,2560]{1,2,0:T(8,128)(2,1)}, bf16[2,256,2560]{1,2,0:T(8,128)(2,1)}, u32[]{:S(2)}, u32[]{:S(2)}) collective-permute-start(bf16[2,256,2560]{1,2,0:T(8,128)(2,1)} %broadcast_select_fusion), channel_id=1, source_target_pairs={{0,1},{4,5},{8,9},{12,13},{2,3},{6,7},{10,11},{14,15},{1,4},{5,8},... | collective-permute-start | bytes 7864328 | tf_op jit(solution)/shard_map/ppermute | solution.py:31
  24.2 73.1 %collective-permute-start.1 = (bf16[2,256,2560]{1,2,0:T(8,128)(2,1)}, bf16[2,256,2560]{1,2,0:T(8,128)(2,1)}, u32[]{:S(2)}, u32[]{:S(2)}) collective-permute-start(bf16[2,256,2560]{1,2,0:T(8,128)(2,1)} %broadcast_select_fusion), channel_id=1, source_target_pairs={{0,2},{4,6},{8,10},{12,14},{1,3},{5,7},{9,11},{13,15},{2,1},{6,5},... | collective-permute-start | bytes 7864328 | tf_op jit(solution)/shard_map/ppermute | solution.py:31
  42.6 1.1 copy-start.6
  42.6 1.1 copy-start.8
  42.9 1.1 copy-start.9
  102.3 4.6 %copy-start = (bf16[256,2560]{0,1:T(8,128)(2,1)S(1)}, bf16[256,2560]{0,1:T(8,128)(2,1)}, u32[]{:S(2)}) copy-start(bf16[256,2560]{0,1:T(8,128)(2,1)} %copy.28) | copy-start | bytes 3932164
  102.3 42.3 %collective-permute-start.2 = (bf16[2,256,2560]{1,2,0:T(8,128)(2,1)}, bf16[2,256,2560]{1,2,0:T(8,128)(2,1)}, u32[]{:S(2)}, u32[]{:S(2)}) collective-permute-start(bf16[2,256,2560]{1,2,0:T(8,128)(2,1)} %get-tuple-element.29), channel_id=1, source_target_pairs={{3,2},{7,6},{11,10},{15,14},{2,0},{6,4},{10,8},{14,12},{1,5},{5,9}... | collective-permute-start | bytes 7864328 | tf_op jit(solution)/shard_map/ppermute | solution.py:31
  109.4 2.2 %copy-start.2 = (bf16[1,512,2560]{1,2,0:T(8,128)(2,1)S(1)}, bf16[1,512,2560]{1,2,0:T(8,128)(2,1)}, u32[]{:S(2)}) copy-start(bf16[1,512,2560]{1,2,0:T(8,128)(2,1)} %get-tuple-element.18) | copy-start | bytes 7864324
  150.3 24.4 %collective-permute-start.3 = (bf16[2,256,2560]{1,2,0:T(8,128)(2,1)}, bf16[2,256,2560]{1,2,0:T(8,128)(2,1)}, u32[]{:S(2)}, u32[]{:S(2)}) collective-permute-start(bf16[2,256,2560]{1,2,0:T(8,128)(2,1)} %get-tuple-element.27), channel_id=1, source_target_pairs={{0,1},{4,5},{8,9},{12,13},{1,0},{5,4},{9,8},{13,12},{2,3},{6,7},{1... | collective-permute-start | bytes 7864328 | tf_op jit(solution)/shard_map/ppermute | solution.py:31
  159.4 4.5 %copy-start.1 = (bf16[256,2560]{0,1:T(8,128)(2,1)S(1)}, bf16[256,2560]{0,1:T(8,128)(2,1)}, u32[]{:S(2)}) copy-start(bf16[256,2560]{0,1:T(8,128)(2,1)} %copy.28) | copy-start | bytes 3932164
  177.9 1.7 copy-start.3
  177.9 2.5 %copy-start.4 = (f32[20,256,128]{2,1,0:T(8,128)S(1)}, f32[20,256,128]{2,1,0:T(8,128)}, u32[]{:S(2)}) copy-start(f32[20,256,128]{2,1,0:T(8,128)} %fusion.6) | copy-start | bytes 7864324
  187.6 1.7 copy-start.5
Sparse Core Ops, SparseCore 0:
  31.2 121.3 all-reduce.2

commit v10 on v9

--- a/solution.py
+++ b/solution.py
@@ -65,16 +65,24 @@
     )
 
 
-def attend(q, kv, valid, state):
-    k = kv[0].reshape(-1, HG, DH)
-    v = kv[1].reshape(-1, HG, DH)
-    scores = part_stats(q, k, valid, DH ** (-0.5))
-    top = jnp.max(scores, axis=-1, keepdims=True)
+def attend(q, blocks, state):
+    scores = [
+        part_stats(q, kv[0].reshape(-1, HG, DH), valid, DH ** (-0.5)) for kv, valid in blocks
+    ]
+    tops = [jnp.max(s, axis=-1, keepdims=True) for s in scores]
     if state is not None:
-        top = jnp.maximum(state[0], top)
-    weights = jnp.exp(scores - top)
-    total = jnp.sum(weights, axis=-1, keepdims=True)
-    out = weighted(weights, v)
+        tops.append(state[0])
+    top = tops[0]
+    for t in tops[1:]:
+        top = jnp.maximum(top, t)
+    total = None
+    out = None
+    for s, (kv, _) in zip(scores, blocks):
+        weights = jnp.exp(s - top)
+        part_total = jnp.sum(weights, axis=-1, keepdims=True)
+        part_out = weighted(weights, kv[1].reshape(-1, HG, DH))
+        total = part_total if total is None else total + part_total
+        out = part_out if out is None else out + part_out
     if state is not None:
         rescale = jnp.exp(state[0] - top)
         total = state[1] * rescale + total
@@ -120,23 +128,23 @@
         return out
 
     groups = [
-        (jnp.concatenate([keys_values, along], axis=1),
-         jnp.concatenate([valid_list[0], offset_of(3, 1, 3, 1)])),
-        (jnp.concatenate([cross, second], axis=1),
-         jnp.concatenate([offset_of(4, 4, 2, 2), offset_of(1, 3, 1, 4)])),
-        (third, offset_of(2, 2, 4, 3)),
+        [(keys_values, valid_list[0]), (along, offset_of(3, 1, 3, 1))],
+        [(cross, offset_of(4, 4, 2, 2)), (second, offset_of(1, 3, 1, 4))],
+        [(third, offset_of(2, 2, 4, 3))],
     ]
     anchor_valid = (place != anchor) & (row_ids < lengths[anchor])
     heads = [slice(h * HG * DH, (h + 1) * HG * DH) for h in range(H // HG)]
     query_heads = [queries[:, cols].reshape(tok_rows, HG, DH) for cols in heads]
     states = [None] * len(heads)
-    for group_kv, group_valid in groups:
+    for group in groups:
         for h, cols in enumerate(heads):
-            states[h] = attend(query_heads[h], group_kv[:, :, cols], group_valid, states[h])
+            states[h] = attend(
+                query_heads[h], [(kv[:, :, cols], valid) for kv, valid in group], states[h]
+            )
     anchor_kv, states = lax.optimization_barrier((anchor_kv, states))
     pieces = []
     for h, cols in enumerate(heads):
-        top, total, out = attend(query_heads[h], anchor_kv[:, :, cols], anchor_valid, states[h])
+        top, total, out = attend(query_heads[h], [(anchor_kv[:, :, cols], anchor_valid)], states[h])
         blended = out / total
         pieces.append(jnp.transpose(blended, (1, 0, 2)).reshape(tok_rows, HG * DH))
     attended = jnp.concatenate(pieces, axis=1)

time: 205 us -> 194 us (0.946)
  other arithmetic: 32.5 us -> 24.1 us
  matrix products: 31.7 us -> 25.4 us
  waiting for transfers between devices: 76 us -> 80.5 us
  starting transfers between devices: 24.4 us -> 26.8 us
  local copies, waits for them, and re-layouts: 21.7 us -> 19.4 us
    concatenate x4 -> x0, other arithmetic: 8.73 us -> none  [the longest x1 5.68 us: shards(): jnp.concatenate([cross, second], axis=1)]
    select_n x0 -> x2, other arithmetic: none -> 5.66 us  [pick(): out = jnp.where(lane == l, options[l], out)]
    unnamed x4, other arithmetic: 5.17 us -> 0.22 us
    ppermute x4, waiting for transfers between devices: 76 us -> 79.8 us  [move(): return lax.ppermute(value, 'span', pairs)]
    dot_general x1, matrix products: 6.09 us -> 2.77 us  [shards(): jnp.dot(columns, conv_weight.reshape(27 * channels, channels), preferred_...]
    dot_general x4 -> x6, matrix products: 18 us -> 14.8 us  [weighted(): jnp.einsum('hqk,khd->hqd', weights.astype(jnp.bfloat16), values, preferre...]
    unnamed x49 -> x51, local copies, waits for them, and re-layouts: 10.4 us -> 7.97 us
    slice x3 -> x6, local copies, waits for them, and re-layouts: 8.27 us -> 9.39 us  [attend(): part_out = weighted(weights, kv[1].reshape(-1, HG, DH))]
  transfers between devices with their start and end apart: 7 -> 7, of which waited for: 3 -> 2; matrix products, arithmetic and copies ran while one was open for 34% -> 27% of each run, Pallas kernels for 0% -> 0%
where the time goes in v10:
time: 194 us
  waiting for transfers between devices  80.5 us (41%)
  starting transfers between devices  26.8 us (14%)
  matrix products  25.4 us (13%)
  other arithmetic  24.1 us (12%)
  local copies, waits for them, and re-layouts  19.4 us (10%)
  between operations  17.4 us (9%)
    ppermute x4, waiting for transfers between devices, move(): return lax.ppermute(value, 'span', pairs)  79.8 us
    ppermute x4, starting transfers between devices, move(): return lax.ppermute(value, 'span', pairs)  21.3 us
    dot_general x6, matrix products, weighted(): jnp.einsum('hqk,khd->hqd', weights.astype(jnp.bfloat16), values, preferre...  14.8 us
    slice x6, local copies, waits for them, and re-layouts, attend(): part_out = weighted(weights, kv[1].reshape(-1, HG, DH))  9.39 us
    unnamed x51, local copies, waits for them, and re-layouts  7.97 us
    dot_general x6, matrix products, part_stats(): jnp.einsum('qhd,khd->hqk', q, k, preferred_element_type=jnp.float32) * scale  7.88 us
    reduce_sum x4, other arithmetic, attend(): part_total = jnp.sum(weights, axis=-1, keepdims=True)  7.25 us
    select_n x2, other arithmetic, pick(): out = jnp.where(lane == l, options[l], out)  5.66 us
  transfers between devices with their start and end apart: 7, of which 2 were waited for; matrix products, arithmetic and copies ran while one was open for 27% of the time, Pallas kernels for 0%

profile of v10, /device:TPU:0, one launch (start us, length us, event | category | flops | bytes accessed | tf_op | source)
XLA Modules:
  0.0 193.6 jit_solution(819332269546636796)
XLA Ops:
  7.2 3.0 %copy.31 = bf16[2,256,2560]{1,2,0:T(8,128)(2,1)S(1)} copy(bf16[2,256,2560]{2,1,0:T(8,128)(2,1)} %param.11) | data formatting | bytes 5242880 | tf_op args[1]
  10.8 1.7 broadcast_select_fusion.1
  12.5 1.8 broadcast_select_fusion
  14.3 0.7 all-reduce.3.cloned.1.call-update
  15.1 6.4 %collective-permute-start = (bf16[2,256,2560]{1,2,0:T(8,128)(2,1)}, bf16[2,256,2560]{1,2,0:T(8,128)(2,1)}, u32[]{:S(2)}, u32[]{:S(2)}) collective-permute-start(bf16[2,256,2560]{1,2,0:T(8,128)(2,1)} %broadcast_select_fusion), channel_id=1, source_target_pairs={{0,2},{4,6},{8,10},{12,14},{1,3},{5,7},{9,11},{13,15},{2,1},{6,5},... | collective-permute-start | bytes 7864328 | tf_op jit(solution)/shard_map/ppermute | solution.py:31
  21.8 0.7 pad_maximum_fusion
  22.5 1.3 collective-permute-start.5
  23.8 4.2 %collective-permute-start.4 = (bf16[5,1,52,384]{3,2,0,1:T(8,128)(2,1)}, bf16[5,1,52,384]{3,2,0,1:T(8,128)(2,1)S(1)}, u32[]{:S(2)}, u32[]{:S(2)}) collective-permute-start(bf16[5,1,52,384]{3,2,0,1:T(8,128)(2,1)} %pad_maximum_fusion), channel_id=1, source_target_pairs={{0,1},{1,2},{2,3},{3,4},{4,5},{5,6},{6,7},{7,8},{8,9},{9,10},{10,1... | collective-permute-start | bytes 599048 | tf_op jit(solution)/shard_map/ppermute | solution.py:22
  28.1 1.7 fusion.111
  29.8 0.7 constant_dynamic-slice_fusion.2
  31.8 1.6 copy.33
  34.1 0.7 fusion.114
  34.8 0.6 iota_compare_fusion.2
  35.4 0.6 compare_and_fusion
  36.1 1.3 fusion.5
  37.4 1.3 select_select_fusion.5
  38.7 1.3 fusion.95
  40.0 2.0 %fusion.94 = (pred[256]{0:T(512)(128)(4,1)S(1)}, pred[256]{0:T(512)(128)(4,1)S(1)}) fusion(pred[]{:T(512)S(6)} %eq.61, pred[]{:T(512)S(6)} %and.94, pred[]{:T(512)S(6)} %eq.56, pred[]{:T(512)S(6)} %eq.53, s32[]{:T(128)} %bitcast.13, s32[]{:T(128)} %bitcast.3, pred[]{:T(512)S(6)} %and.86, s32[]{:T(128)} %bitcast.5, pred[]{:T(512)S(6)} %and.90), kind=kLoop, calls=%fused_computation.149 | loop fusion | flops 2816 | bytes 530 | tf_op jit(solution)/shard_map/jit(_where)/select_n | solution.py:127
  43.5 45.7 %collective-permute-done = bf16[2,256,2560]{1,2,0:T(8,128)(2,1)} collective-permute-done((bf16[2,256,2560]{1,2,0:T(8,128)(2,1)}, bf16[2,256,2560]{1,2,0:T(8,128)(2,1)}, u32[]{:S(2)}, u32[]{:S(2)}) %collective-permute-start) | collective-permute-done | bytes 2621472 | tf_op jit(solution)/shard_map/ppermute | solution.py:31
  89.1 2.0 %select_select_fusion.1 = bf16[2,256,2560]{1,2,0:T(8,128)(2,1)S(1)} fusion(bf16[2,256,2560]{1,2,0:T(8,128)(2,1)} %collective-permute-done, bf16[2,256,2560]{1,2,0:T(8,128)(2,1)} %collective-permute-done.1, pred[]{:T(512)S(6)} %eq.56, pred[]{:T(512)S(6)} %eq.53), kind=kLoop, calls=%fused_computation.36 | loop fusion | flops 2621440 | bytes 7864322 | tf_op jit(solution)/shard_map/jit(_where)/select_n | solution.py:47
  91.2 1.3 collective-permute-start.2
  92.5 2.8 %fusion.69 = bf16[3,1,52,384]{3,2,1,0:T(8,128)(2,1)} fusion(bf16[10368,384,1]{1,0,2:T(8,128)(2,1)S(1)} %bitcast.202, bf16[3,1,52,10368]{3,2,0,1:T(8,128)(2,1)S(1)} %slice_dynamic-update-slice_fusion, bf16[3,1,52,384]{3,2,1,0:T(8,128)(2,1)S(1)} %copy-done.4, f32[384]{0:T(512)S(1)} %copy-done.8), kind=kOutput, calls=%fused_computation.81 | convolution fusion | flops 1242408960 | bytes 11438592 | tf_op jit(solution)/shard_map/dot_general | solution.py:176
  95.3 1.9 fusion.113
  97.2 1.3 bitcast_reduce_fusion.3
  98.5 1.9 fusion.110
  100.4 1.3 bitcast_reduce_fusion.1
  101.7 34.1 %collective-permute-done.2 = bf16[2,256,2560]{1,2,0:T(8,128)(2,1)S(1)} collective-permute-done((bf16[2,256,2560]{1,2,0:T(8,128)(2,1)S(1)}, bf16[2,256,2560]{1,2,0:T(8,128)(2,1)S(1)}, u32[]{:S(2)}, u32[]{:S(2)}) %collective-permute-start.2) | collective-permute-done | bytes 2621472 | tf_op jit(solution)/shard_map/ppermute | solution.py:31
  135.8 3.6 %select_select_fusion = bf16[2,256,2560]{1,2,0:T(8,128)(2,1)} fusion(bf16[2,256,2560]{1,2,0:T(8,128)(2,1)} %collective-permute-done, bf16[2,256,2560]{1,2,0:T(8,128)(2,1)S(1)} %collective-permute-done.2, pred[]{:T(512)S(6)} %eq.56, pred[]{:T(512)S(6)} %eq.53), kind=kLoop, calls=%fused_computation.35 | loop fusion | flops 2621440 | bytes 7864322 | tf_op jit(solution)/shard_map/jit(_where)/select_n | solution.py:47
  139.4 13.6 %collective-permute-start.3 = (bf16[2,256,2560]{1,2,0:T(8,128)(2,1)}, bf16[2,256,2560]{1,2,0:T(8,128)(2,1)}, u32[]{:S(2)}, u32[]{:S(2)}) collective-permute-start(bf16[2,256,2560]{1,2,0:T(8,128)(2,1)} %select_select_fusion), channel_id=1, source_target_pairs={{0,1},{4,5},{8,9},{12,13},{1,0},{5,4},{9,8},{13,12},{2,3},{6,7},{1... | collective-permute-start | bytes 7864328 | tf_op jit(solution)/shard_map/ppermute | solution.py:31
  153.2 1.3 bitcast_reduce_fusion.2
  154.6 1.6 fusion.26
  156.2 1.6 fusion.24
  157.8 1.6 fusion.30
  159.3 3.1 %fusion.22 = f32[20,256,128]{2,1,0:T(8,128)} fusion(bf16[256,20,128]{0,2,1:T(8,128)(2,1)S(1)} %bitcast.210, f32[20,256,256]{2,1,0:T(8,128)S(1)} %get-tuple-element.54, f32[20,256]{1,0:T(8,128)S(1)} %get-tuple-element.20, pred[256]{0:T(512)(128)(4,1)S(1)} %get-tuple-element.59), kind=kOutput, calls=%fused_computation.40 | convolution fusion | flops 340787200 | bytes 9195776 | tf_op jit(solution)/shard_map/hqk,khd->hqd/dot_general | solution.py:63
  162.4 2.5 %fusion.13 = (f32[20,256]{1,0:T(8,128)S(1)}, f32[20,256]{1,0:T(8,128)S(1)}) fusion(f32[20,256,256]{2,1,0:T(8,128)S(1)} %get-tuple-element.50, f32[20,256]{1,0:T(8,128)S(1)} %get-tuple-element.19, pred[256]{0:T(512)(128)(4,1)S(1)} %fusion.95, f32[20,256,256]{2,1,0:T(8,128)S(1)} %get-tuple-element.48, pred[256]{0:T(512)(128)(4,1)S(1)} %get-tuple-element.60), kind=kLoop, calls=%fused_computation.30 | loop fusion | flops 10475520 | bytes 10547712 | tf_op jit(solution)/shard_map/reduce_sum | solution.py:82
  164.9 2.4 %fusion.15 = (f32[20,256]{1,0:T(8,128)S(1)}, f32[20,256]{1,0:T(8,128)S(1)}) fusion(f32[20,256,256]{2,1,0:T(8,128)S(1)} %get-tuple-element.54, f32[20,256]{1,0:T(8,128)S(1)} %get-tuple-element.20, pred[256]{0:T(512)(128)(4,1)S(1)} %get-tuple-element.59, f32[20,256,256]{1,2,0:T(8,128)S(1)} %get-tuple-element.52, pred[256]{0:T(512)(128)(4,1)S(1)} %iota_compare_fusion.2), kind=kLoop, calls=%fused_computation.32 | loop fusion | flops 10475520 | bytes 10547712 | tf_op jit(solution)/shard_map/reduce_sum | solution.py:82
  167.4 1.9 fusion.109
  169.2 1.3 bitcast_reduce_fusion.4
  170.6 1.2 fusion.9
  171.8 0.5 copy-done
  172.3 4.1 %multiply_add_fusion = f32[20,256,128]{2,1,0:T(8,128)} fusion(f32[20,256,128]{2,1,0:T(8,128)S(1)} %fusion.26, f32[20,256,128]{2,1,0:T(8,128)S(1)} %fusion.24, f32[20,256,128]{2,1,0:T(8,128)S(1)} %fusion.30, f32[20,256,128]{2,1,0:T(8,128)S(1)} %copy-done, bf16[256,20,128]{0,2,1:T(8,128)(2,1)S(1)} %bitcast.212, f32[20,256,256]{2,1,0:T(8,128)S(1)} %get-tuple-element.56, ...), kind=kOutput, calls=%fused_computation.51 | convolution fusion | flops 344719360 | bytes 19722496 | tf_op jit(solution)/shard_map/hqk,khd->hqd/dot_general | solution.py:63
  176.4 1.9 fusion.108
  178.3 1.3 bitcast_reduce_fusion
  179.6 1.2 fusion.16
  180.8 0.5 copy-done.3
  181.3 2.9 %divide_bitcast_fusion = bf16[256,20,128]{2,0,1:T(8,128)(2,1)S(1)} fusion(f32[20,256,128]{2,1,0:T(8,128)S(1)} %copy-done.3, f32[20,256]{1,0:T(8,128)S(1)} %get-tuple-element.38, f32[20,256]{1,0:T(8,128)S(1)} %get-tuple-element.37, bf16[256,20,128]{0,2,1:T(8,128)(2,1)S(1)} %bitcast.214, f32[20,256,256]{2,1,0:T(8,128)S(1)} %get-tuple-element.58, ...), kind=kOutput, calls=%fused_computation.49 | convolution fusion | flops 343408640 | bytes 10547456 | tf_op jit(solution)/shard_map/hqk,khd->hqd/dot_general | solution.py:63
  184.3 0.6 copy.62
  185.2 1.6 copy.65
  (69 shorter events, 2.1 us)
Async XLA Ops:
  12.5 9.0 %copy-start.5 = (bf16[2,1,52,384]{3,0,2,1:T(2,128)(2,1)S(1)}, bf16[2,1,52,384]{3,0,2,1:T(2,128)(2,1)}, u32[]{:S(2)}) copy-start(bf16[2,1,52,384]{3,0,2,1:T(2,128)(2,1)} %param.16) | copy-start | bytes 239620
  12.5 9.0 %copy-start.4 = (bf16[3,1,52,384]{3,2,1,0:T(8,128)(2,1)S(1)}, bf16[3,1,52,384]{3,2,1,0:T(8,128)(2,1)}, u32[]{:S(2)}) copy-start(bf16[3,1,52,384]{3,2,1,0:T(8,128)(2,1)} %param.15) | copy-start | bytes 359428
  12.5 9.1 %copy-start.7 = (f32[384]{0:T(512)S(1)}, f32[384]{0:T(512)}, u32[]{:S(2)}) copy-start(f32[384]{0:T(512)} %param.17) | copy-start | bytes 4612
  14.3 162.1 %all-reduce.3.cloned.1.call-start = ((), (), s32[]{:S(2)}) async-start(), calls=%async_computation | async-start | bytes 5242880 | tf_op jit(solution)/shard_map/psum | solution.py:113
  15.0 14.8 %copy-start.9 = (s32[16,3]{0,1:T(4,128)S(1)}, s32[16,3]{0,1:T(4,128)}, u32[]{:S(2)}) copy-start(s32[16,3]{0,1:T(4,128)} %param.13) | copy-start | bytes 580
  15.1 74.1 %collective-permute-start = (bf16[2,256,2560]{1,2,0:T(8,128)(2,1)}, bf16[2,256,2560]{1,2,0:T(8,128)(2,1)}, u32[]{:S(2)}, u32[]{:S(2)}) collective-permute-start(bf16[2,256,2560]{1,2,0:T(8,128)(2,1)} %broadcast_select_fusion), channel_id=1, source_target_pairs={{0,2},{4,6},{8,10},{12,14},{1,3},{5,7},{9,11},{13,15},{2,1},{6,5},... | collective-permute-start | bytes 7864328 | tf_op jit(solution)/shard_map/ppermute | solution.py:31
  21.4 67.7 %collective-permute-start.1 = (bf16[2,256,2560]{1,2,0:T(8,128)(2,1)}, bf16[2,256,2560]{1,2,0:T(8,128)(2,1)}, u32[]{:S(2)}, u32[]{:S(2)}) collective-permute-start(bf16[2,256,2560]{1,2,0:T(8,128)(2,1)} %broadcast_select_fusion), channel_id=1, source_target_pairs={{0,1},{4,5},{8,9},{12,13},{2,3},{6,7},{10,11},{14,15},{1,4},{5,8},... | collective-permute-start | bytes 7864328 | tf_op jit(solution)/shard_map/ppermute | solution.py:31
  22.5 19.5 %collective-permute-start.5 = (bf16[5,1,52,384]{3,2,0,1:T(8,128)(2,1)}, bf16[5,1,52,384]{3,2,0,1:T(8,128)(2,1)S(1)}, u32[]{:S(2)}, u32[]{:S(2)}) collective-permute-start(bf16[5,1,52,384]{3,2,0,1:T(8,128)(2,1)} %pad_maximum_fusion), channel_id=1, source_target_pairs={{1,0},{2,1},{3,2},{4,3},{5,4},{6,5},{7,6},{8,7},{9,8},{10,9},{11,1... | collective-permute-start | bytes 599048 | tf_op jit(solution)/shard_map/ppermute | solution.py:25
  23.8 18.3 %collective-permute-start.4 = (bf16[5,1,52,384]{3,2,0,1:T(8,128)(2,1)}, bf16[5,1,52,384]{3,2,0,1:T(8,128)(2,1)S(1)}, u32[]{:S(2)}, u32[]{:S(2)}) collective-permute-start(bf16[5,1,52,384]{3,2,0,1:T(8,128)(2,1)} %pad_maximum_fusion), channel_id=1, source_target_pairs={{0,1},{1,2},{2,3},{3,4},{4,5},{5,6},{6,7},{7,8},{8,9},{9,10},{10,1... | collective-permute-start | bytes 599048 | tf_op jit(solution)/shard_map/ppermute | solution.py:22
  28.1 6.0 %copy-start.6 = (s32[16]{0:T(128)S(1)}, s32[16]{0:T(128)}, u32[]{:S(2)}) copy-start(s32[16]{0:T(128)} %param.14) | copy-start | bytes 196
  29.8 6.3 %copy-start.1 = (bf16[1,256,2560]{1,2,0:T(8,128)(2,1)S(1)}, bf16[1,256,2560]{1,2,0:T(8,128)(2,1)}, u32[]{:S(2)}) copy-start(bf16[1,256,2560]{1,2,0:T(8,128)(2,1)} %get-tuple-element.30) | copy-start | bytes 3932164
  42.3 50.1 %slice-start = ((s8[7962624]{0:T(1024)(128)(4,1)}), s8[4194304]{0:T(1024)(128)(4,1)S(1)}, s32[]{:S(2)}) async-start(s8[7962624]{0:T(1024)(128)(4,1)} %bitcast.200), calls=%async_computation.1 | async-start | bytes 8388608
  43.4 49.0 %slice-start.1 = ((s8[7962624]{0:T(1024)(128)(4,1)}), s8[3768320]{0:T(1024)(128)(4,1)S(1)}, s32[]{:S(2)}) async-start(s8[7962624]{0:T(1024)(128)(4,1)} %bitcast.200), calls=%async_computation.2 | async-start | bytes 7536640
  43.5 49.0 %copy-start.8 = (f32[384]{0:T(512)S(1)}, f32[384]{0:T(512)}, u32[]{:S(2)}) copy-start(f32[384]{0:T(512)} %param.19) | copy-start | bytes 4612
  91.2 44.6 %collective-permute-start.2 = (bf16[2,256,2560]{1,2,0:T(8,128)(2,1)S(1)}, bf16[2,256,2560]{1,2,0:T(8,128)(2,1)S(1)}, u32[]{:S(2)}, u32[]{:S(2)}) collective-permute-start(bf16[2,256,2560]{1,2,0:T(8,128)(2,1)S(1)} %select_select_fusion.1), channel_id=1, source_target_pairs={{3,2},{7,6},{11,10},{15,14},{2,0},{6,4},{10,8},{14,12},{1,5},{5,9}... | collective-permute-start | bytes 7864328 | tf_op jit(solution)/shard_map/ppermute | solution.py:31
  139.4 27.9 %collective-permute-start.3 = (bf16[2,256,2560]{1,2,0:T(8,128)(2,1)}, bf16[2,256,2560]{1,2,0:T(8,128)(2,1)}, u32[]{:S(2)}, u32[]{:S(2)}) collective-permute-start(bf16[2,256,2560]{1,2,0:T(8,128)(2,1)} %select_select_fusion), channel_id=1, source_target_pairs={{0,1},{4,5},{8,9},{12,13},{1,0},{5,4},{9,8},{13,12},{2,3},{6,7},{1... | collective-permute-start | bytes 7864328 | tf_op jit(solution)/shard_map/ppermute | solution.py:31
  156.2 1.6 copy-start.2
  170.6 1.7 copy-start
  179.6 1.7 copy-start.3
Sparse Core Ops, SparseCore 0:
  18.8 129.5 all-reduce.2

commit v11 on v10

--- a/solution.py
+++ b/solution.py
@@ -50,8 +50,12 @@
     cross = move(kv, pairs((0, 2, 0), (1, 3, 0), (2, 1, 0)))
     along = move(kv, pairs((0, 1, 0), (2, 3, 0), (1, 0, 1), (3, 2, 1)))
     second = move(pick(cross, cross, along, cross), pairs((3, 2, 0), (2, 0, 0), (1, 1, 1)))
-    third = move(pick(second, second, cross, cross), pairs((0, 1, 0), (1, 0, 0), (2, 3, 0)))
-    return along, cross, second, third
+
+    def round_three(ready):
+        payload, ready = lax.optimization_barrier((pick(second, second, cross, cross), ready))
+        return move(payload, pairs((0, 1, 0), (1, 0, 0), (2, 3, 0))), ready
+
+    return along, cross, second, round_three
 
 
 def part_stats(q, k, valid, scale):
@@ -112,7 +116,7 @@
     masked = jnp.where(is_anchor, keys_values, jnp.zeros_like(keys_values))
     anchor_kv = lax.psum(masked, "span")
     sent = jnp.where(is_anchor, lax.optimization_barrier(masked), keys_values)
-    along, cross, second, third = window_blocks(sent, devices)
+    along, cross, second, round_three = window_blocks(sent, devices)
     valid_list = [row_ids < lengths[place]]
     for offset in range(1, WIN):
         source = (place - offset) % devices
@@ -130,7 +134,6 @@
     groups = [
         [(keys_values, valid_list[0]), (along, offset_of(3, 1, 3, 1))],
         [(cross, offset_of(4, 4, 2, 2)), (second, offset_of(1, 3, 1, 4))],
-        [(third, offset_of(2, 2, 4, 3))],
     ]
     anchor_valid = (place != anchor) & (row_ids < lengths[anchor])
     heads = [slice(h * HG * DH, (h + 1) * HG * DH) for h in range(H // HG)]
@@ -141,6 +144,10 @@
             states[h] = attend(
                 query_heads[h], [(kv[:, :, cols], valid) for kv, valid in group], states[h]
             )
+    third, states = round_three(states)
+    third_valid = offset_of(2, 2, 4, 3)
+    for h, cols in enumerate(heads):
+        states[h] = attend(query_heads[h], [(third[:, :, cols], third_valid)], states[h])
     anchor_kv, states = lax.optimization_barrier((anchor_kv, states))
     pieces = []
     for h, cols in enumerate(heads):

time: 194 us -> 201 us (1.036)
  matrix products: 25.4 us -> 31.4 us
  waiting for transfers between devices: 80.5 us -> 83.3 us
  other arithmetic: 24.1 us -> 21.4 us
    dot_general x6, matrix products: 14.8 us -> 21 us  [weighted(): jnp.einsum('hqk,khd->hqd', weights.astype(jnp.bfloat16), values, preferre...]
    ppermute x4, waiting for transfers between devices: 79.8 us -> 82.6 us  [move(): return lax.ppermute(value, 'span', pairs)]
    unnamed x51 -> x59, local copies, waits for them, and re-layouts: 7.97 us -> 8.09 us
  transfers between devices with their start and end apart: 7 -> 7, of which waited for: 2 -> 3; matrix products, arithmetic and copies ran while one was open for 27% -> 28% of each run, Pallas kernels for 0% -> 0%
where the time goes in v11:
time: 201 us
  waiting for transfers between devices  83.3 us (41%)
  matrix products  31.4 us (16%)
  starting transfers between devices  27.3 us (14%)
  other arithmetic  21.4 us (11%)
  local copies, waits for them, and re-layouts  20.1 us (10%)
  between operations  17.2 us (9%)
    ppermute x4, waiting for transfers between devices, move(): return lax.ppermute(value, 'span', pairs)  82.6 us
    ppermute x4, starting transfers between devices, move(): return lax.ppermute(value, 'span', pairs)  21.8 us
    dot_general x6, matrix products, weighted(): jnp.einsum('hqk,khd->hqd', weights.astype(jnp.bfloat16), values, preferre...  21 us
    slice x6, local copies, waits for them, and re-layouts, attend(): part_out = weighted(weights, kv[1].reshape(-1, HG, DH))  10 us
    unnamed x59, local copies, waits for them, and re-layouts  8.09 us
    dot_general x6, matrix products, part_stats(): jnp.einsum('qhd,khd->hqk', q, k, preferred_element_type=jnp.float32) * scale  7.8 us
    reduce_sum x4, other arithmetic, attend(): part_total = jnp.sum(weights, axis=-1, keepdims=True)  7.4 us
    select_n x2, other arithmetic, pick(): out = jnp.where(lane == l, options[l], out)  4.28 us
  transfers between devices with their start and end apart: 7, of which 3 were waited for; matrix products, arithmetic and copies ran while one was open for 28% of the time, Pallas kernels for 0%

profile of v11, /device:TPU:0, one launch (start us, length us, event | category | flops | bytes accessed | tf_op | source)
XLA Modules:
  0.0 200.8 jit_solution(16108878899451777461)
XLA Ops:
  7.2 3.0 %copy.31 = bf16[2,256,2560]{1,2,0:T(8,128)(2,1)S(1)} copy(bf16[2,256,2560]{2,1,0:T(8,128)(2,1)} %param.11) | data formatting | bytes 5242880 | tf_op args[1]
  10.8 1.7 broadcast_select_fusion.1
  12.5 1.8 broadcast_select_fusion
  14.3 0.7 all-reduce.3.cloned.1.call-update
  15.0 6.5 %collective-permute-start = (bf16[2,256,2560]{1,2,0:T(8,128)(2,1)}, bf16[2,256,2560]{1,2,0:T(8,128)(2,1)}, u32[]{:S(2)}, u32[]{:S(2)}) collective-permute-start(bf16[2,256,2560]{1,2,0:T(8,128)(2,1)} %broadcast_select_fusion), channel_id=1, source_target_pairs={{0,2},{4,6},{8,10},{12,14},{1,3},{5,7},{9,11},{13,15},{2,1},{6,5},... | collective-permute-start | bytes 7864328 | tf_op jit(solution)/shard_map/ppermute | solution.py:31
  21.8 0.7 pad_maximum_fusion
  22.5 1.3 collective-permute-start.5
  23.8 4.2 %collective-permute-start.4 = (bf16[5,1,52,384]{3,2,0,1:T(8,128)(2,1)}, bf16[5,1,52,384]{3,2,0,1:T(8,128)(2,1)S(1)}, u32[]{:S(2)}, u32[]{:S(2)}) collective-permute-start(bf16[5,1,52,384]{3,2,0,1:T(8,128)(2,1)} %pad_maximum_fusion), channel_id=1, source_target_pairs={{0,1},{1,2},{2,3},{3,4},{4,5},{5,6},{6,7},{7,8},{8,9},{9,10},{10,1... | collective-permute-start | bytes 599048 | tf_op jit(solution)/shard_map/ppermute | solution.py:22
  28.2 1.7 fusion.114
  29.8 1.7 copy.33
  31.6 0.7 constant_dynamic-slice_fusion.1
  34.0 0.7 fusion.116
  34.7 0.6 iota_compare_fusion.2
  35.3 0.7 select_select_fusion.4
  36.0 1.3 select_select_fusion.5
  37.3 1.3 fusion.5
  38.7 0.6 compare_and_fusion
  39.3 1.2 fusion.96
  41.4 47.7 %collective-permute-done = bf16[2,256,2560]{1,2,0:T(8,128)(2,1)} collective-permute-done((bf16[2,256,2560]{1,2,0:T(8,128)(2,1)}, bf16[2,256,2560]{1,2,0:T(8,128)(2,1)}, u32[]{:S(2)}, u32[]{:S(2)}) %collective-permute-start) | collective-permute-done | bytes 2621472 | tf_op jit(solution)/shard_map/ppermute | solution.py:31
  89.1 2.0 %select_select_fusion.1 = bf16[2,256,2560]{1,2,0:T(8,128)(2,1)S(1)} fusion(bf16[2,256,2560]{1,2,0:T(8,128)(2,1)} %collective-permute-done, bf16[2,256,2560]{1,2,0:T(8,128)(2,1)} %collective-permute-done.1, pred[]{:T(512)S(6)} %eq.56, pred[]{:T(512)S(6)} %eq.53), kind=kLoop, calls=%fused_computation.36 | loop fusion | flops 2621440 | bytes 7864322 | tf_op jit(solution)/shard_map/jit(_where)/select_n | solution.py:47
  91.1 1.3 collective-permute-start.2
  92.5 3.2 %fusion.112 = (bf16[1,256,2560]{1,2,0:T(8,128)(2,1)S(1)}, bf16[1,256,2560]{1,2,0:T(8,128)(2,1)S(1)}) fusion(bf16[2,256,2560]{1,2,0:T(8,128)(2,1)} %collective-permute-done), kind=kLoop, calls=%fused_computation.179 | loop fusion | bytes 5242880 | tf_op jit(solution)/shard_map/slice | solution.py:87
  95.7 1.3 bitcast_reduce_fusion.4
  97.0 3.0 %fusion.113 = (bf16[1,256,2560]{1,2,0:T(8,128)(2,1)}, bf16[1,256,2560]{1,2,0:T(8,128)(2,1)S(1)}) fusion(bf16[2,256,2560]{1,2,0:T(8,128)(2,1)} %collective-permute-done.1), kind=kLoop, calls=%fused_computation.180 | loop fusion | bytes 5242880 | tf_op jit(solution)/shard_map/slice | solution.py:87
  99.9 1.3 bitcast_reduce_fusion.2
  101.2 33.7 %collective-permute-done.2 = bf16[2,256,2560]{1,2,0:T(8,128)(2,1)S(1)} collective-permute-done((bf16[2,256,2560]{1,2,0:T(8,128)(2,1)S(1)}, bf16[2,256,2560]{1,2,0:T(8,128)(2,1)S(1)}, u32[]{:S(2)}, u32[]{:S(2)}) %collective-permute-start.2) | collective-permute-done | bytes 2621472 | tf_op jit(solution)/shard_map/ppermute | solution.py:31
  135.1 1.3 bitcast_reduce_fusion.3
  136.5 2.6 %fusion.11 = (f32[20,256]{1,0:T(8,128)S(1)}, f32[20,256]{1,0:T(8,128)S(1)}) fusion(f32[20,256,256]{2,1,0:T(8,128)S(1)} %get-tuple-element.58, f32[20,256]{1,0:T(8,128)S(1)} %get-tuple-element.29, pred[256]{0:T(512)(128)(4,1)S(1)} %get-tuple-element.68, f32[20,256,256]{2,1,0:T(8,128)S(1)} %get-tuple-element.56, pred[256]{0:T(512)(128)(4,1)S(1)} %select_select_fusion.4), kind=kLoop, calls=%fused_computation.28 | loop fusion | flops 10475520 | bytes 10547712 | tf_op jit(solution)/shard_map/reduce_sum | solution.py:86
  139.1 3.2 %fusion.26 = f32[20,256,128]{2,1,0:T(8,128)} fusion(bf16[256,20,128]{0,2,1:T(8,128)(2,1)S(1)} %bitcast.203, f32[20,256,256]{2,1,0:T(8,128)S(1)} %get-tuple-element.58, f32[20,256]{1,0:T(8,128)S(1)} %get-tuple-element.29, pred[256]{0:T(512)(128)(4,1)S(1)} %get-tuple-element.68), kind=kOutput, calls=%fused_computation.42 | convolution fusion | flops 340787200 | bytes 9195776 | tf_op jit(solution)/shard_map/hqk,khd->hqd/dot_general | solution.py:67
  142.3 2.5 %fusion.13 = (f32[20,256]{1,0:T(8,128)S(1)}, f32[20,256]{1,0:T(8,128)S(1)}) fusion(f32[20,256,256]{2,1,0:T(8,128)S(1)} %get-tuple-element.62, f32[20,256]{1,0:T(8,128)S(1)} %get-tuple-element.30, pred[256]{0:T(512)(128)(4,1)S(1)} %get-tuple-element.67, f32[20,256,256]{1,2,0:T(8,128)S(1)} %get-tuple-element.60, pred[256]{0:T(512)(128)(4,1)S(1)} %iota_compare_fusion.2), kind=kLoop, calls=%fused_computation.30 | loop fusion | flops 10475520 | bytes 10547712 | tf_op jit(solution)/shard_map/reduce_sum | solution.py:86
  144.8 3.1 %fusion.30 = f32[20,256,128]{2,1,0:T(8,128)} fusion(bf16[256,20,128]{0,2,1:T(8,128)(2,1)S(1)} %bitcast.201, f32[20,256,256]{1,2,0:T(8,128)S(1)} %get-tuple-element.60, f32[20,256]{1,0:T(8,128)S(1)} %get-tuple-element.30, pred[256]{0:T(512)(128)(4,1)S(1)} %iota_compare_fusion.2), kind=kOutput, calls=%fused_computation.44 | convolution fusion | flops 340787200 | bytes 9195776 | tf_op jit(solution)/shard_map/hqk,khd->hqd/dot_general | solution.py:67
  147.8 3.1 %fusion.24 = f32[20,256,128]{2,1,0:T(8,128)} fusion(bf16[256,20,128]{0,2,1:T(8,128)(2,1)S(1)} %bitcast.202, f32[20,256,256]{2,1,0:T(8,128)S(1)} %get-tuple-element.62, f32[20,256]{1,0:T(8,128)S(1)} %get-tuple-element.30, pred[256]{0:T(512)(128)(4,1)S(1)} %get-tuple-element.67), kind=kOutput, calls=%fused_computation.41 | convolution fusion | flops 340787200 | bytes 9195776 | tf_op jit(solution)/shard_map/hqk,khd->hqd/dot_general | solution.py:67
  151.0 5.4 %add_add_fusion = f32[20,256,128]{2,1,0:T(8,128)} fusion(f32[20,256,128]{2,1,0:T(8,128)S(1)} %copy-done.1, f32[20,256,128]{2,1,0:T(8,128)} %fusion.30, f32[20,256,128]{2,1,0:T(8,128)} %fusion.24, bf16[256,20,128]{0,2,1:T(8,128)(2,1)S(1)} %bitcast.193, f32[20,256,256]{2,1,0:T(8,128)S(1)} %get-tuple-element.56, f32[20,256]{1,0:T(8,128)S(1)} %get-tuple-element.29, ...), kind=kOutput, calls=%fused_computation.53 | convolution fusion | flops 343408640 | bytes 17080576 | tf_op jit(solution)/shard_map/hqk,khd->hqd/dot_general | solution.py:67
  156.3 2.3 %select_select_fusion = bf16[2,256,2560]{1,2,0:T(8,128)(2,1)S(1)} fusion(bf16[2,256,2560]{1,2,0:T(8,128)(2,1)} %collective-permute-done, bf16[2,256,2560]{1,2,0:T(8,128)(2,1)S(1)} %collective-permute-done.2, pred[]{:T(512)S(6)} %eq.56, pred[]{:T(512)S(6)} %eq.53), kind=kLoop, calls=%fused_computation.35 | loop fusion | flops 2621440 | bytes 7864322 | tf_op jit(solution)/shard_map/jit(_where)/select_n | solution.py:47
  158.6 14.0 %collective-permute-start.3 = (bf16[2,256,2560]{1,2,0:T(8,128)(2,1)S(1)}, bf16[2,256,2560]{1,2,0:T(8,128)(2,1)S(1)}, u32[]{:S(2)}, u32[]{:S(2)}) collective-permute-start(bf16[2,256,2560]{1,2,0:T(8,128)(2,1)S(1)} %select_select_fusion), channel_id=1, source_target_pairs={{0,1},{4,5},{8,9},{12,13},{1,0},{5,4},{9,8},{13,12},{2,3},{6,7},{1... | collective-permute-start | bytes 7864328 | tf_op jit(solution)/shard_map/ppermute | solution.py:31
  173.1 2.7 %fusion.71 = bf16[3,1,52,384]{3,2,1,0:T(8,128)(2,1)} fusion(bf16[10368,384,1]{1,0,2:T(8,128)(2,1)S(1)} %bitcast.192, bf16[3,1,52,10368]{3,2,0,1:T(8,128)(2,1)S(1)} %slice_dynamic-update-slice_fusion, bf16[3,1,52,384]{3,2,1,0:T(8,128)(2,1)S(1)} %copy-done.8, f32[384]{0:T(512)S(1)} %copy-done.12), kind=kOutput, calls=%fused_computation.82 | convolution fusion | flops 1242408960 | bytes 11438592 | tf_op jit(solution)/shard_map/dot_general | solution.py:183
  175.8 1.1 collective-permute-done.3
  177.1 1.3 bitcast_reduce_fusion.1
  178.4 1.2 fusion.15
  179.6 0.5 copy-done
  180.1 3.4 %multiply_add_fusion = f32[20,256,128]{2,1,0:T(8,128)} fusion(f32[20,256,128]{2,1,0:T(8,128)S(1)} %copy-done, bf16[256,20,128]{0,2,1:T(8,128)(2,1)S(1)} %bitcast.195, f32[20,256,256]{2,1,0:T(8,128)S(1)} %get-tuple-element.64, f32[20,256]{1,0:T(8,128)S(1)} %bitcast.206, pred[256]{0:T(512)(128)(4,1)S(1)} %select_select_fusion.5, ...), kind=kOutput, calls=%fused_computation.51 | convolution fusion | flops 342097920 | bytes 11837696 | tf_op jit(solution)/shard_map/hqk,khd->hqd/dot_general | solution.py:67
  183.5 1.9 fusion.110
  185.4 1.3 bitcast_reduce_fusion
  186.7 1.2 fusion.16
  187.9 0.5 copy-done.7
  188.4 2.9 %divide_bitcast_fusion = bf16[256,20,128]{2,0,1:T(8,128)(2,1)S(1)} fusion(f32[20,256,128]{2,1,0:T(8,128)S(1)} %copy-done.7, f32[20,256]{1,0:T(8,128)S(1)} %get-tuple-element.46, f32[20,256]{1,0:T(8,128)S(1)} %get-tuple-element.45, bf16[256,20,128]{0,2,1:T(8,128)(2,1)S(1)} %bitcast.204, f32[20,256,256]{2,1,0:T(8,128)S(1)} %get-tuple-element.66, ...), kind=kOutput, calls=%fused_computation.49 | convolution fusion | flops 343408640 | bytes 10547456 | tf_op jit(solution)/shard_map/hqk,khd->hqd/dot_general | solution.py:67
  191.4 0.6 copy.62
  192.3 1.6 copy.65
  (78 shorter events, 2.3 us)
Async XLA Ops:
  12.5 9.0 %copy-start.9 = (bf16[2,1,52,384]{3,0,2,1:T(2,128)(2,1)S(1)}, bf16[2,1,52,384]{3,0,2,1:T(2,128)(2,1)}, u32[]{:S(2)}) copy-start(bf16[2,1,52,384]{3,0,2,1:T(2,128)(2,1)} %param.16) | copy-start | bytes 239620
  12.5 9.0 %copy-start.8 = (bf16[3,1,52,384]{3,2,1,0:T(8,128)(2,1)S(1)}, bf16[3,1,52,384]{3,2,1,0:T(8,128)(2,1)}, u32[]{:S(2)}) copy-start(bf16[3,1,52,384]{3,2,1,0:T(8,128)(2,1)} %param.15) | copy-start | bytes 359428
  12.5 9.1 %copy-start.11 = (f32[384]{0:T(512)S(1)}, f32[384]{0:T(512)}, u32[]{:S(2)}) copy-start(f32[384]{0:T(512)} %param.17) | copy-start | bytes 4612
  14.3 169.2 %all-reduce.3.cloned.1.call-start = ((), (), s32[]{:S(2)}) async-start(), calls=%async_computation | async-start | bytes 5242880 | tf_op jit(solution)/shard_map/psum | solution.py:117
  15.0 74.1 %collective-permute-start = (bf16[2,256,2560]{1,2,0:T(8,128)(2,1)}, bf16[2,256,2560]{1,2,0:T(8,128)(2,1)}, u32[]{:S(2)}, u32[]{:S(2)}) collective-permute-start(bf16[2,256,2560]{1,2,0:T(8,128)(2,1)} %broadcast_select_fusion), channel_id=1, source_target_pairs={{0,2},{4,6},{8,10},{12,14},{1,3},{5,7},{9,11},{13,15},{2,1},{6,5},... | collective-permute-start | bytes 7864328 | tf_op jit(solution)/shard_map/ppermute | solution.py:31
  21.5 67.6 %collective-permute-start.1 = (bf16[2,256,2560]{1,2,0:T(8,128)(2,1)}, bf16[2,256,2560]{1,2,0:T(8,128)(2,1)}, u32[]{:S(2)}, u32[]{:S(2)}) collective-permute-start(bf16[2,256,2560]{1,2,0:T(8,128)(2,1)} %broadcast_select_fusion), channel_id=1, source_target_pairs={{0,1},{4,5},{8,9},{12,13},{2,3},{6,7},{10,11},{14,15},{1,4},{5,8},... | collective-permute-start | bytes 7864328 | tf_op jit(solution)/shard_map/ppermute | solution.py:31
  22.5 18.0 %collective-permute-start.5 = (bf16[5,1,52,384]{3,2,0,1:T(8,128)(2,1)}, bf16[5,1,52,384]{3,2,0,1:T(8,128)(2,1)S(1)}, u32[]{:S(2)}, u32[]{:S(2)}) collective-permute-start(bf16[5,1,52,384]{3,2,0,1:T(8,128)(2,1)} %pad_maximum_fusion), channel_id=1, source_target_pairs={{1,0},{2,1},{3,2},{4,3},{5,4},{6,5},{7,6},{8,7},{9,8},{10,9},{11,1... | collective-permute-start | bytes 599048 | tf_op jit(solution)/shard_map/ppermute | solution.py:25
  23.8 16.7 %collective-permute-start.4 = (bf16[5,1,52,384]{3,2,0,1:T(8,128)(2,1)}, bf16[5,1,52,384]{3,2,0,1:T(8,128)(2,1)S(1)}, u32[]{:S(2)}, u32[]{:S(2)}) collective-permute-start(bf16[5,1,52,384]{3,2,0,1:T(8,128)(2,1)} %pad_maximum_fusion), channel_id=1, source_target_pairs={{0,1},{1,2},{2,3},{3,4},{4,5},{5,6},{6,7},{7,8},{8,9},{9,10},{10,1... | collective-permute-start | bytes 599048 | tf_op jit(solution)/shard_map/ppermute | solution.py:22
  28.1 3.4 %copy-start.13 = (s32[16,3]{0,1:T(4,128)S(1)}, s32[16,3]{0,1:T(4,128)}, u32[]{:S(2)}) copy-start(s32[16,3]{0,1:T(4,128)} %param.13) | copy-start | bytes 580
  28.2 5.9 %copy-start.10 = (s32[16]{0:T(128)S(1)}, s32[16]{0:T(128)}, u32[]{:S(2)}) copy-start(s32[16]{0:T(128)} %param.14) | copy-start | bytes 196
  29.8 7.5 %copy-start.4 = (bf16[1,256,2560]{1,2,0:T(8,128)(2,1)S(1)}, bf16[1,256,2560]{1,2,0:T(8,128)(2,1)}, u32[]{:S(2)}) copy-start(bf16[1,256,2560]{1,2,0:T(8,128)(2,1)} %get-tuple-element.42) | copy-start | bytes 3932164
  91.1 43.8 %collective-permute-start.2 = (bf16[2,256,2560]{1,2,0:T(8,128)(2,1)S(1)}, bf16[2,256,2560]{1,2,0:T(8,128)(2,1)S(1)}, u32[]{:S(2)}, u32[]{:S(2)}) collective-permute-start(bf16[2,256,2560]{1,2,0:T(8,128)(2,1)S(1)} %select_select_fusion.1), channel_id=1, source_target_pairs={{3,2},{7,6},{11,10},{15,14},{2,0},{6,4},{10,8},{14,12},{1,5},{5,9}... | collective-permute-start | bytes 7864328 | tf_op jit(solution)/shard_map/ppermute | solution.py:31
  92.5 4.5 %copy-start.2 = (bf16[3,1,52,10368]{3,2,0,1:T(8,128)(2,1)}, bf16[3,1,52,10368]{3,2,0,1:T(8,128)(2,1)S(1)}, u32[]{:S(2)}) copy-start(bf16[3,1,52,10368]{3,2,0,1:T(8,128)(2,1)S(1)} %slice_dynamic-update-slice_fusion.8) | copy-start | bytes 9704452
  142.3 2.5 %copy-start.5 = (bf16[1,256,2560]{1,2,0:T(8,128)(2,1)S(1)}, bf16[1,256,2560]{1,2,0:T(8,128)(2,1)}, u32[]{:S(2)}) copy-start(bf16[1,256,2560]{1,2,0:T(8,128)(2,1)} %get-tuple-element.41) | copy-start | bytes 3932164
  144.8 3.1 %copy-start.6 = (bf16[1,256,2560]{1,2,0:T(8,128)(2,1)S(1)}, bf16[1,256,2560]{1,2,0:T(8,128)(2,1)}, u32[]{:S(2)}) copy-start(bf16[1,256,2560]{1,2,0:T(8,128)(2,1)} %get-tuple-element.39) | copy-start | bytes 3932164
  147.8 3.1 %copy-start.1 = (f32[20,256,128]{2,1,0:T(8,128)S(1)}, f32[20,256,128]{2,1,0:T(8,128)}, u32[]{:S(2)}) copy-start(f32[20,256,128]{2,1,0:T(8,128)} %fusion.26) | copy-start | bytes 7864324
  147.8 25.3 %slice-start = ((s8[7962624]{0:T(1024)(128)(4,1)}), s8[3768320]{0:T(1024)(128)(4,1)S(1)}, s32[]{:S(2)}) async-start(s8[7962624]{0:T(1024)(128)(4,1)} %bitcast.190), calls=%async_computation.1 | async-start | bytes 7536640
  150.9 22.2 %slice-start.1 = ((s8[7962624]{0:T(1024)(128)(4,1)}), s8[4194304]{0:T(1024)(128)(4,1)S(1)}, s32[]{:S(2)}) async-start(s8[7962624]{0:T(1024)(128)(4,1)} %bitcast.190), calls=%async_computation.2 | async-start | bytes 8388608
  156.3 16.3 %copy-start.3 = (bf16[3,1,52,10368]{3,2,0,1:T(8,128)(2,1)S(1)}, bf16[3,1,52,10368]{3,2,0,1:T(8,128)(2,1)}, u32[]{:S(2)}) copy-start(bf16[3,1,52,10368]{3,2,0,1:T(8,128)(2,1)} %copy-done.2) | copy-start | bytes 9704452
  156.3 16.8 %copy-start.12 = (f32[384]{0:T(512)S(1)}, f32[384]{0:T(512)}, u32[]{:S(2)}) copy-start(f32[384]{0:T(512)} %param.19) | copy-start | bytes 4612
  158.6 18.3 %collective-permute-start.3 = (bf16[2,256,2560]{1,2,0:T(8,128)(2,1)S(1)}, bf16[2,256,2560]{1,2,0:T(8,128)(2,1)S(1)}, u32[]{:S(2)}, u32[]{:S(2)}) collective-permute-start(bf16[2,256,2560]{1,2,0:T(8,128)(2,1)S(1)} %select_select_fusion), channel_id=1, source_target_pairs={{0,1},{4,5},{8,9},{12,13},{1,0},{5,4},{9,8},{13,12},{2,3},{6,7},{1... | collective-permute-start | bytes 7864328 | tf_op jit(solution)/shard_map/ppermute | solution.py:31
  178.4 1.7 copy-start
  186.7 1.7 copy-start.7
Sparse Core Ops, SparseCore 0:
  18.7 129.1 all-reduce.2

commit v12 on v10

--- a/solution.py
+++ b/solution.py
@@ -127,10 +127,12 @@
             out = jnp.where(lane == l, valid_list[per_lane[l]], out)
         return out
 
+    early = jnp.where(lane < 2, second, cross)
+    late = jnp.where(lane == 2, second, third)
     groups = [
         [(keys_values, valid_list[0]), (along, offset_of(3, 1, 3, 1))],
-        [(cross, offset_of(4, 4, 2, 2)), (second, offset_of(1, 3, 1, 4))],
-        [(third, offset_of(2, 2, 4, 3))],
+        [(early, offset_of(1, 3, 2, 2))],
+        [(late, offset_of(2, 2, 1, 3))],
     ]
     anchor_valid = (place != anchor) & (row_ids < lengths[anchor])
     heads = [slice(h * HG * DH, (h + 1) * HG * DH) for h in range(H // HG)]

time: 194 us -> 188 us (0.969)
  matrix products: 25.4 us -> 21 us
  local copies, waits for them, and re-layouts: 19.4 us -> 15.2 us
  waiting for transfers between devices: 80.5 us -> 83.6 us
    select_n x0 -> x2, other arithmetic: none -> 3.93 us  [the longest x1 3.65 us: shards(): early = jnp.where(lane < 2, second, cross)]
    select_n x2 -> x1, other arithmetic: 5.66 us -> 2.01 us  [pick(): out = jnp.where(lane == l, options[l], out)]
    slice x6 -> x5, local copies, waits for them, and re-layouts: 9.39 us -> 5.77 us  [attend(): part_out = weighted(weights, kv[1].reshape(-1, HG, DH))]
    ppermute x4, waiting for transfers between devices: 79.8 us -> 82.9 us  [move(): return lax.ppermute(value, 'span', pairs)]
    dot_general x6 -> x5, matrix products: 14.8 us -> 11.7 us  [weighted(): jnp.einsum('hqk,khd->hqd', weights.astype(jnp.bfloat16), values, preferre...]
    ppermute x4, starting transfers between devices: 21.3 us -> 23.5 us  [move(): return lax.ppermute(value, 'span', pairs)]
    dot_general x6 -> x5, matrix products: 7.88 us -> 6.52 us  [part_stats(): jnp.einsum('qhd,khd->hqk', q, k, preferred_element_type=jnp.float32) * scale]
    select_n x3 -> x2, other arithmetic: 4.61 us -> 3.85 us  [offset_of(): out = jnp.where(lane == l, valid_list[per_lane[l]], out)]
  transfers between devices with their start and end apart: 7 -> 7, of which waited for: 2 -> 2; matrix products, arithmetic and copies ran while one was open for 27% -> 22% of each run, Pallas kernels for 0% -> 0%
where the time goes in v12:
time: 188 us
  waiting for transfers between devices  83.6 us (44%)
  starting transfers between devices  27.8 us (15%)
  other arithmetic  22.6 us (12%)
  matrix products  21 us (11%)
  between operations  17.4 us (9%)
  local copies, waits for them, and re-layouts  15.2 us (8%)
    ppermute x4, waiting for transfers between devices, move(): return lax.ppermute(value, 'span', pairs)  82.9 us
    ppermute x4, starting transfers between devices, move(): return lax.ppermute(value, 'span', pairs)  23.5 us
    dot_general x5, matrix products, weighted(): jnp.einsum('hqk,khd->hqd', weights.astype(jnp.bfloat16), values, preferre...  11.7 us
    unnamed x49, local copies, waits for them, and re-layouts  7.46 us
    dot_general x5, matrix products, part_stats(): jnp.einsum('qhd,khd->hqk', q, k, preferred_element_type=jnp.float32) * scale  6.52 us
    reduce_sum x4, other arithmetic, attend(): part_total = jnp.sum(weights, axis=-1, keepdims=True)  6.2 us
    slice x5, local copies, waits for them, and re-layouts, attend(): part_out = weighted(weights, kv[1].reshape(-1, HG, DH))  5.77 us
    select_n x2, other arithmetic, offset_of(): out = jnp.where(lane == l, valid_list[per_lane[l]], out)  3.85 us
  transfers between devices with their start and end apart: 7, of which 2 were waited for; matrix products, arithmetic and copies ran while one was open for 22% of the time, Pallas kernels for 0%

profile of v12, /device:TPU:0, one launch (start us, length us, event | category | flops | bytes accessed | tf_op | source)
XLA Modules:
  0.0 187.6 jit_solution(10701188257814439373)
XLA Ops:
  7.2 3.0 %copy.29 = bf16[2,256,2560]{1,2,0:T(8,128)(2,1)S(1)} copy(bf16[2,256,2560]{2,1,0:T(8,128)(2,1)} %param.11) | data formatting | bytes 5242880 | tf_op args[1]
  10.8 1.7 broadcast_select_fusion.3
  12.5 1.8 broadcast_select_fusion.2
  14.3 0.7 all-reduce.3.cloned.1.call-update
  15.1 8.2 %collective-permute-start = (bf16[2,256,2560]{1,2,0:T(8,128)(2,1)}, bf16[2,256,2560]{1,2,0:T(8,128)(2,1)}, u32[]{:S(2)}, u32[]{:S(2)}) collective-permute-start(bf16[2,256,2560]{1,2,0:T(8,128)(2,1)} %broadcast_select_fusion.2), channel_id=1, source_target_pairs={{0,2},{4,6},{8,10},{12,14},{1,3},{5,7},{9,11},{13,15},{2,1},{6,5},... | collective-permute-start | bytes 7864328 | tf_op jit(solution)/shard_map/ppermute | solution.py:31
  23.5 0.7 pad_maximum_fusion
  24.2 1.3 collective-permute-start.5
  25.5 3.0 %collective-permute-start.4 = (bf16[5,1,52,384]{3,2,0,1:T(8,128)(2,1)}, bf16[5,1,52,384]{3,2,0,1:T(8,128)(2,1)S(1)}, u32[]{:S(2)}, u32[]{:S(2)}) collective-permute-start(bf16[5,1,52,384]{3,2,0,1:T(8,128)(2,1)} %pad_maximum_fusion), channel_id=1, source_target_pairs={{0,1},{1,2},{2,3},{3,4},{4,5},{5,6},{6,7},{7,8},{8,9},{9,10},{10,1... | collective-permute-start | bytes 599048 | tf_op jit(solution)/shard_map/ppermute | solution.py:22
  28.7 1.7 fusion.99
  30.4 0.7 constant_dynamic-slice_fusion.2
  32.9 1.6 copy.31
  34.6 0.7 fusion.101
  35.3 0.6 iota_compare_fusion.2
  35.9 0.7 compare_and_fusion
  36.6 1.3 fusion.4
  37.9 1.9 %select_select_fusion.4 = pred[256]{0:T(512)(128)(4,1)S(1)} fusion(pred[]{:T(512)S(6)} %and.97, pred[]{:T(512)S(6)} %eq.54, pred[]{:T(512)S(6)} %eq.51, s32[]{:T(128)} %bitcast.7, s32[]{:T(128)} %bitcast.3, pred[]{:T(512)S(6)} %and.89, s32[]{:T(128)} %bitcast.5, pred[]{:T(512)S(6)} %and.93), kind=kLoop, calls=%fused_computation.144 | loop fusion | flops 2048 | bytes 273 | tf_op jit(solution)/shard_map/jit(_where)/select_n | solution.py:127
  39.8 1.9 %fusion.85 = (pred[256]{0:T(512)(128)(4,1)S(1)}, pred[256]{0:T(512)(128)(4,1)S(1)}) fusion(pred[]{:T(512)S(6)} %eq.59, pred[]{:T(512)S(6)} %eq.54, pred[]{:T(512)S(6)} %eq.51, s32[]{:T(128)} %bitcast.3, pred[]{:T(512)S(6)} %and.89, s32[]{:T(128)} %bitcast.5, pred[]{:T(512)S(6)} %and.93, s32[]{:T(128)} %bitcast.7, pred[]{:T(512)S(6)} %and.97), kind=kLoop, calls=%fused_computation.140 | loop fusion | flops 3072 | bytes 530 | tf_op jit(solution)/shard_map/jit(_where)/select_n | solution.py:127
  41.8 0.2 select_maximum_fusion
  42.8 0.2 constant_dynamic-update-slice_fusion
  43.0 47.3 %collective-permute-done = bf16[2,256,2560]{1,2,0:T(8,128)(2,1)} collective-permute-done((bf16[2,256,2560]{1,2,0:T(8,128)(2,1)}, bf16[2,256,2560]{1,2,0:T(8,128)(2,1)}, u32[]{:S(2)}, u32[]{:S(2)}) %collective-permute-start) | collective-permute-done | bytes 2621472 | tf_op jit(solution)/shard_map/ppermute | solution.py:31
  90.3 2.0 %select_select_fusion.1 = bf16[2,256,2560]{1,2,0:T(8,128)(2,1)S(1)} fusion(bf16[2,256,2560]{1,2,0:T(8,128)(2,1)} %collective-permute-done, bf16[2,256,2560]{1,2,0:T(8,128)(2,1)} %collective-permute-done.1, pred[]{:T(512)S(6)} %eq.51, pred[]{:T(512)S(6)} %eq.54), kind=kLoop, calls=%fused_computation.30 | loop fusion | flops 2621440 | bytes 7864322 | tf_op jit(solution)/shard_map/jit(_where)/select_n | solution.py:47
  92.3 1.3 collective-permute-start.2
  93.8 2.7 %fusion.60 = bf16[3,1,52,384]{3,2,1,0:T(8,128)(2,1)} fusion(bf16[10368,384,1]{1,0,2:T(8,128)(2,1)S(1)} %bitcast.186, bf16[3,1,52,10368]{3,2,0,1:T(8,128)(2,1)S(1)} %slice_dynamic-update-slice_fusion, bf16[3,1,52,384]{3,2,1,0:T(8,128)(2,1)S(1)} %copy-done.3, f32[384]{0:T(512)S(1)} %copy-done.7), kind=kOutput, calls=%fused_computation.72 | convolution fusion | flops 1242408960 | bytes 11438592 | tf_op jit(solution)/shard_map/dot_general | solution.py:178
  96.5 1.9 %fusion.98 = (bf16[1,256,2560]{1,2,0:T(8,128)(2,1)S(1)}, bf16[1,256,2560]{1,2,0:T(8,128)(2,1)S(1)}) fusion(bf16[2,256,2560]{1,2,0:T(8,128)(2,1)} %collective-permute-done.1), kind=kLoop, calls=%fused_computation.164 | loop fusion | bytes 5242880 | tf_op jit(solution)/shard_map/slice | solution.py:83
  98.4 1.3 bitcast_reduce_fusion.1
  99.7 35.6 %collective-permute-done.2 = bf16[2,256,2560]{1,2,0:T(8,128)(2,1)S(1)} collective-permute-done((bf16[2,256,2560]{1,2,0:T(8,128)(2,1)S(1)}, bf16[2,256,2560]{1,2,0:T(8,128)(2,1)S(1)}, u32[]{:S(2)}, u32[]{:S(2)}) %collective-permute-start.2) | collective-permute-done | bytes 2621472 | tf_op jit(solution)/shard_map/ppermute | solution.py:31
  135.3 3.7 %broadcast_select_fusion = (bf16[2,256,2560]{1,2,0:T(8,128)(2,1)S(1)}, bf16[2,256,2560]{1,2,0:T(8,128)(2,1)}) fusion(bf16[2,256,2560]{1,2,0:T(8,128)(2,1)S(1)} %collective-permute-done.2, bf16[2,256,2560]{1,2,0:T(8,128)(2,1)} %collective-permute-done, pred[]{:T(512)S(6)} %lt.138, pred[]{:T(512)S(6)} %eq.54, pred[]{:T(512)S(6)} %eq.51), kind=kLoop, calls=%fused_computation.62 | loop fusion | flops 3932160 | bytes 10485763 | tf_op jit(solution)/shard_map/jit(_where)/select_n | solution.py:130
  139.0 14.0 %collective-permute-start.3 = (bf16[2,256,2560]{1,2,0:T(8,128)(2,1)}, bf16[2,256,2560]{1,2,0:T(8,128)(2,1)S(1)}, u32[]{:S(2)}, u32[]{:S(2)}) collective-permute-start(bf16[2,256,2560]{1,2,0:T(8,128)(2,1)} %get-tuple-element.22), channel_id=1, source_target_pairs={{0,1},{4,5},{8,9},{12,13},{1,0},{5,4},{9,8},{13,12},{2,3},{6,7},{1... | collective-permute-start | bytes 7864328 | tf_op jit(solution)/shard_map/ppermute | solution.py:31
  153.0 0.2 fusion.100
  153.2 1.3 bitcast_reduce_fusion.2
  154.6 1.2 fusion.10
  155.7 1.6 fusion.21
  157.3 1.6 fusion.25
  158.9 1.6 fusion.19
  160.5 2.7 %fusion.12 = (f32[20,256]{1,0:T(8,128)S(1)}, f32[20,256]{1,0:T(8,128)S(1)}) fusion(f32[20,256,256]{2,1,0:T(8,128)S(1)} %get-tuple-element.50, f32[20,256]{1,0:T(8,128)S(1)} %get-tuple-element.18, pred[256]{0:T(512)(128)(4,1)S(1)} %get-tuple-element.55, f32[20,256,256]{1,2,0:T(8,128)S(1)} %get-tuple-element.48, pred[256]{0:T(512)(128)(4,1)S(1)} %iota_compare_fusion.2), kind=kLoop, calls=%fused_computation.26 | loop fusion | flops 10475520 | bytes 10547712 | tf_op jit(solution)/shard_map/reduce_sum | solution.py:82
  163.2 0.3 broadcast_select_fusion.1
  163.5 0.2 fusion.97
  163.6 1.3 bitcast_reduce_fusion.3
  165.0 1.2 fusion.8
  166.2 4.1 %multiply_add_fusion = f32[20,256,128]{2,1,0:T(8,128)} fusion(f32[20,256,128]{2,1,0:T(8,128)S(1)} %fusion.21, f32[20,256,128]{2,1,0:T(8,128)S(1)} %fusion.25, f32[20,256,128]{2,1,0:T(8,128)S(1)} %fusion.19, bf16[256,20,128]{0,2,1:T(8,128)(2,1)S(1)} %bitcast.187, f32[20,256,256]{2,1,0:T(8,128)S(1)} %get-tuple-element.52, ...), kind=kOutput, calls=%fused_computation.44 | convolution fusion | flops 344064000 | bytes 17101056 | tf_op jit(solution)/shard_map/hqk,khd->hqd/dot_general | solution.py:63
  170.3 1.9 %fusion.96 = (bf16[1,256,2560]{1,2,0:T(8,128)(2,1)S(1)}, bf16[1,256,2560]{1,2,0:T(8,128)(2,1)S(1)}) fusion(bf16[2,256,2560]{1,2,0:T(8,128)(2,1)} %all-reduce.3.cloned.1.call-done), kind=kLoop, calls=%fused_computation.162 | loop fusion | bytes 5242880 | tf_op jit(solution)/shard_map/slice | solution.py:83
  172.2 1.3 bitcast_reduce_fusion
  173.5 1.2 fusion.13
  174.7 0.5 copy-done.2
  175.2 2.9 %divide_bitcast_fusion = bf16[256,20,128]{2,0,1:T(8,128)(2,1)S(1)} fusion(f32[20,256,128]{2,1,0:T(8,128)S(1)} %copy-done.2, f32[20,256]{1,0:T(8,128)S(1)} %get-tuple-element.36, f32[20,256]{1,0:T(8,128)S(1)} %get-tuple-element.35, bf16[256,20,128]{0,2,1:T(8,128)(2,1)S(1)} %bitcast.196, f32[20,256,256]{2,1,0:T(8,128)S(1)} %get-tuple-element.54, ...), kind=kOutput, calls=%fused_computation.42 | convolution fusion | flops 343408640 | bytes 10547456 | tf_op jit(solution)/shard_map/hqk,khd->hqd/dot_general | solution.py:63
  178.2 0.6 copy.56
  178.8 0.3 fusion.29
  179.1 1.6 copy.59
  (64 shorter events, 1.2 us)
Async XLA Ops:
  12.5 10.7 %copy-start.4 = (bf16[2,1,52,384]{3,0,2,1:T(2,128)(2,1)S(1)}, bf16[2,1,52,384]{3,0,2,1:T(2,128)(2,1)}, u32[]{:S(2)}) copy-start(bf16[2,1,52,384]{3,0,2,1:T(2,128)(2,1)} %param.16) | copy-start | bytes 239620
  12.5 10.7 %copy-start.3 = (bf16[3,1,52,384]{3,2,1,0:T(8,128)(2,1)S(1)}, bf16[3,1,52,384]{3,2,1,0:T(8,128)(2,1)}, u32[]{:S(2)}) copy-start(bf16[3,1,52,384]{3,2,1,0:T(8,128)(2,1)} %param.15) | copy-start | bytes 359428
  12.5 10.9 %copy-start.6 = (f32[384]{0:T(512)S(1)}, f32[384]{0:T(512)}, u32[]{:S(2)}) copy-start(f32[384]{0:T(512)} %param.17) | copy-start | bytes 4612
  14.3 156.0 %all-reduce.3.cloned.1.call-start = ((), (), s32[]{:S(2)}) async-start(), calls=%async_computation | async-start | bytes 5242880 | tf_op jit(solution)/shard_map/psum | solution.py:113
  15.1 15.3 %copy-start.8 = (s32[16,3]{0,1:T(4,128)S(1)}, s32[16,3]{0,1:T(4,128)}, u32[]{:S(2)}) copy-start(s32[16,3]{0,1:T(4,128)} %param.13) | copy-start | bytes 580
  15.1 75.2 %collective-permute-start = (bf16[2,256,2560]{1,2,0:T(8,128)(2,1)}, bf16[2,256,2560]{1,2,0:T(8,128)(2,1)}, u32[]{:S(2)}, u32[]{:S(2)}) collective-permute-start(bf16[2,256,2560]{1,2,0:T(8,128)(2,1)} %broadcast_select_fusion.2), channel_id=1, source_target_pairs={{0,2},{4,6},{8,10},{12,14},{1,3},{5,7},{9,11},{13,15},{2,1},{6,5},... | collective-permute-start | bytes 7864328 | tf_op jit(solution)/shard_map/ppermute | solution.py:31
  23.2 67.1 %collective-permute-start.1 = (bf16[2,256,2560]{1,2,0:T(8,128)(2,1)}, bf16[2,256,2560]{1,2,0:T(8,128)(2,1)}, u32[]{:S(2)}, u32[]{:S(2)}) collective-permute-start(bf16[2,256,2560]{1,2,0:T(8,128)(2,1)} %broadcast_select_fusion.2), channel_id=1, source_target_pairs={{0,1},{4,5},{8,9},{12,13},{2,3},{6,7},{10,11},{14,15},{1,4},{5,8},... | collective-permute-start | bytes 7864328 | tf_op jit(solution)/shard_map/ppermute | solution.py:31
  24.2 17.5 %collective-permute-start.5 = (bf16[5,1,52,384]{3,2,0,1:T(8,128)(2,1)}, bf16[5,1,52,384]{3,2,0,1:T(8,128)(2,1)S(1)}, u32[]{:S(2)}, u32[]{:S(2)}) collective-permute-start(bf16[5,1,52,384]{3,2,0,1:T(8,128)(2,1)} %pad_maximum_fusion), channel_id=1, source_target_pairs={{1,0},{2,1},{3,2},{4,3},{5,4},{6,5},{7,6},{8,7},{9,8},{10,9},{11,1... | collective-permute-start | bytes 599048 | tf_op jit(solution)/shard_map/ppermute | solution.py:25
  25.5 16.2 %collective-permute-start.4 = (bf16[5,1,52,384]{3,2,0,1:T(8,128)(2,1)}, bf16[5,1,52,384]{3,2,0,1:T(8,128)(2,1)S(1)}, u32[]{:S(2)}, u32[]{:S(2)}) collective-permute-start(bf16[5,1,52,384]{3,2,0,1:T(8,128)(2,1)} %pad_maximum_fusion), channel_id=1, source_target_pairs={{0,1},{1,2},{2,3},{3,4},{4,5},{5,6},{6,7},{7,8},{8,9},{9,10},{10,1... | collective-permute-start | bytes 599048 | tf_op jit(solution)/shard_map/ppermute | solution.py:22
  28.7 5.9 %copy-start.5 = (s32[16]{0:T(128)S(1)}, s32[16]{0:T(128)}, u32[]{:S(2)}) copy-start(s32[16]{0:T(128)} %param.14) | copy-start | bytes 196
  30.4 6.2 %copy-start = (bf16[1,256,2560]{1,2,0:T(8,128)(2,1)S(1)}, bf16[1,256,2560]{1,2,0:T(8,128)(2,1)}, u32[]{:S(2)}) copy-start(bf16[1,256,2560]{1,2,0:T(8,128)(2,1)} %get-tuple-element.30) | copy-start | bytes 3932164
  42.0 51.8 %slice-start = ((s8[7962624]{0:T(1024)(128)(4,1)}), s8[4194304]{0:T(1024)(128)(4,1)S(1)}, s32[]{:S(2)}) async-start(s8[7962624]{0:T(1024)(128)(4,1)} %bitcast.184), calls=%async_computation.1 | async-start | bytes 8388608
  43.0 50.8 %slice-start.1 = ((s8[7962624]{0:T(1024)(128)(4,1)}), s8[3768320]{0:T(1024)(128)(4,1)S(1)}, s32[]{:S(2)}) async-start(s8[7962624]{0:T(1024)(128)(4,1)} %bitcast.184), calls=%async_computation.2 | async-start | bytes 7536640
  43.0 50.8 %copy-start.7 = (f32[384]{0:T(512)S(1)}, f32[384]{0:T(512)}, u32[]{:S(2)}) copy-start(f32[384]{0:T(512)} %param.19) | copy-start | bytes 4612
  92.3 43.0 %collective-permute-start.2 = (bf16[2,256,2560]{1,2,0:T(8,128)(2,1)S(1)}, bf16[2,256,2560]{1,2,0:T(8,128)(2,1)S(1)}, u32[]{:S(2)}, u32[]{:S(2)}) collective-permute-start(bf16[2,256,2560]{1,2,0:T(8,128)(2,1)S(1)} %select_select_fusion.1), channel_id=1, source_target_pairs={{3,2},{7,6},{11,10},{15,14},{2,0},{6,4},{10,8},{14,12},{1,5},{5,9}... | collective-permute-start | bytes 7864328 | tf_op jit(solution)/shard_map/ppermute | solution.py:31
  139.0 24.2 %collective-permute-start.3 = (bf16[2,256,2560]{1,2,0:T(8,128)(2,1)}, bf16[2,256,2560]{1,2,0:T(8,128)(2,1)S(1)}, u32[]{:S(2)}, u32[]{:S(2)}) collective-permute-start(bf16[2,256,2560]{1,2,0:T(8,128)(2,1)} %get-tuple-element.22), channel_id=1, source_target_pairs={{0,1},{4,5},{8,9},{12,13},{1,0},{5,4},{9,8},{13,12},{2,3},{6,7},{1... | collective-permute-start | bytes 7864328 | tf_op jit(solution)/shard_map/ppermute | solution.py:31
  155.7 1.6 copy-start.1
  173.5 1.7 copy-start.2
Sparse Core Ops, SparseCore 0:
  18.8 129.5 all-reduce.2

commit v13 on v12

--- a/solution.py
+++ b/solution.py
@@ -50,7 +50,8 @@
     cross = move(kv, pairs((0, 2, 0), (1, 3, 0), (2, 1, 0)))
     along = move(kv, pairs((0, 1, 0), (2, 3, 0), (1, 0, 1), (3, 2, 1)))
     second = move(pick(cross, cross, along, cross), pairs((3, 2, 0), (2, 0, 0), (1, 1, 1)))
-    third = move(pick(second, second, cross, cross), pairs((0, 1, 0), (1, 0, 0), (2, 3, 0)))
+    onchip = move(cross, pairs((2, 3, 0)))
+    third = jnp.where(lane == 3, onchip, move(second, pairs((0, 1, 0), (1, 0, 0))))
     return along, cross, second, third
 
 

time: 188 us -> 193 us (1.027)
  waiting for transfers between devices: 83.6 us -> 87.9 us
    ppermute x4 -> x5, waiting for transfers between devices: 82.9 us -> 87.2 us  [move(): return lax.ppermute(value, 'span', pairs)]
    ppermute x4 -> x5, starting transfers between devices: 23.5 us -> 23.8 us  [move(): return lax.ppermute(value, 'span', pairs)]
    slice x5 -> x4, local copies, waits for them, and re-layouts: 5.77 us -> 5.76 us  [attend(): part_out = weighted(weights, kv[1].reshape(-1, HG, DH))]
    unnamed x49 -> x51, local copies, waits for them, and re-layouts: 7.46 us -> 7.47 us
  transfers between devices with their start and end apart: 7 -> 8, of which waited for: 2 -> 2; matrix products, arithmetic and copies ran while one was open for 22% -> 21% of each run, Pallas kernels for 0% -> 0%
where the time goes in v13:
time: 193 us
  waiting for transfers between devices  87.9 us (46%)
  starting transfers between devices  29.3 us (15%)
  other arithmetic  21.7 us (11%)
  matrix products  21 us (11%)
  between operations  17.3 us (9%)
  local copies, waits for them, and re-layouts  15.2 us (8%)
    ppermute x5, waiting for transfers between devices, move(): return lax.ppermute(value, 'span', pairs)  87.2 us
    ppermute x5, starting transfers between devices, move(): return lax.ppermute(value, 'span', pairs)  23.8 us
    dot_general x5, matrix products, weighted(): jnp.einsum('hqk,khd->hqd', weights.astype(jnp.bfloat16), values, preferre...  11.7 us
    unnamed x51, local copies, waits for them, and re-layouts  7.47 us
    dot_general x5, matrix products, part_stats(): jnp.einsum('qhd,khd->hqk', q, k, preferred_element_type=jnp.float32) * scale  6.57 us
    reduce_sum x4, other arithmetic, attend(): part_total = jnp.sum(weights, axis=-1, keepdims=True)  6.19 us
    slice x4, local copies, waits for them, and re-layouts, attend(): part_out = weighted(weights, kv[1].reshape(-1, HG, DH))  5.76 us
    ppermute x1, starting transfers between devices, extended_2(): lax.ppermute(lax.slice_in_dim(block, block.shape[dim] - width, None, axis...  4.23 us
  transfers between devices with their start and end apart: 8, of which 2 were waited for; matrix products, arithmetic and copies ran while one was open for 21% of the time, Pallas kernels for 0%

profile of v13, /device:TPU:0, one launch (start us, length us, event | category | flops | bytes accessed | tf_op | source)
XLA Modules:
  0.0 192.6 jit_solution(2400524635520131121)
XLA Ops:
  7.2 3.0 %copy.29 = bf16[2,256,2560]{1,2,0:T(8,128)(2,1)S(1)} copy(bf16[2,256,2560]{2,1,0:T(8,128)(2,1)} %param.11) | data formatting | bytes 5242880 | tf_op args[1]
  10.8 1.7 broadcast_select_fusion.2
  12.5 1.8 broadcast_select_fusion.1
  14.3 0.7 all-reduce.3.cloned.1.call-update
  15.0 6.4 %collective-permute-start = (bf16[2,256,2560]{1,2,0:T(8,128)(2,1)}, bf16[2,256,2560]{1,2,0:T(8,128)(2,1)}, u32[]{:S(2)}, u32[]{:S(2)}) collective-permute-start(bf16[2,256,2560]{1,2,0:T(8,128)(2,1)} %broadcast_select_fusion.1), channel_id=1, source_target_pairs={{0,2},{4,6},{8,10},{12,14},{1,3},{5,7},{9,11},{13,15},{2,1},{6,5},... | collective-permute-start | bytes 7864328 | tf_op jit(solution)/shard_map/ppermute | solution.py:31
  21.6 0.1 fusion.75
  21.7 0.7 pad_maximum_fusion
  22.4 1.3 collective-permute-start.6
  23.7 4.2 %collective-permute-start.5 = (bf16[5,1,52,384]{3,2,0,1:T(8,128)(2,1)}, bf16[5,1,52,384]{3,2,0,1:T(8,128)(2,1)S(1)}, u32[]{:S(2)}, u32[]{:S(2)}) collective-permute-start(bf16[5,1,52,384]{3,2,0,1:T(8,128)(2,1)} %pad_maximum_fusion), channel_id=1, source_target_pairs={{0,1},{1,2},{2,3},{3,4},{4,5},{5,6},{6,7},{7,8},{8,9},{9,10},{10,1... | collective-permute-start | bytes 599048 | tf_op jit(solution)/shard_map/ppermute | solution.py:22
  28.1 1.7 fusion.99
  29.8 0.7 constant_dynamic-slice_fusion.2
  32.3 1.6 copy.31
  34.0 0.7 fusion.101
  34.7 0.6 iota_compare_fusion.2
  35.3 1.3 fusion.4
  36.6 2.0 %fusion.85 = (pred[256]{0:T(512)(128)(4,1)S(1)}, pred[256]{0:T(512)(128)(4,1)S(1)}) fusion(pred[]{:T(512)S(6)} %eq.57, pred[]{:T(512)S(6)} %eq.52, pred[]{:T(512)S(6)} %eq.49, s32[]{:T(128)} %bitcast.3, pred[]{:T(512)S(6)} %and.89, s32[]{:T(128)} %bitcast.5, pred[]{:T(512)S(6)} %and.93, s32[]{:T(128)} %bitcast.7, pred[]{:T(512)S(6)} %and.97), kind=kLoop, calls=%fused_computation.139 | loop fusion | flops 3072 | bytes 530 | tf_op jit(solution)/shard_map/jit(_where)/select_n | solution.py:128
  38.6 2.0 %select_select_fusion.4 = pred[256]{0:T(512)(128)(4,1)S(1)} fusion(pred[]{:T(512)S(6)} %and.97, pred[]{:T(512)S(6)} %eq.52, pred[]{:T(512)S(6)} %eq.49, s32[]{:T(128)} %bitcast.7, s32[]{:T(128)} %bitcast.3, pred[]{:T(512)S(6)} %and.89, s32[]{:T(128)} %bitcast.5, pred[]{:T(512)S(6)} %and.93), kind=kLoop, calls=%fused_computation.143 | loop fusion | flops 2048 | bytes 273 | tf_op jit(solution)/shard_map/jit(_where)/select_n | solution.py:128
  40.6 0.6 compare_and_fusion
  41.2 0.2 select_maximum_fusion
  41.9 47.3 %collective-permute-done = bf16[2,256,2560]{1,2,0:T(8,128)(2,1)} collective-permute-done((bf16[2,256,2560]{1,2,0:T(8,128)(2,1)}, bf16[2,256,2560]{1,2,0:T(8,128)(2,1)}, u32[]{:S(2)}, u32[]{:S(2)}) %collective-permute-start) | collective-permute-done | bytes 2621472 | tf_op jit(solution)/shard_map/ppermute | solution.py:31
  89.1 2.0 %select_select_fusion = bf16[2,256,2560]{1,2,0:T(8,128)(2,1)S(1)} fusion(bf16[2,256,2560]{1,2,0:T(8,128)(2,1)} %collective-permute-done, bf16[2,256,2560]{1,2,0:T(8,128)(2,1)} %collective-permute-done.1, pred[]{:T(512)S(6)} %eq.49, pred[]{:T(512)S(6)} %eq.52), kind=kLoop, calls=%fused_computation.29 | loop fusion | flops 2621440 | bytes 7864322 | tf_op jit(solution)/shard_map/jit(_where)/select_n | solution.py:47
  91.2 1.3 collective-permute-start.2
  92.9 0.2 constant_dynamic-update-slice_fusion
  93.0 2.1 %collective-permute-start.3 = (bf16[2,256,2560]{1,2,0:T(8,128)(2,1)}, bf16[2,256,2560]{1,2,0:T(8,128)(2,1)}, u32[]{:S(2)}, u32[]{:S(2)}) collective-permute-start(bf16[2,256,2560]{1,2,0:T(8,128)(2,1)} %collective-permute-done), channel_id=1, source_target_pairs={{2,3},{6,7},{10,11},{14,15},{18,19},{22,23},{26,27},{30,31}} | collective-permute-start | bytes 7864328 | tf_op jit(solution)/shard_map/ppermute | solution.py:31
  95.2 39.9 %collective-permute-done.2 = bf16[2,256,2560]{1,2,0:T(8,128)(2,1)S(1)} collective-permute-done((bf16[2,256,2560]{1,2,0:T(8,128)(2,1)S(1)}, bf16[2,256,2560]{1,2,0:T(8,128)(2,1)S(1)}, u32[]{:S(2)}, u32[]{:S(2)}) %collective-permute-start.2) | collective-permute-done | bytes 2621472 | tf_op jit(solution)/shard_map/ppermute | solution.py:31
  135.1 14.0 %collective-permute-start.4 = (bf16[2,256,2560]{1,2,0:T(8,128)(2,1)S(1)}, bf16[2,256,2560]{1,2,0:T(8,128)(2,1)}, u32[]{:S(2)}, u32[]{:S(2)}) collective-permute-start(bf16[2,256,2560]{1,2,0:T(8,128)(2,1)S(1)} %collective-permute-done.2), channel_id=1, source_target_pairs={{0,1},{4,5},{8,9},{12,13},{1,0},{5,4},{9,8},{13,12},{16,17},{20,21... | collective-permute-start | bytes 7864328 | tf_op jit(solution)/shard_map/ppermute | solution.py:31
  149.3 2.7 %fusion.60 = bf16[3,1,52,384]{3,2,1,0:T(8,128)(2,1)} fusion(bf16[10368,384,1]{1,0,2:T(8,128)(2,1)S(1)} %bitcast.186, bf16[3,1,52,10368]{3,2,0,1:T(8,128)(2,1)S(1)} %slice_dynamic-update-slice_fusion, bf16[3,1,52,384]{3,2,1,0:T(8,128)(2,1)S(1)} %copy-done.4, f32[384]{0:T(512)S(1)} %copy-done.8), kind=kOutput, calls=%fused_computation.71 | convolution fusion | flops 1242408960 | bytes 11438592 | tf_op jit(solution)/shard_map/dot_general | solution.py:179
  152.1 1.9 fusion.98
  154.0 1.3 bitcast_reduce_fusion.1
  155.3 3.1 %broadcast_select_fusion = (bf16[2,256,2560]{1,2,0:T(8,128)(2,1)S(1)}, bf16[2,256,2560]{1,2,0:T(8,128)(2,1)S(1)}) fusion(bf16[2,256,2560]{1,2,0:T(8,128)(2,1)} %copy-done.2, bf16[2,256,2560]{1,2,0:T(8,128)(2,1)} %collective-permute-done, pred[]{:T(512)S(6)} %lt.138, bf16[2,256,2560]{1,2,0:T(8,128)(2,1)} %collective-permute-done.3, ...), kind=kLoop, calls=%fused_computation.62 | loop fusion | flops 3932160 | bytes 15728643 | tf_op jit(solution)/shard_map/jit(_where)/select_n | solution.py:131
  158.4 0.3 fusion.97
  158.7 1.3 bitcast_reduce_fusion.3
  160.1 1.3 bitcast_reduce_fusion.2
  161.4 1.2 fusion.10
  162.6 1.6 fusion.21
  164.2 2.7 %fusion.12 = (f32[20,256]{1,0:T(8,128)S(1)}, f32[20,256]{1,0:T(8,128)S(1)}) fusion(f32[20,256,256]{2,1,0:T(8,128)S(1)} %get-tuple-element.50, f32[20,256]{1,0:T(8,128)S(1)} %get-tuple-element.18, pred[256]{0:T(512)(128)(4,1)S(1)} %get-tuple-element.55, f32[20,256,256]{1,2,0:T(8,128)S(1)} %get-tuple-element.48, pred[256]{0:T(512)(128)(4,1)S(1)} %iota_compare_fusion.2), kind=kLoop, calls=%fused_computation.26 | loop fusion | flops 10475520 | bytes 10547712 | tf_op jit(solution)/shard_map/reduce_sum | solution.py:83
  166.9 1.6 fusion.25
  168.4 1.2 fusion.8
  169.6 1.6 fusion.19
  171.2 4.1 %multiply_add_fusion = f32[20,256,128]{2,1,0:T(8,128)} fusion(f32[20,256,128]{2,1,0:T(8,128)S(1)} %fusion.21, f32[20,256,128]{2,1,0:T(8,128)S(1)} %fusion.25, f32[20,256,128]{2,1,0:T(8,128)S(1)} %fusion.19, bf16[256,20,128]{0,2,1:T(8,128)(2,1)S(1)} %bitcast.187, f32[20,256,256]{2,1,0:T(8,128)S(1)} %get-tuple-element.52, ...), kind=kOutput, calls=%fused_computation.43 | convolution fusion | flops 344064000 | bytes 17101056 | tf_op jit(solution)/shard_map/hqk,khd->hqd/dot_general | solution.py:64
  175.3 1.9 fusion.96
  177.2 1.3 bitcast_reduce_fusion
  178.5 1.2 fusion.13
  179.7 0.5 copy-done.3
  180.2 2.9 %divide_bitcast_fusion = bf16[256,20,128]{2,0,1:T(8,128)(2,1)S(1)} fusion(f32[20,256,128]{2,1,0:T(8,128)S(1)} %copy-done.3, f32[20,256]{1,0:T(8,128)S(1)} %get-tuple-element.36, f32[20,256]{1,0:T(8,128)S(1)} %get-tuple-element.35, bf16[256,20,128]{0,2,1:T(8,128)(2,1)S(1)} %bitcast.196, f32[20,256,256]{2,1,0:T(8,128)S(1)} %get-tuple-element.54, ...), kind=kOutput, calls=%fused_computation.41 | convolution fusion | flops 343408640 | bytes 10547456 | tf_op jit(solution)/shard_map/hqk,khd->hqd/dot_general | solution.py:64
  183.2 0.6 copy.56
  183.8 0.3 fusion.29
  184.1 1.6 copy.59
  (66 shorter events, 1.1 us)
Async XLA Ops:
  12.5 8.9 %copy-start.5 = (bf16[2,1,52,384]{3,0,2,1:T(2,128)(2,1)S(1)}, bf16[2,1,52,384]{3,0,2,1:T(2,128)(2,1)}, u32[]{:S(2)}) copy-start(bf16[2,1,52,384]{3,0,2,1:T(2,128)(2,1)} %param.16) | copy-start | bytes 239620
  12.5 8.9 %copy-start.4 = (bf16[3,1,52,384]{3,2,1,0:T(8,128)(2,1)S(1)}, bf16[3,1,52,384]{3,2,1,0:T(8,128)(2,1)}, u32[]{:S(2)}) copy-start(bf16[3,1,52,384]{3,2,1,0:T(8,128)(2,1)} %param.15) | copy-start | bytes 359428
  12.5 9.1 %copy-start.7 = (f32[384]{0:T(512)S(1)}, f32[384]{0:T(512)}, u32[]{:S(2)}) copy-start(f32[384]{0:T(512)} %param.17) | copy-start | bytes 4612
  14.3 161.0 %all-reduce.3.cloned.1.call-start = ((), (), s32[]{:S(2)}) async-start(), calls=%async_computation | async-start | bytes 5242880 | tf_op jit(solution)/shard_map/psum | solution.py:114
  15.0 14.7 %copy-start.9 = (s32[16,3]{0,1:T(4,128)S(1)}, s32[16,3]{0,1:T(4,128)}, u32[]{:S(2)}) copy-start(s32[16,3]{0,1:T(4,128)} %param.13) | copy-start | bytes 580
  15.0 74.1 %collective-permute-start = (bf16[2,256,2560]{1,2,0:T(8,128)(2,1)}, bf16[2,256,2560]{1,2,0:T(8,128)(2,1)}, u32[]{:S(2)}, u32[]{:S(2)}) collective-permute-start(bf16[2,256,2560]{1,2,0:T(8,128)(2,1)} %broadcast_select_fusion.1), channel_id=1, source_target_pairs={{0,2},{4,6},{8,10},{12,14},{1,3},{5,7},{9,11},{13,15},{2,1},{6,5},... | collective-permute-start | bytes 7864328 | tf_op jit(solution)/shard_map/ppermute | solution.py:31
  21.4 67.7 %collective-permute-start.1 = (bf16[2,256,2560]{1,2,0:T(8,128)(2,1)}, bf16[2,256,2560]{1,2,0:T(8,128)(2,1)}, u32[]{:S(2)}, u32[]{:S(2)}) collective-permute-start(bf16[2,256,2560]{1,2,0:T(8,128)(2,1)} %broadcast_select_fusion.1), channel_id=1, source_target_pairs={{0,1},{4,5},{8,9},{12,13},{2,3},{6,7},{10,11},{14,15},{1,4},{5,8},... | collective-permute-start | bytes 7864328 | tf_op jit(solution)/shard_map/ppermute | solution.py:31
  22.4 18.7 %collective-permute-start.6 = (bf16[5,1,52,384]{3,2,0,1:T(8,128)(2,1)}, bf16[5,1,52,384]{3,2,0,1:T(8,128)(2,1)S(1)}, u32[]{:S(2)}, u32[]{:S(2)}) collective-permute-start(bf16[5,1,52,384]{3,2,0,1:T(8,128)(2,1)} %pad_maximum_fusion), channel_id=1, source_target_pairs={{1,0},{2,1},{3,2},{4,3},{5,4},{6,5},{7,6},{8,7},{9,8},{10,9},{11,1... | collective-permute-start | bytes 599048 | tf_op jit(solution)/shard_map/ppermute | solution.py:25
  23.7 17.5 %collective-permute-start.5 = (bf16[5,1,52,384]{3,2,0,1:T(8,128)(2,1)}, bf16[5,1,52,384]{3,2,0,1:T(8,128)(2,1)S(1)}, u32[]{:S(2)}, u32[]{:S(2)}) collective-permute-start(bf16[5,1,52,384]{3,2,0,1:T(8,128)(2,1)} %pad_maximum_fusion), channel_id=1, source_target_pairs={{0,1},{1,2},{2,3},{3,4},{4,5},{5,6},{6,7},{7,8},{8,9},{9,10},{10,1... | collective-permute-start | bytes 599048 | tf_op jit(solution)/shard_map/ppermute | solution.py:22
  28.1 5.9 %copy-start.6 = (s32[16]{0:T(128)S(1)}, s32[16]{0:T(128)}, u32[]{:S(2)}) copy-start(s32[16]{0:T(128)} %param.14) | copy-start | bytes 196
  29.7 5.6 %copy-start = (bf16[1,256,2560]{1,2,0:T(8,128)(2,1)S(1)}, bf16[1,256,2560]{1,2,0:T(8,128)(2,1)}, u32[]{:S(2)}) copy-start(bf16[1,256,2560]{1,2,0:T(8,128)(2,1)} %get-tuple-element.28) | copy-start | bytes 3932164
  41.5 107.8 %slice-start = ((s8[7962624]{0:T(1024)(128)(4,1)}), s8[4194304]{0:T(1024)(128)(4,1)S(1)}, s32[]{:S(2)}) async-start(s8[7962624]{0:T(1024)(128)(4,1)} %bitcast.184), calls=%async_computation.1 | async-start | bytes 8388608
  41.8 107.5 %slice-start.1 = ((s8[7962624]{0:T(1024)(128)(4,1)}), s8[3768320]{0:T(1024)(128)(4,1)S(1)}, s32[]{:S(2)}) async-start(s8[7962624]{0:T(1024)(128)(4,1)} %bitcast.184), calls=%async_computation.2 | async-start | bytes 7536640
  91.1 58.2 %copy-start.8 = (f32[384]{0:T(512)S(1)}, f32[384]{0:T(512)}, u32[]{:S(2)}) copy-start(f32[384]{0:T(512)} %param.19) | copy-start | bytes 4612
  91.2 44.0 %collective-permute-start.2 = (bf16[2,256,2560]{1,2,0:T(8,128)(2,1)S(1)}, bf16[2,256,2560]{1,2,0:T(8,128)(2,1)S(1)}, u32[]{:S(2)}, u32[]{:S(2)}) collective-permute-start(bf16[2,256,2560]{1,2,0:T(8,128)(2,1)S(1)} %select_select_fusion), channel_id=1, source_target_pairs={{3,2},{7,6},{11,10},{15,14},{2,0},{6,4},{10,8},{14,12},{1,5},{5,9}... | collective-permute-start | bytes 7864328 | tf_op jit(solution)/shard_map/ppermute | solution.py:31
  93.0 62.2 %collective-permute-start.3 = (bf16[2,256,2560]{1,2,0:T(8,128)(2,1)}, bf16[2,256,2560]{1,2,0:T(8,128)(2,1)}, u32[]{:S(2)}, u32[]{:S(2)}) collective-permute-start(bf16[2,256,2560]{1,2,0:T(8,128)(2,1)} %collective-permute-done), channel_id=1, source_target_pairs={{2,3},{6,7},{10,11},{14,15},{18,19},{22,23},{26,27},{30,31}} | collective-permute-start | bytes 7864328 | tf_op jit(solution)/shard_map/ppermute | solution.py:31
  135.1 18.8 %copy-start.2 = (bf16[2,256,2560]{1,2,0:T(8,128)(2,1)}, bf16[2,256,2560]{1,2,0:T(8,128)(2,1)S(1)}, u32[]{:S(2)}) copy-start(bf16[2,256,2560]{1,2,0:T(8,128)(2,1)S(1)} %collective-permute-done.2) | copy-start | bytes 7864324
  135.1 20.2 %collective-permute-start.4 = (bf16[2,256,2560]{1,2,0:T(8,128)(2,1)S(1)}, bf16[2,256,2560]{1,2,0:T(8,128)(2,1)}, u32[]{:S(2)}, u32[]{:S(2)}) collective-permute-start(bf16[2,256,2560]{1,2,0:T(8,128)(2,1)S(1)} %collective-permute-done.2), channel_id=1, source_target_pairs={{0,1},{4,5},{8,9},{12,13},{1,0},{5,4},{9,8},{13,12},{16,17},{20,21... | collective-permute-start | bytes 7864328 | tf_op jit(solution)/shard_map/ppermute | solution.py:31
  164.2 2.7 %copy-start.1 = (bf16[1,256,2560]{1,2,0:T(8,128)(2,1)S(1)}, bf16[1,256,2560]{1,2,0:T(8,128)(2,1)}, u32[]{:S(2)}) copy-start(bf16[1,256,2560]{1,2,0:T(8,128)(2,1)} %get-tuple-element.27) | copy-start | bytes 3932164
  178.5 1.7 copy-start.3
Sparse Core Ops, SparseCore 0:
  18.7 129.2 all-reduce.2

commit v14 on v12

--- a/solution.py
+++ b/solution.py
@@ -132,8 +132,8 @@
     groups = [
         [(keys_values, valid_list[0]), (along, offset_of(3, 1, 3, 1))],
         [(early, offset_of(1, 3, 2, 2))],
-        [(late, offset_of(2, 2, 1, 3))],
     ]
+    late_valid = offset_of(2, 2, 1, 3)
     anchor_valid = (place != anchor) & (row_ids < lengths[anchor])
     heads = [slice(h * HG * DH, (h + 1) * HG * DH) for h in range(H // HG)]
     query_heads = [queries[:, cols].reshape(tok_rows, HG, DH) for cols in heads]
@@ -146,7 +146,8 @@
     anchor_kv, states = lax.optimization_barrier((anchor_kv, states))
     pieces = []
     for h, cols in enumerate(heads):
-        top, total, out = attend(query_heads[h], [(anchor_kv[:, :, cols], anchor_valid)], states[h])
+        last = [(late[:, :, cols], late_valid), (anchor_kv[:, :, cols], anchor_valid)]
+        top, total, out = attend(query_heads[h], last, states[h])
         blended = out / total
         pieces.append(jnp.transpose(blended, (1, 0, 2)).reshape(tok_rows, HG * DH))
     attended = jnp.concatenate(pieces, axis=1)

time: 188 us -> 189 us (level); the launches traced: 188 us -> 187 us
  starting transfers between devices: 27.8 us -> 16.4 us
  waiting for transfers between devices: 83.6 us -> 91.5 us
  other arithmetic: 22.6 us -> 25.7 us
    ppermute x4, starting transfers between devices: 23.5 us -> 10.9 us  [move(): return lax.ppermute(value, 'span', pairs)]
    psum x1, waiting for transfers between devices: 0.01 us -> 12.2 us  [shards(): anchor_kv = lax.psum(masked, 'span')]
    select_n x1 -> x2, other arithmetic: 2.01 us -> 6.91 us  [pick(): out = jnp.where(lane == l, options[l], out)]
    ppermute x4, waiting for transfers between devices: 82.9 us -> 78.5 us  [move(): return lax.ppermute(value, 'span', pairs)]
    select_n x1 -> x0, other arithmetic: 3.65 us -> none  [shards(): early = jnp.where(lane < 2, second, cross)]
    slice x5 -> x4, local copies, waits for them, and re-layouts: 5.77 us -> 3.9 us  [attend(): part_out = weighted(weights, kv[1].reshape(-1, HG, DH))]
    unnamed x49 -> x53, local copies, waits for them, and re-layouts: 7.46 us -> 7.35 us
    reduce_sum x4 -> x3, other arithmetic: 6.2 us -> 6.11 us  [attend(): part_total = jnp.sum(weights, axis=-1, keepdims=True)]
  transfers between devices with their start and end apart: 7 -> 7, of which waited for: 2 -> 3; matrix products, arithmetic and copies ran while one was open for 22% -> 22% of each run, Pallas kernels for 0% -> 0%
where the time goes in v14:
time: 189 us; the launch traced here: 187 us
  waiting for transfers between devices  91.5 us (48%)
  other arithmetic  25.7 us (14%)
  matrix products  20.6 us (11%)
  between operations  17.4 us (9%)
  starting transfers between devices  16.4 us (9%)
  local copies, waits for them, and re-layouts  15.2 us (8%)
    ppermute x4, waiting for transfers between devices, move(): return lax.ppermute(value, 'span', pairs)  78.5 us
    psum x1, waiting for transfers between devices, shards(): anchor_kv = lax.psum(masked, 'span')  12.2 us
    dot_general x5, matrix products, weighted(): jnp.einsum('hqk,khd->hqd', weights.astype(jnp.bfloat16), values, preferre...  11.4 us
    ppermute x4, starting transfers between devices, move(): return lax.ppermute(value, 'span', pairs)  10.9 us
    unnamed x53, local copies, waits for them, and re-layouts  7.35 us
    select_n x2, other arithmetic, pick(): out = jnp.where(lane == l, options[l], out)  6.91 us
    dot_general x5, matrix products, part_stats(): jnp.einsum('qhd,khd->hqk', q, k, preferred_element_type=jnp.float32) * scale  6.5 us
    reduce_sum x3, other arithmetic, attend(): part_total = jnp.sum(weights, axis=-1, keepdims=True)  6.11 us
  transfers between devices with their start and end apart: 7, of which 3 were waited for; matrix products, arithmetic and copies ran while one was open for 22% of the time, Pallas kernels for 0%

profile of v14, /device:TPU:0, one launch (start us, length us, event | category | flops | bytes accessed | tf_op | source)
XLA Modules:
  0.0 186.6 jit_solution(2963885489761789995)
XLA Ops:
  7.2 3.0 %copy.31 = bf16[2,256,2560]{1,2,0:T(8,128)(2,1)S(1)} copy(bf16[2,256,2560]{2,1,0:T(8,128)(2,1)} %param.11) | data formatting | bytes 5242880 | tf_op args[1]
  10.8 1.7 broadcast_select_fusion.3
  12.5 1.8 broadcast_select_fusion.2
  14.3 0.7 all-reduce.3.cloned.1.call-update
  15.1 6.4 %collective-permute-start = (bf16[2,256,2560]{1,2,0:T(8,128)(2,1)}, bf16[2,256,2560]{1,2,0:T(8,128)(2,1)}, u32[]{:S(2)}, u32[]{:S(2)}) collective-permute-start(bf16[2,256,2560]{1,2,0:T(8,128)(2,1)} %broadcast_select_fusion.2), channel_id=1, source_target_pairs={{0,2},{4,6},{8,10},{12,14},{1,3},{5,7},{9,11},{13,15},{2,1},{6,5},... | collective-permute-start | bytes 7864328 | tf_op jit(solution)/shard_map/ppermute | solution.py:31
  21.7 0.7 pad_maximum_fusion
  22.5 1.3 collective-permute-start.5
  23.7 4.2 %collective-permute-start.4 = (bf16[5,1,52,384]{3,2,0,1:T(8,128)(2,1)}, bf16[5,1,52,384]{3,2,0,1:T(8,128)(2,1)S(1)}, u32[]{:S(2)}, u32[]{:S(2)}) collective-permute-start(bf16[5,1,52,384]{3,2,0,1:T(8,128)(2,1)} %pad_maximum_fusion), channel_id=1, source_target_pairs={{0,1},{1,2},{2,3},{3,4},{4,5},{5,6},{6,7},{7,8},{8,9},{9,10},{10,1... | collective-permute-start | bytes 599048 | tf_op jit(solution)/shard_map/ppermute | solution.py:22
  28.1 1.7 fusion.99
  29.8 0.7 constant_dynamic-slice_fusion.2
  32.4 1.6 copy.33
  34.0 0.7 fusion.100
  34.7 0.7 iota_compare_fusion.2
  35.4 0.6 compare_and_fusion
  36.1 1.3 fusion.4
  37.4 2.0 %select_select_fusion.3 = pred[256]{0:T(512)(128)(4,1)S(1)} fusion(pred[]{:T(512)S(6)} %eq.55, pred[]{:T(512)S(6)} %eq.54, pred[]{:T(512)S(6)} %and.89, pred[]{:T(512)S(6)} %eq.51, s32[]{:T(128)} %bitcast.3, s32[]{:T(128)} %bitcast.5, pred[]{:T(512)S(6)} %and.93, s32[]{:T(128)} %bitcast.7, pred[]{:T(512)S(6)} %and.97), kind=kLoop, calls=%fused_computation.136 | loop fusion | flops 2304 | bytes 274 | tf_op jit(solution)/shard_map/jit(_where)/select_n | solution.py:127
  39.3 2.0 %fusion.83 = (pred[256]{0:T(512)(128)(4,1)S(1)}, pred[256]{0:T(512)(128)(4,1)S(1)}) fusion(pred[]{:T(512)S(6)} %eq.55, pred[]{:T(512)S(6)} %eq.54, pred[]{:T(512)S(6)} %eq.51, s32[]{:T(128)} %bitcast.5, pred[]{:T(512)S(6)} %and.93, s32[]{:T(128)} %bitcast.7, pred[]{:T(512)S(6)} %and.97, s32[]{:T(128)} %bitcast.3, pred[]{:T(512)S(6)} %and.89), kind=kLoop, calls=%fused_computation.135 | loop fusion | flops 2816 | bytes 530 | tf_op jit(solution)/shard_map/jit(_where)/select_n | solution.py:127
  41.3 0.2 select_maximum_fusion
  42.4 0.2 constant_dynamic-update-slice_fusion
  42.6 46.6 %collective-permute-done = bf16[2,256,2560]{1,2,0:T(8,128)(2,1)} collective-permute-done((bf16[2,256,2560]{1,2,0:T(8,128)(2,1)}, bf16[2,256,2560]{1,2,0:T(8,128)(2,1)}, u32[]{:S(2)}, u32[]{:S(2)}) %collective-permute-start) | collective-permute-done | bytes 2621472 | tf_op jit(solution)/shard_map/ppermute | solution.py:31
  89.2 2.0 %select_select_fusion.1 = bf16[2,256,2560]{1,2,0:T(8,128)(2,1)S(1)} fusion(bf16[2,256,2560]{1,2,0:T(8,128)(2,1)} %collective-permute-done, bf16[2,256,2560]{1,2,0:T(8,128)(2,1)} %collective-permute-done.1, pred[]{:T(512)S(6)} %eq.54, pred[]{:T(512)S(6)} %eq.51), kind=kLoop, calls=%fused_computation.30 | loop fusion | flops 2621440 | bytes 7864322 | tf_op jit(solution)/shard_map/jit(_where)/select_n | solution.py:47
  91.2 1.5 collective-permute-start.2
  92.9 2.7 %fusion.60 = bf16[3,1,52,384]{3,2,1,0:T(8,128)(2,1)} fusion(bf16[10368,384,1]{1,0,2:T(8,128)(2,1)S(1)} %bitcast.166, bf16[3,1,52,10368]{3,2,0,1:T(8,128)(2,1)S(1)} %slice_dynamic-update-slice_fusion, bf16[3,1,52,384]{3,2,1,0:T(8,128)(2,1)S(1)} %copy-done.5, f32[384]{0:T(512)S(1)} %copy-done.9), kind=kOutput, calls=%fused_computation.72 | convolution fusion | flops 1242408960 | bytes 11438592 | tf_op jit(solution)/shard_map/dot_general | solution.py:179
  95.6 1.9 %fusion.98 = (bf16[1,256,2560]{1,2,0:T(8,128)(2,1)S(1)}, bf16[1,256,2560]{1,2,0:T(8,128)(2,1)S(1)}) fusion(bf16[2,256,2560]{1,2,0:T(8,128)(2,1)} %collective-permute-done.1), kind=kLoop, calls=%fused_computation.161 | loop fusion | bytes 5242880 | tf_op jit(solution)/shard_map/slice | solution.py:83
  97.5 1.3 bitcast_reduce_fusion.2
  98.8 31.9 %collective-permute-done.2 = bf16[2,256,2560]{1,2,0:T(8,128)(2,1)S(1)} collective-permute-done((bf16[2,256,2560]{1,2,0:T(8,128)(2,1)S(1)}, bf16[2,256,2560]{1,2,0:T(8,128)(2,1)S(1)}, u32[]{:S(2)}, u32[]{:S(2)}) %collective-permute-start.2) | collective-permute-done | bytes 2621472 | tf_op jit(solution)/shard_map/ppermute | solution.py:31
  130.7 4.9 %select_select_fusion = (bf16[2,256,2560]{1,2,0:T(8,128)(2,1)}, bf16[2,256,2560]{1,2,0:T(8,128)(2,1)S(1)}) fusion(bf16[2,256,2560]{1,2,0:T(8,128)(2,1)} %collective-permute-done, bf16[2,256,2560]{1,2,0:T(8,128)(2,1)S(1)} %collective-permute-done.2, pred[]{:T(512)S(6)} %eq.54, pred[]{:T(512)S(6)} %eq.51, pred[]{:T(512)S(6)} %lt.138), kind=kLoop, calls=%fused_computation.29 | loop fusion | flops 3932160 | bytes 10485763 | tf_op jit(solution)/shard_map/jit(_where)/select_n | solution.py:47
  135.6 0.2 fusion.97
  135.8 1.3 bitcast_reduce_fusion.3
  137.1 2.4 %fusion.10 = (f32[20,256]{1,0:T(8,128)S(1)}, f32[20,256]{1,0:T(8,128)S(1)}) fusion(f32[20,256,256]{2,1,0:T(8,128)S(1)} %get-tuple-element.50, f32[20,256]{1,0:T(8,128)S(1)} %get-tuple-element.20, pred[256]{0:T(512)(128)(4,1)S(1)} %get-tuple-element.55, f32[20,256,256]{1,2,0:T(8,128)S(1)} %get-tuple-element.48, pred[256]{0:T(512)(128)(4,1)S(1)} %iota_compare_fusion.2), kind=kLoop, calls=%fused_computation.24 | loop fusion | flops 10475520 | bytes 10547712 | tf_op jit(solution)/shard_map/reduce_sum | solution.py:82
  139.6 1.6 fusion.25
  141.2 3.1 %collective-permute-start.3 = (bf16[2,256,2560]{1,2,0:T(8,128)(2,1)}, bf16[2,256,2560]{1,2,0:T(8,128)(2,1)}, u32[]{:S(2)}, u32[]{:S(2)}) collective-permute-start(bf16[2,256,2560]{1,2,0:T(8,128)(2,1)} %get-tuple-element.21), channel_id=1, source_target_pairs={{0,1},{4,5},{8,9},{12,13},{1,0},{5,4},{9,8},{13,12},{2,3},{6,7},{1... | collective-permute-start | bytes 7864328 | tf_op jit(solution)/shard_map/ppermute | solution.py:31
  144.2 1.2 fusion.8
  145.4 1.6 fusion.21
  147.0 3.7 %multiply_add_fusion = f32[20,256,128]{2,1,0:T(8,128)} fusion(f32[20,256,128]{2,1,0:T(8,128)S(1)} %fusion.25, f32[20,256,128]{2,1,0:T(8,128)S(1)} %fusion.21, bf16[256,20,128]{0,2,1:T(8,128)(2,1)S(1)} %bitcast.168, f32[20,256,256]{2,1,0:T(8,128)S(1)} %get-tuple-element.46, f32[20,256]{1,0:T(8,128)S(1)} %get-tuple-element.19, ...), kind=kOutput, calls=%fused_computation.45 | convolution fusion | flops 342753280 | bytes 14459136 | tf_op jit(solution)/shard_map/hqk,khd->hqd/dot_general | solution.py:63
  150.7 12.2 %all-reduce.3.cloned.1.call-done = bf16[2,256,2560]{1,2,0:T(8,128)(2,1)} async-done(((bf16[2,256,2560]{1,2,0:T(8,128)(2,1)}), bf16[2,256,2560]{1,2,0:T(8,128)(2,1)}) %all-reduce.3.cloned.1.call-update) | async-done | bytes 2621456 | tf_op jit(solution)/shard_map/psum | solution.py:113
  162.9 1.9 %fusion.96 = (bf16[1,256,2560]{1,2,0:T(8,128)(2,1)S(1)}, bf16[1,256,2560]{1,2,0:T(8,128)(2,1)S(1)}) fusion(bf16[2,256,2560]{1,2,0:T(8,128)(2,1)} %all-reduce.3.cloned.1.call-done), kind=kLoop, calls=%fused_computation.159 | loop fusion | bytes 5242880 | tf_op jit(solution)/shard_map/slice | solution.py:70
  164.8 1.3 bitcast_reduce_fusion
  166.1 0.4 copy-done.1
  166.5 2.1 %broadcast_select_fusion = bf16[2,256,2560]{1,2,0:T(8,128)(2,1)S(1)} fusion(bf16[2,256,2560]{1,2,0:T(8,128)(2,1)S(1)} %copy-done.1, bf16[2,256,2560]{1,2,0:T(8,128)(2,1)} %collective-permute-done.3, pred[]{:T(512)S(6)} %eq.54), kind=kLoop, calls=%fused_computation.62 | loop fusion | flops 1310720 | bytes 7864321 | tf_op jit(solution)/shard_map/jit(_where)/select_n | solution.py:131
  168.6 0.2 fusion.95
  168.8 1.3 bitcast_reduce_fusion.1
  170.1 1.6 fusion.17
  171.7 2.5 %fusion.13 = (f32[20,256]{1,0:T(8,128)S(1)}, f32[20,256]{1,0:T(8,128)S(1)}) fusion(f32[20,256,256]{2,1,0:T(8,128)S(1)} %get-tuple-element.54, f32[20,256]{1,0:T(8,128)S(1)} %fusion.94, pred[256]{0:T(512)(128)(4,1)S(1)} %compare_and_fusion, f32[20,256,256]{2,1,0:T(8,128)S(1)} %get-tuple-element.52, pred[256]{0:T(512)(128)(4,1)S(1)} %get-tuple-element.56), kind=kLoop, calls=%fused_computation.27 | loop fusion | flops 10475520 | bytes 10547712 | tf_op jit(solution)/shard_map/reduce_sum | solution.py:82
  174.3 3.0 %divide_bitcast_fusion = bf16[256,20,128]{2,0,1:T(8,128)(2,1)S(1)} fusion(f32[20,256,128]{2,1,0:T(8,128)S(1)} %fusion.17, f32[20,256,128]{2,1,0:T(8,128)S(1)} %copy-done.4, f32[20,256]{1,0:T(8,128)S(1)} %get-tuple-element.34, f32[20,256]{1,0:T(8,128)S(1)} %get-tuple-element.33, bf16[256,20,128]{0,2,1:T(8,128)(2,1)S(1)} %bitcast.176, ...), kind=kOutput, calls=%fused_computation.42 | convolution fusion | flops 344064000 | bytes 13168896 | tf_op jit(solution)/shard_map/hqk,khd->hqd/dot_general | solution.py:63
  177.3 0.6 copy.58
  177.9 0.3 fusion.29
  178.2 1.6 copy.61
  (66 shorter events, 1.2 us)
Async XLA Ops:
  12.5 8.9 %copy-start.6 = (bf16[2,1,52,384]{3,0,2,1:T(2,128)(2,1)S(1)}, bf16[2,1,52,384]{3,0,2,1:T(2,128)(2,1)}, u32[]{:S(2)}) copy-start(bf16[2,1,52,384]{3,0,2,1:T(2,128)(2,1)} %param.16) | copy-start | bytes 239620
  12.5 8.9 %copy-start.5 = (bf16[3,1,52,384]{3,2,1,0:T(8,128)(2,1)S(1)}, bf16[3,1,52,384]{3,2,1,0:T(8,128)(2,1)}, u32[]{:S(2)}) copy-start(bf16[3,1,52,384]{3,2,1,0:T(8,128)(2,1)} %param.15) | copy-start | bytes 359428
  12.5 9.1 %copy-start.8 = (f32[384]{0:T(512)S(1)}, f32[384]{0:T(512)}, u32[]{:S(2)}) copy-start(f32[384]{0:T(512)} %param.17) | copy-start | bytes 4612
  14.3 148.6 %all-reduce.3.cloned.1.call-start = ((), (), s32[]{:S(2)}) async-start(), calls=%async_computation | async-start | bytes 5242880 | tf_op jit(solution)/shard_map/psum | solution.py:113
  15.0 14.7 %copy-start.10 = (s32[16,3]{0,1:T(4,128)S(1)}, s32[16,3]{0,1:T(4,128)}, u32[]{:S(2)}) copy-start(s32[16,3]{0,1:T(4,128)} %param.13) | copy-start | bytes 580
  15.1 74.1 %collective-permute-start = (bf16[2,256,2560]{1,2,0:T(8,128)(2,1)}, bf16[2,256,2560]{1,2,0:T(8,128)(2,1)}, u32[]{:S(2)}, u32[]{:S(2)}) collective-permute-start(bf16[2,256,2560]{1,2,0:T(8,128)(2,1)} %broadcast_select_fusion.2), channel_id=1, source_target_pairs={{0,2},{4,6},{8,10},{12,14},{1,3},{5,7},{9,11},{13,15},{2,1},{6,5},... | collective-permute-start | bytes 7864328 | tf_op jit(solution)/shard_map/ppermute | solution.py:31
  21.4 67.7 %collective-permute-start.1 = (bf16[2,256,2560]{1,2,0:T(8,128)(2,1)}, bf16[2,256,2560]{1,2,0:T(8,128)(2,1)}, u32[]{:S(2)}, u32[]{:S(2)}) collective-permute-start(bf16[2,256,2560]{1,2,0:T(8,128)(2,1)} %broadcast_select_fusion.2), channel_id=1, source_target_pairs={{0,1},{4,5},{8,9},{12,13},{2,3},{6,7},{10,11},{14,15},{1,4},{5,8},... | collective-permute-start | bytes 7864328 | tf_op jit(solution)/shard_map/ppermute | solution.py:31
  22.5 18.8 %collective-permute-start.5 = (bf16[5,1,52,384]{3,2,0,1:T(8,128)(2,1)}, bf16[5,1,52,384]{3,2,0,1:T(8,128)(2,1)S(1)}, u32[]{:S(2)}, u32[]{:S(2)}) collective-permute-start(bf16[5,1,52,384]{3,2,0,1:T(8,128)(2,1)} %pad_maximum_fusion), channel_id=1, source_target_pairs={{1,0},{2,1},{3,2},{4,3},{5,4},{6,5},{7,6},{8,7},{9,8},{10,9},{11,1... | collective-permute-start | bytes 599048 | tf_op jit(solution)/shard_map/ppermute | solution.py:25
  23.7 17.6 %collective-permute-start.4 = (bf16[5,1,52,384]{3,2,0,1:T(8,128)(2,1)}, bf16[5,1,52,384]{3,2,0,1:T(8,128)(2,1)S(1)}, u32[]{:S(2)}, u32[]{:S(2)}) collective-permute-start(bf16[5,1,52,384]{3,2,0,1:T(8,128)(2,1)} %pad_maximum_fusion), channel_id=1, source_target_pairs={{0,1},{1,2},{2,3},{3,4},{4,5},{5,6},{6,7},{7,8},{8,9},{9,10},{10,1... | collective-permute-start | bytes 599048 | tf_op jit(solution)/shard_map/ppermute | solution.py:22
  28.1 5.9 %copy-start.7 = (s32[16]{0:T(128)S(1)}, s32[16]{0:T(128)}, u32[]{:S(2)}) copy-start(s32[16]{0:T(128)} %param.14) | copy-start | bytes 196
  29.8 6.3 %copy-start.2 = (bf16[1,256,2560]{1,2,0:T(8,128)(2,1)S(1)}, bf16[1,256,2560]{1,2,0:T(8,128)(2,1)}, u32[]{:S(2)}) copy-start(bf16[1,256,2560]{1,2,0:T(8,128)(2,1)} %get-tuple-element.32) | copy-start | bytes 3932164
  41.6 51.2 %slice-start = ((s8[7962624]{0:T(1024)(128)(4,1)}), s8[4194304]{0:T(1024)(128)(4,1)S(1)}, s32[]{:S(2)}) async-start(s8[7962624]{0:T(1024)(128)(4,1)} %bitcast.164), calls=%async_computation.1 | async-start | bytes 8388608
  42.6 50.3 %slice-start.1 = ((s8[7962624]{0:T(1024)(128)(4,1)}), s8[3768320]{0:T(1024)(128)(4,1)S(1)}, s32[]{:S(2)}) async-start(s8[7962624]{0:T(1024)(128)(4,1)} %bitcast.164), calls=%async_computation.2 | async-start | bytes 7536640
  42.6 50.3 %copy-start.9 = (f32[384]{0:T(512)S(1)}, f32[384]{0:T(512)}, u32[]{:S(2)}) copy-start(f32[384]{0:T(512)} %param.19) | copy-start | bytes 4612
  91.2 39.5 %collective-permute-start.2 = (bf16[2,256,2560]{1,2,0:T(8,128)(2,1)S(1)}, bf16[2,256,2560]{1,2,0:T(8,128)(2,1)S(1)}, u32[]{:S(2)}, u32[]{:S(2)}) collective-permute-start(bf16[2,256,2560]{1,2,0:T(8,128)(2,1)S(1)} %select_select_fusion.1), channel_id=1, source_target_pairs={{3,2},{7,6},{11,10},{15,14},{2,0},{6,4},{10,8},{14,12},{1,5},{5,9}... | collective-permute-start | bytes 7864328 | tf_op jit(solution)/shard_map/ppermute | solution.py:31
  130.7 4.9 %copy-start = (bf16[2,256,2560]{1,2,0:T(8,128)(2,1)}, bf16[2,256,2560]{1,2,0:T(8,128)(2,1)S(1)}, u32[]{:S(2)}) copy-start(bf16[2,256,2560]{1,2,0:T(8,128)(2,1)S(1)} %collective-permute-done.2) | copy-start | bytes 7864324
  137.1 2.5 %copy-start.3 = (bf16[1,256,2560]{1,2,0:T(8,128)(2,1)S(1)}, bf16[1,256,2560]{1,2,0:T(8,128)(2,1)}, u32[]{:S(2)}) copy-start(bf16[1,256,2560]{1,2,0:T(8,128)(2,1)} %get-tuple-element.31) | copy-start | bytes 3932164
  141.2 24.9 %collective-permute-start.3 = (bf16[2,256,2560]{1,2,0:T(8,128)(2,1)}, bf16[2,256,2560]{1,2,0:T(8,128)(2,1)}, u32[]{:S(2)}, u32[]{:S(2)}) collective-permute-start(bf16[2,256,2560]{1,2,0:T(8,128)(2,1)} %get-tuple-element.21), channel_id=1, source_target_pairs={{0,1},{4,5},{8,9},{12,13},{1,0},{5,4},{9,8},{13,12},{2,3},{6,7},{1... | collective-permute-start | bytes 7864328 | tf_op jit(solution)/shard_map/ppermute | solution.py:31
  164.8 1.7 copy-start.1
  171.7 2.6 %copy-start.4 = (f32[20,256,128]{2,1,0:T(8,128)S(1)}, f32[20,256,128]{2,1,0:T(8,128)}, u32[]{:S(2)}) copy-start(f32[20,256,128]{2,1,0:T(8,128)} %multiply_add_fusion) | copy-start | bytes 7864324
Sparse Core Ops, SparseCore 0:
  18.8 144.0 all-reduce.2

commit v15 on v12

--- a/solution.py
+++ b/solution.py
@@ -111,8 +111,7 @@
     is_anchor = place == anchor
     masked = jnp.where(is_anchor, keys_values, jnp.zeros_like(keys_values))
     anchor_kv = lax.psum(masked, "span")
-    sent = jnp.where(is_anchor, lax.optimization_barrier(masked), keys_values)
-    along, cross, second, third = window_blocks(sent, devices)
+    along, cross, second, third = window_blocks(keys_values, devices)
     valid_list = [row_ids < lengths[place]]
     for offset in range(1, WIN):
         source = (place - offset) % devices

time: 188 us -> 183 us (0.973)
  waiting for transfers between devices: 83.6 us -> 80.2 us
  other arithmetic: 22.6 us -> 19.5 us
  local copies, waits for them, and re-layouts: 15.2 us -> 18 us
    ppermute x4, starting transfers between devices: 23.5 us -> 20.7 us  [move(): return lax.ppermute(value, 'span', pairs)]
    ppermute x4, waiting for transfers between devices: 82.9 us -> 80.2 us  [move(): return lax.ppermute(value, 'span', pairs)]
    unnamed x49 -> x47, local copies, waits for them, and re-layouts: 7.46 us -> 8.97 us
  transfers between devices with their start and end apart: 7 -> 7, of which waited for: 2 -> 2; matrix products, arithmetic and copies ran while one was open for 22% -> 24% of each run, Pallas kernels for 0% -> 0%
where the time goes in v15:
time: 183 us; the launch traced here: 182 us
  waiting for transfers between devices  80.2 us (44%)
  starting transfers between devices  26.3 us (14%)
  matrix products  20.3 us (11%)
  other arithmetic  19.5 us (11%)
  local copies, waits for them, and re-layouts  18 us (10%)
  between operations  17.3 us (9%)
    ppermute x4, waiting for transfers between devices, move(): return lax.ppermute(value, 'span', pairs)  80.2 us
    ppermute x4, starting transfers between devices, move(): return lax.ppermute(value, 'span', pairs)  20.7 us
    dot_general x5, matrix products, weighted(): jnp.einsum('hqk,khd->hqd', weights.astype(jnp.bfloat16), values, preferre...  10.8 us
    unnamed x47, local copies, waits for them, and re-layouts  8.97 us
    slice x5, local copies, waits for them, and re-layouts, attend(): part_out = weighted(weights, kv[1].reshape(-1, HG, DH))  7.04 us
    dot_general x5, matrix products, part_stats(): jnp.einsum('qhd,khd->hqk', q, k, preferred_element_type=jnp.float32) * scale  6.81 us
    reduce_sum x4, other arithmetic, attend(): part_total = jnp.sum(weights, axis=-1, keepdims=True)  6.61 us
    ppermute x1, starting transfers between devices, extended_2(): lax.ppermute(lax.slice_in_dim(block, block.shape[dim] - width, None, axis...  4.23 us
  transfers between devices with their start and end apart: 7, of which 2 were waited for; matrix products, arithmetic and copies ran while one was open for 24% of the time, Pallas kernels for 0%

profile of v15, /device:TPU:0, one launch (start us, length us, event | category | flops | bytes accessed | tf_op | source)
XLA Modules:
  0.0 181.7 jit_solution(10990462945819034839)
XLA Ops:
  7.2 4.4 %copy.27 = bf16[2,256,2560]{1,2,0:T(8,128)(2,1)} copy(bf16[2,256,2560]{2,1,0:T(8,128)(2,1)} %param.11) | data formatting | bytes 5242880 | tf_op args[1]
  11.7 6.4 %collective-permute-start = (bf16[2,256,2560]{1,2,0:T(8,128)(2,1)}, bf16[2,256,2560]{1,2,0:T(8,128)(2,1)}, u32[]{:S(2)}, u32[]{:S(2)}) collective-permute-start(bf16[2,256,2560]{1,2,0:T(8,128)(2,1)} %copy.27), channel_id=1, source_target_pairs={{0,2},{4,6},{8,10},{12,14},{1,3},{5,7},{9,11},{13,15},{2,1},{6,5},... | collective-permute-start | bytes 7864328 | tf_op jit(solution)/shard_map/ppermute | solution.py:31
  18.1 0.1 fusion.68
  18.2 0.1 fusion.75
  18.4 0.7 pad_maximum_fusion
  19.1 1.3 collective-permute-start.5
  20.4 4.2 %collective-permute-start.4 = (bf16[5,1,52,384]{3,2,0,1:T(8,128)(2,1)}, bf16[5,1,52,384]{3,2,0,1:T(8,128)(2,1)S(1)}, u32[]{:S(2)}, u32[]{:S(2)}) collective-permute-start(bf16[5,1,52,384]{3,2,0,1:T(8,128)(2,1)} %pad_maximum_fusion), channel_id=1, source_target_pairs={{0,1},{1,2},{2,3},{3,4},{4,5},{5,6},{6,7},{7,8},{8,9},{9,10},{10,1... | collective-permute-start | bytes 599048 | tf_op jit(solution)/shard_map/ppermute | solution.py:22
  25.3 1.7 broadcast_select_fusion.2
  27.2 2.9 %fusion.99 = (bf16[1,256,2560]{1,2,0:T(8,128)(2,1)}, bf16[1,256,2560]{1,2,0:T(8,128)(2,1)S(1)}) fusion(bf16[2,256,2560]{1,2,0:T(8,128)(2,1)} %copy.27), kind=kLoop, calls=%fused_computation.163 | loop fusion | bytes 5242880 | tf_op jit(solution)/shard_map/slice | solution.py:83
  30.1 0.6 constant_dynamic-slice_fusion.2
  32.7 1.6 copy.30
  34.4 0.7 fusion.101
  35.1 0.6 iota_compare_fusion.2
  35.7 0.6 compare_and_fusion
  36.3 1.5 fusion.3
  37.8 1.8 select_select_fusion.4
  39.6 1.8 fusion.85
  41.5 0.2 select_maximum_fusion
  42.5 0.2 constant_dynamic-update-slice_fusion
  42.7 43.0 %collective-permute-done = bf16[2,256,2560]{1,2,0:T(8,128)(2,1)} collective-permute-done((bf16[2,256,2560]{1,2,0:T(8,128)(2,1)}, bf16[2,256,2560]{1,2,0:T(8,128)(2,1)}, u32[]{:S(2)}, u32[]{:S(2)}) %collective-permute-start) | collective-permute-done | bytes 2621472 | tf_op jit(solution)/shard_map/ppermute | solution.py:31
  85.8 2.0 %select_select_fusion.1 = bf16[2,256,2560]{1,2,0:T(8,128)(2,1)S(1)} fusion(bf16[2,256,2560]{1,2,0:T(8,128)(2,1)} %collective-permute-done, bf16[2,256,2560]{1,2,0:T(8,128)(2,1)} %collective-permute-done.1, pred[]{:T(512)S(6)} %eq.51, pred[]{:T(512)S(6)} %eq.54), kind=kLoop, calls=%fused_computation.29 | loop fusion | flops 2621440 | bytes 7864322 | tf_op jit(solution)/shard_map/jit(_where)/select_n | solution.py:47
  87.8 1.3 collective-permute-start.2
  89.3 2.7 %fusion.60 = bf16[3,1,52,384]{3,2,1,0:T(8,128)(2,1)} fusion(bf16[10368,384,1]{1,0,2:T(8,128)(2,1)S(1)} %bitcast.176, bf16[3,1,52,10368]{3,2,0,1:T(8,128)(2,1)S(1)} %slice_dynamic-update-slice_fusion, bf16[3,1,52,384]{3,2,1,0:T(8,128)(2,1)S(1)} %copy-done.1, f32[384]{0:T(512)S(1)} %copy-done.6), kind=kOutput, calls=%fused_computation.70 | convolution fusion | flops 1242408960 | bytes 11438592 | tf_op jit(solution)/shard_map/dot_general | solution.py:177
  92.0 1.9 %fusion.98 = (bf16[1,256,2560]{1,2,0:T(8,128)(2,1)S(1)}, bf16[1,256,2560]{1,2,0:T(8,128)(2,1)S(1)}) fusion(bf16[2,256,2560]{1,2,0:T(8,128)(2,1)} %collective-permute-done.1), kind=kLoop, calls=%fused_computation.162 | loop fusion | bytes 5242880 | tf_op jit(solution)/shard_map/slice | solution.py:83
  93.8 1.4 fusion.4
  95.3 37.2 %collective-permute-done.2 = bf16[2,256,2560]{1,2,0:T(8,128)(2,1)S(1)} collective-permute-done((bf16[2,256,2560]{1,2,0:T(8,128)(2,1)S(1)}, bf16[2,256,2560]{1,2,0:T(8,128)(2,1)S(1)}, u32[]{:S(2)}, u32[]{:S(2)}) %collective-permute-start.2) | collective-permute-done | bytes 2621472 | tf_op jit(solution)/shard_map/ppermute | solution.py:31
  132.4 2.1 %broadcast_select_fusion = (bf16[2,256,2560]{1,2,0:T(8,128)(2,1)S(1)}, bf16[2,256,2560]{1,2,0:T(8,128)(2,1)S(1)}) fusion(bf16[2,256,2560]{1,2,0:T(8,128)(2,1)S(1)} %collective-permute-done.2, bf16[2,256,2560]{1,2,0:T(8,128)(2,1)} %collective-permute-done, pred[]{:T(512)S(6)} %lt.138, pred[]{:T(512)S(6)} %eq.54, pred[]{:T(512)S(6)} %eq.51), kind=kLoop, calls=%fused_computation.61 | loop fusion | flops 3932160 | bytes 10485763 | tf_op jit(solution)/shard_map/jit(_where)/select_n | solution.py:129
  134.5 13.1 %collective-permute-start.3 = (bf16[2,256,2560]{1,2,0:T(8,128)(2,1)S(1)}, bf16[2,256,2560]{1,2,0:T(8,128)(2,1)S(1)}, u32[]{:S(2)}, u32[]{:S(2)}) collective-permute-start(bf16[2,256,2560]{1,2,0:T(8,128)(2,1)S(1)} %get-tuple-element.22), channel_id=1, source_target_pairs={{0,1},{4,5},{8,9},{12,13},{1,0},{5,4},{9,8},{13,12},{2,3},{6,7},{1... | collective-permute-start | bytes 7864328 | tf_op jit(solution)/shard_map/ppermute | solution.py:31
  147.6 0.2 fusion.100
  147.8 1.3 bitcast_reduce_fusion.1
  149.1 1.2 fusion.12
  150.3 1.5 fusion.19
  151.8 1.2 fusion.25
  153.0 1.2 fusion.23
  154.2 3.1 %fusion.8 = (f32[20,256]{1,0:T(8,128)S(1)}, f32[20,256]{1,0:T(8,128)S(1)}) fusion(f32[20,256,256]{2,1,0:T(8,128)S(1)} %get-tuple-element.50, f32[20,256]{1,0:T(8,128)S(1)} %get-tuple-element.18, pred[256]{0:T(512)(128)(4,1)S(1)} %get-tuple-element.55, f32[20,256,256]{2,1,0:T(8,128)S(1)} %get-tuple-element.48, pred[256]{0:T(512)(128)(4,1)S(1)} %iota_compare_fusion.2), kind=kLoop, calls=%fused_computation.21 | loop fusion | flops 10475520 | bytes 10547712 | tf_op jit(solution)/shard_map/reduce_sum | solution.py:82
  157.3 0.3 broadcast_select_fusion.1
  157.6 0.2 fusion.97
  157.8 1.3 bitcast_reduce_fusion.2
  159.2 1.2 fusion.10
  160.4 4.0 %multiply_add_fusion = f32[20,256,128]{2,1,0:T(8,128)} fusion(f32[20,256,128]{2,1,0:T(8,128)S(1)} %fusion.19, f32[20,256,128]{2,1,0:T(8,128)S(1)} %fusion.25, f32[20,256,128]{2,1,0:T(8,128)S(1)} %fusion.23, bf16[256,20,128]{0,2,1:T(8,128)(2,1)S(1)} %bitcast.177, f32[20,256,256]{2,1,0:T(8,128)S(1)} %get-tuple-element.52, ...), kind=kOutput, calls=%fused_computation.41 | convolution fusion | flops 344064000 | bytes 17101056 | tf_op jit(solution)/shard_map/hqk,khd->hqd/dot_general | solution.py:63
  164.4 1.9 %fusion.96 = (bf16[1,256,2560]{1,2,0:T(8,128)(2,1)S(1)}, bf16[1,256,2560]{1,2,0:T(8,128)(2,1)S(1)}) fusion(bf16[2,256,2560]{1,2,0:T(8,128)(2,1)} %all-reduce.3.cloned.1.call-done), kind=kLoop, calls=%fused_computation.160 | loop fusion | bytes 5242880 | tf_op jit(solution)/shard_map/slice | solution.py:83
  166.3 1.3 bitcast_reduce_fusion
  167.6 1.2 fusion.13
  168.8 0.5 copy-done
  169.3 2.9 %divide_bitcast_fusion = bf16[256,20,128]{2,0,1:T(8,128)(2,1)S(1)} fusion(f32[20,256,128]{2,1,0:T(8,128)S(1)} %copy-done, f32[20,256]{1,0:T(8,128)S(1)} %get-tuple-element.36, f32[20,256]{1,0:T(8,128)S(1)} %get-tuple-element.35, bf16[256,20,128]{0,2,1:T(8,128)(2,1)S(1)} %bitcast.186, f32[20,256,256]{2,1,0:T(8,128)S(1)} %get-tuple-element.54, ...), kind=kOutput, calls=%fused_computation.39 | convolution fusion | flops 343408640 | bytes 10547456 | tf_op jit(solution)/shard_map/hqk,khd->hqd/dot_general | solution.py:63
  172.3 0.6 copy.53
  172.9 0.3 fusion.27
  173.2 1.6 copy.56
  (61 shorter events, 1.0 us)
Async XLA Ops:
  7.2 10.9 %copy-start.3 = (bf16[2,1,52,384]{3,0,2,1:T(2,128)(2,1)S(1)}, bf16[2,1,52,384]{3,0,2,1:T(2,128)(2,1)}, u32[]{:S(2)}) copy-start(bf16[2,1,52,384]{3,0,2,1:T(2,128)(2,1)} %param.16) | copy-start | bytes 239620
  7.2 10.9 %copy-start.1 = (bf16[3,1,52,384]{3,2,1,0:T(8,128)(2,1)S(1)}, bf16[3,1,52,384]{3,2,1,0:T(8,128)(2,1)}, u32[]{:S(2)}) copy-start(bf16[3,1,52,384]{3,2,1,0:T(8,128)(2,1)} %param.15) | copy-start | bytes 359428
  7.2 11.0 %copy-start.5 = (f32[384]{0:T(512)S(1)}, f32[384]{0:T(512)}, u32[]{:S(2)}) copy-start(f32[384]{0:T(512)} %param.17) | copy-start | bytes 4612
  7.2 157.2 %all-reduce.3.cloned.1.call-start = ((), (), s32[]{:S(2)}) async-start(), calls=%async_computation | async-start | bytes 5242880 | tf_op jit(solution)/shard_map/psum | solution.py:113
  11.7 74.1 %collective-permute-start = (bf16[2,256,2560]{1,2,0:T(8,128)(2,1)}, bf16[2,256,2560]{1,2,0:T(8,128)(2,1)}, u32[]{:S(2)}, u32[]{:S(2)}) collective-permute-start(bf16[2,256,2560]{1,2,0:T(8,128)(2,1)} %copy.27), channel_id=1, source_target_pairs={{0,2},{4,6},{8,10},{12,14},{1,3},{5,7},{9,11},{13,15},{2,1},{6,5},... | collective-permute-start | bytes 7864328 | tf_op jit(solution)/shard_map/ppermute | solution.py:31
  18.1 67.7 %collective-permute-start.1 = (bf16[2,256,2560]{1,2,0:T(8,128)(2,1)}, bf16[2,256,2560]{1,2,0:T(8,128)(2,1)}, u32[]{:S(2)}, u32[]{:S(2)}) collective-permute-start(bf16[2,256,2560]{1,2,0:T(8,128)(2,1)} %copy.27), channel_id=1, source_target_pairs={{0,1},{4,5},{8,9},{12,13},{2,3},{6,7},{10,11},{14,15},{1,4},{5,8},... | collective-permute-start | bytes 7864328 | tf_op jit(solution)/shard_map/ppermute | solution.py:31
  19.1 22.3 %collective-permute-start.5 = (bf16[5,1,52,384]{3,2,0,1:T(8,128)(2,1)}, bf16[5,1,52,384]{3,2,0,1:T(8,128)(2,1)S(1)}, u32[]{:S(2)}, u32[]{:S(2)}) collective-permute-start(bf16[5,1,52,384]{3,2,0,1:T(8,128)(2,1)} %pad_maximum_fusion), channel_id=1, source_target_pairs={{1,0},{2,1},{3,2},{4,3},{5,4},{6,5},{7,6},{8,7},{9,8},{10,9},{11,1... | collective-permute-start | bytes 599048 | tf_op jit(solution)/shard_map/ppermute | solution.py:25
  20.4 21.1 %collective-permute-start.4 = (bf16[5,1,52,384]{3,2,0,1:T(8,128)(2,1)}, bf16[5,1,52,384]{3,2,0,1:T(8,128)(2,1)S(1)}, u32[]{:S(2)}, u32[]{:S(2)}) collective-permute-start(bf16[5,1,52,384]{3,2,0,1:T(8,128)(2,1)} %pad_maximum_fusion), channel_id=1, source_target_pairs={{0,1},{1,2},{2,3},{3,4},{4,5},{5,6},{6,7},{7,8},{8,9},{9,10},{10,1... | collective-permute-start | bytes 599048 | tf_op jit(solution)/shard_map/ppermute | solution.py:22
  27.0 3.1 %copy-start.7 = (s32[16,3]{0,1:T(4,128)S(1)}, s32[16,3]{0,1:T(4,128)}, u32[]{:S(2)}) copy-start(s32[16,3]{0,1:T(4,128)} %param.13) | copy-start | bytes 580
  27.2 7.2 %copy-start.4 = (s32[16]{0:T(128)S(1)}, s32[16]{0:T(128)}, u32[]{:S(2)}) copy-start(s32[16]{0:T(128)} %param.14) | copy-start | bytes 196
  41.7 47.5 %slice-start = ((s8[7962624]{0:T(1024)(128)(4,1)}), s8[4194304]{0:T(1024)(128)(4,1)S(1)}, s32[]{:S(2)}) async-start(s8[7962624]{0:T(1024)(128)(4,1)} %bitcast.174), calls=%async_computation.1 | async-start | bytes 8388608
  42.7 46.6 %slice-start.1 = ((s8[7962624]{0:T(1024)(128)(4,1)}), s8[3768320]{0:T(1024)(128)(4,1)S(1)}, s32[]{:S(2)}) async-start(s8[7962624]{0:T(1024)(128)(4,1)} %bitcast.174), calls=%async_computation.2 | async-start | bytes 7536640
  42.7 46.6 %copy-start.6 = (f32[384]{0:T(512)S(1)}, f32[384]{0:T(512)}, u32[]{:S(2)}) copy-start(f32[384]{0:T(512)} %param.19) | copy-start | bytes 4612
  87.8 44.7 %collective-permute-start.2 = (bf16[2,256,2560]{1,2,0:T(8,128)(2,1)S(1)}, bf16[2,256,2560]{1,2,0:T(8,128)(2,1)S(1)}, u32[]{:S(2)}, u32[]{:S(2)}) collective-permute-start(bf16[2,256,2560]{1,2,0:T(8,128)(2,1)S(1)} %select_select_fusion.1), channel_id=1, source_target_pairs={{3,2},{7,6},{11,10},{15,14},{2,0},{6,4},{10,8},{14,12},{1,5},{5,9}... | collective-permute-start | bytes 7864328 | tf_op jit(solution)/shard_map/ppermute | solution.py:31
  134.5 22.7 %collective-permute-start.3 = (bf16[2,256,2560]{1,2,0:T(8,128)(2,1)S(1)}, bf16[2,256,2560]{1,2,0:T(8,128)(2,1)S(1)}, u32[]{:S(2)}, u32[]{:S(2)}) collective-permute-start(bf16[2,256,2560]{1,2,0:T(8,128)(2,1)S(1)} %get-tuple-element.22), channel_id=1, source_target_pairs={{0,1},{4,5},{8,9},{12,13},{1,0},{5,4},{9,8},{13,12},{2,3},{6,7},{1... | collective-permute-start | bytes 7864328 | tf_op jit(solution)/shard_map/ppermute | solution.py:31
  150.3 1.5 copy-start.2
  167.6 1.7 copy-start
Sparse Core Ops, SparseCore 0:
  27.2 117.2 all-reduce.2
